TPU v7x, 128 devices: a whole 4x4x4 slice. The times are simulated.
128 devices in a mesh: seq: 16 (over x_lo, z, core), batch: 8 (over y, x_hi).
Axes of the slice: x: 4 (x_hi: 2, x_lo: 2; x = x_hi * 2 + x_lo), y: 4, z: 4, core: 2. Of those that a mesh axis runs over, the one named last changes fastest.
Arguments:
- activations: bfloat16 [2, 8192, 1536], P(None, ('seq', 'batch')), may hold values from -6 to 6
- conv_gain: float32 [1536], replicated, may hold values from 0.25 to 1.75
- conv_weight: bfloat16 [5, 1536, 1536], P(None, 'batch'), may hold values from -0.0625 to 0.0625
- attention_gain: float32 [1536], replicated, may hold values from 0.25 to 1.75
- query_weight: bfloat16 [1536, 1536], P('batch'), may hold values from -3 to 3
- key_weight: bfloat16 [1536, 1536], P('batch'), may hold values from -3 to 3
- value_weight: bfloat16 [1536, 1536], P('batch'), may hold values from -0.15625 to 0.15625
- output_weight: bfloat16 [1536, 1536], P('batch'), may hold values from -0.15625 to 0.15625
Outputs:
- block_out: bfloat16 [2, 8192, 1536], P(None, ('seq', 'batch'))
All inputs are finite; a program needn't handle non-finite values.
Results may differ from a plain program's by a relative error of at most 0.015.
Values may be sent and summed in bfloat16 or wider, within the bound.
No kernel may reach another device: no remote copies, remote signals or barrier semaphores. Data moves between devices by JAX's collectives and lax.ppermute only.
A program may use at most 128 MiB of HBM per device.

v0:
```python
import math

import jax
import jax.numpy as jnp
from jax import lax
from jax.sharding import PartitionSpec as P

HD = 192


def with_halo(cells, sides, width):
    for axis, dim in sides:
        count = lax.axis_size(axis)
        ends = count - 1
        head = lax.slice_in_dim(cells, 0, width, axis=dim)
        tail = lax.slice_in_dim(cells, cells.shape[dim] - width, cells.shape[dim], axis=dim)
        cells = jnp.concatenate(
            [
                lax.ppermute(tail, axis, [(i, (i + 1) % count) for i in range(ends)]),
                cells,
                lax.ppermute(head, axis, [((i + 1) % count, i) for i in range(ends)]),
            ],
            axis=dim,
        )
    return cells


def normalize(rows_in, gain):
    values = rows_in.astype(jnp.float32)
    scale = lax.rsqrt(jnp.mean(values * values, axis=-1, keepdims=True) + 1e-06)
    return values * scale * gain


def shards(
    activations,
    conv_gain,
    conv_weight,
    attention_gain,
    query_weight,
    key_weight,
    value_weight,
    output_weight,
):
    sample_count, own_rows, full_width = activations.shape
    tap_count, local_out, _ = conv_weight.shape
    flank_rows = tap_count // 2
    gathered_in = lax.all_gather(activations, "batch", axis=1, tiled=True)
    seq_rows = gathered_in.shape[1]
    active = jax.nn.gelu(normalize(gathered_in, conv_gain)).astype(jnp.bfloat16)
    framed = with_halo(active, (("seq", 1),), flank_rows)
    conv_sum = jnp.zeros((sample_count, local_out, seq_rows), jnp.float32)
    for offset in range(tap_count):
        conv_sum = conv_sum + jnp.einsum(
            "std,ed->set",
            framed[:, offset : offset + seq_rows],
            conv_weight[offset],
            preferred_element_type=jnp.float32,
        )
    column_start = lax.axis_index("batch") * local_out
    own_columns = lax.dynamic_slice_in_dim(gathered_in, column_start, local_out, 2)
    residual = jnp.transpose(own_columns, (0, 2, 1)).astype(jnp.float32)
    hidden_part = (residual + conv_sum).astype(jnp.bfloat16)
    hidden_full = lax.all_gather(hidden_part, "batch", axis=1, tiled=True)
    hidden_float = hidden_full.astype(jnp.float32)
    norm_scale = lax.rsqrt(jnp.mean(hidden_float * hidden_float, axis=1, keepdims=True) + 1e-06)
    normed = (hidden_float * norm_scale * attention_gain[None, :, None]).astype(jnp.bfloat16)
    queries = (
        jnp.einsum("sdt,ed->set", normed, query_weight, preferred_element_type=jnp.float32)
        * HD ** (-0.5)
    ).astype(jnp.bfloat16)
    key_rows = jnp.einsum(
        "sdt,ed->set", normed, key_weight, preferred_element_type=jnp.float32
    ).astype(jnp.bfloat16)
    value_rows = jnp.einsum(
        "sdt,ed->set", normed, value_weight, preferred_element_type=jnp.float32
    ).astype(jnp.bfloat16)
    heads_here = query_weight.shape[0] // HD
    query_heads = queries.reshape(sample_count, heads_here, HD, seq_rows)
    start_max = jnp.full((sample_count, heads_here, seq_rows), -jnp.inf, jnp.float32)
    start_sum = jnp.zeros((sample_count, heads_here, seq_rows), jnp.float32)
    start_acc = jnp.zeros((sample_count, heads_here, HD, seq_rows), jnp.float32)
    key_tile = lax.all_gather(key_rows, "seq", axis=2, tiled=True)
    value_tile = lax.all_gather(value_rows, "seq", axis=2, tiled=True)
    key_count = key_tile.shape[2]
    block_rows = math.gcd(key_count, 512)

    def consume(block_index, running):
        running_max, weight_sum, summed = running
        begin = block_index * block_rows
        key_block = lax.dynamic_slice_in_dim(key_tile, begin, block_rows, 2).reshape(
            sample_count, heads_here, HD, block_rows
        )
        value_block = lax.dynamic_slice_in_dim(value_tile, begin, block_rows, 2).reshape(
            sample_count, heads_here, HD, block_rows
        )
        scores = jnp.einsum(
            "shdq,shdk->shqk", query_heads, key_block, preferred_element_type=jnp.float32
        )
        new_max = jnp.maximum(running_max, jnp.max(scores, axis=-1))
        weights = jnp.exp(scores - new_max[..., None])
        rescale = jnp.exp(running_max - new_max)
        weight_sum = weight_sum * rescale + jnp.sum(weights, axis=-1)
        summed = summed * rescale[:, :, None, :] + jnp.einsum(
            "shqk,shdk->shdq",
            weights.astype(jnp.bfloat16),
            value_block,
            preferred_element_type=jnp.float32,
        )
        return (new_max, weight_sum, summed)

    final_max, weight_sum, summed = lax.fori_loop(
        0, key_count // block_rows, consume, (start_max, start_sum, start_acc)
    )
    attended = (
        (summed / weight_sum[:, :, None, :])
        .astype(jnp.bfloat16)
        .reshape(sample_count, heads_here * HD, seq_rows)
    )
    row_start = lax.axis_index("batch") * own_rows
    own_hidden = jnp.transpose(
        lax.dynamic_slice_in_dim(hidden_full, row_start, own_rows, 2), (0, 2, 1)
    ).astype(jnp.float32)
    share_rows = lax.psum_scatter(
        jnp.einsum(
            "set,ef->tsf", attended, output_weight, preferred_element_type=jnp.float32
        ).astype(jnp.bfloat16),
        "batch",
        scatter_dimension=0,
        tiled=True,
    ).astype(jnp.float32)
    branch_rows = jnp.transpose(share_rows, (1, 0, 2))
    result = own_hidden + branch_rows
    return result.astype(jnp.bfloat16)


def solution(mesh):
    placed = (
        P(None, ("seq", "batch"), None),
        P(),
        P(None, "batch", None),
        P(),
        P("batch", None),
        P("batch", None),
        P("batch", None),
        P("batch", None),
    )
    return jax.shard_map(
        shards,
        mesh=mesh,
        in_specs=placed,
        out_specs=P(None, ("seq", "batch"), None),
        check_vma=False,
    )
```

profile of v0, /device:TPU:0, one launch (start us, length us, event | category | flops | bytes accessed | tf_op | source)
XLA Modules:
  0.0 400.5 jit_solution(12064633944674675458)
XLA Ops:
  6.5 2.2 copy.40
  8.8 65.9 %all-gather.5.cloned.1.call-done = bf16[2,512,1536]{2,0,1:T(2,128)(2,1)} async-done(((bf16[2,64,1536]{2,0,1:T(2,128)(2,1)}), bf16[2,512,1536]{2,0,1:T(2,128)(2,1)}) %all-gather.5.cloned.1.call-update) | async-done | bytes 3145744 | tf_op jit(solution)/shard_map/all_gather | solution.py:47
  74.7 2.6 fusion.13
  77.3 2.0 constant_dynamic-slice_fusion.1
  79.7 4.3 %fusion.17 = bf16[2,512,1536]{2,1,0:T(8,128)(2,1)S(1)} fusion(f32[1536]{0:T(1024)S(1)} %copy-done.3, f32[2,512]{1,0:T(2,128)S(1)} %add_rsqrt_fusion.1, bf16[2,512,1536]{2,0,1:T(2,128)(2,1)} %all-gather.5.cloned.1.call-done), kind=kLoop, calls=%fused_computation.30 | loop fusion | flops 18874368 | bytes 6301696 | tf_op jit(solution)/shard_map/convert_element_type | solution.py:49
  87.9 2.3 collective-permute-done.1
  96.3 64.2 %all-gather.7.cloned.1.call-done = bf16[2,1536,512]{2,0,1:T(2,128)(2,1)} async-done(((bf16[2,192,512]{2,0,1:T(2,128)(2,1)}), bf16[2,1536,512]{2,0,1:T(2,128)(2,1)}) %all-gather.7.cloned.1.call-update) | async-done | bytes 3145744 | tf_op jit(solution)/shard_map/all_gather | solution.py:63
  160.5 2.7 fusion.22
  167.4 3.5 fusion.57
  171.2 2.7 fusion.58
  173.9 34.0 %all-gather.9.cloned.1.call-done = bf16[2,192,8192]{2,1,0:T(8,128)(2,1)} async-done(((bf16[2,192,512]{2,1,0:T(8,128)(2,1)}), bf16[2,192,8192]{2,1,0:T(8,128)(2,1)}) %all-gather.9.cloned.1.call-update) | async-done | bytes 6291472 | tf_op jit(solution)/shard_map/all_gather | solution.py:82
  207.8 44.8 %all-gather.11.cloned.1.call-done = bf16[2,192,8192]{2,1,0:T(8,128)(2,1)} async-done(((bf16[2,192,512]{2,1,0:T(8,128)(2,1)}), bf16[2,192,8192]{2,1,0:T(8,128)(2,1)}) %all-gather.11.cloned.1.call-update) | async-done | bytes 6291472 | tf_op jit(solution)/shard_map/all_gather | solution.py:83
  252.7 56.6 %while.18 = (s32[]{:T(128)}, f32[2,1,512]{2,0,1:T(2,128)S(1)}, f32[2,1,512]{2,0,1:T(2,128)S(1)}, f32[2,1,192,512]{3,2,0,1:T(8,128)S(1)}, bf16[2,192,8192]{2,1,0:...) while((s32[]{:T(128)}, f32[2,1,512]{2,0,1:T(2,128)S(1)}, ...), condition=%wide.region_5.0_spmd.clone, body=%wide.region_2.0_spmd.clone.sunk | while | flops 405870592 | bytes 9109687 | solution.py:111
  254.5 1.6 fusion.97
  258.0 1.6 fusion.97
  261.6 1.6 fusion.97
  265.1 1.6 fusion.97
  268.6 1.6 fusion.97
  272.2 1.6 fusion.97
  275.7 1.6 fusion.97
  309.2 2.7 fusion.26
  311.9 2.0 constant_dynamic-slice_fusion
  314.5 77.6 %reduce-scatter.2.cloned.1.call-done = bf16[64,2,1536]{2,0,1:T(8,128)(2,1)} async-done(((bf16[512,2,1536]{2,0,1:T(8,128)(2,1)}), bf16[64,2,1536]{2,0,1:T(8,128)(2,1)}) %reduce-scatter.2.cloned.1.call-update) | async-done | bytes 393232 | tf_op jit(solution)/shard_map/reduce_scatter | solution.py:123
  392.2 1.8 fusion.62
  (136 shorter events, 59.5 us)
Async XLA Ops:
  6.5 302.7 %copy-start = (bf16[192,1536]{1,0:T(8,128)(2,1)S(1)}, bf16[192,1536]{1,0:T(8,128)(2,1)}, u32[]{:S(2)}) copy-start(bf16[192,1536]{1,0:T(8,128)(2,1)} %param.17) | copy-start | bytes 1769476
  6.5 73.2 %copy-start.3 = (f32[1536]{0:T(1024)S(1)}, f32[1536]{0:T(1024)}, u32[]{:S(2)}) copy-start(f32[1536]{0:T(1024)} %param.11) | copy-start | bytes 18436
  6.5 68.2 %all-gather.5.cloned.1.call-start = ((), (), s32[]{:S(2)}) async-start(), calls=%async_computation.1 | async-start | bytes 3538944 | tf_op jit(solution)/shard_map/all_gather | solution.py:47
  8.8 151.7 %all-gather.7.cloned.1.call-start = ((), (), s32[]{:S(2)}) async-start(), calls=%async_computation.2 | async-start | bytes 3538944 | tf_op jit(solution)/shard_map/all_gather | solution.py:63
  79.7 7.0 %copy-start.5 = (bf16[5,192,1536]{2,1,0:T(8,128)(2,1)S(1)}, bf16[5,192,1536]{2,1,0:T(8,128)(2,1)}, u32[]{:S(2)}) copy-start(bf16[5,192,1536]{2,1,0:T(8,128)(2,1)} %param.12) | copy-start | bytes 8847364
  84.1 8.5 %collective-permute-start = (bf16[2,2,1536]{2,1,0:T(2,128)(2,1)S(1)}, bf16[2,2,1536]{2,1,0:T(2,128)(2,1)S(1)}, u32[]{:S(2)}, u32[]{:S(2)}) collective-permute-start(bf16[2,2,1536]{2,1,0:T(2,128)(2,1)S(1)} %get-tuple-element.174), channel_id=1, source_target_pairs={{0,8},{8,16},{16,24},{24,32},{32,40},{40,48},{48,56},{56,64},{64,7... | collective-permute-start | bytes 36872 | tf_op jit(solution)/shard_map/ppermute | solution.py:19
  85.4 4.8 %collective-permute-start.1 = (bf16[2,2,1536]{2,1,0:T(2,128)(2,1)S(1)}, bf16[2,2,1536]{2,1,0:T(2,128)(2,1)S(1)}, u32[]{:S(2)}, u32[]{:S(2)}) collective-permute-start(bf16[2,2,1536]{2,1,0:T(2,128)(2,1)S(1)} %get-tuple-element.175), channel_id=1, source_target_pairs={{8,0},{16,8},{24,16},{32,24},{40,32},{48,40},{56,48},{64,56},{72,6... | collective-permute-start | bytes 36872 | tf_op jit(solution)/shard_map/ppermute | solution.py:21
  95.1 68.2 %copy-start.4 = (f32[1536]{0:T(1024)S(1)}, f32[1536]{0:T(1024)}, u32[]{:S(2)}) copy-start(f32[1536]{0:T(1024)} %param.13) | copy-start | bytes 18436
  96.3 111.6 %all-gather.9.cloned.1.call-start = ((), (), s32[]{:S(2)}) async-start(), calls=%async_computation.3 | async-start | bytes 6684672 | tf_op jit(solution)/shard_map/all_gather | solution.py:82
  160.5 2.8 copy-start.1
  163.4 2.4 copy-start.6
  164.1 1.7 copy-start.2
  165.8 1.6 copy-start.7
  167.3 3.8 copy-start.8
  167.4 85.3 %all-gather.11.cloned.1.call-start = ((), (), s32[]{:S(2)}) async-start(), calls=%async_computation.4 | async-start | bytes 6684672 | tf_op jit(solution)/shard_map/all_gather | solution.py:83
  170.9 221.3 %reduce-scatter.2.cloned.1.call-start = ((), (), s32[]{:S(2)}) async-start(), calls=%async_computation.5 | async-start | bytes 3538944 | tf_op jit(solution)/shard_map/reduce_scatter | solution.py:123
Sparse Core Ops, SparseCore 0:
  9.7 65.0 all-gather.4
  96.4 64.0 all-gather.6
  167.5 40.3 all-gather.8
  209.4 43.2 all-gather.10
  312.1 80.0 reduce-scatter.1
where the time goes:
time: 402 us; the launch traced here: 401 us
  waiting for transfers between devices  289 us (72%)
  matrix products  66.6 us (17%)
  other arithmetic  17.6 us (4%)
  between operations  13.4 us (3%)
  local copies, waits for them, and re-layouts  10.2 us (3%)
    reduce_scatter x1, waiting for transfers between devices, shards(): lax.psum_scatter(jnp.einsum('set,ef->tsf', attended, output_weight, prefe...  77.6 us
    all_gather x1, waiting for transfers between devices, shards(): gathered_in = lax.all_gather(activations, 'batch', axis=1, tiled=True)  65.9 us
    all_gather x1, waiting for transfers between devices, shards(): hidden_full = lax.all_gather(hidden_part, 'batch', axis=1, tiled=True)  64.2 us
    all_gather x1, waiting for transfers between devices, shards(): value_tile = lax.all_gather(value_rows, 'seq', axis=2, tiled=True)  44.8 us
    all_gather x1, waiting for transfers between devices, shards(): key_tile = lax.all_gather(key_rows, 'seq', axis=2, tiled=True)  34 us
    dot_general x16, matrix products, consume(): jnp.einsum('shqk,shdk->shdq', weights.astype(jnp.bfloat16), value_block,...  26.3 us
    dot_general x16, matrix products, consume(): jnp.einsum('shdq,shdk->shqk', query_heads, key_block, preferred_element_t...  24 us
  transfers between devices with their start and end apart: 7, of which 6 were waited for; matrix products, arithmetic and copies ran while one was open for 3% of the time, Pallas kernels for 0%

commit v1 on v0

--- a/solution.py
+++ b/solution.py
@@ -25,6 +25,13 @@
     return cells
 
 
+def gather_batch(block, axis):
+    count = lax.axis_size("batch")
+    copies = jnp.broadcast_to(block[None], (count,) + block.shape)
+    arrived = jnp.moveaxis(lax.all_to_all(copies, "batch", 0, 0, tiled=False), 0, axis)
+    return arrived.reshape(block.shape[:axis] + (count * block.shape[axis],) + block.shape[axis + 1 :])
+
+
 def normalize(rows_in, gain):
     values = rows_in.astype(jnp.float32)
     scale = lax.rsqrt(jnp.mean(values * values, axis=-1, keepdims=True) + 1e-06)
@@ -44,7 +51,7 @@
     sample_count, own_rows, full_width = activations.shape
     tap_count, local_out, _ = conv_weight.shape
     flank_rows = tap_count // 2
-    gathered_in = lax.all_gather(activations, "batch", axis=1, tiled=True)
+    gathered_in = gather_batch(activations, 1)
     seq_rows = gathered_in.shape[1]
     active = jax.nn.gelu(normalize(gathered_in, conv_gain)).astype(jnp.bfloat16)
     framed = with_halo(active, (("seq", 1),), flank_rows)
@@ -60,7 +67,7 @@
     own_columns = lax.dynamic_slice_in_dim(gathered_in, column_start, local_out, 2)
     residual = jnp.transpose(own_columns, (0, 2, 1)).astype(jnp.float32)
     hidden_part = (residual + conv_sum).astype(jnp.bfloat16)
-    hidden_full = lax.all_gather(hidden_part, "batch", axis=1, tiled=True)
+    hidden_full = gather_batch(hidden_part, 1)
     hidden_float = hidden_full.astype(jnp.float32)
     norm_scale = lax.rsqrt(jnp.mean(hidden_float * hidden_float, axis=1, keepdims=True) + 1e-06)
     normed = (hidden_float * norm_scale * attention_gain[None, :, None]).astype(jnp.bfloat16)
@@ -120,14 +127,14 @@
     own_hidden = jnp.transpose(
         lax.dynamic_slice_in_dim(hidden_full, row_start, own_rows, 2), (0, 2, 1)
     ).astype(jnp.float32)
-    share_rows = lax.psum_scatter(
-        jnp.einsum(
-            "set,ef->tsf", attended, output_weight, preferred_element_type=jnp.float32
-        ).astype(jnp.bfloat16),
-        "batch",
-        scatter_dimension=0,
-        tiled=True,
-    ).astype(jnp.float32)
+    batch_count = lax.axis_size("batch")
+    partial_rows = jnp.einsum(
+        "set,ef->tsf", attended, output_weight, preferred_element_type=jnp.float32
+    ).astype(jnp.bfloat16)
+    partial_rows = partial_rows.reshape(batch_count, own_rows, sample_count, full_width)
+    share_rows = jnp.sum(
+        lax.all_to_all(partial_rows, "batch", 0, 0, tiled=False).astype(jnp.float32), axis=0
+    )
     branch_rows = jnp.transpose(share_rows, (1, 0, 2))
     result = own_hidden + branch_rows
     return result.astype(jnp.bfloat16)

time: 402 us -> 337 us (0.84)
  waiting for transfers between devices: 289 us -> 158 us
  blocking collectives: 0 us -> 43.2 us
  starting transfers between devices: 2.98 us -> 18.3 us
    all_gather x2 -> x0, waiting for transfers between devices: 130 us -> none  [the longest x1 65.9 us: shards(): gathered_in = lax.all_gather(activations, 'batch', axis=1, tiled=True)]
    all_to_all x0 -> x2, waiting for transfers between devices: none -> 78.3 us  [the longest x1 39.8 us: gather_batch(): lax.all_to_all(copies, 'batch', 0, 0, tiled=False)]
    reduce_scatter x1 -> x0, waiting for transfers between devices: 77.6 us -> none  [shards(): lax.psum_scatter(jnp.einsum('set,ef->tsf', attended, output_weight, prefe...]
    all_to_all x0 -> x1, blocking collectives: none -> 43.2 us  [gather_batch(): lax.all_to_all(copies, 'batch', 0, 0, tiled=False)]
    all_to_all x0 -> x2, starting transfers between devices: none -> 13.6 us  [the longest x1 7.01 us: gather_batch(): lax.all_to_all(copies, 'batch', 0, 0, tiled=False)]
  transfers between devices with their start and end apart: 7 -> 6, of which waited for: 6 -> 4; matrix products, arithmetic and copies ran while one was open for 3% -> 6% of each run, Pallas kernels for 0% -> 0%
where the time goes in v1:
time: 337 us; the launch traced here: 335 us
  waiting for transfers between devices  158 us (47%)
  matrix products  68.1 us (20%)
  blocking collectives  43.2 us (13%)
  other arithmetic  19.8 us (6%)
  starting transfers between devices  18.3 us (5%)
  between operations  13.7 us (4%)
  local copies, waits for them, and re-layouts  12.9 us (4%)
    all_gather x1, waiting for transfers between devices, shards(): value_tile = lax.all_gather(value_rows, 'seq', axis=2, tiled=True)  45 us
    all_to_all x1, blocking collectives, gather_batch(): lax.all_to_all(copies, 'batch', 0, 0, tiled=False)  43.2 us
    all_to_all x1, waiting for transfers between devices, gather_batch(): lax.all_to_all(copies, 'batch', 0, 0, tiled=False)  39.8 us
    all_to_all x1, waiting for transfers between devices, shards(): lax.all_to_all(partial_rows, 'batch', 0, 0, tiled=False).astype(jnp.float32)  38.6 us
    all_gather x1, waiting for transfers between devices, shards(): key_tile = lax.all_gather(key_rows, 'seq', axis=2, tiled=True)  34.8 us
    dot_general x16, matrix products, consume(): jnp.einsum('shqk,shdk->shdq', weights.astype(jnp.bfloat16), value_block,...  26.3 us
    dot_general x16, matrix products, consume(): jnp.einsum('shdq,shdk->shqk', query_heads, key_block, preferred_element_t...  24 us
    dot_general x5, matrix products, shards(): jnp.einsum('std,ed->set', framed[:, offset:offset + seq_rows], conv_weigh...  9.08 us
  transfers between devices with their start and end apart: 6, of which 4 were waited for; matrix products, arithmetic and copies ran while one was open for 6% of the time, Pallas kernels for 0%

profile of v1, /device:TPU:0, one launch (start us, length us, event | category | flops | bytes accessed | tf_op | source)
XLA Modules:
  0.0 335.0 jit_solution(1888584935394674766)
XLA Ops:
  6.5 3.0 broadcast_in_dim.14
  9.6 7.0 %all-to-all-start = ((bf16[8,2,64,1536]{3,2,1,0:T(8,128)(2,1)}), bf16[8,2,64,1536]{3,2,1,0:T(8,128)(2,1)}, u32[]{:S(2)}, u32[]{:S(2)}) async-start(bf16[8,2,64,1536]{3,2,1,0:T(8,128)(2,1)} %broadcast_in_dim.14), calls=%async_computation | async-start | bytes 6291456 | tf_op jit(solution)/shard_map/all_to_all | solution.py:31
  16.6 39.8 %all-to-all-done = bf16[8,2,64,1536]{3,2,1,0:T(8,128)(2,1)} async-done(((bf16[8,2,64,1536]{3,2,1,0:T(8,128)(2,1)}), bf16[8,2,64,1536]{3,2,1,0:T(8,128)(2,1)}, u32[]{:S(2)}, u32[]{:S(2)}) %all-to-all-start) | async-done | bytes 3145760 | tf_op jit(solution)/shard_map/all_to_all | solution.py:31
  56.4 2.6 fusion.13
  59.1 2.2 copy.63
  61.3 3.0 fusion.29
  65.6 4.2 %fusion.17 = bf16[2,8,64,1536]{3,2,1,0:T(8,128)(2,1)S(1)} fusion(f32[1536]{0:T(1024)S(1)} %copy-done.5, f32[2,8,64]{2,1,0:T(8,128)S(1)} %add_rsqrt_fusion, bf16[8,2,64,1536]{3,2,1,0:T(8,128)(2,1)} %all-to-all-done), kind=kLoop, calls=%fused_computation.29 | loop fusion | flops 18874368 | bytes 6301696 | tf_op jit(solution)/shard_map/convert_element_type | solution.py:56
  69.8 2.2 fusion.73
  72.5 3.3 collective-permute-start
  75.9 3.2 fusion.32
  83.1 43.2 %all_to_all.15 = bf16[8,2,192,512]{3,2,1,0:T(8,128)(2,1)S(1)} all-to-all(bf16[8,2,192,512]{3,2,1,0:T(8,128)(2,1)S(1)} %broadcast_in_dim.15), channel_id=1, replica_groups=mesh['seq'=16,'batch'=8] {'batch'}, dimensions={0} | all-to-all | bytes 6291456 | tf_op jit(solution)/shard_map/all_to_all | solution.py:31
  132.5 3.5 %fusion.61 = bf16[2,192,512]{2,1,0:T(8,128)(2,1)} fusion(bf16[2,1536,512]{2,1,0:T(8,128)(2,1)} %copy-done.4, bf16[192,1536]{1,0:T(8,128)(2,1)S(1)} %copy-done.9), kind=kOutput, calls=%fused_computation.72 | convolution fusion | flops 604176384 | bytes 4128768 | tf_op jit(solution)/shard_map/sdt,ed->set/dot_general | solution.py:81
  136.1 2.7 fusion.62
  138.7 34.8 %all-gather.3.cloned.1.call-done = bf16[2,192,8192]{2,1,0:T(8,128)(2,1)} async-done(((bf16[2,192,512]{2,1,0:T(8,128)(2,1)}), bf16[2,192,8192]{2,1,0:T(8,128)(2,1)}) %all-gather.3.cloned.1.call-update) | async-done | bytes 6291472 | tf_op jit(solution)/shard_map/all_gather | solution.py:89
  173.6 45.0 %all-gather.5.cloned.1.call-done = bf16[2,192,8192]{2,1,0:T(8,128)(2,1)} async-done(((bf16[2,192,512]{2,1,0:T(8,128)(2,1)}), bf16[2,192,8192]{2,1,0:T(8,128)(2,1)}) %all-gather.5.cloned.1.call-update) | async-done | bytes 6291472 | tf_op jit(solution)/shard_map/all_gather | solution.py:90
  218.5 56.6 %while.18 = (s32[]{:T(128)}, f32[2,1,512]{2,0,1:T(2,128)S(1)}, f32[2,1,512]{2,0,1:T(2,128)S(1)}, f32[2,1,192,512]{3,2,0,1:T(8,128)S(1)}, bf16[2,192,8192]{2,1,0:...) while((s32[]{:T(128)}, f32[2,1,512]{2,0,1:T(2,128)S(1)}, ...), condition=%wide.region_5.0_spmd.clone, body=%wide.region_2.0_spmd.clone.sunk | while | flops 405870592 | bytes 9109687 | solution.py:118
  220.4 1.6 fusion.101
  223.9 1.6 fusion.101
  227.4 1.6 fusion.101
  231.0 1.6 fusion.101
  276.1 2.0 copy.67
  278.1 6.6 %all-to-all-start.2 = ((bf16[8,64,2,1536]{3,1,2,0:T(8,128)(2,1)}), bf16[8,64,2,1536]{3,1,2,0:T(8,128)(2,1)}, u32[]{:S(2)}, u32[]{:S(2)}) async-start(bf16[8,64,2,1536]{3,1,2,0:T(8,128)(2,1)} %copy.67), calls=%async_computation.2 | async-start | bytes 6291456 | tf_op jit(solution)/shard_map/all_to_all | solution.py:136
  286.4 38.6 %all-to-all-done.2 = bf16[8,64,2,1536]{3,1,2,0:T(8,128)(2,1)} async-done(((bf16[8,64,2,1536]{3,1,2,0:T(8,128)(2,1)}), bf16[8,64,2,1536]{3,1,2,0:T(8,128)(2,1)}, u32[]{:S(2)}, u32[]{:S(2)}) %all-to-all-start.2) | async-done | bytes 3145760 | tf_op jit(solution)/shard_map/all_to_all | solution.py:136
  324.9 2.4 convert_reduce_fusion
  (142 shorter events, 64.8 us)
Async XLA Ops:
  6.5 268.6 %copy-start = (bf16[192,1536]{1,0:T(8,128)(2,1)S(1)}, bf16[192,1536]{1,0:T(8,128)(2,1)}, u32[]{:S(2)}) copy-start(bf16[192,1536]{1,0:T(8,128)(2,1)} %param.17) | copy-start | bytes 1769476
  9.6 46.8 %all-to-all-start = ((bf16[8,2,64,1536]{3,2,1,0:T(8,128)(2,1)}), bf16[8,2,64,1536]{3,2,1,0:T(8,128)(2,1)}, u32[]{:S(2)}, u32[]{:S(2)}) async-start(bf16[8,2,64,1536]{3,2,1,0:T(8,128)(2,1)} %broadcast_in_dim.14), calls=%async_computation | async-start | bytes 6291456 | tf_op jit(solution)/shard_map/all_to_all | solution.py:31
  16.6 157.0 %all-gather.3.cloned.1.call-start = ((), (), s32[]{:S(2)}) async-start(), calls=%async_computation.3 | async-start | bytes 6684672 | tf_op jit(solution)/shard_map/all_gather | solution.py:89
  59.1 2.2 copy-start.5
  64.3 5.6 %copy-start.2 = (bf16[2,512,1536]{2,1,0:T(8,128)(2,1)}, bf16[2,512,1536]{2,1,0:T(8,128)(2,1)S(1)}, u32[]{:S(2)}) copy-start(bf16[2,512,1536]{2,1,0:T(8,128)(2,1)S(1)} %fusion.29) | copy-start | bytes 9437188
  64.3 11.5 %collective-permute-start.1 = (bf16[2,2,1536]{2,1,0:T(2,128)(2,1)S(1)}, bf16[2,2,1536]{2,1,0:T(2,128)(2,1)S(1)}, u32[]{:S(2)}, u32[]{:S(2)}) collective-permute-start(bf16[2,2,1536]{2,1,0:T(2,128)(2,1)S(1)} %get-tuple-element.175), channel_id=1, source_target_pairs={{8,0},{16,8},{24,16},{32,24},{40,32},{48,40},{56,48},{64,56},{72,6... | collective-permute-start | bytes 36872 | tf_op jit(solution)/shard_map/ppermute | solution.py:21
  72.5 6.5 %copy-start.3 = (bf16[2,512,1536]{2,1,0:T(8,128)(2,1)S(1)}, bf16[2,512,1536]{2,1,0:T(8,128)(2,1)}, u32[]{:S(2)}) copy-start(bf16[2,512,1536]{2,1,0:T(8,128)(2,1)} %copy-done.2) | copy-start | bytes 9437188
  72.5 6.5 %copy-start.7 = (bf16[5,192,1536]{2,1,0:T(8,128)(2,1)S(1)}, bf16[5,192,1536]{2,1,0:T(8,128)(2,1)}, u32[]{:S(2)}) copy-start(bf16[5,192,1536]{2,1,0:T(8,128)(2,1)} %param.12) | copy-start | bytes 8847364
  72.5 7.7 %collective-permute-start = (bf16[2,2,1536]{2,1,0:T(2,128)(2,1)S(1)}, bf16[2,2,1536]{2,1,0:T(2,128)(2,1)S(1)}, u32[]{:S(2)}, u32[]{:S(2)}) collective-permute-start(bf16[2,2,1536]{2,1,0:T(2,128)(2,1)S(1)} %get-tuple-element.174), channel_id=1, source_target_pairs={{0,8},{8,16},{16,24},{24,32},{32,40},{40,48},{48,56},{56,64},{64,7... | collective-permute-start | bytes 36872 | tf_op jit(solution)/shard_map/ppermute | solution.py:19
  126.9 0.7 copy-start.6
  127.6 1.6 copy-start.1
  127.6 3.3 copy-start.8
  129.3 1.6 copy-start.4
  130.9 1.6 copy-start.9
  132.5 3.6 %copy-start.10 = (bf16[192,1536]{1,0:T(8,128)(2,1)S(1)}, bf16[192,1536]{1,0:T(8,128)(2,1)}, u32[]{:S(2)}) copy-start(bf16[192,1536]{1,0:T(8,128)(2,1)} %param.14) | copy-start | bytes 1769476
  132.5 86.0 %all-gather.5.cloned.1.call-start = ((), (), s32[]{:S(2)}) async-start(), calls=%async_computation.4 | async-start | bytes 6684672 | tf_op jit(solution)/shard_map/all_gather | solution.py:90
  278.1 46.8 %all-to-all-start.2 = ((bf16[8,64,2,1536]{3,1,2,0:T(8,128)(2,1)}), bf16[8,64,2,1536]{3,1,2,0:T(8,128)(2,1)}, u32[]{:S(2)}, u32[]{:S(2)}) async-start(bf16[8,64,2,1536]{3,1,2,0:T(8,128)(2,1)} %copy.67), calls=%async_computation.2 | async-start | bytes 6291456 | tf_op jit(solution)/shard_map/all_to_all | solution.py:136
Sparse Core Ops, SparseCore 0:
  132.6 40.9 all-gather.2
  175.2 43.2 all-gather.4

commit v2 on v1

--- a/solution.py
+++ b/solution.py
@@ -38,7 +38,7 @@
     return values * scale * gain
 
 
-def shards(
+def one_sample(
     activations,
     conv_gain,
     conv_weight,
@@ -140,6 +140,14 @@
     return result.astype(jnp.bfloat16)
 
 
+def shards(activations, *weights):
+    pieces = [
+        one_sample(activations[sample : sample + 1], *weights)
+        for sample in range(activations.shape[0])
+    ]
+    return jnp.concatenate(pieces, axis=0)
+
+
 def solution(mesh):
     placed = (
         P(None, ("seq", "batch"), None),

time: 337 us -> 393 us (1.17)
  matrix products: 68.1 us -> 108 us
  starting transfers between devices: 18.3 us -> 36.5 us
  blocking collectives: 43.2 us -> 29.6 us
  other arithmetic: 19.8 us -> 25.9 us
  waiting for transfers between devices: 158 us -> 164 us
    all_to_all x1 -> x2, waiting for transfers between devices: 38.6 us -> 20.4 us  [one_sample(): lax.all_to_all(partial_rows, 'batch', 0, 0, tiled=False).astype(jnp.float32)]
    dot_general x16 -> x32, matrix products: 24 us -> 40.8 us  [consume(): jnp.einsum('shdq,shdk->shqk', query_heads, key_block, preferred_element_t...]
    dot_general x16 -> x32, matrix products: 26.3 us -> 42.8 us  [consume(): jnp.einsum('shqk,shdk->shdq', weights.astype(jnp.bfloat16), value_block,...]
    all_to_all x1, blocking collectives: 43.2 us -> 29.6 us  [gather_batch(): lax.all_to_all(copies, 'batch', 0, 0, tiled=False)]
    all_gather x2 -> x4, waiting for transfers between devices: 79.8 us -> 92.4 us  [the longest x2 63.6 us: one_sample(): value_tile = lax.all_gather(value_rows, 'seq', axis=2, tiled=True)]
    all_to_all x1 -> x3, waiting for transfers between devices: 39.8 us -> 51.4 us  [gather_batch(): lax.all_to_all(copies, 'batch', 0, 0, tiled=False)]
    all_to_all x1 -> x3, starting transfers between devices: 7.01 us -> 13.5 us  [gather_batch(): lax.all_to_all(copies, 'batch', 0, 0, tiled=False)]
    dot_general x9 -> x18, matrix products: 17.8 us -> 24.2 us  [the longest x10 9.88 us: one_sample(): jnp.einsum('std,ed->set', framed[:, offset:offset + seq_rows], conv_weigh...]
  transfers between devices with their start and end apart: 6 -> 13, of which waited for: 4 -> 7; matrix products, arithmetic and copies ran while one was open for 6% -> 32% of each run, Pallas kernels for 0% -> 0%
where the time goes in v2:
time: 393 us; the launch traced here: 390 us
  waiting for transfers between devices  164 us (42%)
  matrix products  108 us (27%)
  starting transfers between devices  36.5 us (9%)
  blocking collectives  29.6 us (8%)
  other arithmetic  25.9 us (7%)
  between operations  13.6 us (3%)
  local copies, waits for them, and re-layouts  11.1 us (3%)
    all_gather x2, waiting for transfers between devices, one_sample(): value_tile = lax.all_gather(value_rows, 'seq', axis=2, tiled=True)  63.6 us
    all_to_all x3, waiting for transfers between devices, gather_batch(): lax.all_to_all(copies, 'batch', 0, 0, tiled=False)  51.4 us
    dot_general x32, matrix products, consume(): jnp.einsum('shqk,shdk->shdq', weights.astype(jnp.bfloat16), value_block,...  42.8 us
    dot_general x32, matrix products, consume(): jnp.einsum('shdq,shdk->shqk', query_heads, key_block, preferred_element_t...  40.8 us
    all_to_all x1, blocking collectives, gather_batch(): lax.all_to_all(copies, 'batch', 0, 0, tiled=False)  29.6 us
    all_gather x2, waiting for transfers between devices, one_sample(): key_tile = lax.all_gather(key_rows, 'seq', axis=2, tiled=True)  28.8 us
    all_to_all x2, waiting for transfers between devices, one_sample(): lax.all_to_all(partial_rows, 'batch', 0, 0, tiled=False).astype(jnp.float32)  20.4 us
    all_to_all x3, starting transfers between devices, gather_batch(): lax.all_to_all(copies, 'batch', 0, 0, tiled=False)  13.5 us
  transfers between devices with their start and end apart: 13, of which 7 were waited for; matrix products, arithmetic and copies ran while one was open for 32% of the time, Pallas kernels for 0%

profile of v2, /device:TPU:0, one launch (start us, length us, event | category | flops | bytes accessed | tf_op | source)
XLA Modules:
  0.0 390.3 jit_solution(14848912916177011553)
XLA Ops:
  7.8 29.6 %all_to_all.30 = bf16[8,1,64,1536]{3,2,1,0:T(8,128)(2,1)S(1)} all-to-all(bf16[8,1,64,1536]{3,2,1,0:T(8,128)(2,1)S(1)} %broadcast_in_dim.27), channel_id=1, replica_groups=mesh['seq'=16,'batch'=8] {'batch'}, dimensions={0} | all-to-all | bytes 3145728 | tf_op jit(solution)/shard_map/all_to_all | solution.py:31
  38.7 4.4 %all-to-all-start.3 = ((bf16[8,1,64,1536]{3,2,1,0:T(8,128)(2,1)}), bf16[8,1,64,1536]{3,2,1,0:T(8,128)(2,1)}, u32[]{:S(2)}, u32[]{:S(2)}) async-start(bf16[8,1,64,1536]{3,2,1,0:T(8,128)(2,1)} %broadcast_in_dim.33), calls=%async_computation.3 | async-start | bytes 3145728 | tf_op jit(solution)/shard_map/all_to_all | solution.py:31
  43.6 21.5 %all-to-all-done.3 = bf16[8,1,64,1536]{3,2,1,0:T(8,128)(2,1)} async-done(((bf16[8,1,64,1536]{3,2,1,0:T(8,128)(2,1)}), bf16[8,1,64,1536]{3,2,1,0:T(8,128)(2,1)}, u32[]{:S(2)}, u32[]{:S(2)}) %all-to-all-start.3) | async-done | bytes 1572896 | tf_op jit(solution)/shard_map/all_to_all | solution.py:31
  68.3 4.0 %fusion.57 = (bf16[1,512,1536]{2,1,0:T(8,128)(2,1)S(1)}, bf16[1,512,1536]{2,1,0:T(8,128)(2,1)S(1)}) fusion(bf16[1,512,1536]{2,1,0:T(8,128)(2,1)S(1)} %bitcast.299, f32[1536]{0:T(1024)S(1)} %copy-done.7, f32[512]{0:T(512)S(1)} %rsqrt.41, f32[512]{0:T(512)S(1)} %rsqrt.44, bf16[1,512,1536]{2,1,0:T(8,128)(2,1)} %bitcast.37), kind=kLoop, calls=%fused_computation.75 | loop fusion | flops 18874368 | bytes 6301696 | tf_op jit(solution)/shard_map/convert_element_type | solution.py:56
  76.5 4.8 %fusion.36 = (bf16[8,1,64,1536]{3,2,0,1:T(8,128)(2,1)}, bf16[8,1,64,1536]{3,2,0,1:T(8,128)(2,1)S(1)}) fusion(bf16[8,1,64,1536]{3,2,1,0:T(8,128)(2,1)S(1)} %all_to_all.30, f32[1536]{0:T(1024)S(1)} %copy-done.7, f32[8,64]{1,0:T(8,128)S(1)} %add_rsqrt_fusion.1, f32[8,64]{1,0:T(8,128)S(1)} %add_rsqrt_fusion, bf16[8,1,64,1536]{3,2,1,0:T(8,128)(2,1)} %all-to-all-done.3), kind=kLoop, calls=%fused_computation.54 | loop fusion | flops 18874368 | bytes 6301696 | tf_op jit(solution)/shard_map/convert_element_type | solution.py:56
  85.9 4.3 %all-to-all-start.4 = ((bf16[8,1,192,512]{3,2,1,0:T(8,128)(2,1)}), bf16[8,1,192,512]{3,2,1,0:T(8,128)(2,1)}, u32[]{:S(2)}, u32[]{:S(2)}) async-start(bf16[8,1,192,512]{3,2,1,0:T(8,128)(2,1)} %broadcast_in_dim.61), calls=%async_computation.4 | async-start | bytes 3145728 | tf_op jit(solution)/shard_map/all_to_all | solution.py:31
  90.3 2.2 fusion.166
  92.8 6.1 %collective-permute-start = (bf16[1,2,1536]{2,1,0:T(2,128)(2,1)S(1)}, bf16[1,2,1536]{2,1,0:T(2,128)(2,1)S(1)}, u32[]{:S(2)}, u32[]{:S(2)}) collective-permute-start(bf16[1,2,1536]{2,1,0:T(2,128)(2,1)S(1)} %get-tuple-element.343), channel_id=1, source_target_pairs={{0,8},{8,16},{16,24},{24,32},{32,40},{40,48},{48,56},{56,64},{64,7... | collective-permute-start | bytes 18440 | tf_op jit(solution)/shard_map/ppermute | solution.py:19
  98.9 2.2 fusion.97
  103.2 8.3 %all-to-all-done.4 = bf16[8,1,192,512]{3,2,1,0:T(8,128)(2,1)} async-done(((bf16[8,1,192,512]{3,2,1,0:T(8,128)(2,1)}), bf16[8,1,192,512]{3,2,1,0:T(8,128)(2,1)}, u32[]{:S(2)}, u32[]{:S(2)}) %all-to-all-start.4) | async-done | bytes 1572896 | tf_op jit(solution)/shard_map/all_to_all | solution.py:31
  112.8 4.8 %all-to-all-start.1 = ((bf16[8,1,192,512]{3,2,1,0:T(8,128)(2,1)}), bf16[8,1,192,512]{3,2,1,0:T(8,128)(2,1)S(1)}, u32[]{:S(2)}, u32[]{:S(2)}) async-start(bf16[8,1,192,512]{3,2,1,0:T(8,128)(2,1)} %broadcast_in_dim.29), calls=%async_computation.1 | async-start | bytes 3145728 | tf_op jit(solution)/shard_map/all_to_all | solution.py:31
  119.7 21.7 %all-to-all-done.1 = bf16[8,1,192,512]{3,2,1,0:T(8,128)(2,1)S(1)} async-done(((bf16[8,1,192,512]{3,2,1,0:T(8,128)(2,1)}), bf16[8,1,192,512]{3,2,1,0:T(8,128)(2,1)S(1)}, u32[]{:S(2)}, u32[]{:S(2)}) %all-to-all-start.1) | async-done | bytes 1572896 | tf_op jit(solution)/shard_map/all_to_all | solution.py:31
  147.4 2.5 fusion.159
  152.8 2.1 fusion.148
  154.9 2.2 fusion.157
  157.2 28.8 %all-gather.13.cloned.1.call-done = bf16[192,8192]{1,0:T(8,128)(2,1)} async-done(((bf16[192,512]{1,0:T(8,128)(2,1)}), bf16[192,8192]{1,0:T(8,128)(2,1)}) %all-gather.13.cloned.1.call-update) | async-done | bytes 3145744 | tf_op jit(solution)/shard_map/all_gather | solution.py:89
  186.0 37.6 %all-gather.15.cloned.1.call-done = bf16[192,8192]{1,0:T(8,128)(2,1)} async-done(((bf16[192,512]{1,0:T(8,128)(2,1)}), bf16[192,8192]{1,0:T(8,128)(2,1)}) %all-gather.15.cloned.1.call-update) | async-done | bytes 3145744 | tf_op jit(solution)/shard_map/all_gather | solution.py:90
  223.6 46.2 %while.37 = (s32[]{:T(128)}, f32[1,1,512]{2,1,0:T(1,128)S(1)}, f32[1,1,512]{2,1,0:T(1,128)S(1)}, f32[1,1,192,512]{3,2,1,0:T(8,128)S(1)}, bf16[1,192,8192]{2,1,0:...) while((s32[]{:T(128)}, f32[1,1,512]{2,1,0:T(1,128)S(1)}, ...), condition=%wide.region_12.0_spmd.clone, body=%wide.region_9.0_spmd.clone.sunk | while | flops 202934784 | bytes 4554935 | solution.py:118
  271.6 6.4 %all-to-all-start.5 = ((bf16[8,64,1,1536]{3,1,2,0:T(8,128)(2,1)}), bf16[8,64,1,1536]{3,1,2,0:T(8,128)(2,1)S(1)}, u32[]{:S(2)}, u32[]{:S(2)}) async-start(bf16[8,64,1,1536]{3,1,2,0:T(8,128)(2,1)} %bitcast.302), calls=%async_computation.5 | async-start | bytes 3145728 | tf_op jit(solution)/shard_map/all_to_all | solution.py:136
  278.0 25.9 %all-gather.11.cloned.1.call-done = bf16[192,8192]{1,0:T(8,128)(2,1)} async-done(((bf16[192,512]{1,0:T(8,128)(2,1)}), bf16[192,8192]{1,0:T(8,128)(2,1)}) %all-gather.11.cloned.1.call-update) | async-done | bytes 3145744 | tf_op jit(solution)/shard_map/all_gather | solution.py:90
  303.9 46.1 %while.36 = (s32[]{:T(128)}, f32[1,1,512]{2,1,0:T(1,128)S(1)}, f32[1,1,512]{2,1,0:T(1,128)S(1)}, f32[1,1,192,512]{3,2,1,0:T(8,128)S(1)}, bf16[1,192,8192]{2,1,0:...) while((s32[]{:T(128)}, f32[1,1,512]{2,1,0:T(1,128)S(1)}, ...), condition=%wide.region_5.0_spmd.clone, body=%wide.region_2.0_spmd.clone.sunk | while | flops 202934784 | bytes 4554935 | solution.py:118
  350.0 1.9 convolution_convert_fusion.1
  351.9 6.0 %all-to-all-start.2 = ((bf16[8,64,1,1536]{3,1,2,0:T(8,128)(2,1)}), bf16[8,64,1,1536]{3,1,2,0:T(8,128)(2,1)}, u32[]{:S(2)}, u32[]{:S(2)}) async-start(bf16[8,64,1,1536]{3,1,2,0:T(8,128)(2,1)} %bitcast.303), calls=%async_computation.2 | async-start | bytes 3145728 | tf_op jit(solution)/shard_map/all_to_all | solution.py:136
  360.8 20.4 %all-to-all-done.2 = bf16[8,64,1,1536]{3,1,2,0:T(8,128)(2,1)} async-done(((bf16[8,64,1,1536]{3,1,2,0:T(8,128)(2,1)}), bf16[8,64,1,1536]{3,1,2,0:T(8,128)(2,1)}, u32[]{:S(2)}, u32[]{:S(2)}) %all-to-all-start.2) | async-done | bytes 1572896 | tf_op jit(solution)/shard_map/all_to_all | solution.py:136
  (282 shorter events, 127.4 us)
Async XLA Ops:
  6.5 263.3 %copy-start = (bf16[192,1536]{1,0:T(8,128)(2,1)S(1)}, bf16[192,1536]{1,0:T(8,128)(2,1)}, u32[]{:S(2)}) copy-start(bf16[192,1536]{1,0:T(8,128)(2,1)} %param.19) | copy-start | bytes 1769476
  38.7 29.5 %copy-start.7 = (f32[1536]{0:T(1024)S(1)}, f32[1536]{0:T(1024)}, u32[]{:S(2)}) copy-start(f32[1536]{0:T(1024)} %param.13) | copy-start | bytes 18436
  38.7 26.4 %all-to-all-start.3 = ((bf16[8,1,64,1536]{3,2,1,0:T(8,128)(2,1)}), bf16[8,1,64,1536]{3,2,1,0:T(8,128)(2,1)}, u32[]{:S(2)}, u32[]{:S(2)}) async-start(bf16[8,1,64,1536]{3,2,1,0:T(8,128)(2,1)} %broadcast_in_dim.33), calls=%async_computation.3 | async-start | bytes 3145728 | tf_op jit(solution)/shard_map/all_to_all | solution.py:31
  72.2 9.0 %copy-start.5 = (bf16[1,512,1536]{2,1,0:T(8,128)(2,1)}, bf16[1,512,1536]{2,1,0:T(8,128)(2,1)S(1)}, u32[]{:S(2)}) copy-start(bf16[1,512,1536]{2,1,0:T(8,128)(2,1)S(1)} %get-tuple-element.353) | copy-start | bytes 4718596
  72.3 11.0 %collective-permute-start.2 = (bf16[1,2,1536]{2,1,0:T(2,128)(2,1)S(1)}, bf16[1,2,1536]{2,1,0:T(2,128)(2,1)S(1)}, u32[]{:S(2)}, u32[]{:S(2)}) collective-permute-start(bf16[1,2,1536]{2,1,0:T(2,128)(2,1)S(1)} %get-tuple-element.345), channel_id=1, source_target_pairs={{0,8},{8,16},{16,24},{24,32},{32,40},{40,48},{48,56},{56,64},{64,7... | collective-permute-start | bytes 18440 | tf_op jit(solution)/shard_map/ppermute | solution.py:19
  73.6 8.3 %collective-permute-start.3 = (bf16[1,2,1536]{2,1,0:T(2,128)(2,1)S(1)}, bf16[1,2,1536]{2,1,0:T(2,128)(2,1)S(1)}, u32[]{:S(2)}, u32[]{:S(2)}) collective-permute-start(bf16[1,2,1536]{2,1,0:T(2,128)(2,1)S(1)} %get-tuple-element.346), channel_id=1, source_target_pairs={{8,0},{16,8},{24,16},{32,24},{40,32},{48,40},{56,48},{64,56},{72,6... | collective-permute-start | bytes 18440 | tf_op jit(solution)/shard_map/ppermute | solution.py:21
  74.9 6.4 %copy-start.9 = (bf16[5,192,1536]{2,1,0:T(8,128)(2,1)S(1)}, bf16[5,192,1536]{2,1,0:T(8,128)(2,1)}, u32[]{:S(2)}) copy-start(bf16[5,192,1536]{2,1,0:T(8,128)(2,1)} %param.14) | copy-start | bytes 8847364
  74.9 24.0 %collective-permute-start.1 = (bf16[1,2,1536]{2,1,0:T(2,128)(2,1)S(1)}, bf16[1,2,1536]{2,1,0:T(2,128)(2,1)S(1)}, u32[]{:S(2)}, u32[]{:S(2)}) collective-permute-start(bf16[1,2,1536]{2,1,0:T(2,128)(2,1)S(1)} %get-tuple-element.344), channel_id=1, source_target_pairs={{8,0},{16,8},{24,16},{32,24},{40,32},{48,40},{56,48},{64,56},{72,6... | collective-permute-start | bytes 18440 | tf_op jit(solution)/shard_map/ppermute | solution.py:21
  85.9 25.6 %all-to-all-start.4 = ((bf16[8,1,192,512]{3,2,1,0:T(8,128)(2,1)}), bf16[8,1,192,512]{3,2,1,0:T(8,128)(2,1)}, u32[]{:S(2)}, u32[]{:S(2)}) async-start(bf16[8,1,192,512]{3,2,1,0:T(8,128)(2,1)} %broadcast_in_dim.61), calls=%async_computation.4 | async-start | bytes 3145728 | tf_op jit(solution)/shard_map/all_to_all | solution.py:31
  92.6 8.5 %copy-start.6 = (bf16[1,512,1536]{2,1,0:T(8,128)(2,1)S(1)}, bf16[1,512,1536]{2,1,0:T(8,128)(2,1)}, u32[]{:S(2)}) copy-start(bf16[1,512,1536]{2,1,0:T(8,128)(2,1)} %copy-done.5) | copy-start | bytes 4718596
  92.8 8.4 %copy-start.10 = (bf16[5,192,1536]{2,1,0:T(8,128)(2,1)S(1)}, bf16[5,192,1536]{2,1,0:T(8,128)(2,1)}, u32[]{:S(2)}) copy-start(bf16[5,192,1536]{2,1,0:T(8,128)(2,1)} %param.14) | copy-start | bytes 8847364
  92.8 8.3 %collective-permute-start = (bf16[1,2,1536]{2,1,0:T(2,128)(2,1)S(1)}, bf16[1,2,1536]{2,1,0:T(2,128)(2,1)S(1)}, u32[]{:S(2)}, u32[]{:S(2)}) collective-permute-start(bf16[1,2,1536]{2,1,0:T(2,128)(2,1)S(1)} %get-tuple-element.343), channel_id=1, source_target_pairs={{0,8},{8,16},{16,24},{24,32},{32,40},{40,48},{48,56},{56,64},{64,7... | collective-permute-start | bytes 18440 | tf_op jit(solution)/shard_map/ppermute | solution.py:19
  112.8 28.6 %all-to-all-start.1 = ((bf16[8,1,192,512]{3,2,1,0:T(8,128)(2,1)}), bf16[8,1,192,512]{3,2,1,0:T(8,128)(2,1)S(1)}, u32[]{:S(2)}, u32[]{:S(2)}) async-start(bf16[8,1,192,512]{3,2,1,0:T(8,128)(2,1)} %broadcast_in_dim.29), calls=%async_computation.1 | async-start | bytes 3145728 | tf_op jit(solution)/shard_map/all_to_all | solution.py:31
  117.6 68.4 %all-gather.13.cloned.1.call-start = ((), (), s32[]{:S(2)}) async-start(), calls=%async_computation.8 | async-start | bytes 3342336 | tf_op jit(solution)/shard_map/all_gather | solution.py:89
  141.4 1.2 copy-start.2
  142.5 1.9 copy-start.8
  144.4 1.8 copy-start.3
  144.4 3.0 copy-start.4
  145.0 1.2 copy-start.1
  147.3 76.3 %all-gather.15.cloned.1.call-start = ((), (), s32[]{:S(2)}) async-start(), calls=%async_computation.9 | async-start | bytes 3342336 | tf_op jit(solution)/shard_map/all_gather | solution.py:90
  150.0 128.0 %all-gather.9.cloned.1.call-start = ((), (), s32[]{:S(2)}) async-start(), calls=%async_computation.6 | async-start | bytes 3342336 | tf_op jit(solution)/shard_map/all_gather | solution.py:89
  151.2 152.7 %all-gather.11.cloned.1.call-start = ((), (), s32[]{:S(2)}) async-start(), calls=%async_computation.7 | async-start | bytes 3342336 | tf_op jit(solution)/shard_map/all_gather | solution.py:90
  271.6 80.3 %all-to-all-start.5 = ((bf16[8,64,1,1536]{3,1,2,0:T(8,128)(2,1)}), bf16[8,64,1,1536]{3,1,2,0:T(8,128)(2,1)S(1)}, u32[]{:S(2)}, u32[]{:S(2)}) async-start(bf16[8,64,1,1536]{3,1,2,0:T(8,128)(2,1)} %bitcast.302), calls=%async_computation.5 | async-start | bytes 3145728 | tf_op jit(solution)/shard_map/all_to_all | solution.py:136
  351.9 29.4 %all-to-all-start.2 = ((bf16[8,64,1,1536]{3,1,2,0:T(8,128)(2,1)}), bf16[8,64,1,1536]{3,1,2,0:T(8,128)(2,1)}, u32[]{:S(2)}, u32[]{:S(2)}) async-start(bf16[8,64,1,1536]{3,1,2,0:T(8,128)(2,1)} %bitcast.303), calls=%async_computation.2 | async-start | bytes 3145728 | tf_op jit(solution)/shard_map/all_to_all | solution.py:136
Sparse Core Ops, SparseCore 0:
  147.5 38.4 all-gather.12
  187.7 35.9 all-gather.14
  225.3 35.9 all-gather.8
  262.8 41.0 all-gather.10

commit v3 on v1

--- a/solution.py
+++ b/solution.py
@@ -3,6 +3,8 @@
 import jax
 import jax.numpy as jnp
 from jax import lax
+from jax.experimental import pallas as pl
+from jax.experimental.pallas import tpu as pltpu
 from jax.sharding import PartitionSpec as P
 
 HD = 192
@@ -30,6 +32,54 @@
     copies = jnp.broadcast_to(block[None], (count,) + block.shape)
     arrived = jnp.moveaxis(lax.all_to_all(copies, "batch", 0, 0, tiled=False), 0, axis)
     return arrived.reshape(block.shape[:axis] + (count * block.shape[axis],) + block.shape[axis + 1 :])
+
+
+def flash_step(query_ref, key_ref, value_ref, out_ref, peak_ref, total_ref, summed_ref):
+    block = pl.program_id(1)
+
+    @pl.when(block == 0)
+    def _():
+        peak_ref[...] = jnp.full(peak_ref.shape, -jnp.inf, jnp.float32)
+        total_ref[...] = jnp.zeros(total_ref.shape, jnp.float32)
+        summed_ref[...] = jnp.zeros(summed_ref.shape, jnp.float32)
+
+    scores = jnp.dot(query_ref[0], key_ref[0], preferred_element_type=jnp.float32)
+    old_peak = peak_ref[...]
+    new_peak = jnp.maximum(old_peak, jnp.max(scores, axis=1, keepdims=True))
+    weights = jnp.exp(scores - new_peak)
+    rescale = jnp.exp(old_peak - new_peak)
+    total_ref[...] = total_ref[...] * rescale + jnp.sum(weights, axis=1, keepdims=True)
+    summed_ref[...] = summed_ref[...] * rescale + jnp.dot(
+        weights.astype(jnp.bfloat16), value_ref[0], preferred_element_type=jnp.float32
+    )
+    peak_ref[...] = new_peak
+
+    @pl.when(block == pl.num_programs(1) - 1)
+    def _():
+        out_ref[0] = (summed_ref[...] / total_ref[...]).astype(out_ref.dtype)
+
+
+def flash_attention(queries, keys, values, key_block=1024):
+    sample_count, query_count, head_width = queries.shape
+    key_count = keys.shape[2]
+    key_block = math.gcd(key_count, key_block)
+    return pl.pallas_call(
+        flash_step,
+        grid=(sample_count, key_count // key_block),
+        in_specs=[
+            pl.BlockSpec((1, query_count, head_width), lambda s, k: (s, 0, 0)),
+            pl.BlockSpec((1, head_width, key_block), lambda s, k: (s, 0, k)),
+            pl.BlockSpec((1, key_block, head_width), lambda s, k: (s, k, 0)),
+        ],
+        out_specs=pl.BlockSpec((1, query_count, head_width), lambda s, k: (s, 0, 0)),
+        out_shape=jax.ShapeDtypeStruct(queries.shape, jnp.bfloat16),
+        scratch_shapes=[
+            pltpu.VMEM((query_count, 1), jnp.float32),
+            pltpu.VMEM((query_count, 1), jnp.float32),
+            pltpu.VMEM((query_count, head_width), jnp.float32),
+        ],
+        compiler_params=pltpu.CompilerParams(dimension_semantics=("parallel", "arbitrary")),
+    )(queries, keys, values)
 
 
 def normalize(rows_in, gain):
@@ -72,64 +122,25 @@
     norm_scale = lax.rsqrt(jnp.mean(hidden_float * hidden_float, axis=1, keepdims=True) + 1e-06)
     normed = (hidden_float * norm_scale * attention_gain[None, :, None]).astype(jnp.bfloat16)
     queries = (
-        jnp.einsum("sdt,ed->set", normed, query_weight, preferred_element_type=jnp.float32)
+        jnp.einsum("sdt,ed->ste", normed, query_weight, preferred_element_type=jnp.float32)
         * HD ** (-0.5)
     ).astype(jnp.bfloat16)
     key_rows = jnp.einsum(
         "sdt,ed->set", normed, key_weight, preferred_element_type=jnp.float32
     ).astype(jnp.bfloat16)
     value_rows = jnp.einsum(
-        "sdt,ed->set", normed, value_weight, preferred_element_type=jnp.float32
+        "sdt,ed->ste", normed, value_weight, preferred_element_type=jnp.float32
     ).astype(jnp.bfloat16)
-    heads_here = query_weight.shape[0] // HD
-    query_heads = queries.reshape(sample_count, heads_here, HD, seq_rows)
-    start_max = jnp.full((sample_count, heads_here, seq_rows), -jnp.inf, jnp.float32)
-    start_sum = jnp.zeros((sample_count, heads_here, seq_rows), jnp.float32)
-    start_acc = jnp.zeros((sample_count, heads_here, HD, seq_rows), jnp.float32)
     key_tile = lax.all_gather(key_rows, "seq", axis=2, tiled=True)
-    value_tile = lax.all_gather(value_rows, "seq", axis=2, tiled=True)
-    key_count = key_tile.shape[2]
-    block_rows = math.gcd(key_count, 512)
-
-    def consume(block_index, running):
-        running_max, weight_sum, summed = running
-        begin = block_index * block_rows
-        key_block = lax.dynamic_slice_in_dim(key_tile, begin, block_rows, 2).reshape(
-            sample_count, heads_here, HD, block_rows
-        )
-        value_block = lax.dynamic_slice_in_dim(value_tile, begin, block_rows, 2).reshape(
-            sample_count, heads_here, HD, block_rows
-        )
-        scores = jnp.einsum(
-            "shdq,shdk->shqk", query_heads, key_block, preferred_element_type=jnp.float32
-        )
-        new_max = jnp.maximum(running_max, jnp.max(scores, axis=-1))
-        weights = jnp.exp(scores - new_max[..., None])
-        rescale = jnp.exp(running_max - new_max)
-        weight_sum = weight_sum * rescale + jnp.sum(weights, axis=-1)
-        summed = summed * rescale[:, :, None, :] + jnp.einsum(
-            "shqk,shdk->shdq",
-            weights.astype(jnp.bfloat16),
-            value_block,
-            preferred_element_type=jnp.float32,
-        )
-        return (new_max, weight_sum, summed)
-
-    final_max, weight_sum, summed = lax.fori_loop(
-        0, key_count // block_rows, consume, (start_max, start_sum, start_acc)
-    )
-    attended = (
-        (summed / weight_sum[:, :, None, :])
-        .astype(jnp.bfloat16)
-        .reshape(sample_count, heads_here * HD, seq_rows)
-    )
+    value_tile = lax.all_gather(value_rows, "seq", axis=1, tiled=True)
+    attended = flash_attention(queries, key_tile, value_tile)
     row_start = lax.axis_index("batch") * own_rows
     own_hidden = jnp.transpose(
         lax.dynamic_slice_in_dim(hidden_full, row_start, own_rows, 2), (0, 2, 1)
     ).astype(jnp.float32)
     batch_count = lax.axis_size("batch")
     partial_rows = jnp.einsum(
-        "set,ef->tsf", attended, output_weight, preferred_element_type=jnp.float32
+        "ste,ef->tsf", attended, output_weight, preferred_element_type=jnp.float32
     ).astype(jnp.bfloat16)
     partial_rows = partial_rows.reshape(batch_count, own_rows, sample_count, full_width)
     share_rows = jnp.sum(

time: 337 us -> 318 us (0.944)
  matrix products: 68.1 us -> 19 us
  Pallas kernels: 0 us -> 28.3 us
  waiting for transfers between devices: 158 us -> 167 us
  other arithmetic: 19.8 us -> 14.5 us
    dot_general x35 -> x3, matrix products: 57.5 us -> 8.43 us  [the longest x1 3.71 us: shards(): jnp.einsum('sdt,ed->ste', normed, query_weight, preferred_element_type=jn...]
    pallas_call x0 -> x1, Pallas kernels: none -> 28.3 us  [flash_attention(): pl.pallas_call(flash_step, grid=(sample_count, key_count // key_block), i...]
    all_gather x1, waiting for transfers between devices: 45 us -> 54.7 us  [shards(): value_tile = lax.all_gather(value_rows, 'seq', axis=1, tiled=True)]
    reduce_sum x16 -> x0, other arithmetic: 4.82 us -> none  [consume(): weight_sum = weight_sum * rescale + jnp.sum(weights, axis=-1)]
where the time goes in v3:
time: 318 us
  waiting for transfers between devices  167 us (53%)
  blocking collectives  43.2 us (14%)
  Pallas kernels  28.3 us (9%)
  matrix products  19 us (6%)
  starting transfers between devices  18.4 us (6%)
  other arithmetic  14.5 us (5%)
  local copies, waits for them, and re-layouts  13.9 us (4%)
  between operations  13.7 us (4%)
    all_gather x1, waiting for transfers between devices, shards(): value_tile = lax.all_gather(value_rows, 'seq', axis=1, tiled=True)  54.7 us
    all_to_all x1, blocking collectives, gather_batch(): lax.all_to_all(copies, 'batch', 0, 0, tiled=False)  43.2 us
    all_to_all x1, waiting for transfers between devices, gather_batch(): lax.all_to_all(copies, 'batch', 0, 0, tiled=False)  39.8 us
    all_to_all x1, waiting for transfers between devices, shards(): lax.all_to_all(partial_rows, 'batch', 0, 0, tiled=False).astype(jnp.float32)  38.6 us
    all_gather x1, waiting for transfers between devices, shards(): key_tile = lax.all_gather(key_rows, 'seq', axis=2, tiled=True)  33.6 us
    pallas_call x1, Pallas kernels, flash_attention(): pl.pallas_call(flash_step, grid=(sample_count, key_count // key_block), i...  28.3 us
    dot_general x5, matrix products, shards(): jnp.einsum('std,ed->set', framed[:, offset:offset + seq_rows], conv_weigh...  9.08 us
    convert_element_type x2, other arithmetic, shards(): active = jax.nn.gelu(normalize(gathered_in, conv_gain)).astype(jnp.bfloat16)  7.21 us
  transfers between devices with their start and end apart: 6, of which 4 were waited for; matrix products, arithmetic and copies ran while one was open for 6% of the time, Pallas kernels for 0%

profile of v3, /device:TPU:0, one launch (start us, length us, event | category | flops | bytes accessed | tf_op | source)
XLA Modules:
  0.0 317.6 jit_solution(10177289463700784070)
XLA Ops:
  6.5 3.0 broadcast_in_dim.4
  9.6 7.0 %all-to-all-start = ((bf16[8,2,64,1536]{3,2,1,0:T(8,128)(2,1)}), bf16[8,2,64,1536]{3,2,1,0:T(8,128)(2,1)}, u32[]{:S(2)}, u32[]{:S(2)}) async-start(bf16[8,2,64,1536]{3,2,1,0:T(8,128)(2,1)} %broadcast_in_dim.4), calls=%async_computation | async-start | bytes 6291456 | tf_op jit(solution)/shard_map/all_to_all | solution.py:33
  16.6 39.8 %all-to-all-done = bf16[8,2,64,1536]{3,2,1,0:T(8,128)(2,1)} async-done(((bf16[8,2,64,1536]{3,2,1,0:T(8,128)(2,1)}), bf16[8,2,64,1536]{3,2,1,0:T(8,128)(2,1)}, u32[]{:S(2)}, u32[]{:S(2)}) %all-to-all-start) | async-done | bytes 3145760 | tf_op jit(solution)/shard_map/all_to_all | solution.py:33
  56.4 2.6 fusion
  59.1 2.2 copy.66
  61.3 3.0 fusion.16
  65.6 4.2 %fusion.4 = bf16[2,8,64,1536]{3,2,1,0:T(8,128)(2,1)S(1)} fusion(f32[1536]{0:T(1024)S(1)} %copy-done.5, f32[2,8,64]{2,1,0:T(8,128)S(1)} %add_rsqrt_fusion, bf16[8,2,64,1536]{3,2,1,0:T(8,128)(2,1)} %all-to-all-done), kind=kLoop, calls=%fused_computation.8 | loop fusion | flops 18874368 | bytes 6301696 | tf_op jit(solution)/shard_map/convert_element_type | solution.py:106
  69.8 2.2 fusion.58
  72.5 3.3 %collective-permute-start = (bf16[2,2,1536]{2,1,0:T(2,128)(2,1)S(1)}, bf16[2,2,1536]{2,1,0:T(2,128)(2,1)S(1)}, u32[]{:S(2)}, u32[]{:S(2)}) collective-permute-start(bf16[2,2,1536]{2,1,0:T(2,128)(2,1)S(1)} %get-tuple-element.5), channel_id=1, source_target_pairs={{0,8},{8,16},{16,24},{24,32},{32,40},{40,48},{48,56},{56,64},{64,7... | collective-permute-start | bytes 36872 | tf_op jit(solution)/shard_map/ppermute | solution.py:21
  75.9 3.2 %fusion.19 = f32[2,512,192]{1,2,0:T(8,128)S(1)} fusion(bf16[2,512,1536]{2,1,0:T(8,128)(2,1)} %copy-done.2, bf16[2,2,1536]{2,1,0:T(2,128)(2,1)S(1)} %collective-permute-done.1, bf16[5,192,1536]{2,1,0:T(8,128)(2,1)} %param.10), kind=kOutput, calls=%fused_computation.31 | convolution fusion | flops 610271232 | bytes 4534272 | tf_op jit(solution)/shard_map/std,ed->set/dot_general | solution.py:110
  83.1 43.2 %all_to_all.15 = bf16[8,2,192,512]{3,2,1,0:T(8,128)(2,1)S(1)} all-to-all(bf16[8,2,192,512]{3,2,1,0:T(8,128)(2,1)S(1)} %broadcast_in_dim.5), channel_id=1, replica_groups=mesh['seq'=16,'batch'=8] {'batch'}, dimensions={0} | all-to-all | bytes 6291456 | tf_op jit(solution)/shard_map/all_to_all | solution.py:33
  129.3 1.6 copy-done.4
  130.9 1.5 fusion.47
  132.5 2.7 convolution_convert_fusion.1
  136.3 3.7 %fusion.28.query_ref = bf16[2,512,192]{2,1,0:T(8,128)(2,1)} fusion(bf16[2,1536,512]{2,1,0:T(8,128)(2,1)} %copy-done.4, bf16[192,1536]{1,0:T(8,128)(2,1)S(1)} %copy-done.10), kind=kOutput, calls=%fused_computation.41 | convolution fusion | flops 604372992 | bytes 4128768 | tf_op jit(solution)/shard_map/sdt,ed->ste/dot_general | solution.py:125
  140.0 33.6 %all-gather.3.cloned.1.call-done.key_ref = bf16[2,192,8192]{2,1,0:T(8,128)(2,1)} async-done(((bf16[2,192,512]{2,1,0:T(8,128)(2,1)}), bf16[2,192,8192]{2,1,0:T(8,128)(2,1)}) %all-gather.3.cloned.1.call-update) | async-done | bytes 6291472 | tf_op jit(solution)/shard_map/all_gather | solution.py:134
  173.6 54.7 %all-gather.5.cloned.1.call-done.value_ref = bf16[2,8192,192]{2,1,0:T(8,128)(2,1)} async-done(((bf16[2,512,192]{2,1,0:T(8,128)(2,1)}), bf16[2,8192,192]{2,1,0:T(8,128)(2,1)}) %all-gather.5.cloned.1.call-update) | async-done | bytes 6291472 | tf_op jit(solution)/shard_map/all_gather | solution.py:135
  228.3 28.3 %shard_map.82 = bf16[2,512,192]{2,1,0:T(8,128)(2,1)} custom-call(bf16[2,512,192]{2,1,0:T(8,128)(2,1)} %fusion.28.query_ref, bf16[2,192,8192]{2,1,0:T(8,128)(2,1)} %all-gather.3.cloned.1.call-done.key_ref, bf16[2,8192,192]{2,1,0:T(8,128)(2,1)} %all-gather.5.cloned.1.call-done.value_ref), custom_call_target="tpu_custom_call" | custom-call | tf_op jit(solution)/shard_map/pallas_call | solution.py:66
  256.6 2.0 convolution_convert_fusion
  258.6 2.0 copy.74
  260.5 6.7 %all-to-all-start.2 = ((bf16[8,64,2,1536]{3,1,2,0:T(8,128)(2,1)}), bf16[8,64,2,1536]{3,1,2,0:T(8,128)(2,1)}, u32[]{:S(2)}, u32[]{:S(2)}) async-start(bf16[8,64,2,1536]{3,1,2,0:T(8,128)(2,1)} %copy.74), calls=%async_computation.2 | async-start | bytes 6291456 | tf_op jit(solution)/shard_map/all_to_all | solution.py:147
  267.2 1.4 constant_dynamic-slice_fusion
  268.9 38.6 %all-to-all-done.2 = bf16[8,64,2,1536]{3,1,2,0:T(8,128)(2,1)} async-done(((bf16[8,64,2,1536]{3,1,2,0:T(8,128)(2,1)}), bf16[8,64,2,1536]{3,1,2,0:T(8,128)(2,1)}, u32[]{:S(2)}, u32[]{:S(2)}) %all-to-all-start.2) | async-done | bytes 3145760 | tf_op jit(solution)/shard_map/all_to_all | solution.py:147
  307.5 2.4 convert_reduce_fusion
  (44 shorter events, 11.0 us)
Async XLA Ops:
  6.5 250.0 %copy-start = (bf16[192,1536]{1,0:T(8,128)(2,1)S(1)}, bf16[192,1536]{1,0:T(8,128)(2,1)}, u32[]{:S(2)}) copy-start(bf16[192,1536]{1,0:T(8,128)(2,1)} %param.15) | copy-start | bytes 1769476
  9.6 46.8 %all-to-all-start = ((bf16[8,2,64,1536]{3,2,1,0:T(8,128)(2,1)}), bf16[8,2,64,1536]{3,2,1,0:T(8,128)(2,1)}, u32[]{:S(2)}, u32[]{:S(2)}) async-start(bf16[8,2,64,1536]{3,2,1,0:T(8,128)(2,1)} %broadcast_in_dim.4), calls=%async_computation | async-start | bytes 6291456 | tf_op jit(solution)/shard_map/all_to_all | solution.py:33
  16.6 157.0 %all-gather.3.cloned.1.call-start = ((), (), s32[]{:S(2)}) async-start(), calls=%async_computation.3 | async-start | bytes 6684672 | tf_op jit(solution)/shard_map/all_gather | solution.py:134
  59.1 2.2 copy-start.5
  64.3 5.6 %copy-start.2 = (bf16[2,512,1536]{2,1,0:T(8,128)(2,1)}, bf16[2,512,1536]{2,1,0:T(8,128)(2,1)S(1)}, u32[]{:S(2)}) copy-start(bf16[2,512,1536]{2,1,0:T(8,128)(2,1)S(1)} %fusion.16) | copy-start | bytes 9437188
  64.3 11.5 %collective-permute-start.1 = (bf16[2,2,1536]{2,1,0:T(2,128)(2,1)S(1)}, bf16[2,2,1536]{2,1,0:T(2,128)(2,1)S(1)}, u32[]{:S(2)}, u32[]{:S(2)}) collective-permute-start(bf16[2,2,1536]{2,1,0:T(2,128)(2,1)S(1)} %get-tuple-element.6), channel_id=1, source_target_pairs={{8,0},{16,8},{24,16},{32,24},{40,32},{48,40},{56,48},{64,56},{72,6... | collective-permute-start | bytes 36872 | tf_op jit(solution)/shard_map/ppermute | solution.py:23
  72.5 6.5 %copy-start.3 = (bf16[2,512,1536]{2,1,0:T(8,128)(2,1)S(1)}, bf16[2,512,1536]{2,1,0:T(8,128)(2,1)}, u32[]{:S(2)}) copy-start(bf16[2,512,1536]{2,1,0:T(8,128)(2,1)} %copy-done.2) | copy-start | bytes 9437188
  72.5 6.5 %copy-start.7 = (bf16[5,192,1536]{2,1,0:T(8,128)(2,1)S(1)}, bf16[5,192,1536]{2,1,0:T(8,128)(2,1)}, u32[]{:S(2)}) copy-start(bf16[5,192,1536]{2,1,0:T(8,128)(2,1)} %param.10) | copy-start | bytes 8847364
  72.5 7.7 %collective-permute-start = (bf16[2,2,1536]{2,1,0:T(2,128)(2,1)S(1)}, bf16[2,2,1536]{2,1,0:T(2,128)(2,1)S(1)}, u32[]{:S(2)}, u32[]{:S(2)}) collective-permute-start(bf16[2,2,1536]{2,1,0:T(2,128)(2,1)S(1)} %get-tuple-element.5), channel_id=1, source_target_pairs={{0,8},{8,16},{16,24},{24,32},{32,40},{40,48},{48,56},{56,64},{64,7... | collective-permute-start | bytes 36872 | tf_op jit(solution)/shard_map/ppermute | solution.py:21
  126.9 0.7 copy-start.6
  127.6 1.6 copy-start.1
  127.6 3.3 %copy-start.8 = (bf16[192,1536]{1,0:T(8,128)(2,1)S(1)}, bf16[192,1536]{1,0:T(8,128)(2,1)}, u32[]{:S(2)}) copy-start(bf16[192,1536]{1,0:T(8,128)(2,1)} %param.13) | copy-start | bytes 1769476
  129.3 1.6 copy-start.4
  130.9 1.6 copy-start.9
  132.4 3.8 %copy-start.10 = (bf16[192,1536]{1,0:T(8,128)(2,1)S(1)}, bf16[192,1536]{1,0:T(8,128)(2,1)}, u32[]{:S(2)}) copy-start(bf16[192,1536]{1,0:T(8,128)(2,1)} %param.12) | copy-start | bytes 1769476
  132.5 95.8 %all-gather.5.cloned.1.call-start = ((), (), s32[]{:S(2)}) async-start(), calls=%async_computation.4 | async-start | bytes 8912896 | tf_op jit(solution)/shard_map/all_gather | solution.py:135
  260.5 46.9 %all-to-all-start.2 = ((bf16[8,64,2,1536]{3,1,2,0:T(8,128)(2,1)}), bf16[8,64,2,1536]{3,1,2,0:T(8,128)(2,1)}, u32[]{:S(2)}, u32[]{:S(2)}) async-start(bf16[8,64,2,1536]{3,1,2,0:T(8,128)(2,1)} %copy.74), calls=%async_computation.2 | async-start | bytes 6291456 | tf_op jit(solution)/shard_map/all_to_all | solution.py:147
Sparse Core Ops, SparseCore 0:
  132.6 40.9 all-gather.2
  175.2 53.0 all-gather.4

commit v4 on v3

--- a/solution.py
+++ b/solution.py
@@ -131,22 +131,40 @@
     value_rows = jnp.einsum(
         "sdt,ed->ste", normed, value_weight, preferred_element_type=jnp.float32
     ).astype(jnp.bfloat16)
-    key_tile = lax.all_gather(key_rows, "seq", axis=2, tiled=True)
-    value_tile = lax.all_gather(value_rows, "seq", axis=1, tiled=True)
-    attended = flash_attention(queries, key_tile, value_tile)
+    seq_count = lax.axis_size("seq")
+    mine = lax.axis_index("seq") % 2
+    pair = [(index, index ^ 1) for index in range(seq_count)]
+    own_queries = lax.dynamic_index_in_dim(queries, mine, 0, keepdims=False)
+    other_queries = lax.dynamic_index_in_dim(queries, 1 - mine, 0, keepdims=False)
+    query_block = jnp.concatenate([own_queries, lax.ppermute(other_queries, "seq", pair)], 0)
+    head_width = key_rows.shape[1]
+    value_flat = value_rows.reshape(sample_count, head_width, seq_rows)
+    outgoing = jnp.broadcast_to(
+        jnp.stack([key_rows, value_flat], axis=1)[None],
+        (seq_count // sample_count, sample_count, 2, head_width, seq_rows),
+    ).reshape(seq_count, 2, head_width, seq_rows)
+    incoming = lax.all_to_all(outgoing, "seq", 0, 0, tiled=False)
+    key_tile = jnp.moveaxis(incoming[:, 0], 0, 1).reshape(1, head_width, seq_count * seq_rows)
+    value_tile = incoming[:, 1].reshape(1, seq_count * seq_rows, head_width)
+    attended = flash_attention(query_block[None], key_tile, value_tile)[0]
     row_start = lax.axis_index("batch") * own_rows
     own_hidden = jnp.transpose(
         lax.dynamic_slice_in_dim(hidden_full, row_start, own_rows, 2), (0, 2, 1)
     ).astype(jnp.float32)
     batch_count = lax.axis_size("batch")
-    partial_rows = jnp.einsum(
-        "ste,ef->tsf", attended, output_weight, preferred_element_type=jnp.float32
-    ).astype(jnp.bfloat16)
-    partial_rows = partial_rows.reshape(batch_count, own_rows, sample_count, full_width)
+    partial_rows = jnp.dot(attended, output_weight, preferred_element_type=jnp.float32)
+    partial_rows = jnp.transpose(
+        partial_rows.astype(jnp.bfloat16).reshape(2, batch_count, own_rows, full_width), (1, 0, 2, 3)
+    )
     share_rows = jnp.sum(
         lax.all_to_all(partial_rows, "batch", 0, 0, tiled=False).astype(jnp.float32), axis=0
     )
-    branch_rows = jnp.transpose(share_rows, (1, 0, 2))
+    from_partner = lax.ppermute(share_rows[1], "seq", pair)
+    branch_rows = jnp.where(
+        mine == 0,
+        jnp.stack([share_rows[0], from_partner]),
+        jnp.stack([from_partner, share_rows[0]]),
+    )
     result = own_hidden + branch_rows
     return result.astype(jnp.bfloat16)
 

time: 318 us -> 333 us (1.047); the launches traced: 318 us -> 326 us
  blocking collectives: 43.2 us -> 85.6 us
  waiting for transfers between devices: 167 us -> 125 us
  local copies, waits for them, and re-layouts: 13.9 us -> 40.6 us
  between operations: 13.7 us -> 0.38 us
  matrix products: 19 us -> 15.3 us
    all_gather x2 -> x0, waiting for transfers between devices: 88.3 us -> none  [the longest x1 54.7 us: shards(): value_tile = lax.all_gather(value_rows, 'seq', axis=1, tiled=True)]
    all_to_all x1, waiting for transfers between devices: 38.6 us -> 83.8 us  [shards(): incoming = lax.all_to_all(outgoing, 'seq', 0, 0, tiled=False)]
    all_to_all x0 -> x1, blocking collectives: none -> 42.4 us  [shards(): lax.all_to_all(partial_rows, 'batch', 0, 0, tiled=False).astype(jnp.float32)]
    another operation x0 -> x3, local copies, waits for them, and re-layouts: none -> 8.9 us  [the longest x1 8.16 us: shards(): value_tile = incoming[:, 1].reshape(1, seq_count * seq_rows, head_width)]
    slice x0 -> x2, local copies, waits for them, and re-layouts: none -> 6.23 us  [the longest x1 6.18 us: shards(): value_tile = incoming[:, 1].reshape(1, seq_count * seq_rows, head_width)]
    transpose x0 -> x1, local copies, waits for them, and re-layouts: none -> 5.29 us  [shards(): jnp.moveaxis(incoming[:, 0], 0, 1)]
    reshape x1 -> x2, local copies, waits for them, and re-layouts: 1.95 us -> 6.17 us  [the longest x1 5.89 us: shards(): jnp.moveaxis(incoming[:, 0], 0, 1)]
    broadcast_in_dim x0 -> x1, local copies, waits for them, and re-layouts: none -> 3.35 us  [shards(): jnp.broadcast_to(jnp.stack([key_rows, value_flat], axis=1)[None], (seq_co...]
  transfers between devices with their start and end apart: 6 -> 6, of which waited for: 4 -> 3; matrix products, arithmetic and copies ran while one was open for 6% -> 5% of each run, Pallas kernels for 0% -> 0%
where the time goes in v4:
time: 333 us; the launch traced here: 326 us
  waiting for transfers between devices  125 us (38%)
  blocking collectives  85.6 us (26%)
  local copies, waits for them, and re-layouts  40.6 us (12%)
  Pallas kernels  27.9 us (8%)
  starting transfers between devices  18.3 us (5%)
  matrix products  15.3 us (5%)
  other arithmetic  13.5 us (4%)
    all_to_all x1, waiting for transfers between devices, shards(): incoming = lax.all_to_all(outgoing, 'seq', 0, 0, tiled=False)  83.8 us
    all_to_all x1, blocking collectives, gather_batch(): lax.all_to_all(copies, 'batch', 0, 0, tiled=False)  43.2 us
    all_to_all x1, blocking collectives, shards(): lax.all_to_all(partial_rows, 'batch', 0, 0, tiled=False).astype(jnp.float32)  42.4 us
    all_to_all x1, waiting for transfers between devices, gather_batch(): lax.all_to_all(copies, 'batch', 0, 0, tiled=False)  39.8 us
    pallas_call x1, Pallas kernels, flash_attention(): pl.pallas_call(flash_step, grid=(sample_count, key_count // key_block), i...  27.9 us
    dot_general x5, matrix products, shards(): jnp.einsum('std,ed->set', framed[:, offset:offset + seq_rows], conv_weigh...  9.08 us
    another operation x1, local copies, waits for them, and re-layouts, shards(): value_tile = incoming[:, 1].reshape(1, seq_count * seq_rows, head_width)  8.16 us
    convert_element_type x2, other arithmetic, shards(): active = jax.nn.gelu(normalize(gathered_in, conv_gain)).astype(jnp.bfloat16)  7.21 us
  transfers between devices with their start and end apart: 6, of which 3 were waited for; matrix products, arithmetic and copies ran while one was open for 5% of the time, Pallas kernels for 0%

profile of v4, /device:TPU:0, one launch (start us, length us, event | category | flops | bytes accessed | tf_op | source)
XLA Modules:
  0.0 326.3 jit_solution(1617301922956444095)
XLA Ops:
  0.0 3.0 broadcast_in_dim.8
  3.0 7.0 %all-to-all-start = ((bf16[8,2,64,1536]{3,2,1,0:T(8,128)(2,1)}), bf16[8,2,64,1536]{3,2,1,0:T(8,128)(2,1)}, u32[]{:S(2)}, u32[]{:S(2)}) async-start(bf16[8,2,64,1536]{3,2,1,0:T(8,128)(2,1)} %broadcast_in_dim.8), calls=%async_computation | async-start | bytes 6291456 | tf_op jit(solution)/shard_map/all_to_all | solution.py:33
  10.0 39.8 %all-to-all-done = bf16[8,2,64,1536]{3,2,1,0:T(8,128)(2,1)} async-done(((bf16[8,2,64,1536]{3,2,1,0:T(8,128)(2,1)}), bf16[8,2,64,1536]{3,2,1,0:T(8,128)(2,1)}, u32[]{:S(2)}, u32[]{:S(2)}) %all-to-all-start) | async-done | bytes 3145760 | tf_op jit(solution)/shard_map/all_to_all | solution.py:33
  49.9 2.6 fusion
  52.5 2.2 copy.80
  54.7 3.0 fusion.16
  59.1 4.2 %fusion.4 = bf16[2,8,64,1536]{3,2,1,0:T(8,128)(2,1)S(1)} fusion(f32[1536]{0:T(1024)S(1)} %copy-done.6, f32[2,8,64]{2,1,0:T(8,128)S(1)} %add_rsqrt_fusion, bf16[8,2,64,1536]{3,2,1,0:T(8,128)(2,1)} %all-to-all-done), kind=kLoop, calls=%fused_computation.8 | loop fusion | flops 18874368 | bytes 6301696 | tf_op jit(solution)/shard_map/convert_element_type | solution.py:106
  63.3 2.2 fusion.58
  66.0 3.3 %collective-permute-start = (bf16[2,2,1536]{2,1,0:T(2,128)(2,1)S(1)}, bf16[2,2,1536]{2,1,0:T(2,128)(2,1)S(1)}, u32[]{:S(2)}, u32[]{:S(2)}) collective-permute-start(bf16[2,2,1536]{2,1,0:T(2,128)(2,1)S(1)} %get-tuple-element.7), channel_id=1, source_target_pairs={{0,8},{8,16},{16,24},{24,32},{32,40},{40,48},{48,56},{56,64},{64,7... | collective-permute-start | bytes 36872 | tf_op jit(solution)/shard_map/ppermute | solution.py:21
  69.3 3.2 fusion.19
  74.9 1.3 fusion.48
  76.5 43.2 %all_to_all.20 = bf16[8,2,192,512]{3,2,1,0:T(8,128)(2,1)S(1)} all-to-all(bf16[8,2,192,512]{3,2,1,0:T(8,128)(2,1)S(1)} %broadcast_in_dim.9), channel_id=1, replica_groups=mesh['seq'=16,'batch'=8] {'batch'}, dimensions={0} | all-to-all | bytes 6291456 | tf_op jit(solution)/shard_map/all_to_all | solution.py:33
  126.2 3.4 %broadcast_in_dim.11 = bf16[8,2,2,192,512]{4,3,2,1,0:T(8,128)(2,1)} broadcast(bf16[2,2,192,512]{3,2,1,0:T(8,128)(2,1)S(1)} %copy.87), dimensions={1,2,3,4} | broadcast | bytes 7077888 | tf_op jit(solution)/shard_map/broadcast_in_dim | solution.py:142
  129.6 6.2 %all-to-all-start.2 = ((bf16[16,2,192,512]{3,2,1,0:T(8,128)(2,1)}), bf16[16,2,192,512]{3,2,1,0:T(8,128)(2,1)}, u32[]{:S(2)}, u32[]{:S(2)}) async-start(bf16[16,2,192,512]{3,2,1,0:T(8,128)(2,1)} %bitcast.75), calls=%async_computation.2 | async-start | bytes 12582912 | tf_op jit(solution)/shard_map/all_to_all | solution.py:146
  135.8 2.7 fusion.46
  141.2 83.8 %all-to-all-done.2 = bf16[16,2,192,512]{3,2,1,0:T(8,128)(2,1)} async-done(((bf16[16,2,192,512]{3,2,1,0:T(8,128)(2,1)}), bf16[16,2,192,512]{3,2,1,0:T(8,128)(2,1)}, u32[]{:S(2)}, u32[]{:S(2)}) %all-to-all-start.2) | async-done | bytes 6291488 | tf_op jit(solution)/shard_map/all_to_all | solution.py:146
  225.0 6.2 %fusion.72 = (bf16[16,1,192,512]{3,2,1,0:T(8,128)(2,1)}, bf16[192,16,512]{2,0,1:T(8,128)(2,1)}) fusion(bf16[16,2,192,512]{3,2,1,0:T(8,128)(2,1)} %all-to-all-done.2), kind=kLoop, calls=%fused_computation.85 | loop fusion | bytes 12582912 | tf_op jit(solution)/shard_map/slice | solution.py:148
  231.2 8.2 %reshape_squeeze.3.value_ref = bf16[1,8192,192]{2,1,0:T(8,128)(2,1)} reshape(bf16[16,1,192,512]{3,2,1,0:T(8,128)(2,1)} %get-tuple-element.5) | data formatting | bytes 6291456 | tf_op jit(solution)/shard_map/reshape;squeeze | solution.py:148
  239.3 5.3 %copy.88 = bf16[192,16,512]{2,1,0:T(8,128)(2,1)} copy(bf16[192,16,512]{2,0,1:T(8,128)(2,1)} %get-tuple-element.6) | data formatting | bytes 6291456 | tf_op jit(solution)/shard_map/transpose | solution.py:147
  244.6 5.9 %reshape.51.key_ref = bf16[1,192,8192]{2,1,0:T(8,128)(2,1)} reshape(bf16[192,16,512]{2,1,0:T(8,128)(2,1)} %copy.88) | data formatting | bytes 6291456 | tf_op jit(solution)/shard_map/reshape | solution.py:147
  250.5 27.9 %shard_map.82 = bf16[1,1024,192]{2,1,0:T(8,128)(2,1)} custom-call(bf16[1,1024,192]{2,1,0:T(8,128)(2,1)} %maximum_bitcast_fusion.query_ref, bf16[1,192,8192]{2,1,0:T(8,128)(2,1)} %reshape.51.key_ref, bf16[1,8192,192]{2,1,0:T(8,128)(2,1)} %reshape_squeeze.3.value_ref), custom_call_target="tpu_custom_call" | custom-call | tf_op jit(solution)/shard_map/pallas_call | solution.py:66
  278.4 2.0 convolution_convert_fusion
  280.7 42.4 %all_to_all.21 = bf16[8,2,64,1536]{3,2,1,0:T(8,128)(2,1)S(1)} all-to-all(bf16[8,2,64,1536]{3,2,1,0:T(8,128)(2,1)S(1)} %bitcast.79), channel_id=1, replica_groups=mesh['seq'=16,'batch'=8] {'batch'}, dimensions={0} | all-to-all | bytes 6291456 | tf_op jit(solution)/shard_map/all_to_all | solution.py:160
  323.7 1.4 constant_dynamic-slice_fusion.2
  (56 shorter events, 15.6 us)
Async XLA Ops:
  0.0 278.4 %copy-start = (bf16[192,1536]{1,0:T(8,128)(2,1)S(1)}, bf16[192,1536]{1,0:T(8,128)(2,1)}, u32[]{:S(2)}) copy-start(bf16[192,1536]{1,0:T(8,128)(2,1)} %param.15) | copy-start | bytes 1769476
  3.0 46.8 %all-to-all-start = ((bf16[8,2,64,1536]{3,2,1,0:T(8,128)(2,1)}), bf16[8,2,64,1536]{3,2,1,0:T(8,128)(2,1)}, u32[]{:S(2)}, u32[]{:S(2)}) async-start(bf16[8,2,64,1536]{3,2,1,0:T(8,128)(2,1)} %broadcast_in_dim.8), calls=%async_computation | async-start | bytes 6291456 | tf_op jit(solution)/shard_map/all_to_all | solution.py:33
  52.5 2.2 copy-start.6
  57.7 5.6 %copy-start.3 = (bf16[2,512,1536]{2,1,0:T(8,128)(2,1)}, bf16[2,512,1536]{2,1,0:T(8,128)(2,1)S(1)}, u32[]{:S(2)}) copy-start(bf16[2,512,1536]{2,1,0:T(8,128)(2,1)S(1)} %fusion.16) | copy-start | bytes 9437188
  57.8 11.5 %collective-permute-start.1 = (bf16[2,2,1536]{2,1,0:T(2,128)(2,1)S(1)}, bf16[2,2,1536]{2,1,0:T(2,128)(2,1)S(1)}, u32[]{:S(2)}, u32[]{:S(2)}) collective-permute-start(bf16[2,2,1536]{2,1,0:T(2,128)(2,1)S(1)} %get-tuple-element.8), channel_id=1, source_target_pairs={{8,0},{16,8},{24,16},{32,24},{40,32},{48,40},{56,48},{64,56},{72,6... | collective-permute-start | bytes 36872 | tf_op jit(solution)/shard_map/ppermute | solution.py:23
  66.0 6.5 %copy-start.4 = (bf16[2,512,1536]{2,1,0:T(8,128)(2,1)S(1)}, bf16[2,512,1536]{2,1,0:T(8,128)(2,1)}, u32[]{:S(2)}) copy-start(bf16[2,512,1536]{2,1,0:T(8,128)(2,1)} %copy-done.3) | copy-start | bytes 9437188
  66.0 6.5 %copy-start.8 = (bf16[5,192,1536]{2,1,0:T(8,128)(2,1)S(1)}, bf16[5,192,1536]{2,1,0:T(8,128)(2,1)}, u32[]{:S(2)}) copy-start(bf16[5,192,1536]{2,1,0:T(8,128)(2,1)} %param.10) | copy-start | bytes 8847364
  66.0 7.7 %collective-permute-start = (bf16[2,2,1536]{2,1,0:T(2,128)(2,1)S(1)}, bf16[2,2,1536]{2,1,0:T(2,128)(2,1)S(1)}, u32[]{:S(2)}, u32[]{:S(2)}) collective-permute-start(bf16[2,2,1536]{2,1,0:T(2,128)(2,1)S(1)} %get-tuple-element.7), channel_id=1, source_target_pairs={{0,8},{8,16},{16,24},{24,32},{32,40},{40,48},{48,56},{56,64},{64,7... | collective-permute-start | bytes 36872 | tf_op jit(solution)/shard_map/ppermute | solution.py:21
  120.4 0.7 copy-start.7
  121.1 1.6 copy-start.1
  121.1 1.6 copy-start.5
  122.7 1.7 copy-start.2
  122.7 1.7 copy-start.9
  129.6 6.2 %copy-start.10 = (bf16[192,1536]{1,0:T(8,128)(2,1)S(1)}, bf16[192,1536]{1,0:T(8,128)(2,1)}, u32[]{:S(2)}) copy-start(bf16[192,1536]{1,0:T(8,128)(2,1)} %param.12) | copy-start | bytes 1769476
  129.6 95.4 %all-to-all-start.2 = ((bf16[16,2,192,512]{3,2,1,0:T(8,128)(2,1)}), bf16[16,2,192,512]{3,2,1,0:T(8,128)(2,1)}, u32[]{:S(2)}, u32[]{:S(2)}) async-start(bf16[16,2,192,512]{3,2,1,0:T(8,128)(2,1)} %bitcast.75), calls=%async_computation.2 | async-start | bytes 12582912 | tf_op jit(solution)/shard_map/all_to_all | solution.py:146
  138.6 1.6 collective-permute-start.2
  323.6 1.8 collective-permute-start.3

commit v5 on v3

--- a/solution.py
+++ b/solution.py
@@ -34,7 +34,7 @@
     return arrived.reshape(block.shape[:axis] + (count * block.shape[axis],) + block.shape[axis + 1 :])
 
 
-def flash_step(query_ref, key_ref, value_ref, out_ref, peak_ref, total_ref, summed_ref):
+def flash_step(query_ref, kv_ref, out_ref, peak_ref, total_ref, summed_ref):
     block = pl.program_id(1)
 
     @pl.when(block == 0)
@@ -43,15 +43,29 @@
         total_ref[...] = jnp.zeros(total_ref.shape, jnp.float32)
         summed_ref[...] = jnp.zeros(summed_ref.shape, jnp.float32)
 
-    scores = jnp.dot(query_ref[0], key_ref[0], preferred_element_type=jnp.float32)
+    query = query_ref[0]
+    pieces = [
+        jnp.dot(query, kv_ref[part, 0, 0], preferred_element_type=jnp.float32)
+        for part in range(kv_ref.shape[0])
+    ]
     old_peak = peak_ref[...]
-    new_peak = jnp.maximum(old_peak, jnp.max(scores, axis=1, keepdims=True))
-    weights = jnp.exp(scores - new_peak)
+    new_peak = old_peak
+    for scores in pieces:
+        new_peak = jnp.maximum(new_peak, jnp.max(scores, axis=1, keepdims=True))
     rescale = jnp.exp(old_peak - new_peak)
-    total_ref[...] = total_ref[...] * rescale + jnp.sum(weights, axis=1, keepdims=True)
-    summed_ref[...] = summed_ref[...] * rescale + jnp.dot(
-        weights.astype(jnp.bfloat16), value_ref[0], preferred_element_type=jnp.float32
-    )
+    total = total_ref[...] * rescale
+    summed = summed_ref[...] * rescale
+    for part, scores in enumerate(pieces):
+        weights = jnp.exp(scores - new_peak)
+        total = total + jnp.sum(weights, axis=1, keepdims=True)
+        summed = summed + lax.dot_general(
+            weights.astype(jnp.bfloat16),
+            kv_ref[part, 0, 1],
+            (((1,), (1,)), ((), ())),
+            preferred_element_type=jnp.float32,
+        )
+    total_ref[...] = total
+    summed_ref[...] = summed
     peak_ref[...] = new_peak
 
     @pl.when(block == pl.num_programs(1) - 1)
@@ -59,17 +73,18 @@
         out_ref[0] = (summed_ref[...] / total_ref[...]).astype(out_ref.dtype)
 
 
-def flash_attention(queries, keys, values, key_block=1024):
+def flash_attention(queries, kv_tile, sources_per_step=2):
     sample_count, query_count, head_width = queries.shape
-    key_count = keys.shape[2]
-    key_block = math.gcd(key_count, key_block)
+    source_count, _, _, _, source_rows = kv_tile.shape
+    sources_per_step = math.gcd(source_count, sources_per_step)
     return pl.pallas_call(
         flash_step,
-        grid=(sample_count, key_count // key_block),
+        grid=(sample_count, source_count // sources_per_step),
         in_specs=[
             pl.BlockSpec((1, query_count, head_width), lambda s, k: (s, 0, 0)),
-            pl.BlockSpec((1, head_width, key_block), lambda s, k: (s, 0, k)),
-            pl.BlockSpec((1, key_block, head_width), lambda s, k: (s, k, 0)),
+            pl.BlockSpec(
+                (sources_per_step, 1, 2, head_width, source_rows), lambda s, k: (k, s, 0, 0, 0)
+            ),
         ],
         out_specs=pl.BlockSpec((1, query_count, head_width), lambda s, k: (s, 0, 0)),
         out_shape=jax.ShapeDtypeStruct(queries.shape, jnp.bfloat16),
@@ -79,7 +94,7 @@
             pltpu.VMEM((query_count, head_width), jnp.float32),
         ],
         compiler_params=pltpu.CompilerParams(dimension_semantics=("parallel", "arbitrary")),
-    )(queries, keys, values)
+    )(queries, kv_tile)
 
 
 def normalize(rows_in, gain):
@@ -129,11 +144,10 @@
         "sdt,ed->set", normed, key_weight, preferred_element_type=jnp.float32
     ).astype(jnp.bfloat16)
     value_rows = jnp.einsum(
-        "sdt,ed->ste", normed, value_weight, preferred_element_type=jnp.float32
+        "sdt,ed->set", normed, value_weight, preferred_element_type=jnp.float32
     ).astype(jnp.bfloat16)
-    key_tile = lax.all_gather(key_rows, "seq", axis=2, tiled=True)
-    value_tile = lax.all_gather(value_rows, "seq", axis=1, tiled=True)
-    attended = flash_attention(queries, key_tile, value_tile)
+    kv_tile = lax.all_gather(jnp.stack([key_rows, value_rows], axis=1), "seq", axis=0)
+    attended = flash_attention(queries, kv_tile)
     row_start = lax.axis_index("batch") * own_rows
     own_hidden = jnp.transpose(
         lax.dynamic_slice_in_dim(hidden_full, row_start, own_rows, 2), (0, 2, 1)

time: 318 us -> 302 us (0.950)
  waiting for transfers between devices: 167 us -> 145 us
  local copies, waits for them, and re-layouts: 13.9 us -> 22.8 us
    all_gather x2 -> x1, waiting for transfers between devices: 88.3 us -> 66.9 us  [shards(): lax.all_gather(jnp.stack([key_rows, value_rows], axis=1), 'seq', axis=0)]
    all_gather x0 -> x1, local copies, waits for them, and re-layouts: none -> 10.8 us  [shards(): lax.all_gather(jnp.stack([key_rows, value_rows], axis=1), 'seq', axis=0)]
  transfers between devices with their start and end apart: 6 -> 5, of which waited for: 4 -> 3; matrix products, arithmetic and copies ran while one was open for 6% -> 6% of each run, Pallas kernels for 0% -> 0%
where the time goes in v5:
time: 302 us; the launch traced here: 301 us
  waiting for transfers between devices  145 us (48%)
  blocking collectives  43.2 us (14%)
  Pallas kernels  26.1 us (9%)
  local copies, waits for them, and re-layouts  22.8 us (8%)
  starting transfers between devices  18.3 us (6%)
  matrix products  16.4 us (5%)
  other arithmetic  15.5 us (5%)
  between operations  13.7 us (5%)
    all_gather x1, waiting for transfers between devices, shards(): lax.all_gather(jnp.stack([key_rows, value_rows], axis=1), 'seq', axis=0)  66.9 us
    all_to_all x1, blocking collectives, gather_batch(): lax.all_to_all(copies, 'batch', 0, 0, tiled=False)  43.2 us
    all_to_all x1, waiting for transfers between devices, gather_batch(): lax.all_to_all(copies, 'batch', 0, 0, tiled=False)  39.8 us
    all_to_all x1, waiting for transfers between devices, shards(): lax.all_to_all(partial_rows, 'batch', 0, 0, tiled=False).astype(jnp.float32)  38.6 us
    pallas_call x1, Pallas kernels, flash_attention(): pl.pallas_call(flash_step, grid=(sample_count, source_count // sources_pe...  26.1 us
    all_gather x1, local copies, waits for them, and re-layouts, shards(): lax.all_gather(jnp.stack([key_rows, value_rows], axis=1), 'seq', axis=0)  10.8 us
    dot_general x5, matrix products, shards(): jnp.einsum('std,ed->set', framed[:, offset:offset + seq_rows], conv_weigh...  9.08 us
    convert_element_type x2, other arithmetic, shards(): active = jax.nn.gelu(normalize(gathered_in, conv_gain)).astype(jnp.bfloat16)  7.21 us
  transfers between devices with their start and end apart: 5, of which 3 were waited for; matrix products, arithmetic and copies ran while one was open for 6% of the time, Pallas kernels for 0%

profile of v5, /device:TPU:0, one launch (start us, length us, event | category | flops | bytes accessed | tf_op | source)
XLA Modules:
  0.0 301.1 jit_solution(14283379070390212692)
XLA Ops:
  6.5 3.0 %broadcast_in_dim.4 = bf16[8,2,64,1536]{3,2,1,0:T(8,128)(2,1)} broadcast(bf16[2,64,1536]{2,1,0:T(8,128)(2,1)} %param.8), dimensions={1,2,3} | broadcast | bytes 3538944 | tf_op jit(solution)/shard_map/broadcast_in_dim | solution.py:32
  9.6 7.0 %all-to-all-start = ((bf16[8,2,64,1536]{3,2,1,0:T(8,128)(2,1)}), bf16[8,2,64,1536]{3,2,1,0:T(8,128)(2,1)}, u32[]{:S(2)}, u32[]{:S(2)}) async-start(bf16[8,2,64,1536]{3,2,1,0:T(8,128)(2,1)} %broadcast_in_dim.4), calls=%async_computation | async-start | bytes 6291456 | tf_op jit(solution)/shard_map/all_to_all | solution.py:33
  16.6 39.8 %all-to-all-done = bf16[8,2,64,1536]{3,2,1,0:T(8,128)(2,1)} async-done(((bf16[8,2,64,1536]{3,2,1,0:T(8,128)(2,1)}), bf16[8,2,64,1536]{3,2,1,0:T(8,128)(2,1)}, u32[]{:S(2)}, u32[]{:S(2)}) %all-to-all-start) | async-done | bytes 3145760 | tf_op jit(solution)/shard_map/all_to_all | solution.py:33
  56.4 2.6 fusion
  59.1 2.2 copy.70
  61.3 3.0 fusion.16
  64.3 1.3 collective-permute-start.1
  65.6 4.2 %fusion.4 = bf16[2,8,64,1536]{3,2,1,0:T(8,128)(2,1)S(1)} fusion(f32[1536]{0:T(1024)S(1)} %copy-done.7, f32[2,8,64]{2,1,0:T(8,128)S(1)} %add_rsqrt_fusion, bf16[8,2,64,1536]{3,2,1,0:T(8,128)(2,1)} %all-to-all-done), kind=kLoop, calls=%fused_computation.8 | loop fusion | flops 18874368 | bytes 6301696 | tf_op jit(solution)/shard_map/convert_element_type | solution.py:121
  69.8 2.2 fusion.59
  72.5 3.3 %collective-permute-start = (bf16[2,2,1536]{2,1,0:T(2,128)(2,1)S(1)}, bf16[2,2,1536]{2,1,0:T(2,128)(2,1)S(1)}, u32[]{:S(2)}, u32[]{:S(2)}) collective-permute-start(bf16[2,2,1536]{2,1,0:T(2,128)(2,1)S(1)} %get-tuple-element.5), channel_id=1, source_target_pairs={{0,8},{8,16},{16,24},{24,32},{32,40},{40,48},{48,56},{56,64},{64,7... | collective-permute-start | bytes 36872 | tf_op jit(solution)/shard_map/ppermute | solution.py:21
  75.9 3.2 %fusion.19 = f32[2,512,192]{1,2,0:T(8,128)S(1)} fusion(bf16[2,512,1536]{2,1,0:T(8,128)(2,1)} %copy-done.3, bf16[2,2,1536]{2,1,0:T(2,128)(2,1)S(1)} %collective-permute-done.1, bf16[5,192,1536]{2,1,0:T(8,128)(2,1)} %param.10), kind=kOutput, calls=%fused_computation.31 | convolution fusion | flops 610271232 | bytes 4534272 | tf_op jit(solution)/shard_map/std,ed->set/dot_general | solution.py:125
  79.1 1.2 fusion.24
  81.4 1.3 fusion.49
  83.1 43.2 %all_to_all.15 = bf16[8,2,192,512]{3,2,1,0:T(8,128)(2,1)S(1)} all-to-all(bf16[8,2,192,512]{3,2,1,0:T(8,128)(2,1)S(1)} %broadcast_in_dim.5), channel_id=1, replica_groups=mesh['seq'=16,'batch'=8] {'batch'}, dimensions={0} | all-to-all | bytes 6291456 | tf_op jit(solution)/shard_map/all_to_all | solution.py:33
  132.6 3.7 %fusion.28.query_ref = bf16[2,512,192]{2,1,0:T(8,128)(2,1)} fusion(bf16[2,1536,512]{2,1,0:T(8,128)(2,1)} %copy-done.1, bf16[192,1536]{1,0:T(8,128)(2,1)S(1)} %copy-done.10), kind=kOutput, calls=%fused_computation.41 | convolution fusion | flops 604372992 | bytes 4128768 | tf_op jit(solution)/shard_map/sdt,ed->ste/dot_general | solution.py:140
  136.4 66.9 %all-gather.3.cloned.1.call-done = bf16[32,2,192,512]{3,2,0,1:T(8,128)(2,1)} async-done(((bf16[2,2,192,512]{3,2,0,1:T(8,128)(2,1)}), bf16[32,2,192,512]{3,2,0,1:T(8,128)(2,1)}) %all-gather.3.cloned.1.call-update) | async-done | bytes 12582928 | tf_op jit(solution)/shard_map/all_gather | solution.py:149
  203.2 10.8 %copy.76 = bf16[32,2,192,512]{3,2,1,0:T(8,128)(2,1)} copy(bf16[32,2,192,512]{3,2,0,1:T(8,128)(2,1)} %all-gather.3.cloned.1.call-done) | data formatting | bytes 25165824 | tf_op jit(solution)/shard_map/all_gather | solution.py:149
  214.0 26.1 %shard_map.82 = bf16[2,512,192]{2,1,0:T(8,128)(2,1)} custom-call(bf16[2,512,192]{2,1,0:T(8,128)(2,1)} %fusion.28.query_ref, bf16[16,2,2,192,512]{4,3,2,1,0:T(8,128)(2,1)} %bitcast.69), custom_call_target="tpu_custom_call" | custom-call | tf_op jit(solution)/shard_map/pallas_call | solution.py:80
  240.1 2.0 convolution_convert_fusion
  242.1 2.0 copy.78
  244.1 6.7 %all-to-all-start.2 = ((bf16[8,64,2,1536]{3,1,2,0:T(8,128)(2,1)}), bf16[8,64,2,1536]{3,1,2,0:T(8,128)(2,1)}, u32[]{:S(2)}, u32[]{:S(2)}) async-start(bf16[8,64,2,1536]{3,1,2,0:T(8,128)(2,1)} %copy.78), calls=%async_computation.2 | async-start | bytes 6291456 | tf_op jit(solution)/shard_map/all_to_all | solution.py:161
  250.8 1.4 constant_dynamic-slice_fusion
  252.5 38.6 %all-to-all-done.2 = bf16[8,64,2,1536]{3,1,2,0:T(8,128)(2,1)} async-done(((bf16[8,64,2,1536]{3,1,2,0:T(8,128)(2,1)}), bf16[8,64,2,1536]{3,1,2,0:T(8,128)(2,1)}, u32[]{:S(2)}, u32[]{:S(2)}) %all-to-all-start.2) | async-done | bytes 3145760 | tf_op jit(solution)/shard_map/all_to_all | solution.py:161
  291.0 2.4 convert_reduce_fusion
  (42 shorter events, 9.5 us)
Async XLA Ops:
  6.5 233.6 %copy-start = (bf16[192,1536]{1,0:T(8,128)(2,1)S(1)}, bf16[192,1536]{1,0:T(8,128)(2,1)}, u32[]{:S(2)}) copy-start(bf16[192,1536]{1,0:T(8,128)(2,1)} %param.15) | copy-start | bytes 1769476
  9.6 46.8 %all-to-all-start = ((bf16[8,2,64,1536]{3,2,1,0:T(8,128)(2,1)}), bf16[8,2,64,1536]{3,2,1,0:T(8,128)(2,1)}, u32[]{:S(2)}, u32[]{:S(2)}) async-start(bf16[8,2,64,1536]{3,2,1,0:T(8,128)(2,1)} %broadcast_in_dim.4), calls=%async_computation | async-start | bytes 6291456 | tf_op jit(solution)/shard_map/all_to_all | solution.py:33
  16.6 186.6 %all-gather.3.cloned.1.call-start = ((), (), s32[]{:S(2)}) async-start(), calls=%async_computation.3 | async-start | bytes 13369344 | tf_op jit(solution)/shard_map/all_gather | solution.py:149
  59.1 2.2 copy-start.7
  64.3 5.6 %copy-start.3 = (bf16[2,512,1536]{2,1,0:T(8,128)(2,1)}, bf16[2,512,1536]{2,1,0:T(8,128)(2,1)S(1)}, u32[]{:S(2)}) copy-start(bf16[2,512,1536]{2,1,0:T(8,128)(2,1)S(1)} %fusion.16) | copy-start | bytes 9437188
  64.3 11.5 %collective-permute-start.1 = (bf16[2,2,1536]{2,1,0:T(2,128)(2,1)S(1)}, bf16[2,2,1536]{2,1,0:T(2,128)(2,1)S(1)}, u32[]{:S(2)}, u32[]{:S(2)}) collective-permute-start(bf16[2,2,1536]{2,1,0:T(2,128)(2,1)S(1)} %get-tuple-element.6), channel_id=1, source_target_pairs={{8,0},{16,8},{24,16},{32,24},{40,32},{48,40},{56,48},{64,56},{72,6... | collective-permute-start | bytes 36872 | tf_op jit(solution)/shard_map/ppermute | solution.py:23
  72.5 6.5 %copy-start.4 = (bf16[2,512,1536]{2,1,0:T(8,128)(2,1)S(1)}, bf16[2,512,1536]{2,1,0:T(8,128)(2,1)}, u32[]{:S(2)}) copy-start(bf16[2,512,1536]{2,1,0:T(8,128)(2,1)} %copy-done.3) | copy-start | bytes 9437188
  72.5 6.5 %copy-start.9 = (bf16[5,192,1536]{2,1,0:T(8,128)(2,1)S(1)}, bf16[5,192,1536]{2,1,0:T(8,128)(2,1)}, u32[]{:S(2)}) copy-start(bf16[5,192,1536]{2,1,0:T(8,128)(2,1)} %param.10) | copy-start | bytes 8847364
  72.5 7.7 %collective-permute-start = (bf16[2,2,1536]{2,1,0:T(2,128)(2,1)S(1)}, bf16[2,2,1536]{2,1,0:T(2,128)(2,1)S(1)}, u32[]{:S(2)}, u32[]{:S(2)}) collective-permute-start(bf16[2,2,1536]{2,1,0:T(2,128)(2,1)S(1)} %get-tuple-element.5), channel_id=1, source_target_pairs={{0,8},{8,16},{16,24},{24,32},{32,40},{40,48},{48,56},{56,64},{64,7... | collective-permute-start | bytes 36872 | tf_op jit(solution)/shard_map/ppermute | solution.py:21
  126.9 0.7 copy-start.8
  127.6 1.7 copy-start.2
  127.6 1.7 copy-start.5
  129.3 2.3 copy-start.1
  129.3 1.5 copy-start.6
  130.8 1.8 copy-start.10
  244.1 46.9 %all-to-all-start.2 = ((bf16[8,64,2,1536]{3,1,2,0:T(8,128)(2,1)}), bf16[8,64,2,1536]{3,1,2,0:T(8,128)(2,1)}, u32[]{:S(2)}, u32[]{:S(2)}) async-start(bf16[8,64,2,1536]{3,1,2,0:T(8,128)(2,1)} %copy.78), calls=%async_computation.2 | async-start | bytes 6291456 | tf_op jit(solution)/shard_map/all_to_all | solution.py:161
Sparse Core Ops, SparseCore 0:
  132.8 70.4 all-gather.2

commit v6 on v5

--- a/solution.py
+++ b/solution.py
@@ -34,7 +34,7 @@
     return arrived.reshape(block.shape[:axis] + (count * block.shape[axis],) + block.shape[axis + 1 :])
 
 
-def flash_step(query_ref, kv_ref, out_ref, peak_ref, total_ref, summed_ref):
+def flash_step(query_ref, key_ref, value_ref, out_ref, peak_ref, total_ref, summed_ref):
     block = pl.program_id(1)
 
     @pl.when(block == 0)
@@ -45,8 +45,8 @@
 
     query = query_ref[0]
     pieces = [
-        jnp.dot(query, kv_ref[part, 0, 0], preferred_element_type=jnp.float32)
-        for part in range(kv_ref.shape[0])
+        jnp.dot(query, key_ref[0, part, 0], preferred_element_type=jnp.float32)
+        for part in range(key_ref.shape[1])
     ]
     old_peak = peak_ref[...]
     new_peak = old_peak
@@ -60,7 +60,7 @@
         total = total + jnp.sum(weights, axis=1, keepdims=True)
         summed = summed + lax.dot_general(
             weights.astype(jnp.bfloat16),
-            kv_ref[part, 0, 1],
+            value_ref[0, part, 0],
             (((1,), (1,)), ((), ())),
             preferred_element_type=jnp.float32,
         )
@@ -75,7 +75,7 @@
 
 def flash_attention(queries, kv_tile, sources_per_step=2):
     sample_count, query_count, head_width = queries.shape
-    source_count, _, _, _, source_rows = kv_tile.shape
+    _, source_count, _, _, source_rows = kv_tile.shape
     sources_per_step = math.gcd(source_count, sources_per_step)
     return pl.pallas_call(
         flash_step,
@@ -83,7 +83,10 @@
         in_specs=[
             pl.BlockSpec((1, query_count, head_width), lambda s, k: (s, 0, 0)),
             pl.BlockSpec(
-                (sources_per_step, 1, 2, head_width, source_rows), lambda s, k: (k, s, 0, 0, 0)
+                (1, sources_per_step, 1, head_width, source_rows), lambda s, k: (0, k, s, 0, 0)
+            ),
+            pl.BlockSpec(
+                (1, sources_per_step, 1, head_width, source_rows), lambda s, k: (1, k, s, 0, 0)
             ),
         ],
         out_specs=pl.BlockSpec((1, query_count, head_width), lambda s, k: (s, 0, 0)),
@@ -94,7 +97,7 @@
             pltpu.VMEM((query_count, head_width), jnp.float32),
         ],
         compiler_params=pltpu.CompilerParams(dimension_semantics=("parallel", "arbitrary")),
-    )(queries, kv_tile)
+    )(queries, kv_tile, kv_tile)
 
 
 def normalize(rows_in, gain):
@@ -146,7 +149,7 @@
     value_rows = jnp.einsum(
         "sdt,ed->set", normed, value_weight, preferred_element_type=jnp.float32
     ).astype(jnp.bfloat16)
-    kv_tile = lax.all_gather(jnp.stack([key_rows, value_rows], axis=1), "seq", axis=0)
+    kv_tile = lax.all_gather(jnp.stack([key_rows, value_rows]), "seq", axis=1)
     attended = flash_attention(queries, kv_tile)
     row_start = lax.axis_index("batch") * own_rows
     own_hidden = jnp.transpose(

time: 302 us -> 291 us (0.964)
  local copies, waits for them, and re-layouts: 22.8 us -> 11.9 us
    all_gather x1 -> x0, local copies, waits for them, and re-layouts: 10.8 us -> none  [shards(): lax.all_gather(jnp.stack([key_rows, value_rows], axis=1), 'seq', axis=0)]
where the time goes in v6:
time: 291 us; the launch traced here: 290 us
  waiting for transfers between devices  145 us (50%)
  blocking collectives  43.2 us (15%)
  Pallas kernels  26.3 us (9%)
  starting transfers between devices  18.3 us (6%)
  matrix products  16.4 us (6%)
  other arithmetic  15.4 us (5%)
  between operations  13.7 us (5%)
  local copies, waits for them, and re-layouts  11.9 us (4%)
    all_gather x1, waiting for transfers between devices, shards(): kv_tile = lax.all_gather(jnp.stack([key_rows, value_rows]), 'seq', axis=1)  66.8 us
    all_to_all x1, blocking collectives, gather_batch(): lax.all_to_all(copies, 'batch', 0, 0, tiled=False)  43.2 us
    all_to_all x1, waiting for transfers between devices, gather_batch(): lax.all_to_all(copies, 'batch', 0, 0, tiled=False)  39.8 us
    all_to_all x1, waiting for transfers between devices, shards(): lax.all_to_all(partial_rows, 'batch', 0, 0, tiled=False).astype(jnp.float32)  38.6 us
    pallas_call x1, Pallas kernels, flash_attention(): pl.pallas_call(flash_step, grid=(sample_count, source_count // sources_pe...  26.3 us
    dot_general x5, matrix products, shards(): jnp.einsum('std,ed->set', framed[:, offset:offset + seq_rows], conv_weigh...  9.08 us
    convert_element_type x2, other arithmetic, shards(): active = jax.nn.gelu(normalize(gathered_in, conv_gain)).astype(jnp.bfloat16)  7.21 us
    all_to_all x1, starting transfers between devices, gather_batch(): lax.all_to_all(copies, 'batch', 0, 0, tiled=False)  7.01 us
  transfers between devices with their start and end apart: 5, of which 3 were waited for; matrix products, arithmetic and copies ran while one was open for 6% of the time, Pallas kernels for 0%

profile of v6, /device:TPU:0, one launch (start us, length us, event | category | flops | bytes accessed | tf_op | source)
XLA Modules:
  0.0 290.4 jit_solution(4541780289981695082)
XLA Ops:
  6.5 3.0 %broadcast_in_dim.4 = bf16[8,2,64,1536]{3,2,1,0:T(8,128)(2,1)} broadcast(bf16[2,64,1536]{2,1,0:T(8,128)(2,1)} %param.8), dimensions={1,2,3} | broadcast | bytes 3538944 | tf_op jit(solution)/shard_map/broadcast_in_dim | solution.py:32
  9.6 7.0 %all-to-all-start = ((bf16[8,2,64,1536]{3,2,1,0:T(8,128)(2,1)}), bf16[8,2,64,1536]{3,2,1,0:T(8,128)(2,1)}, u32[]{:S(2)}, u32[]{:S(2)}) async-start(bf16[8,2,64,1536]{3,2,1,0:T(8,128)(2,1)} %broadcast_in_dim.4), calls=%async_computation | async-start | bytes 6291456 | tf_op jit(solution)/shard_map/all_to_all | solution.py:33
  16.6 39.8 %all-to-all-done = bf16[8,2,64,1536]{3,2,1,0:T(8,128)(2,1)} async-done(((bf16[8,2,64,1536]{3,2,1,0:T(8,128)(2,1)}), bf16[8,2,64,1536]{3,2,1,0:T(8,128)(2,1)}, u32[]{:S(2)}, u32[]{:S(2)}) %all-to-all-start) | async-done | bytes 3145760 | tf_op jit(solution)/shard_map/all_to_all | solution.py:33
  56.4 2.6 fusion
  59.1 2.2 copy.65
  61.3 3.0 %fusion.16 = bf16[2,512,1536]{2,1,0:T(8,128)(2,1)S(1)} fusion(f32[1536]{0:T(1024)S(1)} %copy-done.7, f32[2,512]{1,0:T(2,128)S(1)} %rsqrt.21, bf16[8,2,64,1536]{3,2,0,1:T(8,128)(2,1)S(1)} %copy.65), kind=kLoop, calls=%fused_computation.20 | loop fusion | flops 18874368 | bytes 6301696 | tf_op jit(solution)/shard_map/convert_element_type | solution.py:124
  64.3 1.3 collective-permute-start.1
  65.6 4.2 %fusion.4 = bf16[2,8,64,1536]{3,2,1,0:T(8,128)(2,1)S(1)} fusion(f32[1536]{0:T(1024)S(1)} %copy-done.7, f32[2,8,64]{2,1,0:T(8,128)S(1)} %add_rsqrt_fusion, bf16[8,2,64,1536]{3,2,1,0:T(8,128)(2,1)} %all-to-all-done), kind=kLoop, calls=%fused_computation.8 | loop fusion | flops 18874368 | bytes 6301696 | tf_op jit(solution)/shard_map/convert_element_type | solution.py:124
  69.8 2.2 fusion.59
  72.5 3.3 %collective-permute-start = (bf16[2,2,1536]{2,1,0:T(2,128)(2,1)S(1)}, bf16[2,2,1536]{2,1,0:T(2,128)(2,1)S(1)}, u32[]{:S(2)}, u32[]{:S(2)}) collective-permute-start(bf16[2,2,1536]{2,1,0:T(2,128)(2,1)S(1)} %get-tuple-element.5), channel_id=1, source_target_pairs={{0,8},{8,16},{16,24},{24,32},{32,40},{40,48},{48,56},{56,64},{64,7... | collective-permute-start | bytes 36872 | tf_op jit(solution)/shard_map/ppermute | solution.py:21
  75.9 3.2 %fusion.19 = f32[2,512,192]{1,2,0:T(8,128)S(1)} fusion(bf16[2,512,1536]{2,1,0:T(8,128)(2,1)} %copy-done.3, bf16[2,2,1536]{2,1,0:T(2,128)(2,1)S(1)} %collective-permute-done.1, bf16[5,192,1536]{2,1,0:T(8,128)(2,1)} %param.10), kind=kOutput, calls=%fused_computation.31 | convolution fusion | flops 610271232 | bytes 4534272 | tf_op jit(solution)/shard_map/std,ed->set/dot_general | solution.py:128
  79.1 1.2 fusion.24
  80.3 1.2 fusion.26
  81.4 1.3 fusion.49
  83.1 43.2 %all_to_all.15 = bf16[8,2,192,512]{3,2,1,0:T(8,128)(2,1)S(1)} all-to-all(bf16[8,2,192,512]{3,2,1,0:T(8,128)(2,1)S(1)} %broadcast_in_dim.5), channel_id=1, replica_groups=mesh['seq'=16,'batch'=8] {'batch'}, dimensions={0} | all-to-all | bytes 6291456 | tf_op jit(solution)/shard_map/all_to_all | solution.py:33
  132.5 3.7 %fusion.28.query_ref = bf16[2,512,192]{2,1,0:T(8,128)(2,1)} fusion(bf16[2,1536,512]{2,1,0:T(8,128)(2,1)} %copy-done.1, bf16[192,1536]{1,0:T(8,128)(2,1)S(1)} %copy-done.10), kind=kOutput, calls=%fused_computation.41 | convolution fusion | flops 604372992 | bytes 4128768 | tf_op jit(solution)/shard_map/sdt,ed->ste/dot_general | solution.py:143
  136.3 66.8 %all-gather.3.cloned.1.call-done = bf16[2,32,192,512]{3,2,1,0:T(8,128)(2,1)} async-done(((bf16[2,2,192,512]{3,2,1,0:T(8,128)(2,1)}), bf16[2,32,192,512]{3,2,1,0:T(8,128)(2,1)}) %all-gather.3.cloned.1.call-update) | async-done | bytes 12582928 | tf_op jit(solution)/shard_map/all_gather | solution.py:152
  203.1 26.3 %shard_map.82 = bf16[2,512,192]{2,1,0:T(8,128)(2,1)} custom-call(bf16[2,512,192]{2,1,0:T(8,128)(2,1)} %fusion.28.query_ref, bf16[2,16,2,192,512]{4,3,2,1,0:T(8,128)(2,1)} %bitcast.69, bf16[2,16,2,192,512]{4,3,2,1,0:T(8,128)(2,1)} %bitcast.70), custom_call_target="tpu_custom_call" | custom-call | tf_op jit(solution)/shard_map/pallas_call | solution.py:80
  229.4 2.0 convolution_convert_fusion
  231.5 2.0 copy.72
  233.4 6.7 %all-to-all-start.2 = ((bf16[8,64,2,1536]{3,1,2,0:T(8,128)(2,1)}), bf16[8,64,2,1536]{3,1,2,0:T(8,128)(2,1)}, u32[]{:S(2)}, u32[]{:S(2)}) async-start(bf16[8,64,2,1536]{3,1,2,0:T(8,128)(2,1)} %copy.72), calls=%async_computation.2 | async-start | bytes 6291456 | tf_op jit(solution)/shard_map/all_to_all | solution.py:164
  240.1 1.4 constant_dynamic-slice_fusion
  241.8 38.6 %all-to-all-done.2 = bf16[8,64,2,1536]{3,1,2,0:T(8,128)(2,1)} async-done(((bf16[8,64,2,1536]{3,1,2,0:T(8,128)(2,1)}), bf16[8,64,2,1536]{3,1,2,0:T(8,128)(2,1)}, u32[]{:S(2)}, u32[]{:S(2)}) %all-to-all-start.2) | async-done | bytes 3145760 | tf_op jit(solution)/shard_map/all_to_all | solution.py:164
  280.4 2.4 convert_reduce_fusion
  (41 shorter events, 8.2 us)
Async XLA Ops:
  6.5 222.9 %copy-start = (bf16[192,1536]{1,0:T(8,128)(2,1)S(1)}, bf16[192,1536]{1,0:T(8,128)(2,1)}, u32[]{:S(2)}) copy-start(bf16[192,1536]{1,0:T(8,128)(2,1)} %param.15) | copy-start | bytes 1769476
  9.6 46.8 %all-to-all-start = ((bf16[8,2,64,1536]{3,2,1,0:T(8,128)(2,1)}), bf16[8,2,64,1536]{3,2,1,0:T(8,128)(2,1)}, u32[]{:S(2)}, u32[]{:S(2)}) async-start(bf16[8,2,64,1536]{3,2,1,0:T(8,128)(2,1)} %broadcast_in_dim.4), calls=%async_computation | async-start | bytes 6291456 | tf_op jit(solution)/shard_map/all_to_all | solution.py:33
  16.6 186.5 %all-gather.3.cloned.1.call-start = ((), (), s32[]{:S(2)}) async-start(), calls=%async_computation.3 | async-start | bytes 13369344 | tf_op jit(solution)/shard_map/all_gather | solution.py:152
  59.1 2.2 copy-start.7
  64.3 5.6 %copy-start.3 = (bf16[2,512,1536]{2,1,0:T(8,128)(2,1)}, bf16[2,512,1536]{2,1,0:T(8,128)(2,1)S(1)}, u32[]{:S(2)}) copy-start(bf16[2,512,1536]{2,1,0:T(8,128)(2,1)S(1)} %fusion.16) | copy-start | bytes 9437188
  64.3 11.5 %collective-permute-start.1 = (bf16[2,2,1536]{2,1,0:T(2,128)(2,1)S(1)}, bf16[2,2,1536]{2,1,0:T(2,128)(2,1)S(1)}, u32[]{:S(2)}, u32[]{:S(2)}) collective-permute-start(bf16[2,2,1536]{2,1,0:T(2,128)(2,1)S(1)} %get-tuple-element.6), channel_id=1, source_target_pairs={{8,0},{16,8},{24,16},{32,24},{40,32},{48,40},{56,48},{64,56},{72,6... | collective-permute-start | bytes 36872 | tf_op jit(solution)/shard_map/ppermute | solution.py:23
  72.5 6.5 %copy-start.4 = (bf16[2,512,1536]{2,1,0:T(8,128)(2,1)S(1)}, bf16[2,512,1536]{2,1,0:T(8,128)(2,1)}, u32[]{:S(2)}) copy-start(bf16[2,512,1536]{2,1,0:T(8,128)(2,1)} %copy-done.3) | copy-start | bytes 9437188
  72.5 6.5 %copy-start.9 = (bf16[5,192,1536]{2,1,0:T(8,128)(2,1)S(1)}, bf16[5,192,1536]{2,1,0:T(8,128)(2,1)}, u32[]{:S(2)}) copy-start(bf16[5,192,1536]{2,1,0:T(8,128)(2,1)} %param.10) | copy-start | bytes 8847364
  72.5 7.7 %collective-permute-start = (bf16[2,2,1536]{2,1,0:T(2,128)(2,1)S(1)}, bf16[2,2,1536]{2,1,0:T(2,128)(2,1)S(1)}, u32[]{:S(2)}, u32[]{:S(2)}) collective-permute-start(bf16[2,2,1536]{2,1,0:T(2,128)(2,1)S(1)} %get-tuple-element.5), channel_id=1, source_target_pairs={{0,8},{8,16},{16,24},{24,32},{32,40},{40,48},{48,56},{56,64},{64,7... | collective-permute-start | bytes 36872 | tf_op jit(solution)/shard_map/ppermute | solution.py:21
  126.9 0.7 copy-start.8
  127.6 1.6 copy-start.2
  127.6 1.6 copy-start.5
  129.3 2.3 copy-start.1
  129.3 1.5 copy-start.6
  130.7 1.8 copy-start.10
  233.4 46.9 %all-to-all-start.2 = ((bf16[8,64,2,1536]{3,1,2,0:T(8,128)(2,1)}), bf16[8,64,2,1536]{3,1,2,0:T(8,128)(2,1)}, u32[]{:S(2)}, u32[]{:S(2)}) async-start(bf16[8,64,2,1536]{3,1,2,0:T(8,128)(2,1)} %copy.72), calls=%async_computation.2 | async-start | bytes 6291456 | tf_op jit(solution)/shard_map/all_to_all | solution.py:164
Sparse Core Ops, SparseCore 0:
  132.7 70.4 all-gather.2

commit v7 on v6

--- a/solution.py
+++ b/solution.py
@@ -106,7 +106,7 @@
     return values * scale * gain
 
 
-def shards(
+def one_sample(
     activations,
     conv_gain,
     conv_weight,
@@ -168,6 +168,14 @@
     return result.astype(jnp.bfloat16)
 
 
+def shards(activations, *weights):
+    pieces = [
+        one_sample(activations[sample : sample + 1], *weights)
+        for sample in range(activations.shape[0])
+    ]
+    return jnp.concatenate(pieces, axis=0)
+
+
 def solution(mesh):
     placed = (
         P(None, ("seq", "batch"), None),

time: 291 us -> 312 us (1.072)
  starting transfers between devices: 18.3 us -> 37 us
  blocking collectives: 43.2 us -> 29.6 us
  matrix products: 16.4 us -> 25.7 us
  other arithmetic: 15.4 us -> 23 us
    all_to_all x1 -> x2, waiting for transfers between devices: 38.6 us -> 20 us  [one_sample(): lax.all_to_all(partial_rows, 'batch', 0, 0, tiled=False).astype(jnp.float32)]
    all_to_all x1, blocking collectives: 43.2 us -> 29.6 us  [gather_batch(): lax.all_to_all(copies, 'batch', 0, 0, tiled=False)]
    all_to_all x1 -> x3, waiting for transfers between devices: 39.8 us -> 51.4 us  [gather_batch(): lax.all_to_all(copies, 'batch', 0, 0, tiled=False)]
    dot_general x9 -> x18, matrix products: 16.4 us -> 25.7 us  [the longest x10 9.88 us: one_sample(): jnp.einsum('std,ed->set', framed[:, offset:offset + seq_rows], conv_weigh...]
    all_to_all x1 -> x3, starting transfers between devices: 7.01 us -> 13.5 us  [gather_batch(): lax.all_to_all(copies, 'batch', 0, 0, tiled=False)]
    all_to_all x1 -> x2, starting transfers between devices: 6.7 us -> 13 us  [one_sample(): lax.all_to_all(partial_rows, 'batch', 0, 0, tiled=False).astype(jnp.float32)]
    all_gather x1 -> x2, waiting for transfers between devices: 66.8 us -> 73.1 us  [one_sample(): kv_tile = lax.all_gather(jnp.stack([key_rows, value_rows]), 'seq', axis=1)]
    ppermute x1 -> x2, starting transfers between devices: 3.29 us -> 7.37 us  [with_halo(): lax.ppermute(tail, axis, [(i, (i + 1) % count) for i in range(ends)])]
  transfers between devices with their start and end apart: 5 -> 11, of which waited for: 3 -> 6; matrix products, arithmetic and copies ran while one was open for 6% -> 12% of each run, Pallas kernels for 0% -> 9%
where the time goes in v7:
time: 312 us; the launch traced here: 310 us
  waiting for transfers between devices  144 us (46%)
  starting transfers between devices  37 us (12%)
  blocking collectives  29.6 us (9%)
  Pallas kernels  27.7 us (9%)
  matrix products  25.7 us (8%)
  other arithmetic  23 us (7%)
  between operations  13.8 us (4%)
  local copies, waits for them, and re-layouts  9.21 us (3%)
    all_gather x2, waiting for transfers between devices, one_sample(): kv_tile = lax.all_gather(jnp.stack([key_rows, value_rows]), 'seq', axis=1)  73.1 us
    all_to_all x3, waiting for transfers between devices, gather_batch(): lax.all_to_all(copies, 'batch', 0, 0, tiled=False)  51.4 us
    all_to_all x1, blocking collectives, gather_batch(): lax.all_to_all(copies, 'batch', 0, 0, tiled=False)  29.6 us
    pallas_call x2, Pallas kernels, flash_attention(): pl.pallas_call(flash_step, grid=(sample_count, source_count // sources_pe...  27.7 us
    all_to_all x2, waiting for transfers between devices, one_sample(): lax.all_to_all(partial_rows, 'batch', 0, 0, tiled=False).astype(jnp.float32)  20 us
    all_to_all x3, starting transfers between devices, gather_batch(): lax.all_to_all(copies, 'batch', 0, 0, tiled=False)  13.5 us
    all_to_all x2, starting transfers between devices, one_sample(): lax.all_to_all(partial_rows, 'batch', 0, 0, tiled=False).astype(jnp.float32)  13 us
    dot_general x10, matrix products, one_sample(): jnp.einsum('std,ed->set', framed[:, offset:offset + seq_rows], conv_weigh...  9.88 us
  transfers between devices with their start and end apart: 11, of which 6 were waited for; matrix products, arithmetic and copies ran while one was open for 12% of the time, Pallas kernels for 9%

profile of v7, /device:TPU:0, one launch (start us, length us, event | category | flops | bytes accessed | tf_op | source)
XLA Modules:
  0.0 310.5 jit_solution(4289569448016324856)
XLA Ops:
  7.8 29.6 %all_to_all.30 = bf16[8,1,64,1536]{3,2,1,0:T(8,128)(2,1)S(1)} all-to-all(bf16[8,1,64,1536]{3,2,1,0:T(8,128)(2,1)S(1)} %broadcast_in_dim.17), channel_id=1, replica_groups=mesh['seq'=16,'batch'=8] {'batch'}, dimensions={0} | all-to-all | bytes 3145728 | tf_op jit(solution)/shard_map/all_to_all | solution.py:33
  38.7 4.4 %all-to-all-start.3 = ((bf16[8,1,64,1536]{3,2,1,0:T(8,128)(2,1)}), bf16[8,1,64,1536]{3,2,1,0:T(8,128)(2,1)}, u32[]{:S(2)}, u32[]{:S(2)}) async-start(bf16[8,1,64,1536]{3,2,1,0:T(8,128)(2,1)} %broadcast_in_dim.21), calls=%async_computation.3 | async-start | bytes 3145728 | tf_op jit(solution)/shard_map/all_to_all | solution.py:33
  43.6 21.5 %all-to-all-done.3 = bf16[8,1,64,1536]{3,2,1,0:T(8,128)(2,1)} async-done(((bf16[8,1,64,1536]{3,2,1,0:T(8,128)(2,1)}), bf16[8,1,64,1536]{3,2,1,0:T(8,128)(2,1)}, u32[]{:S(2)}, u32[]{:S(2)}) %all-to-all-start.3) | async-done | bytes 1572896 | tf_op jit(solution)/shard_map/all_to_all | solution.py:33
  68.3 4.0 %fusion.25 = (bf16[1,512,1536]{2,1,0:T(8,128)(2,1)S(1)}, bf16[1,512,1536]{2,1,0:T(8,128)(2,1)S(1)}) fusion(bf16[1,512,1536]{2,1,0:T(8,128)(2,1)S(1)} %bitcast.225, f32[1536]{0:T(1024)S(1)} %copy-done.6, f32[512]{0:T(512)S(1)} %rsqrt.41, f32[512]{0:T(512)S(1)} %rsqrt.44, bf16[1,512,1536]{2,1,0:T(8,128)(2,1)} %bitcast.36), kind=kLoop, calls=%fused_computation.33 | loop fusion | flops 18874368 | bytes 6301696 | tf_op jit(solution)/shard_map/convert_element_type | solution.py:124
  76.5 4.8 %fusion.4 = (bf16[8,1,64,1536]{3,2,0,1:T(8,128)(2,1)}, bf16[8,1,64,1536]{3,2,0,1:T(8,128)(2,1)S(1)}) fusion(bf16[8,1,64,1536]{3,2,1,0:T(8,128)(2,1)S(1)} %all_to_all.30, f32[1536]{0:T(1024)S(1)} %copy-done.6, f32[8,64]{1,0:T(8,128)S(1)} %add_rsqrt_fusion.1, f32[8,64]{1,0:T(8,128)S(1)} %add_rsqrt_fusion, bf16[8,1,64,1536]{3,2,1,0:T(8,128)(2,1)} %all-to-all-done.3), kind=kLoop, calls=%fused_computation.12 | loop fusion | flops 18874368 | bytes 6301696 | tf_op jit(solution)/shard_map/convert_element_type | solution.py:124
  85.9 4.3 %all-to-all-start.4 = ((bf16[8,1,192,512]{3,2,1,0:T(8,128)(2,1)}), bf16[8,1,192,512]{3,2,1,0:T(8,128)(2,1)}, u32[]{:S(2)}, u32[]{:S(2)}) async-start(bf16[8,1,192,512]{3,2,1,0:T(8,128)(2,1)} %broadcast_in_dim.23), calls=%async_computation.4 | async-start | bytes 3145728 | tf_op jit(solution)/shard_map/all_to_all | solution.py:33
  90.3 2.2 fusion.134
  92.8 6.1 %collective-permute-start = (bf16[1,2,1536]{2,1,0:T(2,128)(2,1)S(1)}, bf16[1,2,1536]{2,1,0:T(2,128)(2,1)S(1)}, u32[]{:S(2)}, u32[]{:S(2)}) collective-permute-start(bf16[1,2,1536]{2,1,0:T(2,128)(2,1)S(1)} %get-tuple-element.5), channel_id=1, source_target_pairs={{0,8},{8,16},{16,24},{24,32},{32,40},{40,48},{48,56},{56,64},{64,7... | collective-permute-start | bytes 18440 | tf_op jit(solution)/shard_map/ppermute | solution.py:21
  98.9 2.2 fusion.65
  103.2 8.3 %all-to-all-done.4 = bf16[8,1,192,512]{3,2,1,0:T(8,128)(2,1)} async-done(((bf16[8,1,192,512]{3,2,1,0:T(8,128)(2,1)}), bf16[8,1,192,512]{3,2,1,0:T(8,128)(2,1)}, u32[]{:S(2)}, u32[]{:S(2)}) %all-to-all-start.4) | async-done | bytes 1572896 | tf_op jit(solution)/shard_map/all_to_all | solution.py:33
  112.8 4.8 %all-to-all-start.1 = ((bf16[8,1,192,512]{3,2,1,0:T(8,128)(2,1)}), bf16[8,1,192,512]{3,2,1,0:T(8,128)(2,1)S(1)}, u32[]{:S(2)}, u32[]{:S(2)}) async-start(bf16[8,1,192,512]{3,2,1,0:T(8,128)(2,1)} %broadcast_in_dim.19), calls=%async_computation.1 | async-start | bytes 3145728 | tf_op jit(solution)/shard_map/all_to_all | solution.py:33
  119.7 21.7 %all-to-all-done.1 = bf16[8,1,192,512]{3,2,1,0:T(8,128)(2,1)S(1)} async-done(((bf16[8,1,192,512]{3,2,1,0:T(8,128)(2,1)}), bf16[8,1,192,512]{3,2,1,0:T(8,128)(2,1)S(1)}, u32[]{:S(2)}, u32[]{:S(2)}) %all-to-all-start.1) | async-done | bytes 1572896 | tf_op jit(solution)/shard_map/all_to_all | solution.py:33
  148.3 1.9 fusion.124
  152.9 2.9 fusion.116.query_ref
  155.8 37.5 %all-gather.7.cloned.1.call-done = bf16[2,16,192,512]{3,2,1,0:T(8,128)(2,1)} async-done(((bf16[2,1,192,512]{3,2,1,0:T(8,128)(2,1)}), bf16[2,16,192,512]{3,2,1,0:T(8,128)(2,1)}) %all-gather.7.cloned.1.call-update) | async-done | bytes 6291472 | tf_op jit(solution)/shard_map/all_gather | solution.py:152
  193.3 13.9 %shard_map.83 = bf16[1,512,192]{2,1,0:T(8,128)(2,1)} custom-call(bf16[1,512,192]{2,1,0:T(8,128)(2,1)} %fusion.116.query_ref, bf16[2,16,1,192,512]{4,3,2,1,0:T(8,128)(2,1)} %bitcast.227, bf16[2,16,1,192,512]{4,3,2,1,0:T(8,128)(2,1)} %bitcast.228), custom_call_target="tpu_custom_call" | custom-call | tf_op jit(solution)/shard_map/pallas_call | solution.py:80
  207.2 2.8 convolution_convert_fusion
  210.0 6.6 %all-to-all-start.5 = ((bf16[8,64,1,1536]{3,1,2,0:T(8,128)(2,1)}), bf16[8,64,1,1536]{3,1,2,0:T(8,128)(2,1)}, u32[]{:S(2)}, u32[]{:S(2)}) async-start(bf16[8,64,1,1536]{3,1,2,0:T(8,128)(2,1)} %bitcast.233), calls=%async_computation.5 | async-start | bytes 3145728 | tf_op jit(solution)/shard_map/all_to_all | solution.py:164
  216.6 2.8 fusion.117.query_ref
  219.3 35.5 %all-gather.5.cloned.1.call-done = bf16[2,16,192,512]{3,2,1,0:T(8,128)(2,1)} async-done(((bf16[2,1,192,512]{3,2,1,0:T(8,128)(2,1)}), bf16[2,16,192,512]{3,2,1,0:T(8,128)(2,1)}) %all-gather.5.cloned.1.call-update) | async-done | bytes 6291472 | tf_op jit(solution)/shard_map/all_gather | solution.py:152
  254.8 13.8 %shard_map.82 = bf16[1,512,192]{2,1,0:T(8,128)(2,1)} custom-call(bf16[1,512,192]{2,1,0:T(8,128)(2,1)} %fusion.117.query_ref, bf16[2,16,1,192,512]{4,3,2,1,0:T(8,128)(2,1)} %bitcast.229, bf16[2,16,1,192,512]{4,3,2,1,0:T(8,128)(2,1)} %bitcast.230), custom_call_target="tpu_custom_call" | custom-call | tf_op jit(solution)/shard_map/pallas_call | solution.py:80
  268.7 2.6 convolution_convert_fusion.1
  271.3 6.4 %all-to-all-start.2 = ((bf16[8,64,1,1536]{3,1,2,0:T(8,128)(2,1)}), bf16[8,64,1,1536]{3,1,2,0:T(8,128)(2,1)}, u32[]{:S(2)}, u32[]{:S(2)}) async-start(bf16[8,64,1,1536]{3,1,2,0:T(8,128)(2,1)} %bitcast.232), calls=%async_computation.2 | async-start | bytes 3145728 | tf_op jit(solution)/shard_map/all_to_all | solution.py:164
  281.2 19.9 %all-to-all-done.2 = bf16[8,64,1,1536]{3,1,2,0:T(8,128)(2,1)} async-done(((bf16[8,64,1,1536]{3,1,2,0:T(8,128)(2,1)}), bf16[8,64,1,1536]{3,1,2,0:T(8,128)(2,1)}, u32[]{:S(2)}, u32[]{:S(2)}) %all-to-all-start.2) | async-done | bytes 1572896 | tf_op jit(solution)/shard_map/all_to_all | solution.py:164
  (80 shorter events, 36.1 us)
Async XLA Ops:
  6.5 200.6 %copy-start = (bf16[192,1536]{1,0:T(8,128)(2,1)S(1)}, bf16[192,1536]{1,0:T(8,128)(2,1)}, u32[]{:S(2)}) copy-start(bf16[192,1536]{1,0:T(8,128)(2,1)} %param.15) | copy-start | bytes 1769476
  38.7 29.5 %copy-start.6 = (f32[1536]{0:T(1024)S(1)}, f32[1536]{0:T(1024)}, u32[]{:S(2)}) copy-start(f32[1536]{0:T(1024)} %param.9) | copy-start | bytes 18436
  38.7 26.4 %all-to-all-start.3 = ((bf16[8,1,64,1536]{3,2,1,0:T(8,128)(2,1)}), bf16[8,1,64,1536]{3,2,1,0:T(8,128)(2,1)}, u32[]{:S(2)}, u32[]{:S(2)}) async-start(bf16[8,1,64,1536]{3,2,1,0:T(8,128)(2,1)} %broadcast_in_dim.21), calls=%async_computation.3 | async-start | bytes 3145728 | tf_op jit(solution)/shard_map/all_to_all | solution.py:33
  72.2 9.0 %copy-start.4 = (bf16[1,512,1536]{2,1,0:T(8,128)(2,1)}, bf16[1,512,1536]{2,1,0:T(8,128)(2,1)S(1)}, u32[]{:S(2)}) copy-start(bf16[1,512,1536]{2,1,0:T(8,128)(2,1)S(1)} %get-tuple-element.15) | copy-start | bytes 4718596
  72.3 11.0 %collective-permute-start.2 = (bf16[1,2,1536]{2,1,0:T(2,128)(2,1)S(1)}, bf16[1,2,1536]{2,1,0:T(2,128)(2,1)S(1)}, u32[]{:S(2)}, u32[]{:S(2)}) collective-permute-start(bf16[1,2,1536]{2,1,0:T(2,128)(2,1)S(1)} %get-tuple-element.7), channel_id=1, source_target_pairs={{0,8},{8,16},{16,24},{24,32},{32,40},{40,48},{48,56},{56,64},{64,7... | collective-permute-start | bytes 18440 | tf_op jit(solution)/shard_map/ppermute | solution.py:21
  73.6 8.3 %collective-permute-start.3 = (bf16[1,2,1536]{2,1,0:T(2,128)(2,1)S(1)}, bf16[1,2,1536]{2,1,0:T(2,128)(2,1)S(1)}, u32[]{:S(2)}, u32[]{:S(2)}) collective-permute-start(bf16[1,2,1536]{2,1,0:T(2,128)(2,1)S(1)} %get-tuple-element.8), channel_id=1, source_target_pairs={{8,0},{16,8},{24,16},{32,24},{40,32},{48,40},{56,48},{64,56},{72,6... | collective-permute-start | bytes 18440 | tf_op jit(solution)/shard_map/ppermute | solution.py:23
  74.9 6.4 %copy-start.8 = (bf16[5,192,1536]{2,1,0:T(8,128)(2,1)S(1)}, bf16[5,192,1536]{2,1,0:T(8,128)(2,1)}, u32[]{:S(2)}) copy-start(bf16[5,192,1536]{2,1,0:T(8,128)(2,1)} %param.10) | copy-start | bytes 8847364
  74.9 24.0 %collective-permute-start.1 = (bf16[1,2,1536]{2,1,0:T(2,128)(2,1)S(1)}, bf16[1,2,1536]{2,1,0:T(2,128)(2,1)S(1)}, u32[]{:S(2)}, u32[]{:S(2)}) collective-permute-start(bf16[1,2,1536]{2,1,0:T(2,128)(2,1)S(1)} %get-tuple-element.6), channel_id=1, source_target_pairs={{8,0},{16,8},{24,16},{32,24},{40,32},{48,40},{56,48},{64,56},{72,6... | collective-permute-start | bytes 18440 | tf_op jit(solution)/shard_map/ppermute | solution.py:23
  85.9 25.6 %all-to-all-start.4 = ((bf16[8,1,192,512]{3,2,1,0:T(8,128)(2,1)}), bf16[8,1,192,512]{3,2,1,0:T(8,128)(2,1)}, u32[]{:S(2)}, u32[]{:S(2)}) async-start(bf16[8,1,192,512]{3,2,1,0:T(8,128)(2,1)} %broadcast_in_dim.23), calls=%async_computation.4 | async-start | bytes 3145728 | tf_op jit(solution)/shard_map/all_to_all | solution.py:33
  92.6 8.5 %copy-start.5 = (bf16[1,512,1536]{2,1,0:T(8,128)(2,1)S(1)}, bf16[1,512,1536]{2,1,0:T(8,128)(2,1)}, u32[]{:S(2)}) copy-start(bf16[1,512,1536]{2,1,0:T(8,128)(2,1)} %copy-done.4) | copy-start | bytes 4718596
  92.8 8.4 %copy-start.9 = (bf16[5,192,1536]{2,1,0:T(8,128)(2,1)S(1)}, bf16[5,192,1536]{2,1,0:T(8,128)(2,1)}, u32[]{:S(2)}) copy-start(bf16[5,192,1536]{2,1,0:T(8,128)(2,1)} %param.10) | copy-start | bytes 8847364
  92.8 8.3 %collective-permute-start = (bf16[1,2,1536]{2,1,0:T(2,128)(2,1)S(1)}, bf16[1,2,1536]{2,1,0:T(2,128)(2,1)S(1)}, u32[]{:S(2)}, u32[]{:S(2)}) collective-permute-start(bf16[1,2,1536]{2,1,0:T(2,128)(2,1)S(1)} %get-tuple-element.5), channel_id=1, source_target_pairs={{0,8},{8,16},{16,24},{24,32},{32,40},{40,48},{48,56},{56,64},{64,7... | collective-permute-start | bytes 18440 | tf_op jit(solution)/shard_map/ppermute | solution.py:21
  112.8 28.6 %all-to-all-start.1 = ((bf16[8,1,192,512]{3,2,1,0:T(8,128)(2,1)}), bf16[8,1,192,512]{3,2,1,0:T(8,128)(2,1)S(1)}, u32[]{:S(2)}, u32[]{:S(2)}) async-start(bf16[8,1,192,512]{3,2,1,0:T(8,128)(2,1)} %broadcast_in_dim.19), calls=%async_computation.1 | async-start | bytes 3145728 | tf_op jit(solution)/shard_map/all_to_all | solution.py:33
  117.6 75.7 %all-gather.7.cloned.1.call-start = ((), (), s32[]{:S(2)}) async-start(), calls=%async_computation.7 | async-start | bytes 6684672 | tf_op jit(solution)/shard_map/all_gather | solution.py:152
  142.2 1.9 copy-start.7
  144.1 1.8 copy-start.2
  144.1 2.9 copy-start.3
  145.9 1.1 copy-start.1
  148.3 106.6 %all-gather.5.cloned.1.call-start = ((), (), s32[]{:S(2)}) async-start(), calls=%async_computation.6 | async-start | bytes 6684672 | tf_op jit(solution)/shard_map/all_gather | solution.py:152
  207.2 9.4 %copy-start.10 = (bf16[192,1536]{1,0:T(8,128)(2,1)S(1)}, bf16[192,1536]{1,0:T(8,128)(2,1)}, u32[]{:S(2)}) copy-start(bf16[192,1536]{1,0:T(8,128)(2,1)} %param.12) | copy-start | bytes 1769476
  210.0 61.4 %all-to-all-start.5 = ((bf16[8,64,1,1536]{3,1,2,0:T(8,128)(2,1)}), bf16[8,64,1,1536]{3,1,2,0:T(8,128)(2,1)}, u32[]{:S(2)}, u32[]{:S(2)}) async-start(bf16[8,64,1,1536]{3,1,2,0:T(8,128)(2,1)} %bitcast.233), calls=%async_computation.5 | async-start | bytes 3145728 | tf_op jit(solution)/shard_map/all_to_all | solution.py:164
  271.3 29.8 %all-to-all-start.2 = ((bf16[8,64,1,1536]{3,1,2,0:T(8,128)(2,1)}), bf16[8,64,1,1536]{3,1,2,0:T(8,128)(2,1)}, u32[]{:S(2)}, u32[]{:S(2)}) async-start(bf16[8,64,1,1536]{3,1,2,0:T(8,128)(2,1)} %bitcast.232), calls=%async_computation.2 | async-start | bytes 3145728 | tf_op jit(solution)/shard_map/all_to_all | solution.py:164
Sparse Core Ops, SparseCore 0:
  148.4 44.8 all-gather.6
  195.0 59.8 all-gather.4

commit v8 on v6

--- a/solution.py
+++ b/solution.py
@@ -8,6 +8,9 @@
 from jax.sharding import PartitionSpec as P
 
 HD = 192
+SEQ = ("chip_x", "chip_z", "core")
+BATCH = ("peer_y", "peer_x")
+CHIPS = ("chip_x", "chip_z")
 
 
 def with_halo(cells, sides, width):
@@ -28,9 +31,9 @@
 
 
 def gather_batch(block, axis):
-    count = lax.axis_size("batch")
+    count = lax.axis_size(BATCH)
     copies = jnp.broadcast_to(block[None], (count,) + block.shape)
-    arrived = jnp.moveaxis(lax.all_to_all(copies, "batch", 0, 0, tiled=False), 0, axis)
+    arrived = jnp.moveaxis(lax.all_to_all(copies, BATCH, 0, 0, tiled=False), 0, axis)
     return arrived.reshape(block.shape[:axis] + (count * block.shape[axis],) + block.shape[axis + 1 :])
 
 
@@ -122,7 +125,7 @@
     gathered_in = gather_batch(activations, 1)
     seq_rows = gathered_in.shape[1]
     active = jax.nn.gelu(normalize(gathered_in, conv_gain)).astype(jnp.bfloat16)
-    framed = with_halo(active, (("seq", 1),), flank_rows)
+    framed = with_halo(active, ((SEQ, 1),), flank_rows)
     conv_sum = jnp.zeros((sample_count, local_out, seq_rows), jnp.float32)
     for offset in range(tap_count):
         conv_sum = conv_sum + jnp.einsum(
@@ -131,7 +134,7 @@
             conv_weight[offset],
             preferred_element_type=jnp.float32,
         )
-    column_start = lax.axis_index("batch") * local_out
+    column_start = lax.axis_index(BATCH) * local_out
     own_columns = lax.dynamic_slice_in_dim(gathered_in, column_start, local_out, 2)
     residual = jnp.transpose(own_columns, (0, 2, 1)).astype(jnp.float32)
     hidden_part = (residual + conv_sum).astype(jnp.bfloat16)
@@ -149,40 +152,59 @@
     value_rows = jnp.einsum(
         "sdt,ed->set", normed, value_weight, preferred_element_type=jnp.float32
     ).astype(jnp.bfloat16)
-    kv_tile = lax.all_gather(jnp.stack([key_rows, value_rows]), "seq", axis=1)
-    attended = flash_attention(queries, kv_tile)
-    row_start = lax.axis_index("batch") * own_rows
+    mine = lax.axis_index("core")
+    swap = [(0, 1), (1, 0)]
+    own_queries = lax.dynamic_index_in_dim(queries, mine, 0, keepdims=False)
+    other_queries = lax.dynamic_index_in_dim(queries, 1 - mine, 0, keepdims=False)
+    query_block = jnp.concatenate([own_queries, lax.ppermute(other_queries, "core", swap)], 0)
+    kv_rows = jnp.stack([key_rows, value_rows])
+    own_kv = lax.dynamic_index_in_dim(kv_rows, mine, 1, keepdims=False)
+    other_kv = lax.dynamic_index_in_dim(kv_rows, 1 - mine, 1, keepdims=False)
+    chip_kv = jnp.stack([own_kv, lax.ppermute(other_kv, "core", swap)], axis=1)
+    kv_tile = lax.all_gather(chip_kv, CHIPS, axis=1)
+    kv_tile = kv_tile.reshape((2, -1, 1) + kv_tile.shape[3:])
+    attended = flash_attention(query_block[None], kv_tile)[0]
+    row_start = lax.axis_index(BATCH) * own_rows
     own_hidden = jnp.transpose(
         lax.dynamic_slice_in_dim(hidden_full, row_start, own_rows, 2), (0, 2, 1)
     ).astype(jnp.float32)
-    batch_count = lax.axis_size("batch")
-    partial_rows = jnp.einsum(
-        "ste,ef->tsf", attended, output_weight, preferred_element_type=jnp.float32
-    ).astype(jnp.bfloat16)
-    partial_rows = partial_rows.reshape(batch_count, own_rows, sample_count, full_width)
+    batch_count = lax.axis_size(BATCH)
+    partial_rows = jnp.dot(attended, output_weight, preferred_element_type=jnp.float32)
+    partial_rows = jnp.transpose(
+        partial_rows.astype(jnp.bfloat16).reshape(2, batch_count, own_rows, full_width), (1, 0, 2, 3)
+    )
     share_rows = jnp.sum(
-        lax.all_to_all(partial_rows, "batch", 0, 0, tiled=False).astype(jnp.float32), axis=0
-    )
-    branch_rows = jnp.transpose(share_rows, (1, 0, 2))
+        lax.all_to_all(partial_rows, BATCH, 0, 0, tiled=False).astype(jnp.float32), axis=0
+    )
+    from_partner = lax.ppermute(share_rows[1], "core", swap)
+    branch_rows = jnp.where(
+        mine == 0,
+        jnp.stack([share_rows[0], from_partner]),
+        jnp.stack([from_partner, share_rows[0]]),
+    )
     result = own_hidden + branch_rows
     return result.astype(jnp.bfloat16)
 
 
 def solution(mesh):
+    fine = jax.sharding.Mesh(
+        mesh.devices.reshape(2, mesh.shape["seq"] // 4, 2, mesh.shape["batch"] // 2, 2),
+        SEQ + BATCH,
+    )
     placed = (
-        P(None, ("seq", "batch"), None),
+        P(None, SEQ + BATCH, None),
         P(),
-        P(None, "batch", None),
+        P(None, BATCH, None),
         P(),
-        P("batch", None),
-        P("batch", None),
-        P("batch", None),
-        P("batch", None),
+        P(BATCH, None),
+        P(BATCH, None),
+        P(BATCH, None),
+        P(BATCH, None),
     )
     return jax.shard_map(
         shards,
-        mesh=mesh,
+        mesh=fine,
         in_specs=placed,
-        out_specs=P(None, ("seq", "batch"), None),
+        out_specs=P(None, SEQ + BATCH, None),
         check_vma=False,
     )

time: 291 us -> 300 us (1.031)
  waiting for transfers between devices: 145 us -> 149 us
  transfers between devices with their start and end apart: 5 -> 8, of which waited for: 3 -> 5; matrix products, arithmetic and copies ran while one was open for 6% -> 6% of each run, Pallas kernels for 0% -> 0%
where the time goes in v8:
time: 300 us; the launch traced here: 298 us
  waiting for transfers between devices  149 us (50%)
  blocking collectives  45.9 us (15%)
  Pallas kernels  27 us (9%)
  starting transfers between devices  17.1 us (6%)
  other arithmetic  16.4 us (5%)
  matrix products  15.3 us (5%)
  local copies, waits for them, and re-layouts  13.8 us (5%)
  between operations  13.7 us (5%)
    all_to_all x2, waiting for transfers between devices, gather_batch(): lax.all_to_all(copies, BATCH, 0, 0, tiled=False)  80.2 us
    all_gather x1, waiting for transfers between devices, shards(): kv_tile = lax.all_gather(chip_kv, CHIPS, axis=1)  65.7 us
    all_to_all x1, blocking collectives, shards(): lax.all_to_all(partial_rows, BATCH, 0, 0, tiled=False).astype(jnp.float32)  45.9 us
    pallas_call x1, Pallas kernels, flash_attention(): pl.pallas_call(flash_step, grid=(sample_count, source_count // sources_pe...  27 us
    all_to_all x2, starting transfers between devices, gather_batch(): lax.all_to_all(copies, BATCH, 0, 0, tiled=False)  11.5 us
    dot_general x5, matrix products, shards(): jnp.einsum('std,ed->set', framed[:, offset:offset + seq_rows], conv_weigh...  9.07 us
    convert_element_type x2, other arithmetic, shards(): active = jax.nn.gelu(normalize(gathered_in, conv_gain)).astype(jnp.bfloat16)  7.21 us
  transfers between devices with their start and end apart: 8, of which 5 were waited for; matrix products, arithmetic and copies ran while one was open for 6% of the time, Pallas kernels for 0%

profile of v8, /device:TPU:0, one launch (start us, length us, event | category | flops | bytes accessed | tf_op | source)
XLA Modules:
  0.0 297.8 jit_solution(9075446491550092158)
XLA Ops:
  6.5 3.0 %broadcast_in_dim.6 = bf16[8,2,64,1536]{3,2,1,0:T(8,128)(2,1)} broadcast(bf16[2,64,1536]{2,1,0:T(8,128)(2,1)} %param.8), dimensions={1,2,3} | broadcast | bytes 3538944 | tf_op jit(solution)/shard_map/broadcast_in_dim | solution.py:35
  9.6 7.0 %all-to-all-start = ((bf16[8,2,64,1536]{3,2,1,0:T(8,128)(2,1)}), bf16[8,2,64,1536]{3,2,1,0:T(8,128)(2,1)}, u32[]{:S(2)}, u32[]{:S(2)}) async-start(bf16[8,2,64,1536]{3,2,1,0:T(8,128)(2,1)} %broadcast_in_dim.6), calls=%async_computation | async-start | bytes 6291456 | tf_op jit(solution)/shard_map/all_to_all | solution.py:36
  16.6 39.8 %all-to-all-done = bf16[8,2,64,1536]{3,2,1,0:T(8,128)(2,1)} async-done(((bf16[8,2,64,1536]{3,2,1,0:T(8,128)(2,1)}), bf16[8,2,64,1536]{3,2,1,0:T(8,128)(2,1)}, u32[]{:S(2)}, u32[]{:S(2)}) %all-to-all-start) | async-done | bytes 3145760 | tf_op jit(solution)/shard_map/all_to_all | solution.py:36
  56.4 2.6 fusion
  59.1 2.2 copy.67
  61.3 3.0 %fusion.16 = bf16[2,512,1536]{2,1,0:T(8,128)(2,1)S(1)} fusion(f32[1536]{0:T(1024)S(1)} %copy-done.7, f32[2,512]{1,0:T(2,128)S(1)} %rsqrt.21, bf16[8,2,64,1536]{3,2,0,1:T(8,128)(2,1)S(1)} %copy.67), kind=kLoop, calls=%fused_computation.20 | loop fusion | flops 18874368 | bytes 6301696 | tf_op jit(solution)/shard_map/convert_element_type | solution.py:127
  64.3 1.3 collective-permute-start.1
  65.6 4.2 %fusion.4 = bf16[2,8,64,1536]{3,2,1,0:T(8,128)(2,1)S(1)} fusion(f32[1536]{0:T(1024)S(1)} %copy-done.7, f32[2,8,64]{2,1,0:T(8,128)S(1)} %add_rsqrt_fusion, bf16[8,2,64,1536]{3,2,1,0:T(8,128)(2,1)} %all-to-all-done), kind=kLoop, calls=%fused_computation.8 | loop fusion | flops 18874368 | bytes 6301696 | tf_op jit(solution)/shard_map/convert_element_type | solution.py:127
  69.8 2.2 fusion.59
  72.5 3.3 %collective-permute-start = (bf16[2,2,1536]{2,1,0:T(2,128)(2,1)S(1)}, bf16[2,2,1536]{2,1,0:T(2,128)(2,1)S(1)}, u32[]{:S(2)}, u32[]{:S(2)}) collective-permute-start(bf16[2,2,1536]{2,1,0:T(2,128)(2,1)S(1)} %get-tuple-element.5), channel_id=1, source_target_pairs={{0,8},{8,16},{16,24},{24,32},{32,40},{40,48},{48,56},{56,64},{64,7... | collective-permute-start | bytes 36872 | tf_op jit(solution)/shard_map/ppermute | solution.py:24
  75.9 3.2 %fusion.19 = f32[2,512,192]{1,2,0:T(8,128)S(1)} fusion(bf16[2,512,1536]{2,1,0:T(8,128)(2,1)} %copy-done.3, bf16[2,2,1536]{2,1,0:T(2,128)(2,1)S(1)} %collective-permute-done.1, bf16[5,192,1536]{2,1,0:T(8,128)(2,1)} %param.10), kind=kOutput, calls=%fused_computation.31 | convolution fusion | flops 610271232 | bytes 4534272 | tf_op jit(solution)/shard_map/std,ed->set/dot_general | solution.py:131
  81.5 1.3 fusion.49
  82.8 2.0 broadcast_in_dim.7
  84.8 4.5 %all-to-all-start.1 = ((bf16[8,2,192,512]{3,2,1,0:T(8,128)(2,1)}), bf16[8,2,192,512]{3,2,1,0:T(8,128)(2,1)}, u32[]{:S(2)}, u32[]{:S(2)}) async-start(bf16[8,2,192,512]{3,2,1,0:T(8,128)(2,1)} %broadcast_in_dim.7), calls=%async_computation.1 | async-start | bytes 6291456 | tf_op jit(solution)/shard_map/all_to_all | solution.py:36
  89.4 40.4 %all-to-all-done.1 = bf16[8,2,192,512]{3,2,1,0:T(8,128)(2,1)} async-done(((bf16[8,2,192,512]{3,2,1,0:T(8,128)(2,1)}), bf16[8,2,192,512]{3,2,1,0:T(8,128)(2,1)}, u32[]{:S(2)}, u32[]{:S(2)}) %all-to-all-start.1) | async-done | bytes 3145760 | tf_op jit(solution)/shard_map/all_to_all | solution.py:36
  129.9 2.5 multiply_reduce_fusion
  132.4 2.1 copy.69
  139.0 1.4 collective-permute-done.3
  141.5 2.7 fusion.46
  146.9 65.7 %all-gather.3.cloned.1.call-done = bf16[2,16,192,512]{3,2,1,0:T(8,128)(2,1)} async-done(((bf16[2,2,192,512]{3,2,1,0:T(8,128)(2,1)}), bf16[2,16,192,512]{3,2,1,0:T(8,128)(2,1)}) %all-gather.3.cloned.1.call-update) | async-done | bytes 6291472 | tf_op jit(solution)/shard_map/all_gather | solution.py:164
  212.6 27.0 %shard_map.82 = bf16[1,1024,192]{2,1,0:T(8,128)(2,1)} custom-call(bf16[1,1024,192]{2,1,0:T(8,128)(2,1)} %maximum_bitcast_fusion.query_ref, bf16[2,16,1,192,512]{4,3,2,1,0:T(8,128)(2,1)} %bitcast.76, bf16[2,16,1,192,512]{4,3,2,1,0:T(8,128)(2,1)} %bitcast.77), custom_call_target="tpu_custom_call" | custom-call | tf_op jit(solution)/shard_map/pallas_call | solution.py:83
  239.6 2.0 convolution_convert_fusion
  241.9 45.9 %all_to_all.15 = bf16[8,2,64,1536]{3,2,1,0:T(8,128)(2,1)S(1)} all-to-all(bf16[8,2,64,1536]{3,2,1,0:T(8,128)(2,1)S(1)} %bitcast.81), channel_id=1, replica_groups=mesh['chip_x'=2,'chip_z'=4,'core'=2,'peer_y'=4,'peer_x'=2] {'peer_y','pe..., dimensions={0} | all-to-all | bytes 6291456 | tf_op jit(solution)/shard_map/all_to_all | solution.py:177
  288.4 1.4 constant_dynamic-slice_fusion.2
  (53 shorter events, 13.2 us)
Async XLA Ops:
  6.5 233.1 %copy-start = (bf16[192,1536]{1,0:T(8,128)(2,1)S(1)}, bf16[192,1536]{1,0:T(8,128)(2,1)}, u32[]{:S(2)}) copy-start(bf16[192,1536]{1,0:T(8,128)(2,1)} %param.15) | copy-start | bytes 1769476
  9.6 46.8 %all-to-all-start = ((bf16[8,2,64,1536]{3,2,1,0:T(8,128)(2,1)}), bf16[8,2,64,1536]{3,2,1,0:T(8,128)(2,1)}, u32[]{:S(2)}, u32[]{:S(2)}) async-start(bf16[8,2,64,1536]{3,2,1,0:T(8,128)(2,1)} %broadcast_in_dim.6), calls=%async_computation | async-start | bytes 6291456 | tf_op jit(solution)/shard_map/all_to_all | solution.py:36
  59.1 2.2 copy-start.7
  64.3 5.6 %copy-start.3 = (bf16[2,512,1536]{2,1,0:T(8,128)(2,1)}, bf16[2,512,1536]{2,1,0:T(8,128)(2,1)S(1)}, u32[]{:S(2)}) copy-start(bf16[2,512,1536]{2,1,0:T(8,128)(2,1)S(1)} %fusion.16) | copy-start | bytes 9437188
  64.3 11.5 %collective-permute-start.1 = (bf16[2,2,1536]{2,1,0:T(2,128)(2,1)S(1)}, bf16[2,2,1536]{2,1,0:T(2,128)(2,1)S(1)}, u32[]{:S(2)}, u32[]{:S(2)}) collective-permute-start(bf16[2,2,1536]{2,1,0:T(2,128)(2,1)S(1)} %get-tuple-element.6), channel_id=1, source_target_pairs={{8,0},{16,8},{24,16},{32,24},{40,32},{48,40},{56,48},{64,56},{72,6... | collective-permute-start | bytes 36872 | tf_op jit(solution)/shard_map/ppermute | solution.py:26
  72.5 6.6 %copy-start.4 = (bf16[2,512,1536]{2,1,0:T(8,128)(2,1)S(1)}, bf16[2,512,1536]{2,1,0:T(8,128)(2,1)}, u32[]{:S(2)}) copy-start(bf16[2,512,1536]{2,1,0:T(8,128)(2,1)} %copy-done.3) | copy-start | bytes 9437188
  72.5 6.6 %copy-start.9 = (bf16[5,192,1536]{2,1,0:T(8,128)(2,1)S(1)}, bf16[5,192,1536]{2,1,0:T(8,128)(2,1)}, u32[]{:S(2)}) copy-start(bf16[5,192,1536]{2,1,0:T(8,128)(2,1)} %param.10) | copy-start | bytes 8847364
  72.5 7.7 %collective-permute-start = (bf16[2,2,1536]{2,1,0:T(2,128)(2,1)S(1)}, bf16[2,2,1536]{2,1,0:T(2,128)(2,1)S(1)}, u32[]{:S(2)}, u32[]{:S(2)}) collective-permute-start(bf16[2,2,1536]{2,1,0:T(2,128)(2,1)S(1)} %get-tuple-element.5), channel_id=1, source_target_pairs={{0,8},{8,16},{16,24},{24,32},{32,40},{40,48},{48,56},{56,64},{64,7... | collective-permute-start | bytes 36872 | tf_op jit(solution)/shard_map/ppermute | solution.py:24
  84.8 45.1 %all-to-all-start.1 = ((bf16[8,2,192,512]{3,2,1,0:T(8,128)(2,1)}), bf16[8,2,192,512]{3,2,1,0:T(8,128)(2,1)}, u32[]{:S(2)}, u32[]{:S(2)}) async-start(bf16[8,2,192,512]{3,2,1,0:T(8,128)(2,1)} %broadcast_in_dim.7), calls=%async_computation.1 | async-start | bytes 6291456 | tf_op jit(solution)/shard_map/all_to_all | solution.py:36
  89.2 123.4 %all-gather.3.cloned.1.call-start = ((), (), s32[]{:S(2)}) async-start(), calls=%async_computation.3 | async-start | bytes 7077888 | tf_op jit(solution)/shard_map/all_gather | solution.py:164
  132.4 2.1 copy-start.8
  134.6 1.7 copy-start.2
  134.6 1.7 copy-start.5
  136.3 2.3 copy-start.1
  136.3 1.5 copy-start.6
  137.7 3.7 %copy-start.10 = (bf16[192,1536]{1,0:T(8,128)(2,1)S(1)}, bf16[192,1536]{1,0:T(8,128)(2,1)}, u32[]{:S(2)}) copy-start(bf16[192,1536]{1,0:T(8,128)(2,1)} %param.12) | copy-start | bytes 1769476
  138.6 1.8 collective-permute-start.3
  144.3 1.6 collective-permute-start.2
  288.3 1.8 collective-permute-start.4
Sparse Core Ops, SparseCore 0:
  141.6 70.9 all-gather.2

commit v9 on v6

--- a/solution.py
+++ b/solution.py
@@ -119,6 +119,7 @@
     sample_count, own_rows, full_width = activations.shape
     tap_count, local_out, _ = conv_weight.shape
     flank_rows = tap_count // 2
+    full_output_weight = lax.all_gather(output_weight, "batch", axis=0, tiled=True)
     gathered_in = gather_batch(activations, 1)
     seq_rows = gathered_in.shape[1]
     active = jax.nn.gelu(normalize(gathered_in, conv_gain)).astype(jnp.bfloat16)
@@ -149,21 +150,27 @@
     value_rows = jnp.einsum(
         "sdt,ed->set", normed, value_weight, preferred_element_type=jnp.float32
     ).astype(jnp.bfloat16)
-    kv_tile = lax.all_gather(jnp.stack([key_rows, value_rows]), "seq", axis=1)
+    kv_rows, full_output_weight = lax.optimization_barrier(
+        (jnp.stack([key_rows, value_rows]), full_output_weight)
+    )
+    kv_tile = lax.all_gather(kv_rows, "seq", axis=1)
     attended = flash_attention(queries, kv_tile)
     row_start = lax.axis_index("batch") * own_rows
     own_hidden = jnp.transpose(
         lax.dynamic_slice_in_dim(hidden_full, row_start, own_rows, 2), (0, 2, 1)
     ).astype(jnp.float32)
     batch_count = lax.axis_size("batch")
-    partial_rows = jnp.einsum(
-        "ste,ef->tsf", attended, output_weight, preferred_element_type=jnp.float32
-    ).astype(jnp.bfloat16)
-    partial_rows = partial_rows.reshape(batch_count, own_rows, sample_count, full_width)
-    share_rows = jnp.sum(
-        lax.all_to_all(partial_rows, "batch", 0, 0, tiled=False).astype(jnp.float32), axis=0
+    head_width = attended.shape[2]
+    outgoing = jnp.transpose(
+        attended.reshape(sample_count, batch_count, own_rows, head_width), (1, 0, 2, 3)
     )
-    branch_rows = jnp.transpose(share_rows, (1, 0, 2))
+    arrived = lax.all_to_all(outgoing, "batch", 0, 0, tiled=False)
+    heads_side_by_side = jnp.transpose(arrived, (1, 2, 0, 3)).reshape(
+        sample_count, own_rows, batch_count * head_width
+    )
+    branch_rows = jnp.einsum(
+        "std,df->stf", heads_side_by_side, full_output_weight, preferred_element_type=jnp.float32
+    )
     result = own_hidden + branch_rows
     return result.astype(jnp.bfloat16)
 

time: 291 us -> 277 us (0.952)
  waiting for transfers between devices: 145 us -> 125 us
  blocking collectives: 43.2 us -> 50.9 us
    all_to_all x1, waiting for transfers between devices: 38.6 us -> 10.3 us  [shards(): arrived = lax.all_to_all(outgoing, 'batch', 0, 0, tiled=False)]
    all_to_all x1, blocking collectives: 43.2 us -> 50.9 us  [gather_batch(): lax.all_to_all(copies, 'batch', 0, 0, tiled=False)]
    all_to_all x1, waiting for transfers between devices: 39.8 us -> 45.5 us  [gather_batch(): lax.all_to_all(copies, 'batch', 0, 0, tiled=False)]
    all_gather x1 -> x2, waiting for transfers between devices: 66.8 us -> 68.4 us  [the longest x1 68.4 us: shards(): kv_tile = lax.all_gather(kv_rows, 'seq', axis=1)]
  transfers between devices with their start and end apart: 5 -> 6, of which waited for: 3 -> 3; matrix products, arithmetic and copies ran while one was open for 6% -> 12% of each run, Pallas kernels for 0% -> 0%
where the time goes in v9:
time: 277 us; the launch traced here: 276 us
  waiting for transfers between devices  125 us (45%)
  blocking collectives  50.9 us (18%)
  Pallas kernels  26.3 us (9%)
  matrix products  18.3 us (7%)
  starting transfers between devices  18.1 us (7%)
  between operations  13.7 us (5%)
  other arithmetic  12.5 us (5%)
  local copies, waits for them, and re-layouts  11.4 us (4%)
    all_gather x1, waiting for transfers between devices, shards(): kv_tile = lax.all_gather(kv_rows, 'seq', axis=1)  68.4 us
    all_to_all x1, blocking collectives, gather_batch(): lax.all_to_all(copies, 'batch', 0, 0, tiled=False)  50.9 us
    all_to_all x1, waiting for transfers between devices, gather_batch(): lax.all_to_all(copies, 'batch', 0, 0, tiled=False)  45.5 us
    pallas_call x1, Pallas kernels, flash_attention(): pl.pallas_call(flash_step, grid=(sample_count, source_count // sources_pe...  26.3 us
    all_to_all x1, waiting for transfers between devices, shards(): arrived = lax.all_to_all(outgoing, 'batch', 0, 0, tiled=False)  10.3 us
    dot_general x5, matrix products, shards(): jnp.einsum('std,ed->set', framed[:, offset:offset + seq_rows], conv_weigh...  9.14 us
    convert_element_type x2, other arithmetic, shards(): active = jax.nn.gelu(normalize(gathered_in, conv_gain)).astype(jnp.bfloat16)  7.48 us
    all_to_all x1, starting transfers between devices, gather_batch(): lax.all_to_all(copies, 'batch', 0, 0, tiled=False)  7.01 us
  transfers between devices with their start and end apart: 6, of which 3 were waited for; matrix products, arithmetic and copies ran while one was open for 12% of the time, Pallas kernels for 0%

profile of v9, /device:TPU:0, one launch (start us, length us, event | category | flops | bytes accessed | tf_op | source)
XLA Modules:
  0.0 276.1 jit_solution(17634972505270420978)
XLA Ops:
  6.5 3.0 %broadcast_in_dim.4 = bf16[8,2,64,1536]{3,2,1,0:T(8,128)(2,1)} broadcast(bf16[2,64,1536]{2,1,0:T(8,128)(2,1)} %param.8), dimensions={1,2,3} | broadcast | bytes 3538944 | tf_op jit(solution)/shard_map/broadcast_in_dim | solution.py:32
  9.6 7.0 %all-to-all-start = ((bf16[8,2,64,1536]{3,2,1,0:T(8,128)(2,1)}), bf16[8,2,64,1536]{3,2,1,0:T(8,128)(2,1)}, u32[]{:S(2)}, u32[]{:S(2)}) async-start(bf16[8,2,64,1536]{3,2,1,0:T(8,128)(2,1)} %broadcast_in_dim.4), calls=%async_computation | async-start | bytes 6291456 | tf_op jit(solution)/shard_map/all_to_all | solution.py:33
  17.4 45.5 %all-to-all-done = bf16[8,2,64,1536]{3,2,1,0:T(8,128)(2,1)} async-done(((bf16[8,2,64,1536]{3,2,1,0:T(8,128)(2,1)}), bf16[8,2,64,1536]{3,2,1,0:T(8,128)(2,1)}, u32[]{:S(2)}, u32[]{:S(2)}) %all-to-all-start) | async-done | bytes 3145760 | tf_op jit(solution)/shard_map/all_to_all | solution.py:33
  62.8 2.6 fusion
  65.5 2.2 copy.65
  67.7 3.0 %fusion.16 = bf16[2,512,1536]{2,1,0:T(8,128)(2,1)S(1)} fusion(f32[1536]{0:T(1024)S(1)} %copy-done.6, f32[2,512]{1,0:T(2,128)S(1)} %rsqrt.21, bf16[8,2,64,1536]{3,2,0,1:T(8,128)(2,1)S(1)} %copy.65), kind=kLoop, calls=%fused_computation.20 | loop fusion | flops 18874368 | bytes 6301696 | tf_op jit(solution)/shard_map/convert_element_type | solution.py:125
  70.8 1.3 collective-permute-start.1
  72.1 4.5 %fusion.4 = bf16[2,8,64,1536]{3,2,1,0:T(8,128)(2,1)S(1)} fusion(f32[1536]{0:T(1024)S(1)} %copy-done.6, f32[2,8,64]{2,1,0:T(8,128)S(1)} %add_rsqrt_fusion, bf16[8,2,64,1536]{3,2,1,0:T(8,128)(2,1)} %all-to-all-done), kind=kLoop, calls=%fused_computation.8 | loop fusion | flops 18874368 | bytes 6301696 | tf_op jit(solution)/shard_map/convert_element_type | solution.py:125
  76.5 2.2 fusion.65
  79.2 3.0 %collective-permute-start = (bf16[2,2,1536]{2,1,0:T(2,128)(2,1)S(1)}, bf16[2,2,1536]{2,1,0:T(2,128)(2,1)S(1)}, u32[]{:S(2)}, u32[]{:S(2)}) collective-permute-start(bf16[2,2,1536]{2,1,0:T(2,128)(2,1)S(1)} %get-tuple-element.9), channel_id=1, source_target_pairs={{0,8},{8,16},{16,24},{24,32},{32,40},{40,48},{48,56},{56,64},{64,7... | collective-permute-start | bytes 36872 | tf_op jit(solution)/shard_map/ppermute | solution.py:21
  82.3 3.3 %fusion.26 = f32[2,512,192]{1,2,0:T(8,128)S(1)} fusion(bf16[2,2,1536]{2,1,0:T(2,128)(2,1)S(1)} %collective-permute-done.1, bf16[2,512,1536]{2,1,0:T(8,128)(2,1)} %copy-done.3, bf16[5,192,1536]{2,1,0:T(8,128)(2,1)} %param.10), kind=kOutput, calls=%fused_computation.35 | convolution fusion | flops 610271232 | bytes 4534272 | tf_op jit(solution)/shard_map/std,ed->set/dot_general | solution.py:129
  85.6 1.2 fusion.28
  86.8 1.2 fusion.21
  88.0 1.3 fusion.57
  89.6 50.9 %all_to_all.15 = bf16[8,2,192,512]{3,2,1,0:T(8,128)(2,1)S(1)} all-to-all(bf16[8,2,192,512]{3,2,1,0:T(8,128)(2,1)S(1)} %broadcast_in_dim.5), channel_id=1, replica_groups=mesh['seq'=16,'batch'=8] {'batch'}, dimensions={0} | all-to-all | bytes 6291456 | tf_op jit(solution)/shard_map/all_to_all | solution.py:33
  144.6 1.0 pad_maximum_fusion.4
  145.6 3.7 %fusion.36.query_ref = bf16[2,512,192]{2,1,0:T(8,128)(2,1)} fusion(bf16[2,1536,512]{2,1,0:T(8,128)(2,1)} %copy-done.1, bf16[192,1536]{1,0:T(8,128)(2,1)S(1)} %copy-done.9), kind=kOutput, calls=%fused_computation.43 | convolution fusion | flops 604372992 | bytes 4128768 | tf_op jit(solution)/shard_map/sdt,ed->ste/dot_general | solution.py:144
  149.4 68.4 %all-gather.6.cloned.1.call-done = bf16[2,32,192,512]{3,2,1,0:T(8,128)(2,1)} async-done(((bf16[2,2,192,512]{3,2,1,0:T(8,128)(2,1)}), bf16[2,32,192,512]{3,2,1,0:T(8,128)(2,1)}) %all-gather.6.cloned.1.call-update) | async-done | bytes 12582928 | tf_op jit(solution)/shard_map/all_gather | solution.py:156
  217.8 26.3 %shard_map.82 = bf16[2,512,192]{2,1,0:T(8,128)(2,1)} custom-call(bf16[2,512,192]{2,1,0:T(8,128)(2,1)} %fusion.36.query_ref, bf16[2,16,2,192,512]{4,3,2,1,0:T(8,128)(2,1)} %bitcast.73, bf16[2,16,2,192,512]{4,3,2,1,0:T(8,128)(2,1)} %bitcast.74), custom_call_target="tpu_custom_call" | custom-call | tf_op jit(solution)/shard_map/pallas_call | solution.py:80
  244.0 1.9 copy.80
  245.9 6.7 %all-to-all-start.2 = ((bf16[8,2,64,192]{3,2,1,0:T(8,128)(2,1)}), bf16[8,2,64,192]{3,2,1,0:T(8,128)(2,1)S(1)}, u32[]{:S(2)}, u32[]{:S(2)}) async-start(bf16[8,2,64,192]{3,2,1,0:T(8,128)(2,1)} %bitcast.72), calls=%async_computation.2 | async-start | bytes 1048576 | tf_op jit(solution)/shard_map/all_to_all | solution.py:167
  252.6 1.4 constant_dynamic-slice_fusion
  254.3 10.3 %all-to-all-done.2 = bf16[8,2,64,192]{3,2,1,0:T(8,128)(2,1)S(1)} async-done(((bf16[8,2,64,192]{3,2,1,0:T(8,128)(2,1)}), bf16[8,2,64,192]{3,2,1,0:T(8,128)(2,1)S(1)}, u32[]{:S(2)}, u32[]{:S(2)}) %all-to-all-start.2) | async-done | bytes 393248 | tf_op jit(solution)/shard_map/all_to_all | solution.py:167
  265.4 3.9 %fusion.33 = bf16[2,64,1536]{2,1,0:T(8,128)(2,1)} fusion(bf16[2,64,1536]{2,1,0:T(8,128)(2,1)S(1)} %reshape.47, bf16[1536,1536]{1,0:T(8,128)(2,1)} %all-gather.4.cloned.1.call-done, bf16[2,1536,64]{1,2,0:T(8,128)(2,1)S(1)} %copy.75), kind=kOutput, calls=%fused_computation.41 | convolution fusion | flops 604569600 | bytes 5898240 | tf_op jit(solution)/shard_map/std,df->stf/dot_general | solution.py:171
  (42 shorter events, 6.7 us)
Async XLA Ops:
  6.5 135.8 %copy-start = (bf16[192,1536]{1,0:T(8,128)(2,1)S(1)}, bf16[192,1536]{1,0:T(8,128)(2,1)}, u32[]{:S(2)}) copy-start(bf16[192,1536]{1,0:T(8,128)(2,1)} %param.13) | copy-start | bytes 1769476
  9.6 53.3 %all-to-all-start = ((bf16[8,2,64,1536]{3,2,1,0:T(8,128)(2,1)}), bf16[8,2,64,1536]{3,2,1,0:T(8,128)(2,1)}, u32[]{:S(2)}, u32[]{:S(2)}) async-start(bf16[8,2,64,1536]{3,2,1,0:T(8,128)(2,1)} %broadcast_in_dim.4), calls=%async_computation | async-start | bytes 6291456 | tf_op jit(solution)/shard_map/all_to_all | solution.py:33
  16.6 129.0 %all-gather.4.cloned.1.call-start = ((), (), s32[]{:S(2)}) async-start(), calls=%async_computation.3 | async-start | bytes 5308416 | tf_op jit(solution)/shard_map/all_gather | solution.py:122
  17.3 200.4 %all-gather.6.cloned.1.call-start = ((), (), s32[]{:S(2)}) async-start(), calls=%async_computation.4 | async-start | bytes 13369344 | tf_op jit(solution)/shard_map/all_gather | solution.py:156
  65.5 2.2 copy-start.6
  70.7 5.8 %copy-start.3 = (bf16[2,512,1536]{2,1,0:T(8,128)(2,1)}, bf16[2,512,1536]{2,1,0:T(8,128)(2,1)S(1)}, u32[]{:S(2)}) copy-start(bf16[2,512,1536]{2,1,0:T(8,128)(2,1)S(1)} %fusion.16) | copy-start | bytes 9437188
  70.8 11.5 %collective-permute-start.1 = (bf16[2,2,1536]{2,1,0:T(2,128)(2,1)S(1)}, bf16[2,2,1536]{2,1,0:T(2,128)(2,1)S(1)}, u32[]{:S(2)}, u32[]{:S(2)}) collective-permute-start(bf16[2,2,1536]{2,1,0:T(2,128)(2,1)S(1)} %get-tuple-element.10), channel_id=1, source_target_pairs={{8,0},{16,8},{24,16},{32,24},{40,32},{48,40},{56,48},{64,56},{72,6... | collective-permute-start | bytes 36872 | tf_op jit(solution)/shard_map/ppermute | solution.py:23
  79.2 6.4 %copy-start.4 = (bf16[2,512,1536]{2,1,0:T(8,128)(2,1)S(1)}, bf16[2,512,1536]{2,1,0:T(8,128)(2,1)}, u32[]{:S(2)}) copy-start(bf16[2,512,1536]{2,1,0:T(8,128)(2,1)} %copy-done.3) | copy-start | bytes 9437188
  79.2 6.4 %copy-start.8 = (bf16[5,192,1536]{2,1,0:T(8,128)(2,1)S(1)}, bf16[5,192,1536]{2,1,0:T(8,128)(2,1)}, u32[]{:S(2)}) copy-start(bf16[5,192,1536]{2,1,0:T(8,128)(2,1)} %param.10) | copy-start | bytes 8847364
  79.2 6.3 %collective-permute-start = (bf16[2,2,1536]{2,1,0:T(2,128)(2,1)S(1)}, bf16[2,2,1536]{2,1,0:T(2,128)(2,1)S(1)}, u32[]{:S(2)}, u32[]{:S(2)}) collective-permute-start(bf16[2,2,1536]{2,1,0:T(2,128)(2,1)S(1)} %get-tuple-element.9), channel_id=1, source_target_pairs={{0,8},{8,16},{16,24},{24,32},{32,40},{40,48},{48,56},{56,64},{64,7... | collective-permute-start | bytes 36872 | tf_op jit(solution)/shard_map/ppermute | solution.py:21
  140.7 1.6 copy-start.2
  140.7 0.7 copy-start.7
  142.4 2.3 copy-start.1
  142.4 1.5 copy-start.5
  143.8 1.8 copy-start.9
  245.9 18.7 %all-to-all-start.2 = ((bf16[8,2,64,192]{3,2,1,0:T(8,128)(2,1)}), bf16[8,2,64,192]{3,2,1,0:T(8,128)(2,1)S(1)}, u32[]{:S(2)}, u32[]{:S(2)}) async-start(bf16[8,2,64,192]{3,2,1,0:T(8,128)(2,1)} %bitcast.72), calls=%async_computation.2 | async-start | bytes 1048576 | tf_op jit(solution)/shard_map/all_to_all | solution.py:167
Sparse Core Ops, SparseCore 0:
  19.7 120.4 all-gather.3
  145.7 71.9 all-gather.5

commit v10 on v9

--- a/solution.py
+++ b/solution.py
@@ -73,24 +73,26 @@
         out_ref[0] = (summed_ref[...] / total_ref[...]).astype(out_ref.dtype)
 
 
-def flash_attention(queries, kv_tile, sources_per_step=2):
-    sample_count, query_count, head_width = queries.shape
+def flash_attention(queries, kv_tile, sample, sources_per_step=2):
+    _, query_count, head_width = queries.shape
     _, source_count, _, _, source_rows = kv_tile.shape
     sources_per_step = math.gcd(source_count, sources_per_step)
     return pl.pallas_call(
         flash_step,
-        grid=(sample_count, source_count // sources_per_step),
+        grid=(1, source_count // sources_per_step),
         in_specs=[
-            pl.BlockSpec((1, query_count, head_width), lambda s, k: (s, 0, 0)),
+            pl.BlockSpec((1, query_count, head_width), lambda s, k: (sample, 0, 0)),
             pl.BlockSpec(
-                (1, sources_per_step, 1, head_width, source_rows), lambda s, k: (0, k, s, 0, 0)
+                (1, sources_per_step, 1, head_width, source_rows),
+                lambda s, k: (0, k, sample, 0, 0),
             ),
             pl.BlockSpec(
-                (1, sources_per_step, 1, head_width, source_rows), lambda s, k: (1, k, s, 0, 0)
+                (1, sources_per_step, 1, head_width, source_rows),
+                lambda s, k: (1, k, sample, 0, 0),
             ),
         ],
-        out_specs=pl.BlockSpec((1, query_count, head_width), lambda s, k: (s, 0, 0)),
-        out_shape=jax.ShapeDtypeStruct(queries.shape, jnp.bfloat16),
+        out_specs=pl.BlockSpec((1, query_count, head_width), lambda s, k: (0, 0, 0)),
+        out_shape=jax.ShapeDtypeStruct((1, query_count, head_width), jnp.bfloat16),
         scratch_shapes=[
             pltpu.VMEM((query_count, 1), jnp.float32),
             pltpu.VMEM((query_count, 1), jnp.float32),
@@ -154,25 +156,26 @@
         (jnp.stack([key_rows, value_rows]), full_output_weight)
     )
     kv_tile = lax.all_gather(kv_rows, "seq", axis=1)
-    attended = flash_attention(queries, kv_tile)
     row_start = lax.axis_index("batch") * own_rows
     own_hidden = jnp.transpose(
         lax.dynamic_slice_in_dim(hidden_full, row_start, own_rows, 2), (0, 2, 1)
     ).astype(jnp.float32)
     batch_count = lax.axis_size("batch")
-    head_width = attended.shape[2]
-    outgoing = jnp.transpose(
-        attended.reshape(sample_count, batch_count, own_rows, head_width), (1, 0, 2, 3)
-    )
-    arrived = lax.all_to_all(outgoing, "batch", 0, 0, tiled=False)
-    heads_side_by_side = jnp.transpose(arrived, (1, 2, 0, 3)).reshape(
-        sample_count, own_rows, batch_count * head_width
-    )
-    branch_rows = jnp.einsum(
-        "std,df->stf", heads_side_by_side, full_output_weight, preferred_element_type=jnp.float32
-    )
-    result = own_hidden + branch_rows
-    return result.astype(jnp.bfloat16)
+    pieces = []
+    for sample in range(sample_count):
+        attended = flash_attention(queries, kv_tile, sample)[0]
+        head_width = attended.shape[1]
+        arrived = lax.all_to_all(
+            attended.reshape(batch_count, own_rows, head_width), "batch", 0, 0, tiled=False
+        )
+        heads_side_by_side = jnp.transpose(arrived, (1, 0, 2)).reshape(
+            own_rows, batch_count * head_width
+        )
+        branch_rows = jnp.dot(
+            heads_side_by_side, full_output_weight, preferred_element_type=jnp.float32
+        )
+        pieces.append((own_hidden[sample] + branch_rows).astype(jnp.bfloat16))
+    return jnp.stack(pieces)
 
 
 def solution(mesh):

time: 277 us -> 285 us (1.029)
  starting transfers between devices: 18.1 us -> 25.3 us
    all_to_all x1 -> x2, starting transfers between devices: 6.71 us -> 13.9 us  [shards(): lax.all_to_all(attended.reshape(batch_count, own_rows, head_width), 'batc...]
    dot_general x1 -> x2, matrix products: 3.87 us -> 6.53 us  [shards(): jnp.dot(heads_side_by_side, full_output_weight, preferred_element_type=jn...]
    all_to_all x1 -> x2, waiting for transfers between devices: 10.3 us -> 8.32 us  [shards(): lax.all_to_all(attended.reshape(batch_count, own_rows, head_width), 'batc...]
    pallas_call x1 -> x2, Pallas kernels: 26.3 us -> 27.9 us  [flash_attention(): pl.pallas_call(flash_step, grid=(1, source_count // sources_per_step), in...]
  transfers between devices with their start and end apart: 6 -> 7, of which waited for: 3 -> 3; matrix products, arithmetic and copies ran while one was open for 12% -> 11% of each run, Pallas kernels for 0% -> 5%
where the time goes in v10:
time: 285 us
  waiting for transfers between devices  123 us (43%)
  blocking collectives  50.9 us (18%)
  Pallas kernels  27.9 us (10%)
  starting transfers between devices  25.3 us (9%)
  matrix products  21 us (7%)
  between operations  13.7 us (5%)
  other arithmetic  13.3 us (5%)
  local copies, waits for them, and re-layouts  9.61 us (3%)
    all_gather x1, waiting for transfers between devices, shards(): kv_tile = lax.all_gather(kv_rows, 'seq', axis=1)  68.4 us
    all_to_all x1, blocking collectives, gather_batch(): lax.all_to_all(copies, 'batch', 0, 0, tiled=False)  50.9 us
    all_to_all x1, waiting for transfers between devices, gather_batch(): lax.all_to_all(copies, 'batch', 0, 0, tiled=False)  45.5 us
    pallas_call x2, Pallas kernels, flash_attention(): pl.pallas_call(flash_step, grid=(1, source_count // sources_per_step), in...  27.9 us
    all_to_all x2, starting transfers between devices, shards(): lax.all_to_all(attended.reshape(batch_count, own_rows, head_width), 'batc...  13.9 us
    dot_general x5, matrix products, shards(): jnp.einsum('std,ed->set', framed[:, offset:offset + seq_rows], conv_weigh...  9.14 us
    all_to_all x2, waiting for transfers between devices, shards(): lax.all_to_all(attended.reshape(batch_count, own_rows, head_width), 'batc...  8.32 us
    convert_element_type x2, other arithmetic, shards(): active = jax.nn.gelu(normalize(gathered_in, conv_gain)).astype(jnp.bfloat16)  7.48 us
  transfers between devices with their start and end apart: 7, of which 3 were waited for; matrix products, arithmetic and copies ran while one was open for 11% of the time, Pallas kernels for 5%

profile of v10, /device:TPU:0, one launch (start us, length us, event | category | flops | bytes accessed | tf_op | source)
XLA Modules:
  0.0 284.6 jit_solution(17519573685247850112)
XLA Ops:
  6.5 3.1 %broadcast_in_dim.4 = bf16[8,2,64,1536]{3,2,1,0:T(8,128)(2,1)} broadcast(bf16[2,64,1536]{2,1,0:T(8,128)(2,1)} %param.8), dimensions={1,2,3} | broadcast | bytes 3538944 | tf_op jit(solution)/shard_map/broadcast_in_dim | solution.py:32
  9.6 7.0 %all-to-all-start = ((bf16[8,2,64,1536]{3,2,1,0:T(8,128)(2,1)}), bf16[8,2,64,1536]{3,2,1,0:T(8,128)(2,1)}, u32[]{:S(2)}, u32[]{:S(2)}) async-start(bf16[8,2,64,1536]{3,2,1,0:T(8,128)(2,1)} %broadcast_in_dim.4), calls=%async_computation | async-start | bytes 6291456 | tf_op jit(solution)/shard_map/all_to_all | solution.py:33
  17.4 45.5 %all-to-all-done = bf16[8,2,64,1536]{3,2,1,0:T(8,128)(2,1)} async-done(((bf16[8,2,64,1536]{3,2,1,0:T(8,128)(2,1)}), bf16[8,2,64,1536]{3,2,1,0:T(8,128)(2,1)}, u32[]{:S(2)}, u32[]{:S(2)}) %all-to-all-start) | async-done | bytes 3145760 | tf_op jit(solution)/shard_map/all_to_all | solution.py:33
  62.9 2.6 fusion
  65.5 2.2 copy.64
  67.7 3.0 %fusion.16 = bf16[2,512,1536]{2,1,0:T(8,128)(2,1)S(1)} fusion(f32[1536]{0:T(1024)S(1)} %copy-done.6, f32[2,512]{1,0:T(2,128)S(1)} %rsqrt.21, bf16[8,2,64,1536]{3,2,0,1:T(8,128)(2,1)S(1)} %copy.64), kind=kLoop, calls=%fused_computation.20 | loop fusion | flops 18874368 | bytes 6301696 | tf_op jit(solution)/shard_map/convert_element_type | solution.py:127
  70.8 1.3 collective-permute-start.1
  72.1 4.5 %fusion.4 = bf16[2,8,64,1536]{3,2,1,0:T(8,128)(2,1)S(1)} fusion(f32[1536]{0:T(1024)S(1)} %copy-done.6, f32[2,8,64]{2,1,0:T(8,128)S(1)} %add_rsqrt_fusion, bf16[8,2,64,1536]{3,2,1,0:T(8,128)(2,1)} %all-to-all-done), kind=kLoop, calls=%fused_computation.8 | loop fusion | flops 18874368 | bytes 6301696 | tf_op jit(solution)/shard_map/convert_element_type | solution.py:127
  76.6 2.2 fusion.61
  79.3 3.0 %collective-permute-start = (bf16[2,2,1536]{2,1,0:T(2,128)(2,1)S(1)}, bf16[2,2,1536]{2,1,0:T(2,128)(2,1)S(1)}, u32[]{:S(2)}, u32[]{:S(2)}) collective-permute-start(bf16[2,2,1536]{2,1,0:T(2,128)(2,1)S(1)} %get-tuple-element.9), channel_id=1, source_target_pairs={{0,8},{8,16},{16,24},{24,32},{32,40},{40,48},{48,56},{56,64},{64,7... | collective-permute-start | bytes 36872 | tf_op jit(solution)/shard_map/ppermute | solution.py:21
  82.3 3.3 %fusion.24 = f32[2,512,192]{1,2,0:T(8,128)S(1)} fusion(bf16[2,2,1536]{2,1,0:T(2,128)(2,1)S(1)} %collective-permute-done.1, bf16[2,512,1536]{2,1,0:T(8,128)(2,1)} %copy-done.3, bf16[5,192,1536]{2,1,0:T(8,128)(2,1)} %param.10), kind=kOutput, calls=%fused_computation.33 | convolution fusion | flops 610271232 | bytes 4534272 | tf_op jit(solution)/shard_map/std,ed->set/dot_general | solution.py:131
  86.8 1.2 fusion.19
  88.0 1.3 fusion.53
  89.6 50.9 %all_to_all.20 = bf16[8,2,192,512]{3,2,1,0:T(8,128)(2,1)S(1)} all-to-all(bf16[8,2,192,512]{3,2,1,0:T(8,128)(2,1)S(1)} %broadcast_in_dim.5), channel_id=1, replica_groups=mesh['seq'=16,'batch'=8] {'batch'}, dimensions={0} | all-to-all | bytes 6291456 | tf_op jit(solution)/shard_map/all_to_all | solution.py:33
  145.6 3.8 %fusion.32.query_ref = bf16[2,512,192]{2,1,0:T(8,128)(2,1)} fusion(bf16[2,1536,512]{2,1,0:T(8,128)(2,1)} %copy-done.1, bf16[192,1536]{1,0:T(8,128)(2,1)S(1)} %copy-done.9), kind=kOutput, calls=%fused_computation.45 | convolution fusion | flops 604372992 | bytes 4128768 | tf_op jit(solution)/shard_map/sdt,ed->ste/dot_general | solution.py:146
  149.4 68.4 %all-gather.6.cloned.1.call-done = bf16[2,32,192,512]{3,2,1,0:T(8,128)(2,1)} async-done(((bf16[2,2,192,512]{3,2,1,0:T(8,128)(2,1)}), bf16[2,32,192,512]{3,2,1,0:T(8,128)(2,1)}) %all-gather.6.cloned.1.call-update) | async-done | bytes 12582928 | tf_op jit(solution)/shard_map/all_gather | solution.py:158
  217.8 13.9 %shard_map.83 = bf16[1,512,192]{2,1,0:T(8,128)(2,1)} custom-call(bf16[2,512,192]{2,1,0:T(8,128)(2,1)} %fusion.32.query_ref, bf16[2,16,2,192,512]{4,3,2,1,0:T(8,128)(2,1)} %bitcast.78, bf16[2,16,2,192,512]{4,3,2,1,0:T(8,128)(2,1)} %bitcast.79), custom_call_target="tpu_custom_call" | custom-call | tf_op jit(solution)/shard_map/pallas_call | solution.py:80
  231.7 6.7 %all-to-all-start.3 = ((bf16[8,64,192]{2,1,0:T(8,128)(2,1)}), bf16[8,64,192]{2,1,0:T(8,128)(2,1)S(1)}, u32[]{:S(2)}, u32[]{:S(2)}) async-start(bf16[8,64,192]{2,1,0:T(8,128)(2,1)} %bitcast.86), calls=%async_computation.3 | async-start | bytes 524288 | tf_op jit(solution)/shard_map/all_to_all | solution.py:168
  238.4 1.4 constant_dynamic-slice_fusion
  240.1 13.9 %shard_map.82 = bf16[1,512,192]{2,1,0:T(8,128)(2,1)} custom-call(bf16[2,512,192]{2,1,0:T(8,128)(2,1)} %fusion.32.query_ref, bf16[2,16,2,192,512]{4,3,2,1,0:T(8,128)(2,1)} %bitcast.80, bf16[2,16,2,192,512]{4,3,2,1,0:T(8,128)(2,1)} %bitcast.81), custom_call_target="tpu_custom_call" | custom-call | tf_op jit(solution)/shard_map/pallas_call | solution.py:80
  254.0 7.2 %all-to-all-start.2 = ((bf16[8,64,192]{2,1,0:T(8,128)(2,1)}), bf16[8,64,192]{2,1,0:T(8,128)(2,1)S(1)}, u32[]{:S(2)}, u32[]{:S(2)}) async-start(bf16[8,64,192]{2,1,0:T(8,128)(2,1)} %bitcast.85), calls=%async_computation.2 | async-start | bytes 524288 | tf_op jit(solution)/shard_map/all_to_all | solution.py:168
  261.7 8.3 %all-to-all-done.2 = bf16[8,64,192]{2,1,0:T(8,128)(2,1)S(1)} async-done(((bf16[8,64,192]{2,1,0:T(8,128)(2,1)}), bf16[8,64,192]{2,1,0:T(8,128)(2,1)S(1)}, u32[]{:S(2)}, u32[]{:S(2)}) %all-to-all-start.2) | async-done | bytes 196640 | tf_op jit(solution)/shard_map/all_to_all | solution.py:168
  270.4 3.3 %fusion.30 = bf16[1,64,1536]{2,1,0:T(8,128)(2,1)S(1)} fusion(bf16[64,1536]{1,0:T(8,128)(2,1)S(1)} %reshape.47, bf16[1536,1536]{1,0:T(8,128)(2,1)} %all-gather.4.cloned.1.call-done, f32[2,64,1536]{2,1,0:T(8,128)S(1)} %convert_bitcast_fusion), kind=kOutput, calls=%fused_computation.42 | convolution fusion | flops 302186496 | bytes 5505024 | tf_op jit(solution)/shard_map/dot_general | solution.py:174
  273.7 3.3 %fusion.31 = bf16[1,64,1536]{2,1,0:T(8,128)(2,1)S(1)} fusion(bf16[64,1536]{1,0:T(8,128)(2,1)S(1)} %reshape.46, bf16[1536,1536]{1,0:T(8,128)(2,1)} %all-gather.4.cloned.1.call-done, f32[2,64,1536]{2,1,0:T(8,128)S(1)} %convert_bitcast_fusion), kind=kOutput, calls=%fused_computation.43 | convolution fusion | flops 302186496 | bytes 5505024 | tf_op jit(solution)/shard_map/dot_general | solution.py:174
  (49 shorter events, 9.8 us)
Async XLA Ops:
  6.5 135.8 %copy-start = (bf16[192,1536]{1,0:T(8,128)(2,1)S(1)}, bf16[192,1536]{1,0:T(8,128)(2,1)}, u32[]{:S(2)}) copy-start(bf16[192,1536]{1,0:T(8,128)(2,1)} %param.13) | copy-start | bytes 1769476
  9.6 53.3 %all-to-all-start = ((bf16[8,2,64,1536]{3,2,1,0:T(8,128)(2,1)}), bf16[8,2,64,1536]{3,2,1,0:T(8,128)(2,1)}, u32[]{:S(2)}, u32[]{:S(2)}) async-start(bf16[8,2,64,1536]{3,2,1,0:T(8,128)(2,1)} %broadcast_in_dim.4), calls=%async_computation | async-start | bytes 6291456 | tf_op jit(solution)/shard_map/all_to_all | solution.py:33
  16.6 129.0 %all-gather.4.cloned.1.call-start = ((), (), s32[]{:S(2)}) async-start(), calls=%async_computation.4 | async-start | bytes 5308416 | tf_op jit(solution)/shard_map/all_gather | solution.py:124
  17.3 200.4 %all-gather.6.cloned.1.call-start = ((), (), s32[]{:S(2)}) async-start(), calls=%async_computation.5 | async-start | bytes 13369344 | tf_op jit(solution)/shard_map/all_gather | solution.py:158
  65.5 2.2 copy-start.6
  70.7 5.8 %copy-start.3 = (bf16[2,512,1536]{2,1,0:T(8,128)(2,1)}, bf16[2,512,1536]{2,1,0:T(8,128)(2,1)S(1)}, u32[]{:S(2)}) copy-start(bf16[2,512,1536]{2,1,0:T(8,128)(2,1)S(1)} %fusion.16) | copy-start | bytes 9437188
  70.8 11.5 %collective-permute-start.1 = (bf16[2,2,1536]{2,1,0:T(2,128)(2,1)S(1)}, bf16[2,2,1536]{2,1,0:T(2,128)(2,1)S(1)}, u32[]{:S(2)}, u32[]{:S(2)}) collective-permute-start(bf16[2,2,1536]{2,1,0:T(2,128)(2,1)S(1)} %get-tuple-element.10), channel_id=1, source_target_pairs={{8,0},{16,8},{24,16},{32,24},{40,32},{48,40},{56,48},{64,56},{72,6... | collective-permute-start | bytes 36872 | tf_op jit(solution)/shard_map/ppermute | solution.py:23
  79.2 6.4 %copy-start.4 = (bf16[2,512,1536]{2,1,0:T(8,128)(2,1)S(1)}, bf16[2,512,1536]{2,1,0:T(8,128)(2,1)}, u32[]{:S(2)}) copy-start(bf16[2,512,1536]{2,1,0:T(8,128)(2,1)} %copy-done.3) | copy-start | bytes 9437188
  79.2 6.4 %copy-start.8 = (bf16[5,192,1536]{2,1,0:T(8,128)(2,1)S(1)}, bf16[5,192,1536]{2,1,0:T(8,128)(2,1)}, u32[]{:S(2)}) copy-start(bf16[5,192,1536]{2,1,0:T(8,128)(2,1)} %param.10) | copy-start | bytes 8847364
  79.3 6.3 %collective-permute-start = (bf16[2,2,1536]{2,1,0:T(2,128)(2,1)S(1)}, bf16[2,2,1536]{2,1,0:T(2,128)(2,1)S(1)}, u32[]{:S(2)}, u32[]{:S(2)}) collective-permute-start(bf16[2,2,1536]{2,1,0:T(2,128)(2,1)S(1)} %get-tuple-element.9), channel_id=1, source_target_pairs={{0,8},{8,16},{16,24},{24,32},{32,40},{40,48},{48,56},{56,64},{64,7... | collective-permute-start | bytes 36872 | tf_op jit(solution)/shard_map/ppermute | solution.py:21
  140.7 1.6 copy-start.2
  140.8 0.7 copy-start.7
  142.4 2.3 copy-start.1
  142.4 1.5 copy-start.5
  143.8 1.8 copy-start.9
  231.7 22.3 %all-to-all-start.3 = ((bf16[8,64,192]{2,1,0:T(8,128)(2,1)}), bf16[8,64,192]{2,1,0:T(8,128)(2,1)S(1)}, u32[]{:S(2)}, u32[]{:S(2)}) async-start(bf16[8,64,192]{2,1,0:T(8,128)(2,1)} %bitcast.86), calls=%async_computation.3 | async-start | bytes 524288 | tf_op jit(solution)/shard_map/all_to_all | solution.py:168
  254.0 16.0 %all-to-all-start.2 = ((bf16[8,64,192]{2,1,0:T(8,128)(2,1)}), bf16[8,64,192]{2,1,0:T(8,128)(2,1)S(1)}, u32[]{:S(2)}, u32[]{:S(2)}) async-start(bf16[8,64,192]{2,1,0:T(8,128)(2,1)} %bitcast.85), calls=%async_computation.2 | async-start | bytes 524288 | tf_op jit(solution)/shard_map/all_to_all | solution.py:168
Sparse Core Ops, SparseCore 0:
  19.7 120.4 all-gather.3
  145.7 71.9 all-gather.5

commit v11 on v9

--- a/solution.py
+++ b/solution.py
@@ -29,8 +29,9 @@
 
 def gather_batch(block, axis):
     count = lax.axis_size("batch")
-    copies = jnp.broadcast_to(block[None], (count,) + block.shape)
-    arrived = jnp.moveaxis(lax.all_to_all(copies, "batch", 0, 0, tiled=False), 0, axis)
+    spread = block.shape[:axis] + (count,) + block.shape[axis:]
+    copies = jnp.broadcast_to(jnp.expand_dims(block, axis), spread)
+    arrived = lax.all_to_all(copies, "batch", axis, axis, tiled=False)
     return arrived.reshape(block.shape[:axis] + (count * block.shape[axis],) + block.shape[axis + 1 :])
 
 
@@ -122,7 +123,9 @@
     full_output_weight = lax.all_gather(output_weight, "batch", axis=0, tiled=True)
     gathered_in = gather_batch(activations, 1)
     seq_rows = gathered_in.shape[1]
-    active = jax.nn.gelu(normalize(gathered_in, conv_gain)).astype(jnp.bfloat16)
+    active = lax.optimization_barrier(
+        jax.nn.gelu(normalize(gathered_in, conv_gain)).astype(jnp.bfloat16)
+    )
     framed = with_halo(active, (("seq", 1),), flank_rows)
     conv_sum = jnp.zeros((sample_count, local_out, seq_rows), jnp.float32)
     for offset in range(tap_count):

time: 277 us -> 274 us (0.989)
  waiting for transfers between devices: 125 us -> 129 us
  matrix products: 18.3 us -> 15.1 us
  other arithmetic: 12.5 us -> 9.37 us
    dot_general x5, matrix products: 9.14 us -> 5.96 us  [shards(): jnp.einsum('std,ed->set', framed[:, offset:offset + seq_rows], conv_weigh...]
    convert_element_type x2 -> x1, other arithmetic: 7.48 us -> 4.36 us  [shards(): jax.nn.gelu(normalize(gathered_in, conv_gain)).astype(jnp.bfloat16)]
  transfers between devices with their start and end apart: 6 -> 6, of which waited for: 3 -> 4; matrix products, arithmetic and copies ran while one was open for 12% -> 9% of each run, Pallas kernels for 0% -> 0%
where the time goes in v11:
time: 274 us; the launch traced here: 273 us
  waiting for transfers between devices  129 us (47%)
  blocking collectives  50.5 us (18%)
  Pallas kernels  26.3 us (10%)
  starting transfers between devices  16.4 us (6%)
  matrix products  15.1 us (6%)
  between operations  13.6 us (5%)
  local copies, waits for them, and re-layouts  13.1 us (5%)
  other arithmetic  9.37 us (3%)
    all_gather x1, waiting for transfers between devices, shards(): kv_tile = lax.all_gather(kv_rows, 'seq', axis=1)  69.8 us
    all_to_all x1, blocking collectives, gather_batch(): arrived = lax.all_to_all(copies, 'batch', axis, axis, tiled=False)  50.5 us
    all_to_all x1, waiting for transfers between devices, gather_batch(): arrived = lax.all_to_all(copies, 'batch', axis, axis, tiled=False)  45.5 us
    pallas_call x1, Pallas kernels, flash_attention(): pl.pallas_call(flash_step, grid=(sample_count, source_count // sources_pe...  26.3 us
    all_to_all x1, waiting for transfers between devices, shards(): arrived = lax.all_to_all(outgoing, 'batch', 0, 0, tiled=False)  10.3 us
    all_to_all x1, starting transfers between devices, gather_batch(): arrived = lax.all_to_all(copies, 'batch', axis, axis, tiled=False)  7.01 us
    all_to_all x1, starting transfers between devices, shards(): arrived = lax.all_to_all(outgoing, 'batch', 0, 0, tiled=False)  6.7 us
    dot_general x5, matrix products, shards(): jnp.einsum('std,ed->set', framed[:, offset:offset + seq_rows], conv_weigh...  5.96 us
  transfers between devices with their start and end apart: 6, of which 4 were waited for; matrix products, arithmetic and copies ran while one was open for 9% of the time, Pallas kernels for 0%

profile of v11, /device:TPU:0, one launch (start us, length us, event | category | flops | bytes accessed | tf_op | source)
XLA Modules:
  0.0 273.5 jit_solution(15539304248499924963)
XLA Ops:
  6.5 3.0 %broadcast_in_dim.4 = bf16[2,8,64,1536]{3,2,0,1:T(8,128)(2,1)} broadcast(bf16[2,64,1536]{2,1,0:T(8,128)(2,1)} %param.8), dimensions={0,2,3} | broadcast | bytes 3538944 | tf_op jit(solution)/shard_map/broadcast_in_dim | solution.py:33
  9.6 7.0 %all-to-all-start = ((bf16[2,8,64,1536]{3,2,0,1:T(8,128)(2,1)}), bf16[2,8,64,1536]{3,2,0,1:T(8,128)(2,1)}, u32[]{:S(2)}, u32[]{:S(2)}) async-start(bf16[2,8,64,1536]{3,2,0,1:T(8,128)(2,1)} %broadcast_in_dim.4), calls=%async_computation | async-start | bytes 6291456 | tf_op jit(solution)/shard_map/all_to_all | solution.py:34
  17.4 45.5 %all-to-all-done = bf16[2,8,64,1536]{3,2,0,1:T(8,128)(2,1)} async-done(((bf16[2,8,64,1536]{3,2,0,1:T(8,128)(2,1)}), bf16[2,8,64,1536]{3,2,0,1:T(8,128)(2,1)}, u32[]{:S(2)}, u32[]{:S(2)}) %all-to-all-start) | async-done | bytes 3145760 | tf_op jit(solution)/shard_map/all_to_all | solution.py:34
  62.8 2.6 multiply_reduce_fusion.1
  65.5 2.2 copy.78
  67.7 1.6 copy-done.3
  69.8 4.4 %fusion.7 = bf16[2,512,1536]{2,1,0:T(8,128)(2,1)S(1)} fusion(f32[1536]{0:T(1024)S(1)} %copy-done.5, f32[2,512]{1,0:T(2,128)S(1)} %rsqrt.20, bf16[2,8,64,1536]{3,2,1,0:T(8,128)(2,1)} %copy-done.3), kind=kLoop, calls=%fused_computation.8 | loop fusion | flops 18874368 | bytes 6301696 | tf_op jit(solution)/shard_map/convert_element_type | solution.py:127
  74.2 1.3 collective-permute-start
  75.5 1.3 collective-permute-start.1
  76.8 1.2 fusion.55
  78.0 2.7 %collective-permute-done.1 = bf16[2,2,1536]{2,1,0:T(2,128)(2,1)S(1)} collective-permute-done((bf16[2,2,1536]{2,1,0:T(2,128)(2,1)S(1)}, bf16[2,2,1536]{2,1,0:T(2,128)(2,1)S(1)}, u32[]{:S(2)}, u32[]{:S(2)}) %collective-permute-start.1) | collective-permute-done | bytes 12320 | tf_op jit(solution)/shard_map/ppermute | solution.py:23
  80.7 1.2 fusion.16
  81.9 1.2 fusion.18
  83.1 1.2 fusion.11
  84.3 1.3 fusion.47
  85.9 50.5 %all_to_all.15 = bf16[2,8,192,512]{3,2,0,1:T(8,128)(2,1)S(1)} all-to-all(bf16[2,8,192,512]{3,2,0,1:T(8,128)(2,1)S(1)} %broadcast_in_dim.5), channel_id=1, replica_groups=mesh['seq'=16,'batch'=8] {'batch'}, dimensions={1} | all-to-all | bytes 6291456 | tf_op jit(solution)/shard_map/all_to_all | solution.py:34
  141.6 3.7 %fusion.26.query_ref = bf16[2,512,192]{2,1,0:T(8,128)(2,1)} fusion(bf16[2,1536,512]{2,1,0:T(8,128)(2,1)} %copy-done.1, bf16[192,1536]{1,0:T(8,128)(2,1)S(1)} %copy-done.8), kind=kOutput, calls=%fused_computation.31 | convolution fusion | flops 604372992 | bytes 4128768 | tf_op jit(solution)/shard_map/sdt,ed->ste/dot_general | solution.py:147
  145.4 69.8 %all-gather.6.cloned.1.call-done = bf16[2,32,192,512]{3,2,1,0:T(8,128)(2,1)} async-done(((bf16[2,2,192,512]{3,2,1,0:T(8,128)(2,1)}), bf16[2,32,192,512]{3,2,1,0:T(8,128)(2,1)}) %all-gather.6.cloned.1.call-update) | async-done | bytes 12582928 | tf_op jit(solution)/shard_map/all_gather | solution.py:159
  215.2 26.3 %shard_map.82 = bf16[2,512,192]{2,1,0:T(8,128)(2,1)} custom-call(bf16[2,512,192]{2,1,0:T(8,128)(2,1)} %fusion.26.query_ref, bf16[2,16,2,192,512]{4,3,2,1,0:T(8,128)(2,1)} %bitcast.65, bf16[2,16,2,192,512]{4,3,2,1,0:T(8,128)(2,1)} %bitcast.66), custom_call_target="tpu_custom_call" | custom-call | tf_op jit(solution)/shard_map/pallas_call | solution.py:81
  241.4 1.9 copy.96
  243.3 6.7 %all-to-all-start.2 = ((bf16[8,2,64,192]{3,2,1,0:T(8,128)(2,1)}), bf16[8,2,64,192]{3,2,1,0:T(8,128)(2,1)S(1)}, u32[]{:S(2)}, u32[]{:S(2)}) async-start(bf16[8,2,64,192]{3,2,1,0:T(8,128)(2,1)} %bitcast.64), calls=%async_computation.2 | async-start | bytes 1048576 | tf_op jit(solution)/shard_map/all_to_all | solution.py:170
  250.0 1.4 constant_dynamic-slice_fusion
  251.7 10.3 %all-to-all-done.2 = bf16[8,2,64,192]{3,2,1,0:T(8,128)(2,1)S(1)} async-done(((bf16[8,2,64,192]{3,2,1,0:T(8,128)(2,1)}), bf16[8,2,64,192]{3,2,1,0:T(8,128)(2,1)S(1)}, u32[]{:S(2)}, u32[]{:S(2)}) %all-to-all-start.2) | async-done | bytes 393248 | tf_op jit(solution)/shard_map/all_to_all | solution.py:170
  262.8 3.9 %fusion.23 = bf16[2,64,1536]{2,1,0:T(8,128)(2,1)} fusion(bf16[2,64,1536]{2,1,0:T(8,128)(2,1)S(1)} %reshape.44, bf16[1536,1536]{1,0:T(8,128)(2,1)} %all-gather.4.cloned.1.call-done, bf16[2,1536,64]{1,2,0:T(8,128)(2,1)S(1)} %copy.89), kind=kOutput, calls=%fused_computation.29 | convolution fusion | flops 604569600 | bytes 5898240 | tf_op jit(solution)/shard_map/std,df->stf/dot_general | solution.py:174
  (39 shorter events, 7.7 us)
Async XLA Ops:
  6.5 131.8 %copy-start = (bf16[192,1536]{1,0:T(8,128)(2,1)S(1)}, bf16[192,1536]{1,0:T(8,128)(2,1)}, u32[]{:S(2)}) copy-start(bf16[192,1536]{1,0:T(8,128)(2,1)} %param.13) | copy-start | bytes 1769476
  9.6 53.3 %all-to-all-start = ((bf16[2,8,64,1536]{3,2,0,1:T(8,128)(2,1)}), bf16[2,8,64,1536]{3,2,0,1:T(8,128)(2,1)}, u32[]{:S(2)}, u32[]{:S(2)}) async-start(bf16[2,8,64,1536]{3,2,0,1:T(8,128)(2,1)} %broadcast_in_dim.4), calls=%async_computation | async-start | bytes 6291456 | tf_op jit(solution)/shard_map/all_to_all | solution.py:34
  16.6 125.0 %all-gather.4.cloned.1.call-start = ((), (), s32[]{:S(2)}) async-start(), calls=%async_computation.3 | async-start | bytes 5308416 | tf_op jit(solution)/shard_map/all_gather | solution.py:123
  17.3 197.8 %all-gather.6.cloned.1.call-start = ((), (), s32[]{:S(2)}) async-start(), calls=%async_computation.4 | async-start | bytes 13369344 | tf_op jit(solution)/shard_map/all_gather | solution.py:159
  65.5 4.3 %copy-start.5 = (f32[1536]{0:T(1024)S(1)}, f32[1536]{0:T(1024)}, u32[]{:S(2)}) copy-start(f32[1536]{0:T(1024)} %param.9) | copy-start | bytes 18436
  67.7 1.7 copy-start.3
  69.8 7.0 %copy-start.7 = (bf16[5,192,1536]{2,1,0:T(8,128)(2,1)S(1)}, bf16[5,192,1536]{2,1,0:T(8,128)(2,1)}, u32[]{:S(2)}) copy-start(bf16[5,192,1536]{2,1,0:T(8,128)(2,1)} %param.10) | copy-start | bytes 8847364
  74.2 7.7 %collective-permute-start = (bf16[2,2,1536]{2,1,0:T(2,128)(2,1)S(1)}, bf16[2,2,1536]{2,1,0:T(2,128)(2,1)S(1)}, u32[]{:S(2)}, u32[]{:S(2)}) collective-permute-start(bf16[2,2,1536]{2,1,0:T(2,128)(2,1)S(1)} %get-tuple-element.9), channel_id=1, source_target_pairs={{0,8},{8,16},{16,24},{24,32},{32,40},{40,48},{48,56},{56,64},{64,7... | collective-permute-start | bytes 36872 | tf_op jit(solution)/shard_map/ppermute | solution.py:21
  75.5 5.2 %collective-permute-start.1 = (bf16[2,2,1536]{2,1,0:T(2,128)(2,1)S(1)}, bf16[2,2,1536]{2,1,0:T(2,128)(2,1)S(1)}, u32[]{:S(2)}, u32[]{:S(2)}) collective-permute-start(bf16[2,2,1536]{2,1,0:T(2,128)(2,1)S(1)} %get-tuple-element.10), channel_id=1, source_target_pairs={{8,0},{16,8},{24,16},{32,24},{40,32},{48,40},{56,48},{64,56},{72,6... | collective-permute-start | bytes 36872 | tf_op jit(solution)/shard_map/ppermute | solution.py:23
  136.7 1.6 copy-start.2
  136.7 0.7 copy-start.6
  138.3 2.3 copy-start.1
  138.4 1.5 copy-start.4
  139.8 1.8 copy-start.8
  243.3 18.7 %all-to-all-start.2 = ((bf16[8,2,64,192]{3,2,1,0:T(8,128)(2,1)}), bf16[8,2,64,192]{3,2,1,0:T(8,128)(2,1)S(1)}, u32[]{:S(2)}, u32[]{:S(2)}) async-start(bf16[8,2,64,192]{3,2,1,0:T(8,128)(2,1)} %bitcast.64), calls=%async_computation.2 | async-start | bytes 1048576 | tf_op jit(solution)/shard_map/all_to_all | solution.py:170
Sparse Core Ops, SparseCore 0:
  19.7 118.2 all-gather.3
  141.7 73.3 all-gather.5

commit v12 on v11

--- a/solution.py
+++ b/solution.py
@@ -8,6 +8,9 @@
 from jax.sharding import PartitionSpec as P
 
 HD = 192
+SEQ = ("chip_x", "chip_z", "core")
+BATCH = ("peer_y", "peer_x")
+CHIPS = ("chip_x", "chip_z")
 
 
 def with_halo(cells, sides, width):
@@ -28,10 +31,10 @@
 
 
 def gather_batch(block, axis):
-    count = lax.axis_size("batch")
+    count = lax.axis_size(BATCH)
     spread = block.shape[:axis] + (count,) + block.shape[axis:]
     copies = jnp.broadcast_to(jnp.expand_dims(block, axis), spread)
-    arrived = lax.all_to_all(copies, "batch", axis, axis, tiled=False)
+    arrived = lax.all_to_all(copies, BATCH, axis, axis, tiled=False)
     return arrived.reshape(block.shape[:axis] + (count * block.shape[axis],) + block.shape[axis + 1 :])
 
 
@@ -74,24 +77,24 @@
         out_ref[0] = (summed_ref[...] / total_ref[...]).astype(out_ref.dtype)
 
 
-def flash_attention(queries, kv_tile, sources_per_step=2):
-    sample_count, query_count, head_width = queries.shape
+def flash_attention(queries, kv_tile, sample, sources_per_step=2):
+    _, query_count, head_width = queries.shape
     _, source_count, _, _, source_rows = kv_tile.shape
     sources_per_step = math.gcd(source_count, sources_per_step)
     return pl.pallas_call(
         flash_step,
-        grid=(sample_count, source_count // sources_per_step),
+        grid=(1, source_count // sources_per_step),
         in_specs=[
-            pl.BlockSpec((1, query_count, head_width), lambda s, k: (s, 0, 0)),
+            pl.BlockSpec((1, query_count, head_width), lambda s, k: (sample, 0, 0)),
             pl.BlockSpec(
-                (1, sources_per_step, 1, head_width, source_rows), lambda s, k: (0, k, s, 0, 0)
+                (1, sources_per_step, 1, head_width, source_rows), lambda s, k: (0, k, 0, 0, 0)
             ),
             pl.BlockSpec(
-                (1, sources_per_step, 1, head_width, source_rows), lambda s, k: (1, k, s, 0, 0)
+                (1, sources_per_step, 1, head_width, source_rows), lambda s, k: (1, k, 0, 0, 0)
             ),
         ],
-        out_specs=pl.BlockSpec((1, query_count, head_width), lambda s, k: (s, 0, 0)),
-        out_shape=jax.ShapeDtypeStruct(queries.shape, jnp.bfloat16),
+        out_specs=pl.BlockSpec((1, query_count, head_width), lambda s, k: (0, 0, 0)),
+        out_shape=jax.ShapeDtypeStruct((1, query_count, head_width), jnp.bfloat16),
         scratch_shapes=[
             pltpu.VMEM((query_count, 1), jnp.float32),
             pltpu.VMEM((query_count, 1), jnp.float32),
@@ -120,13 +123,13 @@
     sample_count, own_rows, full_width = activations.shape
     tap_count, local_out, _ = conv_weight.shape
     flank_rows = tap_count // 2
-    full_output_weight = lax.all_gather(output_weight, "batch", axis=0, tiled=True)
+    full_output_weight = lax.all_gather(output_weight, BATCH, axis=0, tiled=True)
     gathered_in = gather_batch(activations, 1)
     seq_rows = gathered_in.shape[1]
     active = lax.optimization_barrier(
         jax.nn.gelu(normalize(gathered_in, conv_gain)).astype(jnp.bfloat16)
     )
-    framed = with_halo(active, (("seq", 1),), flank_rows)
+    framed = with_halo(active, ((SEQ, 1),), flank_rows)
     conv_sum = jnp.zeros((sample_count, local_out, seq_rows), jnp.float32)
     for offset in range(tap_count):
         conv_sum = conv_sum + jnp.einsum(
@@ -135,7 +138,7 @@
             conv_weight[offset],
             preferred_element_type=jnp.float32,
         )
-    column_start = lax.axis_index("batch") * local_out
+    column_start = lax.axis_index(BATCH) * local_out
     own_columns = lax.dynamic_slice_in_dim(gathered_in, column_start, local_out, 2)
     residual = jnp.transpose(own_columns, (0, 2, 1)).astype(jnp.float32)
     hidden_part = (residual + conv_sum).astype(jnp.bfloat16)
@@ -156,18 +159,26 @@
     kv_rows, full_output_weight = lax.optimization_barrier(
         (jnp.stack([key_rows, value_rows]), full_output_weight)
     )
-    kv_tile = lax.all_gather(kv_rows, "seq", axis=1)
-    attended = flash_attention(queries, kv_tile)
-    row_start = lax.axis_index("batch") * own_rows
+    first_tile = lax.all_gather(kv_rows[:, :1], SEQ, axis=1)
+    chip_count = lax.axis_size(CHIPS)
+    second_rows = kv_rows[:, 1:]
+    copies = jnp.broadcast_to(second_rows, (2, chip_count) + second_rows.shape[2:])
+    same_core = lax.all_to_all(copies, CHIPS, 1, 1, tiled=False)
+    other_core = lax.ppermute(same_core, "core", [(0, 1), (1, 0)])
+    second_tile = jnp.concatenate([same_core, other_core], axis=1)[:, :, None]
+    attended = jnp.concatenate(
+        [flash_attention(queries, first_tile, 0), flash_attention(queries, second_tile, 1)]
+    )
+    row_start = lax.axis_index(BATCH) * own_rows
     own_hidden = jnp.transpose(
         lax.dynamic_slice_in_dim(hidden_full, row_start, own_rows, 2), (0, 2, 1)
     ).astype(jnp.float32)
-    batch_count = lax.axis_size("batch")
+    batch_count = lax.axis_size(BATCH)
     head_width = attended.shape[2]
     outgoing = jnp.transpose(
         attended.reshape(sample_count, batch_count, own_rows, head_width), (1, 0, 2, 3)
     )
-    arrived = lax.all_to_all(outgoing, "batch", 0, 0, tiled=False)
+    arrived = lax.all_to_all(outgoing, BATCH, 0, 0, tiled=False)
     heads_side_by_side = jnp.transpose(arrived, (1, 2, 0, 3)).reshape(
         sample_count, own_rows, batch_count * head_width
     )
@@ -179,20 +190,24 @@
 
 
 def solution(mesh):
+    fine = jax.sharding.Mesh(
+        mesh.devices.reshape(2, mesh.shape["seq"] // 4, 2, mesh.shape["batch"] // 2, 2),
+        SEQ + BATCH,
+    )
     placed = (
-        P(None, ("seq", "batch"), None),
+        P(None, SEQ + BATCH, None),
         P(),
-        P(None, "batch", None),
+        P(None, BATCH, None),
         P(),
-        P("batch", None),
-        P("batch", None),
-        P("batch", None),
-        P("batch", None),
+        P(BATCH, None),
+        P(BATCH, None),
+        P(BATCH, None),
+        P(BATCH, None),
     )
     return jax.shard_map(
         shards,
-        mesh=mesh,
+        mesh=fine,
         in_specs=placed,
-        out_specs=P(None, ("seq", "batch"), None),
+        out_specs=P(None, SEQ + BATCH, None),
         check_vma=False,
     )

time: 274 us -> 274 us (level)
  waiting for transfers between devices: 129 us -> 61.4 us
  blocking collectives: 50.5 us -> 115 us
  other arithmetic: 9.37 us -> 12.5 us
    all_gather x2, waiting for transfers between devices: 69.8 us -> 0.02 us  [the longest x1 0.02 us: shards(): lax.all_gather(output_weight, BATCH, axis=0, tiled=True)]
    all_to_all x1 -> x2, blocking collectives: 50.5 us -> 115 us  [the longest x1 64.6 us: shards(): same_core = lax.all_to_all(copies, CHIPS, 1, 1, tiled=False)]
    broadcast_in_dim x0 -> x1, other arithmetic: none -> 2.95 us  [shards(): second_tile = jnp.concatenate([same_core, other_core], axis=1)[:, :, None]]
    pallas_call x1 -> x2, Pallas kernels: 26.3 us -> 27.8 us  [flash_attention(): pl.pallas_call(flash_step, grid=(1, source_count // sources_per_step), in...]
  transfers between devices with their start and end apart: 6 -> 7, of which waited for: 4 -> 4; matrix products, arithmetic and copies ran while one was open for 9% -> 10% of each run, Pallas kernels for 0% -> 5%
where the time goes in v12:
time: 274 us
  blocking collectives  115 us (42%)
  waiting for transfers between devices  61.4 us (22%)
  Pallas kernels  27.8 us (10%)
  starting transfers between devices  15.1 us (6%)
  local copies, waits for them, and re-layouts  14.9 us (5%)
  between operations  13.7 us (5%)
  matrix products  13.2 us (5%)
  other arithmetic  12.5 us (5%)
    all_to_all x1, blocking collectives, shards(): same_core = lax.all_to_all(copies, CHIPS, 1, 1, tiled=False)  64.6 us
    all_to_all x1, blocking collectives, gather_batch(): arrived = lax.all_to_all(copies, BATCH, axis, axis, tiled=False)  50.6 us
    all_to_all x1, waiting for transfers between devices, gather_batch(): arrived = lax.all_to_all(copies, BATCH, axis, axis, tiled=False)  45.5 us
    pallas_call x2, Pallas kernels, flash_attention(): pl.pallas_call(flash_step, grid=(1, source_count // sources_per_step), in...  27.8 us
    all_to_all x1, waiting for transfers between devices, shards(): arrived = lax.all_to_all(outgoing, BATCH, 0, 0, tiled=False)  10.2 us
    all_to_all x1, starting transfers between devices, gather_batch(): arrived = lax.all_to_all(copies, BATCH, axis, axis, tiled=False)  7.01 us
    dot_general x5, matrix products, shards(): jnp.einsum('std,ed->set', framed[:, offset:offset + seq_rows], conv_weigh...  5.95 us
  transfers between devices with their start and end apart: 7, of which 4 were waited for; matrix products, arithmetic and copies ran while one was open for 10% of the time, Pallas kernels for 5%

profile of v12, /device:TPU:0, one launch (start us, length us, event | category | flops | bytes accessed | tf_op | source)
XLA Modules:
  0.0 273.7 jit_solution(11701032619872934165)
XLA Ops:
  6.5 3.0 %broadcast_in_dim.10 = bf16[2,8,64,1536]{3,2,0,1:T(8,128)(2,1)} broadcast(bf16[2,64,1536]{2,1,0:T(8,128)(2,1)} %param.8), dimensions={0,2,3} | broadcast | bytes 3538944 | tf_op jit(solution)/shard_map/broadcast_in_dim | solution.py:36
  9.6 7.0 %all-to-all-start = ((bf16[2,8,64,1536]{3,2,0,1:T(8,128)(2,1)}), bf16[2,8,64,1536]{3,2,0,1:T(8,128)(2,1)}, u32[]{:S(2)}, u32[]{:S(2)}) async-start(bf16[2,8,64,1536]{3,2,0,1:T(8,128)(2,1)} %broadcast_in_dim.10), calls=%async_computation | async-start | bytes 6291456 | tf_op jit(solution)/shard_map/all_to_all | solution.py:37
  17.4 45.5 %all-to-all-done = bf16[2,8,64,1536]{3,2,0,1:T(8,128)(2,1)} async-done(((bf16[2,8,64,1536]{3,2,0,1:T(8,128)(2,1)}), bf16[2,8,64,1536]{3,2,0,1:T(8,128)(2,1)}, u32[]{:S(2)}, u32[]{:S(2)}) %all-to-all-start) | async-done | bytes 3145760 | tf_op jit(solution)/shard_map/all_to_all | solution.py:37
  62.8 2.6 multiply_reduce_fusion.1
  65.5 2.2 copy.85
  67.7 1.6 copy-done.5
  69.8 4.4 %fusion.7 = bf16[2,512,1536]{2,1,0:T(8,128)(2,1)S(1)} fusion(f32[1536]{0:T(1024)S(1)} %copy-done.8, f32[2,512]{1,0:T(2,128)S(1)} %rsqrt.20, bf16[2,8,64,1536]{3,2,1,0:T(8,128)(2,1)} %copy-done.5), kind=kLoop, calls=%fused_computation.8 | loop fusion | flops 18874368 | bytes 6301696 | tf_op jit(solution)/shard_map/convert_element_type | solution.py:130
  74.2 1.3 collective-permute-start
  75.5 1.3 collective-permute-start.1
  78.0 2.7 %collective-permute-done.1 = bf16[2,2,1536]{2,1,0:T(2,128)(2,1)S(1)} collective-permute-done((bf16[2,2,1536]{2,1,0:T(2,128)(2,1)S(1)}, bf16[2,2,1536]{2,1,0:T(2,128)(2,1)S(1)}, u32[]{:S(2)}, u32[]{:S(2)}) %collective-permute-start.1) | collective-permute-done | bytes 12320 | tf_op jit(solution)/shard_map/ppermute | solution.py:26
  83.1 1.2 fusion.11
  84.3 1.3 fusion.47
  85.9 50.6 %all_to_all.20 = bf16[2,8,192,512]{3,2,0,1:T(8,128)(2,1)S(1)} all-to-all(bf16[2,8,192,512]{3,2,0,1:T(8,128)(2,1)S(1)} %broadcast_in_dim.11), channel_id=1, replica_groups=mesh['chip_x'=2,'chip_z'=4,'core'=2,'peer_y'=4,'peer_x'=2] {'peer_y','pe..., dimensions={1} | all-to-all | bytes 6291456 | tf_op jit(solution)/shard_map/all_to_all | solution.py:37
  141.8 64.6 %all_to_all.21 = bf16[2,8,192,512]{3,2,0,1:T(8,128)(2,1)S(1)} all-to-all(bf16[2,8,192,512]{3,2,0,1:T(8,128)(2,1)S(1)} %broadcast_in_dim.13), channel_id=1, replica_groups=mesh['chip_x'=2,'chip_z'=4,'core'=2,'peer_y'=4,'peer_x'=2] {'chip_x','ch..., dimensions={1} | all-to-all | bytes 6291456 | tf_op jit(solution)/shard_map/all_to_all | solution.py:166
  207.0 1.4 copy-done.3
  208.5 1.8 fusion.26.query_ref
  210.3 2.3 collective-permute-done.2
  212.6 3.0 %maximum_bitcast_fusion.key_ref.value_ref = bf16[2,16,1,192,512]{4,3,2,1,0:T(8,128)(2,1)} fusion(bf16[2,8,192,512]{3,2,1,0:T(8,128)(2,1)S(1)} %collective-permute-done.2, bf16[2,8,192,512]{3,2,0,1:T(8,128)(2,1)S(1)} %all_to_all.21), kind=kLoop, calls=%fused_computation.9 | loop fusion | flops 12582912 | bytes 12582912 | tf_op jit(solution)/shard_map/broadcast_in_dim | solution.py:168
  215.6 13.9 %shard_map.83 = bf16[1,512,192]{2,1,0:T(8,128)(2,1)} custom-call(bf16[2,512,192]{2,1,0:T(8,128)(2,1)} %fusion.26.query_ref, bf16[2,16,1,192,512]{4,3,2,1,0:T(8,128)(2,1)} %maximum_bitcast_fusion.key_ref.value_ref, bf16[2,16,1,192,512]{4,3,2,1,0:T(8,128)(2,1)} %maximum_bitcast_fusion.key_ref.value_ref), custom_call_target="tpu_custom_call" | custom-call | tf_op jit(solution)/shard_map/pallas_call | solution.py:84
  229.4 13.9 %shard_map.82 = bf16[1,512,192]{2,1,0:T(8,128)(2,1)} custom-call(bf16[2,512,192]{2,1,0:T(8,128)(2,1)} %fusion.26.query_ref, bf16[2,16,1,192,512]{4,3,2,1,0:T(8,128)(2,1)} %bitcast.69, bf16[2,16,1,192,512]{4,3,2,1,0:T(8,128)(2,1)} %bitcast.70), custom_call_target="tpu_custom_call" | custom-call | tf_op jit(solution)/shard_map/pallas_call | solution.py:84
  245.3 5.1 %all-to-all-start.3 = ((bf16[8,2,64,192]{3,2,1,0:T(8,128)(2,1)}), bf16[8,2,64,192]{3,2,1,0:T(8,128)(2,1)S(1)}, u32[]{:S(2)}, u32[]{:S(2)}) async-start(bf16[8,2,64,192]{3,2,1,0:T(8,128)(2,1)} %bitcast.68), calls=%async_computation.3 | async-start | bytes 1048576 | tf_op jit(solution)/shard_map/all_to_all | solution.py:181
  250.4 1.4 constant_dynamic-slice_fusion
  252.1 10.2 %all-to-all-done.3 = bf16[8,2,64,192]{3,2,1,0:T(8,128)(2,1)S(1)} async-done(((bf16[8,2,64,192]{3,2,1,0:T(8,128)(2,1)}), bf16[8,2,64,192]{3,2,1,0:T(8,128)(2,1)S(1)}, u32[]{:S(2)}, u32[]{:S(2)}) %all-to-all-start.3) | async-done | bytes 393248 | tf_op jit(solution)/shard_map/all_to_all | solution.py:181
  263.0 3.9 %fusion.23 = bf16[2,64,1536]{2,1,0:T(8,128)(2,1)} fusion(bf16[2,64,1536]{2,1,0:T(8,128)(2,1)S(1)} %reshape.44, bf16[1536,1536]{1,0:T(8,128)(2,1)} %all-gather.4.cloned.1.call-done, bf16[2,1536,64]{1,2,0:T(8,128)(2,1)S(1)} %copy.97), kind=kOutput, calls=%fused_computation.30 | convolution fusion | flops 604569600 | bytes 5898240 | tf_op jit(solution)/shard_map/std,df->stf/dot_general | solution.py:185
  (54 shorter events, 14.0 us)
Async XLA Ops:
  6.5 131.8 %copy-start = (bf16[192,1536]{1,0:T(8,128)(2,1)S(1)}, bf16[192,1536]{1,0:T(8,128)(2,1)}, u32[]{:S(2)}) copy-start(bf16[192,1536]{1,0:T(8,128)(2,1)} %param.13) | copy-start | bytes 1769476
  9.6 53.3 %all-to-all-start = ((bf16[2,8,64,1536]{3,2,0,1:T(8,128)(2,1)}), bf16[2,8,64,1536]{3,2,0,1:T(8,128)(2,1)}, u32[]{:S(2)}, u32[]{:S(2)}) async-start(bf16[2,8,64,1536]{3,2,0,1:T(8,128)(2,1)} %broadcast_in_dim.10), calls=%async_computation | async-start | bytes 6291456 | tf_op jit(solution)/shard_map/all_to_all | solution.py:37
  16.6 124.1 %all-gather.4.cloned.1.call-start = ((), (), s32[]{:S(2)}) async-start(), calls=%async_computation.4 | async-start | bytes 5308416 | tf_op jit(solution)/shard_map/all_gather | solution.py:126
  17.3 212.1 %all-gather.6.cloned.1.call-start = ((), (), s32[]{:S(2)}) async-start(), calls=%async_computation.5 | async-start | bytes 6684672 | tf_op jit(solution)/shard_map/all_gather | solution.py:162
  65.5 4.3 %copy-start.8 = (f32[1536]{0:T(1024)S(1)}, f32[1536]{0:T(1024)}, u32[]{:S(2)}) copy-start(f32[1536]{0:T(1024)} %param.9) | copy-start | bytes 18436
  67.7 1.7 copy-start.5
  69.8 7.0 %copy-start.10 = (bf16[5,192,1536]{2,1,0:T(8,128)(2,1)S(1)}, bf16[5,192,1536]{2,1,0:T(8,128)(2,1)}, u32[]{:S(2)}) copy-start(bf16[5,192,1536]{2,1,0:T(8,128)(2,1)} %param.10) | copy-start | bytes 8847364
  74.2 7.7 %collective-permute-start = (bf16[2,2,1536]{2,1,0:T(2,128)(2,1)S(1)}, bf16[2,2,1536]{2,1,0:T(2,128)(2,1)S(1)}, u32[]{:S(2)}, u32[]{:S(2)}) collective-permute-start(bf16[2,2,1536]{2,1,0:T(2,128)(2,1)S(1)} %get-tuple-element.9), channel_id=1, source_target_pairs={{0,8},{8,16},{16,24},{24,32},{32,40},{40,48},{48,56},{56,64},{64,7... | collective-permute-start | bytes 36872 | tf_op jit(solution)/shard_map/ppermute | solution.py:24
  75.5 5.2 %collective-permute-start.1 = (bf16[2,2,1536]{2,1,0:T(2,128)(2,1)S(1)}, bf16[2,2,1536]{2,1,0:T(2,128)(2,1)S(1)}, u32[]{:S(2)}, u32[]{:S(2)}) collective-permute-start(bf16[2,2,1536]{2,1,0:T(2,128)(2,1)S(1)} %get-tuple-element.10), channel_id=1, source_target_pairs={{8,0},{16,8},{24,16},{32,24},{40,32},{48,40},{56,48},{64,56},{72,6... | collective-permute-start | bytes 36872 | tf_op jit(solution)/shard_map/ppermute | solution.py:26
  136.7 1.6 copy-start.4
  136.7 0.7 copy-start.9
  138.3 2.3 copy-start.2
  138.3 1.5 copy-start.7
  206.4 2.0 copy-start.3
  206.4 2.1 copy-start.11
  206.7 5.9 %collective-permute-start.2 = (bf16[2,8,192,512]{3,2,1,0:T(8,128)(2,1)S(1)}, bf16[2,8,192,512]{3,2,1,0:T(8,128)(2,1)S(1)}, u32[]{:S(2)}, u32[]{:S(2)}) collective-permute-start(bf16[2,8,192,512]{3,2,1,0:T(8,128)(2,1)S(1)} %copy.92), channel_id=1, source_target_pairs={{0,8},{8,0},{1,9},{9,1},{2,10},{10,2},{3,11},{11,3},{4,12},{12,4},... | collective-permute-start | bytes 9437192 | tf_op jit(solution)/shard_map/ppermute | solution.py:167
  229.4 13.9 %copy-start.6 = (bf16[1,512,192]{2,1,0:T(8,128)(2,1)S(1)}, bf16[1,512,192]{2,1,0:T(8,128)(2,1)}, u32[]{:S(2)}) copy-start(bf16[1,512,192]{2,1,0:T(8,128)(2,1)} %shard_map.83) | copy-start | bytes 589828
  245.3 17.0 %all-to-all-start.3 = ((bf16[8,2,64,192]{3,2,1,0:T(8,128)(2,1)}), bf16[8,2,64,192]{3,2,1,0:T(8,128)(2,1)S(1)}, u32[]{:S(2)}, u32[]{:S(2)}) async-start(bf16[8,2,64,192]{3,2,1,0:T(8,128)(2,1)} %bitcast.68), calls=%async_computation.3 | async-start | bytes 1048576 | tf_op jit(solution)/shard_map/all_to_all | solution.py:181
  262.6 4.3 %copy-start.1 = (bf16[192,1536]{1,0:T(8,128)(2,1)S(1)}, bf16[192,1536]{1,0:T(8,128)(2,1)}, u32[]{:S(2)}) copy-start(bf16[192,1536]{1,0:T(8,128)(2,1)} %param.13) | copy-start | bytes 1769476
Sparse Core Ops, SparseCore 0:
  19.7 118.2 all-gather.3
  141.7 74.7 all-gather.5

commit v13 on v11

--- a/solution.py
+++ b/solution.py
@@ -74,7 +74,7 @@
         out_ref[0] = (summed_ref[...] / total_ref[...]).astype(out_ref.dtype)
 
 
-def flash_attention(queries, kv_tile, sources_per_step=2):
+def flash_attention(queries, kv_tile, sources_per_step=4):
     sample_count, query_count, head_width = queries.shape
     _, source_count, _, _, source_rows = kv_tile.shape
     sources_per_step = math.gcd(source_count, sources_per_step)

time: 274 us -> 272 us (level)
  no operation moved by 1% of the time
where the time goes in v13:
time: 272 us; the launch traced here: 271 us
  waiting for transfers between devices  129 us (47%)
  blocking collectives  50.5 us (19%)
  Pallas kernels  24.1 us (9%)
  starting transfers between devices  16.4 us (6%)
  matrix products  15.1 us (6%)
  between operations  13.6 us (5%)
  local copies, waits for them, and re-layouts  13.1 us (5%)
  other arithmetic  9.37 us (3%)
    all_gather x1, waiting for transfers between devices, shards(): kv_tile = lax.all_gather(kv_rows, 'seq', axis=1)  69.8 us
    all_to_all x1, blocking collectives, gather_batch(): arrived = lax.all_to_all(copies, 'batch', axis, axis, tiled=False)  50.5 us
    all_to_all x1, waiting for transfers between devices, gather_batch(): arrived = lax.all_to_all(copies, 'batch', axis, axis, tiled=False)  45.5 us
    pallas_call x1, Pallas kernels, flash_attention(): pl.pallas_call(flash_step, grid=(sample_count, source_count // sources_pe...  24.1 us
    all_to_all x1, waiting for transfers between devices, shards(): arrived = lax.all_to_all(outgoing, 'batch', 0, 0, tiled=False)  10.3 us
    all_to_all x1, starting transfers between devices, gather_batch(): arrived = lax.all_to_all(copies, 'batch', axis, axis, tiled=False)  7.01 us
    all_to_all x1, starting transfers between devices, shards(): arrived = lax.all_to_all(outgoing, 'batch', 0, 0, tiled=False)  6.7 us
    dot_general x5, matrix products, shards(): jnp.einsum('std,ed->set', framed[:, offset:offset + seq_rows], conv_weigh...  5.96 us
  transfers between devices with their start and end apart: 6, of which 4 were waited for; matrix products, arithmetic and copies ran while one was open for 9% of the time, Pallas kernels for 0%

profile of v13, /device:TPU:0, one launch (start us, length us, event | category | flops | bytes accessed | tf_op | source)
XLA Modules:
  0.0 271.3 jit_solution(4943253947960271773)
XLA Ops:
  6.5 3.0 %broadcast_in_dim.4 = bf16[2,8,64,1536]{3,2,0,1:T(8,128)(2,1)} broadcast(bf16[2,64,1536]{2,1,0:T(8,128)(2,1)} %param.8), dimensions={0,2,3} | broadcast | bytes 3538944 | tf_op jit(solution)/shard_map/broadcast_in_dim | solution.py:33
  9.6 7.0 %all-to-all-start = ((bf16[2,8,64,1536]{3,2,0,1:T(8,128)(2,1)}), bf16[2,8,64,1536]{3,2,0,1:T(8,128)(2,1)}, u32[]{:S(2)}, u32[]{:S(2)}) async-start(bf16[2,8,64,1536]{3,2,0,1:T(8,128)(2,1)} %broadcast_in_dim.4), calls=%async_computation | async-start | bytes 6291456 | tf_op jit(solution)/shard_map/all_to_all | solution.py:34
  17.4 45.5 %all-to-all-done = bf16[2,8,64,1536]{3,2,0,1:T(8,128)(2,1)} async-done(((bf16[2,8,64,1536]{3,2,0,1:T(8,128)(2,1)}), bf16[2,8,64,1536]{3,2,0,1:T(8,128)(2,1)}, u32[]{:S(2)}, u32[]{:S(2)}) %all-to-all-start) | async-done | bytes 3145760 | tf_op jit(solution)/shard_map/all_to_all | solution.py:34
  62.8 2.6 multiply_reduce_fusion.1
  65.5 2.2 copy.78
  67.7 1.6 copy-done.3
  69.8 4.4 %fusion.7 = bf16[2,512,1536]{2,1,0:T(8,128)(2,1)S(1)} fusion(f32[1536]{0:T(1024)S(1)} %copy-done.5, f32[2,512]{1,0:T(2,128)S(1)} %rsqrt.20, bf16[2,8,64,1536]{3,2,1,0:T(8,128)(2,1)} %copy-done.3), kind=kLoop, calls=%fused_computation.8 | loop fusion | flops 18874368 | bytes 6301696 | tf_op jit(solution)/shard_map/convert_element_type | solution.py:127
  74.2 1.3 collective-permute-start
  75.5 1.3 collective-permute-start.1
  76.8 1.2 fusion.55
  78.0 2.7 %collective-permute-done.1 = bf16[2,2,1536]{2,1,0:T(2,128)(2,1)S(1)} collective-permute-done((bf16[2,2,1536]{2,1,0:T(2,128)(2,1)S(1)}, bf16[2,2,1536]{2,1,0:T(2,128)(2,1)S(1)}, u32[]{:S(2)}, u32[]{:S(2)}) %collective-permute-start.1) | collective-permute-done | bytes 12320 | tf_op jit(solution)/shard_map/ppermute | solution.py:23
  80.7 1.2 fusion.16
  81.9 1.2 fusion.18
  83.1 1.2 fusion.11
  84.3 1.3 fusion.47
  85.9 50.5 %all_to_all.15 = bf16[2,8,192,512]{3,2,0,1:T(8,128)(2,1)S(1)} all-to-all(bf16[2,8,192,512]{3,2,0,1:T(8,128)(2,1)S(1)} %broadcast_in_dim.5), channel_id=1, replica_groups=mesh['seq'=16,'batch'=8] {'batch'}, dimensions={1} | all-to-all | bytes 6291456 | tf_op jit(solution)/shard_map/all_to_all | solution.py:34
  141.6 3.7 %fusion.26.query_ref = bf16[2,512,192]{2,1,0:T(8,128)(2,1)} fusion(bf16[2,1536,512]{2,1,0:T(8,128)(2,1)} %copy-done.1, bf16[192,1536]{1,0:T(8,128)(2,1)S(1)} %copy-done.8), kind=kOutput, calls=%fused_computation.31 | convolution fusion | flops 604372992 | bytes 4128768 | tf_op jit(solution)/shard_map/sdt,ed->ste/dot_general | solution.py:147
  145.4 69.8 %all-gather.6.cloned.1.call-done = bf16[2,32,192,512]{3,2,1,0:T(8,128)(2,1)} async-done(((bf16[2,2,192,512]{3,2,1,0:T(8,128)(2,1)}), bf16[2,32,192,512]{3,2,1,0:T(8,128)(2,1)}) %all-gather.6.cloned.1.call-update) | async-done | bytes 12582928 | tf_op jit(solution)/shard_map/all_gather | solution.py:159
  215.2 24.1 %shard_map.82 = bf16[2,512,192]{2,1,0:T(8,128)(2,1)} custom-call(bf16[2,512,192]{2,1,0:T(8,128)(2,1)} %fusion.26.query_ref, bf16[2,16,2,192,512]{4,3,2,1,0:T(8,128)(2,1)} %bitcast.65, bf16[2,16,2,192,512]{4,3,2,1,0:T(8,128)(2,1)} %bitcast.66), custom_call_target="tpu_custom_call" | custom-call | tf_op jit(solution)/shard_map/pallas_call | solution.py:81
  239.3 1.9 copy.96
  241.1 6.7 %all-to-all-start.2 = ((bf16[8,2,64,192]{3,2,1,0:T(8,128)(2,1)}), bf16[8,2,64,192]{3,2,1,0:T(8,128)(2,1)S(1)}, u32[]{:S(2)}, u32[]{:S(2)}) async-start(bf16[8,2,64,192]{3,2,1,0:T(8,128)(2,1)} %bitcast.64), calls=%async_computation.2 | async-start | bytes 1048576 | tf_op jit(solution)/shard_map/all_to_all | solution.py:170
  247.8 1.4 constant_dynamic-slice_fusion
  249.5 10.3 %all-to-all-done.2 = bf16[8,2,64,192]{3,2,1,0:T(8,128)(2,1)S(1)} async-done(((bf16[8,2,64,192]{3,2,1,0:T(8,128)(2,1)}), bf16[8,2,64,192]{3,2,1,0:T(8,128)(2,1)S(1)}, u32[]{:S(2)}, u32[]{:S(2)}) %all-to-all-start.2) | async-done | bytes 393248 | tf_op jit(solution)/shard_map/all_to_all | solution.py:170
  260.6 3.9 %fusion.23 = bf16[2,64,1536]{2,1,0:T(8,128)(2,1)} fusion(bf16[2,64,1536]{2,1,0:T(8,128)(2,1)S(1)} %reshape.44, bf16[1536,1536]{1,0:T(8,128)(2,1)} %all-gather.4.cloned.1.call-done, bf16[2,1536,64]{1,2,0:T(8,128)(2,1)S(1)} %copy.89), kind=kOutput, calls=%fused_computation.29 | convolution fusion | flops 604569600 | bytes 5898240 | tf_op jit(solution)/shard_map/std,df->stf/dot_general | solution.py:174
  (39 shorter events, 7.7 us)
Async XLA Ops:
  6.5 131.8 %copy-start = (bf16[192,1536]{1,0:T(8,128)(2,1)S(1)}, bf16[192,1536]{1,0:T(8,128)(2,1)}, u32[]{:S(2)}) copy-start(bf16[192,1536]{1,0:T(8,128)(2,1)} %param.13) | copy-start | bytes 1769476
  9.6 53.3 %all-to-all-start = ((bf16[2,8,64,1536]{3,2,0,1:T(8,128)(2,1)}), bf16[2,8,64,1536]{3,2,0,1:T(8,128)(2,1)}, u32[]{:S(2)}, u32[]{:S(2)}) async-start(bf16[2,8,64,1536]{3,2,0,1:T(8,128)(2,1)} %broadcast_in_dim.4), calls=%async_computation | async-start | bytes 6291456 | tf_op jit(solution)/shard_map/all_to_all | solution.py:34
  16.6 125.0 %all-gather.4.cloned.1.call-start = ((), (), s32[]{:S(2)}) async-start(), calls=%async_computation.3 | async-start | bytes 5308416 | tf_op jit(solution)/shard_map/all_gather | solution.py:123
  17.3 197.8 %all-gather.6.cloned.1.call-start = ((), (), s32[]{:S(2)}) async-start(), calls=%async_computation.4 | async-start | bytes 13369344 | tf_op jit(solution)/shard_map/all_gather | solution.py:159
  65.5 4.3 %copy-start.5 = (f32[1536]{0:T(1024)S(1)}, f32[1536]{0:T(1024)}, u32[]{:S(2)}) copy-start(f32[1536]{0:T(1024)} %param.9) | copy-start | bytes 18436
  67.7 1.7 copy-start.3
  69.8 7.0 %copy-start.7 = (bf16[5,192,1536]{2,1,0:T(8,128)(2,1)S(1)}, bf16[5,192,1536]{2,1,0:T(8,128)(2,1)}, u32[]{:S(2)}) copy-start(bf16[5,192,1536]{2,1,0:T(8,128)(2,1)} %param.10) | copy-start | bytes 8847364
  74.2 7.7 %collective-permute-start = (bf16[2,2,1536]{2,1,0:T(2,128)(2,1)S(1)}, bf16[2,2,1536]{2,1,0:T(2,128)(2,1)S(1)}, u32[]{:S(2)}, u32[]{:S(2)}) collective-permute-start(bf16[2,2,1536]{2,1,0:T(2,128)(2,1)S(1)} %get-tuple-element.9), channel_id=1, source_target_pairs={{0,8},{8,16},{16,24},{24,32},{32,40},{40,48},{48,56},{56,64},{64,7... | collective-permute-start | bytes 36872 | tf_op jit(solution)/shard_map/ppermute | solution.py:21
  75.5 5.2 %collective-permute-start.1 = (bf16[2,2,1536]{2,1,0:T(2,128)(2,1)S(1)}, bf16[2,2,1536]{2,1,0:T(2,128)(2,1)S(1)}, u32[]{:S(2)}, u32[]{:S(2)}) collective-permute-start(bf16[2,2,1536]{2,1,0:T(2,128)(2,1)S(1)} %get-tuple-element.10), channel_id=1, source_target_pairs={{8,0},{16,8},{24,16},{32,24},{40,32},{48,40},{56,48},{64,56},{72,6... | collective-permute-start | bytes 36872 | tf_op jit(solution)/shard_map/ppermute | solution.py:23
  136.7 1.6 copy-start.2
  136.7 0.7 copy-start.6
  138.3 2.3 copy-start.1
  138.4 1.5 copy-start.4
  139.8 1.8 copy-start.8
  241.1 18.7 %all-to-all-start.2 = ((bf16[8,2,64,192]{3,2,1,0:T(8,128)(2,1)}), bf16[8,2,64,192]{3,2,1,0:T(8,128)(2,1)S(1)}, u32[]{:S(2)}, u32[]{:S(2)}) async-start(bf16[8,2,64,192]{3,2,1,0:T(8,128)(2,1)} %bitcast.64), calls=%async_computation.2 | async-start | bytes 1048576 | tf_op jit(solution)/shard_map/all_to_all | solution.py:170
Sparse Core Ops, SparseCore 0:
  19.7 118.2 all-gather.3
  141.7 73.3 all-gather.5

commit v14 on v12

--- a/solution.py
+++ b/solution.py
@@ -10,7 +10,6 @@
 HD = 192
 SEQ = ("chip_x", "chip_z", "core")
 BATCH = ("peer_y", "peer_x")
-CHIPS = ("chip_x", "chip_z")
 
 
 def with_halo(cells, sides, width):
@@ -77,24 +76,24 @@
         out_ref[0] = (summed_ref[...] / total_ref[...]).astype(out_ref.dtype)
 
 
-def flash_attention(queries, kv_tile, sample, sources_per_step=2):
-    _, query_count, head_width = queries.shape
+def flash_attention(queries, kv_tile, sources_per_step=4):
+    sample_count, query_count, head_width = queries.shape
     _, source_count, _, _, source_rows = kv_tile.shape
     sources_per_step = math.gcd(source_count, sources_per_step)
     return pl.pallas_call(
         flash_step,
-        grid=(1, source_count // sources_per_step),
+        grid=(sample_count, source_count // sources_per_step),
         in_specs=[
-            pl.BlockSpec((1, query_count, head_width), lambda s, k: (sample, 0, 0)),
+            pl.BlockSpec((1, query_count, head_width), lambda s, k: (s, 0, 0)),
             pl.BlockSpec(
-                (1, sources_per_step, 1, head_width, source_rows), lambda s, k: (0, k, 0, 0, 0)
+                (1, sources_per_step, 1, head_width, source_rows), lambda s, k: (0, k, s, 0, 0)
             ),
             pl.BlockSpec(
-                (1, sources_per_step, 1, head_width, source_rows), lambda s, k: (1, k, 0, 0, 0)
+                (1, sources_per_step, 1, head_width, source_rows), lambda s, k: (1, k, s, 0, 0)
             ),
         ],
-        out_specs=pl.BlockSpec((1, query_count, head_width), lambda s, k: (0, 0, 0)),
-        out_shape=jax.ShapeDtypeStruct((1, query_count, head_width), jnp.bfloat16),
+        out_specs=pl.BlockSpec((1, query_count, head_width), lambda s, k: (s, 0, 0)),
+        out_shape=jax.ShapeDtypeStruct(queries.shape, jnp.bfloat16),
         scratch_shapes=[
             pltpu.VMEM((query_count, 1), jnp.float32),
             pltpu.VMEM((query_count, 1), jnp.float32),
@@ -123,7 +122,14 @@
     sample_count, own_rows, full_width = activations.shape
     tap_count, local_out, _ = conv_weight.shape
     flank_rows = tap_count // 2
-    full_output_weight = lax.all_gather(output_weight, BATCH, axis=0, tiled=True)
+    mine = lax.axis_index("core")
+    half_width = full_width // 2
+    own_half = lax.all_gather(
+        lax.dynamic_slice_in_dim(output_weight, mine * half_width, half_width, 1),
+        BATCH,
+        axis=0,
+        tiled=True,
+    )
     gathered_in = gather_batch(activations, 1)
     seq_rows = gathered_in.shape[1]
     active = lax.optimization_barrier(
@@ -156,19 +162,9 @@
     value_rows = jnp.einsum(
         "sdt,ed->set", normed, value_weight, preferred_element_type=jnp.float32
     ).astype(jnp.bfloat16)
-    kv_rows, full_output_weight = lax.optimization_barrier(
-        (jnp.stack([key_rows, value_rows]), full_output_weight)
-    )
-    first_tile = lax.all_gather(kv_rows[:, :1], SEQ, axis=1)
-    chip_count = lax.axis_size(CHIPS)
-    second_rows = kv_rows[:, 1:]
-    copies = jnp.broadcast_to(second_rows, (2, chip_count) + second_rows.shape[2:])
-    same_core = lax.all_to_all(copies, CHIPS, 1, 1, tiled=False)
-    other_core = lax.ppermute(same_core, "core", [(0, 1), (1, 0)])
-    second_tile = jnp.concatenate([same_core, other_core], axis=1)[:, :, None]
-    attended = jnp.concatenate(
-        [flash_attention(queries, first_tile, 0), flash_attention(queries, second_tile, 1)]
-    )
+    kv_rows, own_half = lax.optimization_barrier((jnp.stack([key_rows, value_rows]), own_half))
+    kv_tile = lax.all_gather(kv_rows, SEQ, axis=1)
+    attended = flash_attention(queries, kv_tile)
     row_start = lax.axis_index(BATCH) * own_rows
     own_hidden = jnp.transpose(
         lax.dynamic_slice_in_dim(hidden_full, row_start, own_rows, 2), (0, 2, 1)
@@ -182,8 +178,17 @@
     heads_side_by_side = jnp.transpose(arrived, (1, 2, 0, 3)).reshape(
         sample_count, own_rows, batch_count * head_width
     )
-    branch_rows = jnp.einsum(
-        "std,df->stf", heads_side_by_side, full_output_weight, preferred_element_type=jnp.float32
+    other_half = lax.ppermute(own_half, "core", [(0, 1), (1, 0)])
+    own_part = jnp.einsum(
+        "std,df->stf", heads_side_by_side, own_half, preferred_element_type=jnp.float32
+    )
+    other_part = jnp.einsum(
+        "std,df->stf", heads_side_by_side, other_half, preferred_element_type=jnp.float32
+    )
+    branch_rows = jnp.where(
+        mine == 0,
+        jnp.concatenate([own_part, other_part], axis=2),
+        jnp.concatenate([other_part, own_part], axis=2),
     )
     result = own_hidden + branch_rows
     return result.astype(jnp.bfloat16)

time: 274 us -> 295 us (1.077)
  waiting for transfers between devices: 61.4 us -> 189 us
  blocking collectives: 115 us -> 0 us
  starting transfers between devices: 15.1 us -> 21.2 us
  Pallas kernels: 27.8 us -> 24.1 us
    all_to_all x2 -> x0, blocking collectives: 115 us -> none  [the longest x1 64.6 us: shards(): same_core = lax.all_to_all(copies, CHIPS, 1, 1, tiled=False)]
    all_gather x2, waiting for transfers between devices: 0.02 us -> 93.9 us  [the longest x1 67.4 us: shards(): kv_tile = lax.all_gather(kv_rows, SEQ, axis=1)]
    all_to_all x1 -> x2, waiting for transfers between devices: 45.5 us -> 81.8 us  [gather_batch(): arrived = lax.all_to_all(copies, BATCH, axis, axis, tiled=False)]
    all_to_all x1 -> x2, starting transfers between devices: 7.01 us -> 11.6 us  [gather_batch(): arrived = lax.all_to_all(copies, BATCH, axis, axis, tiled=False)]
    pallas_call x2 -> x1, Pallas kernels: 27.8 us -> 24.1 us  [flash_attention(): pl.pallas_call(flash_step, grid=(sample_count, source_count // sources_pe...]
    reduce_sum x1, other arithmetic: 0.67 us -> 3.69 us  [shards(): jnp.mean(hidden_float * hidden_float, axis=1, keepdims=True) + 1e-06]
    broadcast_in_dim x1 -> x0, other arithmetic: 2.95 us -> none  [shards(): second_tile = jnp.concatenate([same_core, other_core], axis=1)[:, :, None]]
  transfers between devices with their start and end apart: 7 -> 8, of which waited for: 4 -> 6; matrix products, arithmetic and copies ran while one was open for 10% -> 8% of each run, Pallas kernels for 5% -> 8%
where the time goes in v14:
time: 295 us; the launch traced here: 294 us
  waiting for transfers between devices  189 us (64%)
  Pallas kernels  24.1 us (8%)
  starting transfers between devices  21.2 us (7%)
  local copies, waits for them, and re-layouts  17.2 us (6%)
  matrix products  15.6 us (5%)
  between operations  13.7 us (5%)
  other arithmetic  13.3 us (5%)
    all_to_all x2, waiting for transfers between devices, gather_batch(): arrived = lax.all_to_all(copies, BATCH, axis, axis, tiled=False)  81.8 us
    all_gather x1, waiting for transfers between devices, shards(): kv_tile = lax.all_gather(kv_rows, SEQ, axis=1)  67.4 us
    all_gather x1, waiting for transfers between devices, shards(): lax.all_gather(lax.dynamic_slice_in_dim(output_weight, mine * half_width,...  26.4 us
    pallas_call x1, Pallas kernels, flash_attention(): pl.pallas_call(flash_step, grid=(sample_count, source_count // sources_pe...  24.1 us
    all_to_all x2, starting transfers between devices, gather_batch(): arrived = lax.all_to_all(copies, BATCH, axis, axis, tiled=False)  11.6 us
    all_to_all x1, waiting for transfers between devices, shards(): arrived = lax.all_to_all(outgoing, BATCH, 0, 0, tiled=False)  10.3 us
    all_to_all x1, starting transfers between devices, shards(): arrived = lax.all_to_all(outgoing, BATCH, 0, 0, tiled=False)  6.7 us
    dot_general x5, matrix products, shards(): jnp.einsum('std,ed->set', framed[:, offset:offset + seq_rows], conv_weigh...  5.97 us
  transfers between devices with their start and end apart: 8, of which 6 were waited for; matrix products, arithmetic and copies ran while one was open for 8% of the time, Pallas kernels for 8%

profile of v14, /device:TPU:0, one launch (start us, length us, event | category | flops | bytes accessed | tf_op | source)
XLA Modules:
  0.0 293.8 jit_solution(2088531063752088880)
XLA Ops:
  6.5 3.1 %broadcast_in_dim.4 = bf16[2,8,64,1536]{3,2,0,1:T(8,128)(2,1)} broadcast(bf16[2,64,1536]{2,1,0:T(8,128)(2,1)} %param.8), dimensions={0,2,3} | broadcast | bytes 3538944 | tf_op jit(solution)/shard_map/broadcast_in_dim | solution.py:35
  9.6 7.0 %all-to-all-start = ((bf16[2,8,64,1536]{3,2,0,1:T(8,128)(2,1)}), bf16[2,8,64,1536]{3,2,0,1:T(8,128)(2,1)}, u32[]{:S(2)}, u32[]{:S(2)}) async-start(bf16[2,8,64,1536]{3,2,0,1:T(8,128)(2,1)} %broadcast_in_dim.4), calls=%async_computation | async-start | bytes 6291456 | tf_op jit(solution)/shard_map/all_to_all | solution.py:36
  16.6 39.8 %all-to-all-done = bf16[2,8,64,1536]{3,2,0,1:T(8,128)(2,1)} async-done(((bf16[2,8,64,1536]{3,2,0,1:T(8,128)(2,1)}), bf16[2,8,64,1536]{3,2,0,1:T(8,128)(2,1)}, u32[]{:S(2)}, u32[]{:S(2)}) %all-to-all-start) | async-done | bytes 3145760 | tf_op jit(solution)/shard_map/all_to_all | solution.py:36
  56.4 2.6 multiply_reduce_fusion.1
  59.1 2.2 copy.78
  61.3 1.6 copy-done.3
  63.4 4.4 %fusion.7 = bf16[2,512,1536]{2,1,0:T(8,128)(2,1)S(1)} fusion(f32[1536]{0:T(1024)S(1)} %copy-done.6, f32[2,512]{1,0:T(2,128)S(1)} %rsqrt.20, bf16[2,8,64,1536]{3,2,1,0:T(8,128)(2,1)} %copy-done.3), kind=kLoop, calls=%fused_computation.8 | loop fusion | flops 18874368 | bytes 6301696 | tf_op jit(solution)/shard_map/convert_element_type | solution.py:136
  69.1 1.3 collective-permute-start.1
  71.6 2.7 collective-permute-done.1
  79.2 2.0 broadcast_in_dim.5
  81.2 4.6 %all-to-all-start.1 = ((bf16[2,8,192,512]{3,2,0,1:T(8,128)(2,1)}), bf16[2,8,192,512]{3,2,0,1:T(8,128)(2,1)}, u32[]{:S(2)}, u32[]{:S(2)}) async-start(bf16[2,8,192,512]{3,2,0,1:T(8,128)(2,1)} %broadcast_in_dim.5), calls=%async_computation.1 | async-start | bytes 6291456 | tf_op jit(solution)/shard_map/all_to_all | solution.py:36
  86.6 41.9 %all-to-all-done.1 = bf16[2,8,192,512]{3,2,0,1:T(8,128)(2,1)} async-done(((bf16[2,8,192,512]{3,2,0,1:T(8,128)(2,1)}), bf16[2,8,192,512]{3,2,0,1:T(8,128)(2,1)}, u32[]{:S(2)}, u32[]{:S(2)}) %all-to-all-start.1) | async-done | bytes 3145760 | tf_op jit(solution)/shard_map/all_to_all | solution.py:36
  128.6 2.1 copy.81
  130.7 3.7 %multiply_reduce_fusion = f32[2,512]{1,0:T(2,128)S(1)} fusion(bf16[2,8,192,512]{3,2,0,1:T(8,128)(2,1)} %all-to-all-done.1), kind=kLoop, calls=%fused_computation.10 | loop fusion | flops 4717568 | bytes 3149824 | tf_op jit(solution)/shard_map/reduce_sum | solution.py:153
  138.5 26.4 %all-gather.4.cloned.1.call-done = bf16[1536,768]{1,0:T(8,128)(2,1)} async-done(((bf16[192,768]{1,0:T(8,128)(2,1)}), bf16[1536,768]{1,0:T(8,128)(2,1)}) %all-gather.4.cloned.1.call-update) | async-done | bytes 2359312 | tf_op jit(solution)/shard_map/all_gather | solution.py:127
  165.2 3.8 %fusion.22.query_ref = bf16[2,512,192]{2,1,0:T(8,128)(2,1)} fusion(bf16[2,1536,512]{2,1,0:T(8,128)(2,1)} %copy-done.1, bf16[192,1536]{1,0:T(8,128)(2,1)S(1)} %copy-done.9), kind=kOutput, calls=%fused_computation.31 | convolution fusion | flops 604372992 | bytes 4128768 | tf_op jit(solution)/shard_map/sdt,ed->ste/dot_general | solution.py:156
  168.9 67.4 %all-gather.6.cloned.1.call-done = bf16[2,32,192,512]{3,2,1,0:T(8,128)(2,1)} async-done(((bf16[2,2,192,512]{3,2,1,0:T(8,128)(2,1)}), bf16[2,32,192,512]{3,2,1,0:T(8,128)(2,1)}) %all-gather.6.cloned.1.call-update) | async-done | bytes 12582928 | tf_op jit(solution)/shard_map/all_gather | solution.py:166
  236.4 24.1 %shard_map.82 = bf16[2,512,192]{2,1,0:T(8,128)(2,1)} custom-call(bf16[2,512,192]{2,1,0:T(8,128)(2,1)} %fusion.22.query_ref, bf16[2,16,2,192,512]{4,3,2,1,0:T(8,128)(2,1)} %bitcast.65, bf16[2,16,2,192,512]{4,3,2,1,0:T(8,128)(2,1)} %bitcast.66), custom_call_target="tpu_custom_call" | custom-call | tf_op jit(solution)/shard_map/pallas_call | solution.py:83
  260.5 1.9 copy.96
  262.4 6.7 %all-to-all-start.2 = ((bf16[8,2,64,192]{3,2,1,0:T(8,128)(2,1)}), bf16[8,2,64,192]{3,2,1,0:T(8,128)(2,1)S(1)}, u32[]{:S(2)}, u32[]{:S(2)}) async-start(bf16[8,2,64,192]{3,2,1,0:T(8,128)(2,1)} %bitcast.64), calls=%async_computation.2 | async-start | bytes 1048576 | tf_op jit(solution)/shard_map/all_to_all | solution.py:177
  269.1 1.4 constant_dynamic-slice_fusion.1
  270.8 10.3 %all-to-all-done.2 = bf16[8,2,64,192]{3,2,1,0:T(8,128)(2,1)S(1)} async-done(((bf16[8,2,64,192]{3,2,1,0:T(8,128)(2,1)}), bf16[8,2,64,192]{3,2,1,0:T(8,128)(2,1)S(1)}, u32[]{:S(2)}, u32[]{:S(2)}) %all-to-all-start.2) | async-done | bytes 393248 | tf_op jit(solution)/shard_map/all_to_all | solution.py:177
  281.8 2.1 fusion.20
  284.0 2.1 fusion.18
  (47 shorter events, 14.8 us)
Async XLA Ops:
  6.5 128.7 %copy-start = (bf16[192,1536]{1,0:T(8,128)(2,1)S(1)}, bf16[192,1536]{1,0:T(8,128)(2,1)}, u32[]{:S(2)}) copy-start(bf16[192,1536]{1,0:T(8,128)(2,1)} %param.13) | copy-start | bytes 1769476
  9.6 46.8 %all-to-all-start = ((bf16[2,8,64,1536]{3,2,0,1:T(8,128)(2,1)}), bf16[2,8,64,1536]{3,2,0,1:T(8,128)(2,1)}, u32[]{:S(2)}, u32[]{:S(2)}) async-start(bf16[2,8,64,1536]{3,2,0,1:T(8,128)(2,1)} %broadcast_in_dim.4), calls=%async_computation | async-start | bytes 6291456 | tf_op jit(solution)/shard_map/all_to_all | solution.py:36
  59.1 4.3 %copy-start.6 = (f32[1536]{0:T(1024)S(1)}, f32[1536]{0:T(1024)}, u32[]{:S(2)}) copy-start(f32[1536]{0:T(1024)} %param.9) | copy-start | bytes 18436
  61.3 1.7 copy-start.3
  63.4 7.0 %copy-start.8 = (bf16[5,192,1536]{2,1,0:T(8,128)(2,1)S(1)}, bf16[5,192,1536]{2,1,0:T(8,128)(2,1)}, u32[]{:S(2)}) copy-start(bf16[5,192,1536]{2,1,0:T(8,128)(2,1)} %param.10) | copy-start | bytes 8847364
  67.8 8.9 %collective-permute-start = (bf16[2,2,1536]{2,1,0:T(2,128)(2,1)S(1)}, bf16[2,2,1536]{2,1,0:T(2,128)(2,1)S(1)}, u32[]{:S(2)}, u32[]{:S(2)}) collective-permute-start(bf16[2,2,1536]{2,1,0:T(2,128)(2,1)S(1)} %get-tuple-element.9), channel_id=1, source_target_pairs={{0,8},{8,16},{16,24},{24,32},{32,40},{40,48},{48,56},{56,64},{64,7... | collective-permute-start | bytes 36872 | tf_op jit(solution)/shard_map/ppermute | solution.py:23
  69.1 5.2 %collective-permute-start.1 = (bf16[2,2,1536]{2,1,0:T(2,128)(2,1)S(1)}, bf16[2,2,1536]{2,1,0:T(2,128)(2,1)S(1)}, u32[]{:S(2)}, u32[]{:S(2)}) collective-permute-start(bf16[2,2,1536]{2,1,0:T(2,128)(2,1)S(1)} %get-tuple-element.10), channel_id=1, source_target_pairs={{8,0},{16,8},{24,16},{32,24},{40,32},{48,40},{56,48},{64,56},{72,6... | collective-permute-start | bytes 36872 | tf_op jit(solution)/shard_map/ppermute | solution.py:25
  81.1 4.6 %copy-start.5 = (bf16[192,1536]{1,0:T(8,128)(2,1)S(1)}, bf16[192,1536]{1,0:T(8,128)(2,1)}, u32[]{:S(2)}) copy-start(bf16[192,1536]{1,0:T(8,128)(2,1)} %param.15) | copy-start | bytes 1769476
  81.2 47.4 %all-to-all-start.1 = ((bf16[2,8,192,512]{3,2,0,1:T(8,128)(2,1)}), bf16[2,8,192,512]{3,2,0,1:T(8,128)(2,1)}, u32[]{:S(2)}, u32[]{:S(2)}) async-start(bf16[2,8,192,512]{3,2,0,1:T(8,128)(2,1)} %broadcast_in_dim.5), calls=%async_computation.1 | async-start | bytes 6291456 | tf_op jit(solution)/shard_map/all_to_all | solution.py:36
  85.7 79.1 %all-gather.4.cloned.1.call-start = ((), (), s32[]{:S(2)}) async-start(), calls=%async_computation.3 | async-start | bytes 2654208 | tf_op jit(solution)/shard_map/all_gather | solution.py:127
  86.6 149.8 %all-gather.6.cloned.1.call-start = ((), (), s32[]{:S(2)}) async-start(), calls=%async_computation.4 | async-start | bytes 13369344 | tf_op jit(solution)/shard_map/all_gather | solution.py:166
  130.7 4.5 %copy-start.2 = (bf16[2,8,192,512]{3,2,1,0:T(8,128)(2,1)}, bf16[2,8,192,512]{3,2,1,0:T(8,128)(2,1)S(1)}, u32[]{:S(2)}) copy-start(bf16[2,8,192,512]{3,2,1,0:T(8,128)(2,1)S(1)} %copy.81) | copy-start | bytes 9437188
  130.7 3.7 %copy-start.7 = (f32[1536]{0:T(1024)S(1)}, f32[1536]{0:T(1024)}, u32[]{:S(2)}) copy-start(f32[1536]{0:T(1024)} %param.11) | copy-start | bytes 18436
  135.2 2.3 copy-start.1
  135.2 1.5 copy-start.4
  136.7 28.5 %copy-start.9 = (bf16[192,1536]{1,0:T(8,128)(2,1)S(1)}, bf16[192,1536]{1,0:T(8,128)(2,1)}, u32[]{:S(2)}) copy-start(bf16[192,1536]{1,0:T(8,128)(2,1)} %param.12) | copy-start | bytes 1769476
  164.9 119.1 %collective-permute-start.2 = (bf16[1536,768]{1,0:T(8,128)(2,1)}, bf16[1536,768]{1,0:T(8,128)(2,1)}, u32[]{:S(2)}, u32[]{:S(2)}) collective-permute-start(bf16[1536,768]{1,0:T(8,128)(2,1)} %all-gather.4.cloned.1.call-done), channel_id=1, source_target_pairs={{0,8},{8,0},{1,9},{9,1},{2,10},{10,2},{3,11},{11,3},{4,12},{12,4},... | collective-permute-start | bytes 7077896 | tf_op jit(solution)/shard_map/ppermute | solution.py:181
  262.4 18.7 %all-to-all-start.2 = ((bf16[8,2,64,192]{3,2,1,0:T(8,128)(2,1)}), bf16[8,2,64,192]{3,2,1,0:T(8,128)(2,1)S(1)}, u32[]{:S(2)}, u32[]{:S(2)}) async-start(bf16[8,2,64,192]{3,2,1,0:T(8,128)(2,1)} %bitcast.64), calls=%async_computation.2 | async-start | bytes 1048576 | tf_op jit(solution)/shard_map/all_to_all | solution.py:177
Sparse Core Ops, SparseCore 0:
  88.9 75.9 all-gather.3
  166.5 69.8 all-gather.5

commit v15 on v14

--- a/solution.py
+++ b/solution.py
@@ -76,7 +76,7 @@
         out_ref[0] = (summed_ref[...] / total_ref[...]).astype(out_ref.dtype)
 
 
-def flash_attention(queries, kv_tile, sources_per_step=4):
+def flash_attention(queries, kv_tile, sources_per_step=8):
     sample_count, query_count, head_width = queries.shape
     _, source_count, _, _, source_rows = kv_tile.shape
     sources_per_step = math.gcd(source_count, sources_per_step)
@@ -147,7 +147,9 @@
     column_start = lax.axis_index(BATCH) * local_out
     own_columns = lax.dynamic_slice_in_dim(gathered_in, column_start, local_out, 2)
     residual = jnp.transpose(own_columns, (0, 2, 1)).astype(jnp.float32)
-    hidden_part = (residual + conv_sum).astype(jnp.bfloat16)
+    hidden_part, own_half = lax.optimization_barrier(
+        ((residual + conv_sum).astype(jnp.bfloat16), own_half)
+    )
     hidden_full = gather_batch(hidden_part, 1)
     hidden_float = hidden_full.astype(jnp.float32)
     norm_scale = lax.rsqrt(jnp.mean(hidden_float * hidden_float, axis=1, keepdims=True) + 1e-06)
@@ -162,7 +164,7 @@
     value_rows = jnp.einsum(
         "sdt,ed->set", normed, value_weight, preferred_element_type=jnp.float32
     ).astype(jnp.bfloat16)
-    kv_rows, own_half = lax.optimization_barrier((jnp.stack([key_rows, value_rows]), own_half))
+    kv_rows = jnp.stack([key_rows, value_rows])
     kv_tile = lax.all_gather(kv_rows, SEQ, axis=1)
     attended = flash_attention(queries, kv_tile)
     row_start = lax.axis_index(BATCH) * own_rows

time: 295 us -> 270 us (0.915)
  waiting for transfers between devices: 189 us -> 132 us
  blocking collectives: 0 us -> 42 us
  starting transfers between devices: 21.2 us -> 16.8 us
  other arithmetic: 13.3 us -> 10.2 us
    all_to_all x0 -> x1, blocking collectives: none -> 42 us  [gather_batch(): arrived = lax.all_to_all(copies, BATCH, axis, axis, tiled=False)]
    all_to_all x2 -> x1, waiting for transfers between devices: 81.8 us -> 42.2 us  [gather_batch(): arrived = lax.all_to_all(copies, BATCH, axis, axis, tiled=False)]
    all_gather x1, waiting for transfers between devices: 26.4 us -> 11.5 us  [shards(): lax.all_gather(lax.dynamic_slice_in_dim(output_weight, mine * half_width,...]
    all_to_all x2 -> x1, starting transfers between devices: 11.6 us -> 7.15 us  [gather_batch(): arrived = lax.all_to_all(copies, BATCH, axis, axis, tiled=False)]
    reduce_sum x1, other arithmetic: 3.69 us -> 0.66 us  [shards(): jnp.mean(hidden_float * hidden_float, axis=1, keepdims=True) + 1e-06]
  transfers between devices with their start and end apart: 8 -> 7, of which waited for: 6 -> 5; matrix products, arithmetic and copies ran while one was open for 8% -> 10% of each run, Pallas kernels for 8% -> 9%
where the time goes in v15:
time: 270 us; the launch traced here: 269 us
  waiting for transfers between devices  132 us (49%)
  blocking collectives  42 us (16%)
  Pallas kernels  23.2 us (9%)
  starting transfers between devices  16.8 us (6%)
  matrix products  15.6 us (6%)
  local copies, waits for them, and re-layouts  15 us (6%)
  between operations  13.7 us (5%)
  other arithmetic  10.2 us (4%)
    all_gather x1, waiting for transfers between devices, shards(): kv_tile = lax.all_gather(kv_rows, SEQ, axis=1)  65.7 us
    all_to_all x1, waiting for transfers between devices, gather_batch(): arrived = lax.all_to_all(copies, BATCH, axis, axis, tiled=False)  42.2 us
    all_to_all x1, blocking collectives, gather_batch(): arrived = lax.all_to_all(copies, BATCH, axis, axis, tiled=False)  42 us
    pallas_call x1, Pallas kernels, flash_attention(): pl.pallas_call(flash_step, grid=(sample_count, source_count // sources_pe...  23.2 us
    all_gather x1, waiting for transfers between devices, shards(): lax.all_gather(lax.dynamic_slice_in_dim(output_weight, mine * half_width,...  11.5 us
    all_to_all x1, waiting for transfers between devices, shards(): arrived = lax.all_to_all(outgoing, BATCH, 0, 0, tiled=False)  10.3 us
    all_to_all x1, starting transfers between devices, gather_batch(): arrived = lax.all_to_all(copies, BATCH, axis, axis, tiled=False)  7.15 us
    all_to_all x1, starting transfers between devices, shards(): arrived = lax.all_to_all(outgoing, BATCH, 0, 0, tiled=False)  6.71 us
  transfers between devices with their start and end apart: 7, of which 5 were waited for; matrix products, arithmetic and copies ran while one was open for 10% of the time, Pallas kernels for 9%

profile of v15, /device:TPU:0, one launch (start us, length us, event | category | flops | bytes accessed | tf_op | source)
XLA Modules:
  0.0 269.0 jit_solution(12504845103914914241)
XLA Ops:
  6.5 3.0 %broadcast_in_dim.4 = bf16[2,8,64,1536]{3,2,0,1:T(8,128)(2,1)} broadcast(bf16[2,64,1536]{2,1,0:T(8,128)(2,1)} %param.8), dimensions={0,2,3} | broadcast | bytes 3538944 | tf_op jit(solution)/shard_map/broadcast_in_dim | solution.py:35
  9.6 7.1 %all-to-all-start = ((bf16[2,8,64,1536]{3,2,0,1:T(8,128)(2,1)}), bf16[2,8,64,1536]{3,2,0,1:T(8,128)(2,1)}, u32[]{:S(2)}, u32[]{:S(2)}) async-start(bf16[2,8,64,1536]{3,2,0,1:T(8,128)(2,1)} %broadcast_in_dim.4), calls=%async_computation | async-start | bytes 6291456 | tf_op jit(solution)/shard_map/all_to_all | solution.py:36
  17.6 42.2 %all-to-all-done = bf16[2,8,64,1536]{3,2,0,1:T(8,128)(2,1)} async-done(((bf16[2,8,64,1536]{3,2,0,1:T(8,128)(2,1)}), bf16[2,8,64,1536]{3,2,0,1:T(8,128)(2,1)}, u32[]{:S(2)}, u32[]{:S(2)}) %all-to-all-start) | async-done | bytes 3145760 | tf_op jit(solution)/shard_map/all_to_all | solution.py:36
  59.8 2.6 multiply_reduce_fusion.1
  62.5 2.2 copy.78
  64.6 1.6 copy-done.3
  66.7 4.4 %fusion.7 = bf16[2,512,1536]{2,1,0:T(8,128)(2,1)S(1)} fusion(f32[1536]{0:T(1024)S(1)} %copy-done.6, f32[2,512]{1,0:T(2,128)S(1)} %rsqrt.20, bf16[2,8,64,1536]{3,2,1,0:T(8,128)(2,1)} %copy-done.3), kind=kLoop, calls=%fused_computation.8 | loop fusion | flops 18874368 | bytes 6301696 | tf_op jit(solution)/shard_map/convert_element_type | solution.py:136
  71.1 1.3 collective-permute-start
  72.4 1.3 collective-permute-start.1
  74.9 2.7 %collective-permute-done.1 = bf16[2,2,1536]{2,1,0:T(2,128)(2,1)S(1)} collective-permute-done((bf16[2,2,1536]{2,1,0:T(2,128)(2,1)S(1)}, bf16[2,2,1536]{2,1,0:T(2,128)(2,1)S(1)}, u32[]{:S(2)}, u32[]{:S(2)}) %collective-permute-start.1) | collective-permute-done | bytes 12320 | tf_op jit(solution)/shard_map/ppermute | solution.py:25
  77.7 1.2 fusion.14
  80.0 1.2 fusion.9
  81.2 1.3 fusion.43
  82.5 11.5 %all-gather.4.cloned.1.call-done = bf16[1536,768]{1,0:T(8,128)(2,1)} async-done(((bf16[192,768]{1,0:T(8,128)(2,1)}), bf16[1536,768]{1,0:T(8,128)(2,1)}) %all-gather.4.cloned.1.call-update) | async-done | bytes 2359312 | tf_op jit(solution)/shard_map/all_gather | solution.py:127
  94.3 42.0 %all_to_all.15 = bf16[2,8,192,512]{3,2,0,1:T(8,128)(2,1)S(1)} all-to-all(bf16[2,8,192,512]{3,2,0,1:T(8,128)(2,1)S(1)} %broadcast_in_dim.5), channel_id=1, replica_groups=mesh['chip_x'=2,'chip_z'=4,'core'=2,'peer_y'=4,'peer_x'=2] {'peer_y','pe..., dimensions={1} | all-to-all | bytes 6291456 | tf_op jit(solution)/shard_map/all_to_all | solution.py:36
  142.9 3.8 %fusion.22.query_ref = bf16[2,512,192]{2,1,0:T(8,128)(2,1)} fusion(bf16[2,1536,512]{2,1,0:T(8,128)(2,1)} %copy-done.1, bf16[192,1536]{1,0:T(8,128)(2,1)S(1)} %copy-done.9), kind=kOutput, calls=%fused_computation.31 | convolution fusion | flops 604372992 | bytes 4128768 | tf_op jit(solution)/shard_map/sdt,ed->ste/dot_general | solution.py:158
  146.7 65.7 %all-gather.6.cloned.1.call-done = bf16[2,32,192,512]{3,2,1,0:T(8,128)(2,1)} async-done(((bf16[2,2,192,512]{3,2,1,0:T(8,128)(2,1)}), bf16[2,32,192,512]{3,2,1,0:T(8,128)(2,1)}) %all-gather.6.cloned.1.call-update) | async-done | bytes 12582928 | tf_op jit(solution)/shard_map/all_gather | solution.py:168
  212.4 23.2 %shard_map.82 = bf16[2,512,192]{2,1,0:T(8,128)(2,1)} custom-call(bf16[2,512,192]{2,1,0:T(8,128)(2,1)} %fusion.22.query_ref, bf16[2,16,2,192,512]{4,3,2,1,0:T(8,128)(2,1)} %bitcast.65, bf16[2,16,2,192,512]{4,3,2,1,0:T(8,128)(2,1)} %bitcast.66), custom_call_target="tpu_custom_call" | custom-call | tf_op jit(solution)/shard_map/pallas_call | solution.py:83
  235.6 1.9 copy.96
  237.5 6.7 %all-to-all-start.2 = ((bf16[8,2,64,192]{3,2,1,0:T(8,128)(2,1)}), bf16[8,2,64,192]{3,2,1,0:T(8,128)(2,1)S(1)}, u32[]{:S(2)}, u32[]{:S(2)}) async-start(bf16[8,2,64,192]{3,2,1,0:T(8,128)(2,1)} %bitcast.64), calls=%async_computation.2 | async-start | bytes 1048576 | tf_op jit(solution)/shard_map/all_to_all | solution.py:179
  244.2 1.4 constant_dynamic-slice_fusion
  245.9 10.3 %all-to-all-done.2 = bf16[8,2,64,192]{3,2,1,0:T(8,128)(2,1)S(1)} async-done(((bf16[8,2,64,192]{3,2,1,0:T(8,128)(2,1)}), bf16[8,2,64,192]{3,2,1,0:T(8,128)(2,1)S(1)}, u32[]{:S(2)}, u32[]{:S(2)}) %all-to-all-start.2) | async-done | bytes 393248 | tf_op jit(solution)/shard_map/all_to_all | solution.py:179
  256.9 2.1 fusion.20
  259.1 2.1 fusion.18
  (46 shorter events, 12.3 us)
Async XLA Ops:
  6.5 132.8 %copy-start = (bf16[192,1536]{1,0:T(8,128)(2,1)S(1)}, bf16[192,1536]{1,0:T(8,128)(2,1)}, u32[]{:S(2)}) copy-start(bf16[192,1536]{1,0:T(8,128)(2,1)} %param.13) | copy-start | bytes 1769476
  9.6 7.2 %copy-start.5 = (bf16[192,1536]{1,0:T(8,128)(2,1)S(1)}, bf16[192,1536]{1,0:T(8,128)(2,1)}, u32[]{:S(2)}) copy-start(bf16[192,1536]{1,0:T(8,128)(2,1)} %param.15) | copy-start | bytes 1769476
  9.6 50.2 %all-to-all-start = ((bf16[2,8,64,1536]{3,2,0,1:T(8,128)(2,1)}), bf16[2,8,64,1536]{3,2,0,1:T(8,128)(2,1)}, u32[]{:S(2)}, u32[]{:S(2)}) async-start(bf16[2,8,64,1536]{3,2,0,1:T(8,128)(2,1)} %broadcast_in_dim.4), calls=%async_computation | async-start | bytes 6291456 | tf_op jit(solution)/shard_map/all_to_all | solution.py:36
  16.7 77.3 %all-gather.4.cloned.1.call-start = ((), (), s32[]{:S(2)}) async-start(), calls=%async_computation.3 | async-start | bytes 2654208 | tf_op jit(solution)/shard_map/all_gather | solution.py:127
  17.6 194.8 %all-gather.6.cloned.1.call-start = ((), (), s32[]{:S(2)}) async-start(), calls=%async_computation.4 | async-start | bytes 13369344 | tf_op jit(solution)/shard_map/all_gather | solution.py:168
  62.5 4.3 %copy-start.6 = (f32[1536]{0:T(1024)S(1)}, f32[1536]{0:T(1024)}, u32[]{:S(2)}) copy-start(f32[1536]{0:T(1024)} %param.9) | copy-start | bytes 18436
  64.6 1.6 copy-start.3
  66.7 7.0 %copy-start.8 = (bf16[5,192,1536]{2,1,0:T(8,128)(2,1)S(1)}, bf16[5,192,1536]{2,1,0:T(8,128)(2,1)}, u32[]{:S(2)}) copy-start(bf16[5,192,1536]{2,1,0:T(8,128)(2,1)} %param.10) | copy-start | bytes 8847364
  71.1 7.7 %collective-permute-start = (bf16[2,2,1536]{2,1,0:T(2,128)(2,1)S(1)}, bf16[2,2,1536]{2,1,0:T(2,128)(2,1)S(1)}, u32[]{:S(2)}, u32[]{:S(2)}) collective-permute-start(bf16[2,2,1536]{2,1,0:T(2,128)(2,1)S(1)} %get-tuple-element.9), channel_id=1, source_target_pairs={{0,8},{8,16},{16,24},{24,32},{32,40},{40,48},{48,56},{56,64},{64,7... | collective-permute-start | bytes 36872 | tf_op jit(solution)/shard_map/ppermute | solution.py:23
  72.4 5.2 %collective-permute-start.1 = (bf16[2,2,1536]{2,1,0:T(2,128)(2,1)S(1)}, bf16[2,2,1536]{2,1,0:T(2,128)(2,1)S(1)}, u32[]{:S(2)}, u32[]{:S(2)}) collective-permute-start(bf16[2,2,1536]{2,1,0:T(2,128)(2,1)S(1)} %get-tuple-element.10), channel_id=1, source_target_pairs={{8,0},{16,8},{24,16},{32,24},{40,32},{48,40},{56,48},{64,56},{72,6... | collective-permute-start | bytes 36872 | tf_op jit(solution)/shard_map/ppermute | solution.py:25
  137.0 0.7 copy-start.7
  137.7 1.6 copy-start.2
  139.4 2.3 copy-start.1
  139.4 1.5 copy-start.4
  140.8 2.1 copy-start.9
  142.6 116.5 %collective-permute-start.2 = (bf16[1536,768]{1,0:T(8,128)(2,1)}, bf16[1536,768]{1,0:T(8,128)(2,1)}, u32[]{:S(2)}, u32[]{:S(2)}) collective-permute-start(bf16[1536,768]{1,0:T(8,128)(2,1)} %all-gather.4.cloned.1.call-done), channel_id=1, source_target_pairs={{0,8},{8,0},{1,9},{9,1},{2,10},{10,2},{3,11},{11,3},{4,12},{12,4},... | collective-permute-start | bytes 7077896 | tf_op jit(solution)/shard_map/ppermute | solution.py:183
  237.5 18.7 %all-to-all-start.2 = ((bf16[8,2,64,192]{3,2,1,0:T(8,128)(2,1)}), bf16[8,2,64,192]{3,2,1,0:T(8,128)(2,1)S(1)}, u32[]{:S(2)}, u32[]{:S(2)}) async-start(bf16[8,2,64,192]{3,2,1,0:T(8,128)(2,1)} %bitcast.64), calls=%async_computation.2 | async-start | bytes 1048576 | tf_op jit(solution)/shard_map/all_to_all | solution.py:179
Sparse Core Ops, SparseCore 0:
  19.9 74.1 all-gather.3
  142.7 69.5 all-gather.5

commit v16 on v15

--- a/solution.py
+++ b/solution.py
@@ -147,10 +147,8 @@
     column_start = lax.axis_index(BATCH) * local_out
     own_columns = lax.dynamic_slice_in_dim(gathered_in, column_start, local_out, 2)
     residual = jnp.transpose(own_columns, (0, 2, 1)).astype(jnp.float32)
-    hidden_part, own_half = lax.optimization_barrier(
-        ((residual + conv_sum).astype(jnp.bfloat16), own_half)
-    )
-    hidden_full = gather_batch(hidden_part, 1)
+    hidden_part = (residual + conv_sum).astype(jnp.bfloat16)
+    hidden_full, own_half = lax.optimization_barrier((gather_batch(hidden_part, 1), own_half))
     hidden_float = hidden_full.astype(jnp.float32)
     norm_scale = lax.rsqrt(jnp.mean(hidden_float * hidden_float, axis=1, keepdims=True) + 1e-06)
     normed = (hidden_float * norm_scale * attention_gain[None, :, None]).astype(jnp.bfloat16)

time: 270 us -> 265 us (0.981)
  waiting for transfers between devices: 132 us -> 118 us
  local copies, waits for them, and re-layouts: 15 us -> 19.6 us
    all_gather x1, waiting for transfers between devices: 11.5 us -> 0.01 us  [shards(): lax.all_gather(lax.dynamic_slice_in_dim(output_weight, mine * half_width,...]
    optimization_barrier x0 -> x1, local copies, waits for them, and re-layouts: none -> 4.65 us  [shards(): lax.optimization_barrier((gather_batch(hidden_part, 1), own_half))]
    all_to_all x1, waiting for transfers between devices: 10.3 us -> 7.36 us  [shards(): arrived = lax.all_to_all(outgoing, BATCH, 0, 0, tiled=False)]
  transfers between devices with their start and end apart: 7 -> 7, of which waited for: 5 -> 4; matrix products, arithmetic and copies ran while one was open for 10% -> 12% of each run, Pallas kernels for 9% -> 9%
where the time goes in v16:
time: 265 us; the launch traced here: 264 us
  waiting for transfers between devices  118 us (45%)
  blocking collectives  43.6 us (16%)
  Pallas kernels  23.2 us (9%)
  local copies, waits for them, and re-layouts  19.6 us (7%)
  starting transfers between devices  18.1 us (7%)
  matrix products  14.8 us (6%)
  between operations  13.6 us (5%)
  other arithmetic  12.5 us (5%)
    all_gather x1, waiting for transfers between devices, shards(): kv_tile = lax.all_gather(kv_rows, SEQ, axis=1)  66 us
    all_to_all x1, blocking collectives, gather_batch(): arrived = lax.all_to_all(copies, BATCH, axis, axis, tiled=False)  43.6 us
    all_to_all x1, waiting for transfers between devices, gather_batch(): arrived = lax.all_to_all(copies, BATCH, axis, axis, tiled=False)  42.2 us
    pallas_call x1, Pallas kernels, flash_attention(): pl.pallas_call(flash_step, grid=(sample_count, source_count // sources_pe...  23.2 us
    all_to_all x1, waiting for transfers between devices, shards(): arrived = lax.all_to_all(outgoing, BATCH, 0, 0, tiled=False)  7.36 us
    all_to_all x1, starting transfers between devices, gather_batch(): arrived = lax.all_to_all(copies, BATCH, axis, axis, tiled=False)  7.15 us
    all_to_all x1, starting transfers between devices, shards(): arrived = lax.all_to_all(outgoing, BATCH, 0, 0, tiled=False)  6.71 us
    dot_general x5, matrix products, shards(): jnp.einsum('std,ed->set', framed[:, offset:offset + seq_rows], conv_weigh...  5.97 us
  transfers between devices with their start and end apart: 7, of which 4 were waited for; matrix products, arithmetic and copies ran while one was open for 12% of the time, Pallas kernels for 9%

profile of v16, /device:TPU:0, one launch (start us, length us, event | category | flops | bytes accessed | tf_op | source)
XLA Modules:
  0.0 263.8 jit_solution(6541447408580947307)
XLA Ops:
  6.5 3.0 %broadcast_in_dim.4 = bf16[2,8,64,1536]{3,2,0,1:T(8,128)(2,1)} broadcast(bf16[2,64,1536]{2,1,0:T(8,128)(2,1)} %param.8), dimensions={0,2,3} | broadcast | bytes 3538944 | tf_op jit(solution)/shard_map/broadcast_in_dim | solution.py:35
  9.6 7.1 %all-to-all-start = ((bf16[2,8,64,1536]{3,2,0,1:T(8,128)(2,1)}), bf16[2,8,64,1536]{3,2,0,1:T(8,128)(2,1)}, u32[]{:S(2)}, u32[]{:S(2)}) async-start(bf16[2,8,64,1536]{3,2,0,1:T(8,128)(2,1)} %broadcast_in_dim.4), calls=%async_computation | async-start | bytes 6291456 | tf_op jit(solution)/shard_map/all_to_all | solution.py:36
  17.6 42.2 %all-to-all-done = bf16[2,8,64,1536]{3,2,0,1:T(8,128)(2,1)} async-done(((bf16[2,8,64,1536]{3,2,0,1:T(8,128)(2,1)}), bf16[2,8,64,1536]{3,2,0,1:T(8,128)(2,1)}, u32[]{:S(2)}, u32[]{:S(2)}) %all-to-all-start) | async-done | bytes 3145760 | tf_op jit(solution)/shard_map/all_to_all | solution.py:36
  59.8 2.6 multiply_reduce_fusion
  62.5 2.2 copy.78
  64.6 1.6 copy-done.2
  66.7 4.4 %fusion.10 = bf16[2,512,1536]{2,1,0:T(8,128)(2,1)S(1)} fusion(f32[1536]{0:T(1024)S(1)} %copy-done.5, f32[2,512]{1,0:T(2,128)S(1)} %rsqrt.20, bf16[2,8,64,1536]{3,2,1,0:T(8,128)(2,1)} %copy-done.2), kind=kLoop, calls=%fused_computation.13 | loop fusion | flops 18874368 | bytes 6301696 | tf_op jit(solution)/shard_map/convert_element_type | solution.py:136
  71.1 1.3 collective-permute-start
  72.4 1.3 collective-permute-start.1
  74.9 2.7 %collective-permute-done.1 = bf16[2,2,1536]{2,1,0:T(2,128)(2,1)S(1)} collective-permute-done((bf16[2,2,1536]{2,1,0:T(2,128)(2,1)S(1)}, bf16[2,2,1536]{2,1,0:T(2,128)(2,1)S(1)}, u32[]{:S(2)}, u32[]{:S(2)}) %collective-permute-start.1) | collective-permute-done | bytes 12320 | tf_op jit(solution)/shard_map/ppermute | solution.py:25
  82.8 43.6 %all_to_all.15 = bf16[2,8,192,512]{3,2,0,1:T(8,128)(2,1)S(1)} all-to-all(bf16[2,8,192,512]{3,2,0,1:T(8,128)(2,1)S(1)} %broadcast_in_dim.5), channel_id=1, replica_groups=mesh['chip_x'=2,'chip_z'=4,'core'=2,'peer_y'=4,'peer_x'=2] {'peer_y','pe..., dimensions={1} | all-to-all | bytes 6291456 | tf_op jit(solution)/shard_map/all_to_all | solution.py:36
  126.4 1.9 copy.81
  128.4 2.7 %fusion = f32[2,512]{1,0:T(2,128)S(1)} fusion(bf16[2,1536,512]{2,1,0:T(8,128)(2,1)} %bitcast.63), kind=kLoop, calls=%fused_computation.3 | loop fusion | flops 4717568 | bytes 3149824 | tf_op jit(solution)/shard_map/reduce_sum | solution.py:153
  134.4 1.6 collective-permute-start.2
  136.0 4.1 %fusion.25.query_ref = bf16[2,512,192]{2,1,0:T(8,128)(2,1)} fusion(bf16[192,1536]{1,0:T(8,128)(2,1)S(1)} %copy-done.8, bf16[2,1536,512]{2,1,0:T(8,128)(2,1)} %bitcast.64, f32[1536]{0:T(1024)S(1)} %copy-done.9, f32[2,512]{1,0:T(2,128)S(1)} %add_rsqrt_fusion), kind=kOutput, calls=%fused_computation.34 | convolution fusion | flops 610664448 | bytes 4139008 | tf_op jit(solution)/shard_map/sdt,ed->ste/dot_general | solution.py:156
  140.0 66.0 %all-gather.6.cloned.1.call-done = bf16[2,32,192,512]{3,2,1,0:T(8,128)(2,1)} async-done(((bf16[2,2,192,512]{3,2,1,0:T(8,128)(2,1)}), bf16[2,32,192,512]{3,2,1,0:T(8,128)(2,1)}) %all-gather.6.cloned.1.call-update) | async-done | bytes 12582928 | tf_op jit(solution)/shard_map/all_gather | solution.py:166
  206.0 23.2 %shard_map.82 = bf16[2,512,192]{2,1,0:T(8,128)(2,1)} custom-call(bf16[2,512,192]{2,1,0:T(8,128)(2,1)} %fusion.25.query_ref, bf16[2,16,2,192,512]{4,3,2,1,0:T(8,128)(2,1)} %bitcast.61, bf16[2,16,2,192,512]{4,3,2,1,0:T(8,128)(2,1)} %bitcast.62), custom_call_target="tpu_custom_call" | custom-call | tf_op jit(solution)/shard_map/pallas_call | solution.py:83
  229.2 1.9 copy.95
  231.1 6.7 %all-to-all-start.2 = ((bf16[8,2,64,192]{3,2,1,0:T(8,128)(2,1)}), bf16[8,2,64,192]{3,2,1,0:T(8,128)(2,1)S(1)}, u32[]{:S(2)}, u32[]{:S(2)}) async-start(bf16[8,2,64,192]{3,2,1,0:T(8,128)(2,1)} %bitcast.71), calls=%async_computation.2 | async-start | bytes 1048576 | tf_op jit(solution)/shard_map/all_to_all | solution.py:177
  237.8 4.6 %copy.82 = bf16[2,1536,512]{1,2,0:T(8,128)(2,1)} copy(bf16[2,1536,512]{2,1,0:T(8,128)(2,1)} %bitcast.65) | data formatting | bytes 6291456 | tf_op jit(solution)/shard_map/optimization_barrier | solution.py:151
  242.5 7.4 %all-to-all-done.2 = bf16[8,2,64,192]{3,2,1,0:T(8,128)(2,1)S(1)} async-done(((bf16[8,2,64,192]{3,2,1,0:T(8,128)(2,1)}), bf16[8,2,64,192]{3,2,1,0:T(8,128)(2,1)S(1)}, u32[]{:S(2)}, u32[]{:S(2)}) %all-to-all-start.2) | async-done | bytes 393248 | tf_op jit(solution)/shard_map/all_to_all | solution.py:177
  250.9 1.5 reshape.44
  252.9 2.1 fusion.21
  255.1 1.9 fusion.50
  (44 shorter events, 12.5 us)
Async XLA Ops:
  6.5 124.6 %copy-start = (bf16[192,1536]{1,0:T(8,128)(2,1)S(1)}, bf16[192,1536]{1,0:T(8,128)(2,1)}, u32[]{:S(2)}) copy-start(bf16[192,1536]{1,0:T(8,128)(2,1)} %param.14) | copy-start | bytes 1769476
  9.6 7.2 %copy-start.4 = (bf16[192,1536]{1,0:T(8,128)(2,1)S(1)}, bf16[192,1536]{1,0:T(8,128)(2,1)}, u32[]{:S(2)}) copy-start(bf16[192,1536]{1,0:T(8,128)(2,1)} %param.15) | copy-start | bytes 1769476
  9.6 50.2 %all-to-all-start = ((bf16[2,8,64,1536]{3,2,0,1:T(8,128)(2,1)}), bf16[2,8,64,1536]{3,2,0,1:T(8,128)(2,1)}, u32[]{:S(2)}, u32[]{:S(2)}) async-start(bf16[2,8,64,1536]{3,2,0,1:T(8,128)(2,1)} %broadcast_in_dim.4), calls=%async_computation | async-start | bytes 6291456 | tf_op jit(solution)/shard_map/all_to_all | solution.py:36
  16.7 111.7 %all-gather.4.cloned.1.call-start = ((), (), s32[]{:S(2)}) async-start(), calls=%async_computation.3 | async-start | bytes 2654208 | tf_op jit(solution)/shard_map/all_gather | solution.py:127
  17.6 188.5 %all-gather.6.cloned.1.call-start = ((), (), s32[]{:S(2)}) async-start(), calls=%async_computation.4 | async-start | bytes 13369344 | tf_op jit(solution)/shard_map/all_gather | solution.py:166
  62.5 4.3 %copy-start.5 = (f32[1536]{0:T(1024)S(1)}, f32[1536]{0:T(1024)}, u32[]{:S(2)}) copy-start(f32[1536]{0:T(1024)} %param.9) | copy-start | bytes 18436
  64.6 1.6 copy-start.2
  66.7 7.0 %copy-start.6 = (bf16[5,192,1536]{2,1,0:T(8,128)(2,1)S(1)}, bf16[5,192,1536]{2,1,0:T(8,128)(2,1)}, u32[]{:S(2)}) copy-start(bf16[5,192,1536]{2,1,0:T(8,128)(2,1)} %param.10) | copy-start | bytes 8847364
  71.1 7.7 %collective-permute-start = (bf16[2,2,1536]{2,1,0:T(2,128)(2,1)S(1)}, bf16[2,2,1536]{2,1,0:T(2,128)(2,1)S(1)}, u32[]{:S(2)}, u32[]{:S(2)}) collective-permute-start(bf16[2,2,1536]{2,1,0:T(2,128)(2,1)S(1)} %get-tuple-element.9), channel_id=1, source_target_pairs={{0,8},{8,16},{16,24},{24,32},{32,40},{40,48},{48,56},{56,64},{64,7... | collective-permute-start | bytes 36872 | tf_op jit(solution)/shard_map/ppermute | solution.py:23
  72.4 5.2 %collective-permute-start.1 = (bf16[2,2,1536]{2,1,0:T(2,128)(2,1)S(1)}, bf16[2,2,1536]{2,1,0:T(2,128)(2,1)S(1)}, u32[]{:S(2)}, u32[]{:S(2)}) collective-permute-start(bf16[2,2,1536]{2,1,0:T(2,128)(2,1)S(1)} %get-tuple-element.10), channel_id=1, source_target_pairs={{8,0},{16,8},{24,16},{32,24},{40,32},{48,40},{56,48},{64,56},{72,6... | collective-permute-start | bytes 36872 | tf_op jit(solution)/shard_map/ppermute | solution.py:25
  128.4 2.7 %copy-start.9 = (f32[1536]{0:T(1024)S(1)}, f32[1536]{0:T(1024)}, u32[]{:S(2)}) copy-start(f32[1536]{0:T(1024)} %param.11) | copy-start | bytes 18436
  128.4 2.8 %copy-start.1 = (bf16[2,8,192,512]{3,2,1,0:T(8,128)(2,1)S(1)}, bf16[2,8,192,512]{3,2,1,0:T(8,128)(2,1)}, u32[]{:S(2)}) copy-start(bf16[2,8,192,512]{3,2,1,0:T(8,128)(2,1)} %copy.81) | copy-start | bytes 9437188
  131.2 1.1 copy-start.7
  132.3 2.1 copy-start.3
  132.3 3.7 %copy-start.8 = (bf16[192,1536]{1,0:T(8,128)(2,1)S(1)}, bf16[192,1536]{1,0:T(8,128)(2,1)}, u32[]{:S(2)}) copy-start(bf16[192,1536]{1,0:T(8,128)(2,1)} %param.12) | copy-start | bytes 1769476
  134.4 118.6 %collective-permute-start.2 = (bf16[1536,768]{1,0:T(8,128)(2,1)S(1)}, bf16[1536,768]{1,0:T(8,128)(2,1)}, u32[]{:S(2)}, u32[]{:S(2)}) collective-permute-start(bf16[1536,768]{1,0:T(8,128)(2,1)S(1)} %copy-done.3), channel_id=1, source_target_pairs={{0,8},{8,0},{1,9},{9,1},{2,10},{10,2},{3,11},{11,3},{4,12},{12,4},... | collective-permute-start | bytes 7077896 | tf_op jit(solution)/shard_map/ppermute | solution.py:181
  231.1 18.7 %all-to-all-start.2 = ((bf16[8,2,64,192]{3,2,1,0:T(8,128)(2,1)}), bf16[8,2,64,192]{3,2,1,0:T(8,128)(2,1)S(1)}, u32[]{:S(2)}, u32[]{:S(2)}) async-start(bf16[8,2,64,192]{3,2,1,0:T(8,128)(2,1)} %bitcast.71), calls=%async_computation.2 | async-start | bytes 1048576 | tf_op jit(solution)/shard_map/all_to_all | solution.py:177
Sparse Core Ops, SparseCore 0:
  19.9 79.5 all-gather.3
  134.5 71.4 all-gather.5

commit v17 on v16

--- a/solution.py
+++ b/solution.py
@@ -73,10 +73,11 @@
 
     @pl.when(block == pl.num_programs(1) - 1)
     def _():
-        out_ref[0] = (summed_ref[...] / total_ref[...]).astype(out_ref.dtype)
-
-
-def flash_attention(queries, kv_tile, sources_per_step=8):
+        finished = (summed_ref[...] / total_ref[...]).astype(out_ref.dtype)
+        out_ref[:, 0] = finished.reshape(out_ref.shape[0], out_ref.shape[2], out_ref.shape[3])
+
+
+def flash_attention(queries, kv_tile, peers, sources_per_step=8):
     sample_count, query_count, head_width = queries.shape
     _, source_count, _, _, source_rows = kv_tile.shape
     sources_per_step = math.gcd(source_count, sources_per_step)
@@ -92,8 +93,12 @@
                 (1, sources_per_step, 1, head_width, source_rows), lambda s, k: (1, k, s, 0, 0)
             ),
         ],
-        out_specs=pl.BlockSpec((1, query_count, head_width), lambda s, k: (s, 0, 0)),
-        out_shape=jax.ShapeDtypeStruct(queries.shape, jnp.bfloat16),
+        out_specs=pl.BlockSpec(
+            (peers, 1, query_count // peers, head_width), lambda s, k: (0, s, 0, 0)
+        ),
+        out_shape=jax.ShapeDtypeStruct(
+            (peers, sample_count, query_count // peers, head_width), jnp.bfloat16
+        ),
         scratch_shapes=[
             pltpu.VMEM((query_count, 1), jnp.float32),
             pltpu.VMEM((query_count, 1), jnp.float32),
@@ -164,26 +169,26 @@
     ).astype(jnp.bfloat16)
     kv_rows = jnp.stack([key_rows, value_rows])
     kv_tile = lax.all_gather(kv_rows, SEQ, axis=1)
-    attended = flash_attention(queries, kv_tile)
+    batch_count = lax.axis_size(BATCH)
+    attended = flash_attention(queries, kv_tile, batch_count)
     row_start = lax.axis_index(BATCH) * own_rows
     own_hidden = jnp.transpose(
         lax.dynamic_slice_in_dim(hidden_full, row_start, own_rows, 2), (0, 2, 1)
     ).astype(jnp.float32)
-    batch_count = lax.axis_size(BATCH)
-    head_width = attended.shape[2]
-    outgoing = jnp.transpose(
-        attended.reshape(sample_count, batch_count, own_rows, head_width), (1, 0, 2, 3)
-    )
-    arrived = lax.all_to_all(outgoing, BATCH, 0, 0, tiled=False)
-    heads_side_by_side = jnp.transpose(arrived, (1, 2, 0, 3)).reshape(
-        sample_count, own_rows, batch_count * head_width
-    )
+    head_width = attended.shape[3]
+    arrived = lax.all_to_all(attended, BATCH, 0, 0, tiled=False)
     other_half = lax.ppermute(own_half, "core", [(0, 1), (1, 0)])
     own_part = jnp.einsum(
-        "std,df->stf", heads_side_by_side, own_half, preferred_element_type=jnp.float32
+        "hstd,hdf->stf",
+        arrived,
+        own_half.reshape(batch_count, head_width, -1),
+        preferred_element_type=jnp.float32,
     )
     other_part = jnp.einsum(
-        "std,df->stf", heads_side_by_side, other_half, preferred_element_type=jnp.float32
+        "hstd,hdf->stf",
+        arrived,
+        other_half.reshape(batch_count, head_width, -1),
+        preferred_element_type=jnp.float32,
     )
     branch_rows = jnp.where(
         mine == 0,

time: 265 us -> 260 us (0.981)
  local copies, waits for them, and re-layouts: 19.6 us -> 15.2 us
    reshape x2 -> x0, local copies, waits for them, and re-layouts: 3.39 us -> none  [the longest x1 1.88 us: shards(): attended.reshape(sample_count, batch_count, own_rows, head_width)]
  transfers between devices with their start and end apart: 7 -> 7, of which waited for: 4 -> 4; matrix products, arithmetic and copies ran while one was open for 12% -> 11% of each run, Pallas kernels for 9% -> 9%
where the time goes in v17:
time: 260 us; the launch traced here: 259 us
  waiting for transfers between devices  118 us (45%)
  blocking collectives  43.6 us (17%)
  Pallas kernels  23.3 us (9%)
  starting transfers between devices  18.1 us (7%)
  local copies, waits for them, and re-layouts  15.2 us (6%)
  matrix products  14.9 us (6%)
  between operations  13.6 us (5%)
  other arithmetic  12.5 us (5%)
    all_gather x1, waiting for transfers between devices, shards(): kv_tile = lax.all_gather(kv_rows, SEQ, axis=1)  66 us
    all_to_all x1, blocking collectives, gather_batch(): arrived = lax.all_to_all(copies, BATCH, axis, axis, tiled=False)  43.6 us
    all_to_all x1, waiting for transfers between devices, gather_batch(): arrived = lax.all_to_all(copies, BATCH, axis, axis, tiled=False)  42.2 us
    pallas_call x1, Pallas kernels, flash_attention(): pl.pallas_call(flash_step, grid=(sample_count, source_count // sources_pe...  23.3 us
    all_to_all x1, waiting for transfers between devices, shards(): arrived = lax.all_to_all(attended, BATCH, 0, 0, tiled=False)  7.36 us
    all_to_all x1, starting transfers between devices, gather_batch(): arrived = lax.all_to_all(copies, BATCH, axis, axis, tiled=False)  7.15 us
    all_to_all x1, starting transfers between devices, shards(): arrived = lax.all_to_all(attended, BATCH, 0, 0, tiled=False)  6.7 us
    dot_general x5, matrix products, shards(): jnp.einsum('std,ed->set', framed[:, offset:offset + seq_rows], conv_weigh...  5.97 us
  transfers between devices with their start and end apart: 7, of which 4 were waited for; matrix products, arithmetic and copies ran while one was open for 11% of the time, Pallas kernels for 9%

profile of v17, /device:TPU:0, one launch (start us, length us, event | category | flops | bytes accessed | tf_op | source)
XLA Modules:
  0.0 259.4 jit_solution(2423597966956375300)
XLA Ops:
  6.5 3.0 %broadcast_in_dim.4 = bf16[2,8,64,1536]{3,2,0,1:T(8,128)(2,1)} broadcast(bf16[2,64,1536]{2,1,0:T(8,128)(2,1)} %param.8), dimensions={0,2,3} | broadcast | bytes 3538944 | tf_op jit(solution)/shard_map/broadcast_in_dim | solution.py:35
  9.6 7.1 %all-to-all-start = ((bf16[2,8,64,1536]{3,2,0,1:T(8,128)(2,1)}), bf16[2,8,64,1536]{3,2,0,1:T(8,128)(2,1)}, u32[]{:S(2)}, u32[]{:S(2)}) async-start(bf16[2,8,64,1536]{3,2,0,1:T(8,128)(2,1)} %broadcast_in_dim.4), calls=%async_computation | async-start | bytes 6291456 | tf_op jit(solution)/shard_map/all_to_all | solution.py:36
  17.6 42.2 %all-to-all-done = bf16[2,8,64,1536]{3,2,0,1:T(8,128)(2,1)} async-done(((bf16[2,8,64,1536]{3,2,0,1:T(8,128)(2,1)}), bf16[2,8,64,1536]{3,2,0,1:T(8,128)(2,1)}, u32[]{:S(2)}, u32[]{:S(2)}) %all-to-all-start) | async-done | bytes 3145760 | tf_op jit(solution)/shard_map/all_to_all | solution.py:36
  59.8 2.6 multiply_reduce_fusion
  62.5 2.2 copy.72
  64.6 1.6 copy-done.2
  66.7 4.4 %fusion.10 = bf16[2,512,1536]{2,1,0:T(8,128)(2,1)S(1)} fusion(f32[1536]{0:T(1024)S(1)} %copy-done.5, f32[2,512]{1,0:T(2,128)S(1)} %rsqrt.20, bf16[2,8,64,1536]{3,2,1,0:T(8,128)(2,1)} %copy-done.2), kind=kLoop, calls=%fused_computation.13 | loop fusion | flops 18874368 | bytes 6301696 | tf_op jit(solution)/shard_map/convert_element_type | solution.py:141
  71.1 1.3 collective-permute-start
  72.4 1.3 collective-permute-start.1
  74.9 2.7 %collective-permute-done.1 = bf16[2,2,1536]{2,1,0:T(2,128)(2,1)S(1)} collective-permute-done((bf16[2,2,1536]{2,1,0:T(2,128)(2,1)S(1)}, bf16[2,2,1536]{2,1,0:T(2,128)(2,1)S(1)}, u32[]{:S(2)}, u32[]{:S(2)}) %collective-permute-start.1) | collective-permute-done | bytes 12320 | tf_op jit(solution)/shard_map/ppermute | solution.py:25
  77.7 1.2 fusion.17
  81.2 1.3 fusion.42
  82.8 43.6 %all_to_all.15 = bf16[2,8,192,512]{3,2,0,1:T(8,128)(2,1)S(1)} all-to-all(bf16[2,8,192,512]{3,2,0,1:T(8,128)(2,1)S(1)} %broadcast_in_dim.5), channel_id=1, replica_groups=mesh['chip_x'=2,'chip_z'=4,'core'=2,'peer_y'=4,'peer_x'=2] {'peer_y','pe..., dimensions={1} | all-to-all | bytes 6291456 | tf_op jit(solution)/shard_map/all_to_all | solution.py:36
  126.4 1.9 copy.75
  128.4 2.7 %fusion = f32[2,512]{1,0:T(2,128)S(1)} fusion(bf16[2,1536,512]{2,1,0:T(8,128)(2,1)} %bitcast.66), kind=kLoop, calls=%fused_computation.3 | loop fusion | flops 4717568 | bytes 3149824 | tf_op jit(solution)/shard_map/reduce_sum | solution.py:158
  134.4 1.6 collective-permute-start.2
  136.0 4.1 %fusion.21.query_ref = bf16[2,512,192]{2,1,0:T(8,128)(2,1)} fusion(bf16[192,1536]{1,0:T(8,128)(2,1)S(1)} %copy-done.8, bf16[2,1536,512]{2,1,0:T(8,128)(2,1)} %bitcast.67, f32[1536]{0:T(1024)S(1)} %copy-done.9, f32[2,512]{1,0:T(2,128)S(1)} %add_rsqrt_fusion), kind=kOutput, calls=%fused_computation.30 | convolution fusion | flops 610664448 | bytes 4139008 | tf_op jit(solution)/shard_map/sdt,ed->ste/dot_general | solution.py:161
  140.0 66.0 %all-gather.6.cloned.1.call-done = bf16[2,32,192,512]{3,2,1,0:T(8,128)(2,1)} async-done(((bf16[2,2,192,512]{3,2,1,0:T(8,128)(2,1)}), bf16[2,32,192,512]{3,2,1,0:T(8,128)(2,1)}) %all-gather.6.cloned.1.call-update) | async-done | bytes 12582928 | tf_op jit(solution)/shard_map/all_gather | solution.py:171
  206.0 23.3 %shard_map.82 = bf16[8,2,64,192]{3,2,1,0:T(8,128)(2,1)} custom-call(bf16[2,512,192]{2,1,0:T(8,128)(2,1)} %fusion.21.query_ref, bf16[2,16,2,192,512]{4,3,2,1,0:T(8,128)(2,1)} %bitcast.64, bf16[2,16,2,192,512]{4,3,2,1,0:T(8,128)(2,1)} %bitcast.65), custom_call_target="tpu_custom_call" | custom-call | tf_op jit(solution)/shard_map/pallas_call | solution.py:84
  229.3 6.7 %all-to-all-start.2 = ((bf16[8,2,64,192]{3,2,1,0:T(8,128)(2,1)}), bf16[8,2,64,192]{3,2,1,0:T(8,128)(2,1)S(1)}, u32[]{:S(2)}, u32[]{:S(2)}) async-start(bf16[8,2,64,192]{3,2,1,0:T(8,128)(2,1)} %shard_map.82), calls=%async_computation.2 | async-start | bytes 1048576 | tf_op jit(solution)/shard_map/all_to_all | solution.py:179
  236.0 4.6 %copy.76 = bf16[2,1536,512]{1,2,0:T(8,128)(2,1)} copy(bf16[2,1536,512]{2,1,0:T(8,128)(2,1)} %bitcast.68) | data formatting | bytes 6291456 | tf_op jit(solution)/shard_map/optimization_barrier | solution.py:156
  240.6 7.4 %all-to-all-done.2 = bf16[8,2,64,192]{3,2,1,0:T(8,128)(2,1)S(1)} async-done(((bf16[8,2,64,192]{3,2,1,0:T(8,128)(2,1)}), bf16[8,2,64,192]{3,2,1,0:T(8,128)(2,1)S(1)}, u32[]{:S(2)}, u32[]{:S(2)}) %all-to-all-start.2) | async-done | bytes 393248 | tf_op jit(solution)/shard_map/all_to_all | solution.py:179
  248.5 2.2 convolution_bitcast_fusion
  250.7 1.9 fusion.46
  (41 shorter events, 9.0 us)
Async XLA Ops:
  6.5 124.6 %copy-start = (bf16[192,1536]{1,0:T(8,128)(2,1)S(1)}, bf16[192,1536]{1,0:T(8,128)(2,1)}, u32[]{:S(2)}) copy-start(bf16[192,1536]{1,0:T(8,128)(2,1)} %param.14) | copy-start | bytes 1769476
  9.6 7.2 %copy-start.4 = (bf16[192,1536]{1,0:T(8,128)(2,1)S(1)}, bf16[192,1536]{1,0:T(8,128)(2,1)}, u32[]{:S(2)}) copy-start(bf16[192,1536]{1,0:T(8,128)(2,1)} %param.15) | copy-start | bytes 1769476
  9.6 50.2 %all-to-all-start = ((bf16[2,8,64,1536]{3,2,0,1:T(8,128)(2,1)}), bf16[2,8,64,1536]{3,2,0,1:T(8,128)(2,1)}, u32[]{:S(2)}, u32[]{:S(2)}) async-start(bf16[2,8,64,1536]{3,2,0,1:T(8,128)(2,1)} %broadcast_in_dim.4), calls=%async_computation | async-start | bytes 6291456 | tf_op jit(solution)/shard_map/all_to_all | solution.py:36
  16.7 111.7 %all-gather.4.cloned.1.call-start = ((), (), s32[]{:S(2)}) async-start(), calls=%async_computation.3 | async-start | bytes 2654208 | tf_op jit(solution)/shard_map/all_gather | solution.py:132
  17.6 188.5 %all-gather.6.cloned.1.call-start = ((), (), s32[]{:S(2)}) async-start(), calls=%async_computation.4 | async-start | bytes 13369344 | tf_op jit(solution)/shard_map/all_gather | solution.py:171
  62.5 4.3 %copy-start.5 = (f32[1536]{0:T(1024)S(1)}, f32[1536]{0:T(1024)}, u32[]{:S(2)}) copy-start(f32[1536]{0:T(1024)} %param.9) | copy-start | bytes 18436
  64.6 1.6 copy-start.2
  66.7 7.0 %copy-start.6 = (bf16[5,192,1536]{2,1,0:T(8,128)(2,1)S(1)}, bf16[5,192,1536]{2,1,0:T(8,128)(2,1)}, u32[]{:S(2)}) copy-start(bf16[5,192,1536]{2,1,0:T(8,128)(2,1)} %param.10) | copy-start | bytes 8847364
  71.1 7.7 %collective-permute-start = (bf16[2,2,1536]{2,1,0:T(2,128)(2,1)S(1)}, bf16[2,2,1536]{2,1,0:T(2,128)(2,1)S(1)}, u32[]{:S(2)}, u32[]{:S(2)}) collective-permute-start(bf16[2,2,1536]{2,1,0:T(2,128)(2,1)S(1)} %get-tuple-element.9), channel_id=1, source_target_pairs={{0,8},{8,16},{16,24},{24,32},{32,40},{40,48},{48,56},{56,64},{64,7... | collective-permute-start | bytes 36872 | tf_op jit(solution)/shard_map/ppermute | solution.py:23
  72.4 5.2 %collective-permute-start.1 = (bf16[2,2,1536]{2,1,0:T(2,128)(2,1)S(1)}, bf16[2,2,1536]{2,1,0:T(2,128)(2,1)S(1)}, u32[]{:S(2)}, u32[]{:S(2)}) collective-permute-start(bf16[2,2,1536]{2,1,0:T(2,128)(2,1)S(1)} %get-tuple-element.10), channel_id=1, source_target_pairs={{8,0},{16,8},{24,16},{32,24},{40,32},{48,40},{56,48},{64,56},{72,6... | collective-permute-start | bytes 36872 | tf_op jit(solution)/shard_map/ppermute | solution.py:25
  128.4 2.7 %copy-start.9 = (f32[1536]{0:T(1024)S(1)}, f32[1536]{0:T(1024)}, u32[]{:S(2)}) copy-start(f32[1536]{0:T(1024)} %param.11) | copy-start | bytes 18436
  128.4 2.8 %copy-start.1 = (bf16[2,8,192,512]{3,2,1,0:T(8,128)(2,1)S(1)}, bf16[2,8,192,512]{3,2,1,0:T(8,128)(2,1)}, u32[]{:S(2)}) copy-start(bf16[2,8,192,512]{3,2,1,0:T(8,128)(2,1)} %copy.75) | copy-start | bytes 9437188
  131.2 1.1 copy-start.7
  132.3 2.1 copy-start.3
  132.3 3.7 %copy-start.8 = (bf16[192,1536]{1,0:T(8,128)(2,1)S(1)}, bf16[192,1536]{1,0:T(8,128)(2,1)}, u32[]{:S(2)}) copy-start(bf16[192,1536]{1,0:T(8,128)(2,1)} %param.12) | copy-start | bytes 1769476
  134.4 114.1 %collective-permute-start.2 = (bf16[1536,768]{1,0:T(8,128)(2,1)S(1)}, bf16[1536,768]{1,0:T(8,128)(2,1)}, u32[]{:S(2)}, u32[]{:S(2)}) collective-permute-start(bf16[1536,768]{1,0:T(8,128)(2,1)S(1)} %copy-done.3), channel_id=1, source_target_pairs={{0,8},{8,0},{1,9},{9,1},{2,10},{10,2},{3,11},{11,3},{4,12},{12,4},... | collective-permute-start | bytes 7077896 | tf_op jit(solution)/shard_map/ppermute | solution.py:180
  229.3 18.7 %all-to-all-start.2 = ((bf16[8,2,64,192]{3,2,1,0:T(8,128)(2,1)}), bf16[8,2,64,192]{3,2,1,0:T(8,128)(2,1)S(1)}, u32[]{:S(2)}, u32[]{:S(2)}) async-start(bf16[8,2,64,192]{3,2,1,0:T(8,128)(2,1)} %shard_map.82), calls=%async_computation.2 | async-start | bytes 1048576 | tf_op jit(solution)/shard_map/all_to_all | solution.py:179
Sparse Core Ops, SparseCore 0:
  19.9 79.5 all-gather.3
  134.5 71.4 all-gather.5

commit v18 on v17

--- a/solution.py
+++ b/solution.py
@@ -12,21 +12,14 @@
 BATCH = ("peer_y", "peer_x")
 
 
-def with_halo(cells, sides, width):
-    for axis, dim in sides:
-        count = lax.axis_size(axis)
-        ends = count - 1
-        head = lax.slice_in_dim(cells, 0, width, axis=dim)
-        tail = lax.slice_in_dim(cells, cells.shape[dim] - width, cells.shape[dim], axis=dim)
-        cells = jnp.concatenate(
-            [
-                lax.ppermute(tail, axis, [(i, (i + 1) % count) for i in range(ends)]),
-                cells,
-                lax.ppermute(head, axis, [((i + 1) % count, i) for i in range(ends)]),
-            ],
-            axis=dim,
-        )
-    return cells
+def with_halo(cells, raw, activate, axis, width):
+    count = lax.axis_size(axis)
+    ends = count - 1
+    head = raw[:, :width]
+    tail = raw[:, raw.shape[1] - width :]
+    before = lax.ppermute(tail, axis, [(i, (i + 1) % count) for i in range(ends)])
+    after = lax.ppermute(head, axis, [((i + 1) % count, i) for i in range(ends)])
+    return jnp.concatenate([activate(before), cells, activate(after)], axis=1)
 
 
 def gather_batch(block, axis):
@@ -137,10 +130,11 @@
     )
     gathered_in = gather_batch(activations, 1)
     seq_rows = gathered_in.shape[1]
-    active = lax.optimization_barrier(
-        jax.nn.gelu(normalize(gathered_in, conv_gain)).astype(jnp.bfloat16)
-    )
-    framed = with_halo(active, ((SEQ, 1),), flank_rows)
+    def activate(rows_in):
+        return jax.nn.gelu(normalize(rows_in, conv_gain)).astype(jnp.bfloat16)
+
+    active = lax.optimization_barrier(activate(gathered_in))
+    framed = with_halo(active, gathered_in, activate, SEQ, flank_rows)
     conv_sum = jnp.zeros((sample_count, local_out, seq_rows), jnp.float32)
     for offset in range(tap_count):
         conv_sum = conv_sum + jnp.einsum(

time: 260 us -> 260 us (level)
    ppermute x1, waiting for transfers between devices: 2.74 us -> 0.01 us  [with_halo(): lax.ppermute(head, axis, [((i + 1) % count, i) for i in range(ends)])]
  transfers between devices with their start and end apart: 7 -> 7, of which waited for: 4 -> 3; matrix products, arithmetic and copies ran while one was open for 11% -> 12% of each run, Pallas kernels for 9% -> 9%
where the time goes in v18:
time: 260 us
  waiting for transfers between devices  116 us (45%)
  blocking collectives  44.9 us (17%)
  Pallas kernels  23.2 us (9%)
  starting transfers between devices  17.8 us (7%)
  matrix products  17 us (7%)
  local copies, waits for them, and re-layouts  14.1 us (5%)
  between operations  13.6 us (5%)
  other arithmetic  12.7 us (5%)
    all_gather x1, waiting for transfers between devices, shards(): kv_tile = lax.all_gather(kv_rows, SEQ, axis=1)  66.8 us
    all_to_all x1, blocking collectives, gather_batch(): arrived = lax.all_to_all(copies, BATCH, axis, axis, tiled=False)  44.9 us
    all_to_all x1, waiting for transfers between devices, gather_batch(): arrived = lax.all_to_all(copies, BATCH, axis, axis, tiled=False)  42.2 us
    pallas_call x1, Pallas kernels, flash_attention(): pl.pallas_call(flash_step, grid=(sample_count, source_count // sources_pe...  23.2 us
    dot_general x5, matrix products, shards(): jnp.einsum('std,ed->set', framed[:, offset:offset + seq_rows], conv_weigh...  8.15 us
    all_to_all x1, waiting for transfers between devices, shards(): arrived = lax.all_to_all(attended, BATCH, 0, 0, tiled=False)  7.35 us
    all_to_all x1, starting transfers between devices, gather_batch(): arrived = lax.all_to_all(copies, BATCH, axis, axis, tiled=False)  7.15 us
    all_to_all x1, starting transfers between devices, shards(): arrived = lax.all_to_all(attended, BATCH, 0, 0, tiled=False)  6.71 us
  transfers between devices with their start and end apart: 7, of which 3 were waited for; matrix products, arithmetic and copies ran while one was open for 12% of the time, Pallas kernels for 9%

profile of v18, /device:TPU:0, one launch (start us, length us, event | category | flops | bytes accessed | tf_op | source)
XLA Modules:
  0.0 259.7 jit_solution(17059907903664112716)
XLA Ops:
  6.5 3.0 %broadcast_in_dim.4 = bf16[2,8,64,1536]{3,2,0,1:T(8,128)(2,1)} broadcast(bf16[2,64,1536]{2,1,0:T(8,128)(2,1)} %param.8), dimensions={0,2,3} | broadcast | bytes 3538944 | tf_op jit(solution)/shard_map/broadcast_in_dim | solution.py:28
  9.6 7.1 %all-to-all-start = ((bf16[2,8,64,1536]{3,2,0,1:T(8,128)(2,1)}), bf16[2,8,64,1536]{3,2,0,1:T(8,128)(2,1)}, u32[]{:S(2)}, u32[]{:S(2)}) async-start(bf16[2,8,64,1536]{3,2,0,1:T(8,128)(2,1)} %broadcast_in_dim.4), calls=%async_computation | async-start | bytes 6291456 | tf_op jit(solution)/shard_map/all_to_all | solution.py:29
  17.6 42.2 %all-to-all-done = bf16[2,8,64,1536]{3,2,0,1:T(8,128)(2,1)} async-done(((bf16[2,8,64,1536]{3,2,0,1:T(8,128)(2,1)}), bf16[2,8,64,1536]{3,2,0,1:T(8,128)(2,1)}, u32[]{:S(2)}, u32[]{:S(2)}) %all-to-all-start) | async-done | bytes 3145760 | tf_op jit(solution)/shard_map/all_to_all | solution.py:29
  59.8 2.6 multiply_reduce_fusion
  62.4 2.2 copy.72
  64.7 1.3 collective-permute-start
  66.0 1.3 collective-permute-start.1
  67.3 4.1 %fusion.10 = bf16[2,512,1536]{2,1,0:T(8,128)(2,1)} fusion(f32[1536]{0:T(1024)S(1)} %copy-done.6, f32[2,512]{1,0:T(2,128)S(1)} %rsqrt.37, bf16[2,8,64,1536]{3,2,1,0:T(8,128)(2,1)S(1)} %copy.72), kind=kLoop, calls=%fused_computation.13 | loop fusion | flops 18874368 | bytes 6301696 | tf_op jit(solution)/shard_map/convert_element_type | solution.py:134
  72.3 3.3 %fusion.15 = f32[2,512,192]{1,2,0:T(8,128)S(1)} fusion(bf16[2,2,1536]{2,1,0:T(2,128)(2,1)S(1)} %get-tuple-element.11, bf16[2,512,1536]{2,1,0:T(8,128)(2,1)} %fusion.10, bf16[5,192,1536]{2,1,0:T(8,128)(2,1)} %param.10), kind=kOutput, calls=%fused_computation.22 | convolution fusion | flops 610271232 | bytes 4534272 | tf_op jit(solution)/shard_map/std,ed->set/dot_general | solution.py:140
  76.2 1.2 fusion.17
  77.4 1.2 fusion.24
  79.8 1.2 fusion.29
  81.3 44.9 %all_to_all.15 = bf16[2,8,192,512]{3,2,0,1:T(8,128)(2,1)S(1)} all-to-all(bf16[2,8,192,512]{3,2,0,1:T(8,128)(2,1)S(1)} %broadcast_in_dim.5), channel_id=1, replica_groups=mesh['chip_x'=2,'chip_z'=4,'core'=2,'peer_y'=4,'peer_x'=2] {'peer_y','pe..., dimensions={1} | all-to-all | bytes 6291456 | tf_op jit(solution)/shard_map/all_to_all | solution.py:29
  126.3 1.9 copy.75
  128.2 2.7 %fusion = f32[2,512]{1,0:T(2,128)S(1)} fusion(bf16[2,1536,512]{2,1,0:T(8,128)(2,1)} %bitcast.66), kind=kLoop, calls=%fused_computation.3 | loop fusion | flops 4717568 | bytes 3149824 | tf_op jit(solution)/shard_map/reduce_sum | solution.py:152
  134.2 1.3 collective-permute-start.2
  135.5 4.1 %fusion.21.query_ref = bf16[2,512,192]{2,1,0:T(8,128)(2,1)} fusion(bf16[192,1536]{1,0:T(8,128)(2,1)S(1)} %copy-done.8, bf16[2,1536,512]{2,1,0:T(8,128)(2,1)} %bitcast.67, f32[1536]{0:T(1024)S(1)} %copy-done.9, f32[2,512]{1,0:T(2,128)S(1)} %add_rsqrt_fusion), kind=kOutput, calls=%fused_computation.30 | convolution fusion | flops 610664448 | bytes 4139008 | tf_op jit(solution)/shard_map/sdt,ed->ste/dot_general | solution.py:155
  139.5 66.8 %all-gather.6.cloned.1.call-done = bf16[2,32,192,512]{3,2,1,0:T(8,128)(2,1)} async-done(((bf16[2,2,192,512]{3,2,1,0:T(8,128)(2,1)}), bf16[2,32,192,512]{3,2,1,0:T(8,128)(2,1)}) %all-gather.6.cloned.1.call-update) | async-done | bytes 12582928 | tf_op jit(solution)/shard_map/all_gather | solution.py:165
  206.3 23.2 %shard_map.82 = bf16[8,2,64,192]{3,2,1,0:T(8,128)(2,1)} custom-call(bf16[2,512,192]{2,1,0:T(8,128)(2,1)} %fusion.21.query_ref, bf16[2,16,2,192,512]{4,3,2,1,0:T(8,128)(2,1)} %bitcast.64, bf16[2,16,2,192,512]{4,3,2,1,0:T(8,128)(2,1)} %bitcast.65), custom_call_target="tpu_custom_call" | custom-call | tf_op jit(solution)/shard_map/pallas_call | solution.py:77
  229.6 6.7 %all-to-all-start.2 = ((bf16[8,2,64,192]{3,2,1,0:T(8,128)(2,1)}), bf16[8,2,64,192]{3,2,1,0:T(8,128)(2,1)S(1)}, u32[]{:S(2)}, u32[]{:S(2)}) async-start(bf16[8,2,64,192]{3,2,1,0:T(8,128)(2,1)} %shard_map.82), calls=%async_computation.2 | async-start | bytes 1048576 | tf_op jit(solution)/shard_map/all_to_all | solution.py:173
  236.3 4.7 %copy.76 = bf16[2,1536,512]{1,2,0:T(8,128)(2,1)} copy(bf16[2,1536,512]{2,1,0:T(8,128)(2,1)} %bitcast.68) | data formatting | bytes 6291456 | tf_op jit(solution)/shard_map/optimization_barrier | solution.py:150
  240.9 7.3 %all-to-all-done.2 = bf16[8,2,64,192]{3,2,1,0:T(8,128)(2,1)S(1)} async-done(((bf16[8,2,64,192]{3,2,1,0:T(8,128)(2,1)}), bf16[8,2,64,192]{3,2,1,0:T(8,128)(2,1)S(1)}, u32[]{:S(2)}, u32[]{:S(2)}) %all-to-all-start.2) | async-done | bytes 393248 | tf_op jit(solution)/shard_map/all_to_all | solution.py:173
  248.8 2.2 convolution_bitcast_fusion
  251.0 1.9 fusion.31
  (46 shorter events, 7.6 us)
Async XLA Ops:
  6.5 124.4 %copy-start = (bf16[192,1536]{1,0:T(8,128)(2,1)S(1)}, bf16[192,1536]{1,0:T(8,128)(2,1)}, u32[]{:S(2)}) copy-start(bf16[192,1536]{1,0:T(8,128)(2,1)} %param.14) | copy-start | bytes 1769476
  9.6 7.2 %copy-start.4 = (bf16[192,1536]{1,0:T(8,128)(2,1)S(1)}, bf16[192,1536]{1,0:T(8,128)(2,1)}, u32[]{:S(2)}) copy-start(bf16[192,1536]{1,0:T(8,128)(2,1)} %param.15) | copy-start | bytes 1769476
  9.6 50.2 %all-to-all-start = ((bf16[2,8,64,1536]{3,2,0,1:T(8,128)(2,1)}), bf16[2,8,64,1536]{3,2,0,1:T(8,128)(2,1)}, u32[]{:S(2)}, u32[]{:S(2)}) async-start(bf16[2,8,64,1536]{3,2,0,1:T(8,128)(2,1)} %broadcast_in_dim.4), calls=%async_computation | async-start | bytes 6291456 | tf_op jit(solution)/shard_map/all_to_all | solution.py:29
  16.7 111.5 %all-gather.4.cloned.1.call-start = ((), (), s32[]{:S(2)}) async-start(), calls=%async_computation.3 | async-start | bytes 2654208 | tf_op jit(solution)/shard_map/all_gather | solution.py:125
  17.5 188.8 %all-gather.6.cloned.1.call-start = ((), (), s32[]{:S(2)}) async-start(), calls=%async_computation.4 | async-start | bytes 13369344 | tf_op jit(solution)/shard_map/all_gather | solution.py:165
  62.4 4.8 %copy-start.6 = (f32[1536]{0:T(1024)S(1)}, f32[1536]{0:T(1024)}, u32[]{:S(2)}) copy-start(f32[1536]{0:T(1024)} %param.9) | copy-start | bytes 18436
  64.7 7.2 %collective-permute-start = (bf16[2,2,1536]{2,1,0:T(2,128)(2,1)S(1)}, bf16[2,2,1536]{2,1,0:T(2,128)(2,1)S(1)}, u32[]{:S(2)}, u32[]{:S(2)}) collective-permute-start(bf16[2,2,1536]{2,1,0:T(2,128)(2,1)S(1)} %get-tuple-element.9), channel_id=1, source_target_pairs={{0,8},{8,16},{16,24},{24,32},{32,40},{40,48},{48,56},{56,64},{64,7... | collective-permute-start | bytes 36872 | tf_op jit(solution)/shard_map/ppermute | solution.py:20
  66.0 6.0 %collective-permute-start.1 = (bf16[2,2,1536]{2,1,0:T(2,128)(2,1)S(1)}, bf16[2,2,1536]{2,1,0:T(2,128)(2,1)S(1)}, u32[]{:S(2)}, u32[]{:S(2)}) collective-permute-start(bf16[2,2,1536]{2,1,0:T(2,128)(2,1)S(1)} %get-tuple-element.10), channel_id=1, source_target_pairs={{8,0},{16,8},{24,16},{32,24},{40,32},{48,40},{56,48},{64,56},{72,6... | collective-permute-start | bytes 36872 | tf_op jit(solution)/shard_map/ppermute | solution.py:21
  72.2 3.4 %copy-start.2 = (bf16[2,512,1536]{2,1,0:T(8,128)(2,1)S(1)}, bf16[2,512,1536]{2,1,0:T(8,128)(2,1)}, u32[]{:S(2)}) copy-start(bf16[2,512,1536]{2,1,0:T(8,128)(2,1)} %fusion.10) | copy-start | bytes 9437188
  72.3 3.9 %copy-start.5 = (bf16[5,192,1536]{2,1,0:T(8,128)(2,1)S(1)}, bf16[5,192,1536]{2,1,0:T(8,128)(2,1)}, u32[]{:S(2)}) copy-start(bf16[5,192,1536]{2,1,0:T(8,128)(2,1)} %param.10) | copy-start | bytes 8847364
  128.2 2.7 %copy-start.9 = (f32[1536]{0:T(1024)S(1)}, f32[1536]{0:T(1024)}, u32[]{:S(2)}) copy-start(f32[1536]{0:T(1024)} %param.11) | copy-start | bytes 18436
  128.2 2.8 %copy-start.1 = (bf16[2,8,192,512]{3,2,1,0:T(8,128)(2,1)S(1)}, bf16[2,8,192,512]{3,2,1,0:T(8,128)(2,1)}, u32[]{:S(2)}) copy-start(bf16[2,8,192,512]{3,2,1,0:T(8,128)(2,1)} %copy.75) | copy-start | bytes 9437188
  131.0 1.1 copy-start.7
  132.1 2.1 copy-start.3
  132.1 3.4 %copy-start.8 = (bf16[192,1536]{1,0:T(8,128)(2,1)S(1)}, bf16[192,1536]{1,0:T(8,128)(2,1)}, u32[]{:S(2)}) copy-start(bf16[192,1536]{1,0:T(8,128)(2,1)} %param.12) | copy-start | bytes 1769476
  134.2 114.6 %collective-permute-start.2 = (bf16[1536,768]{1,0:T(8,128)(2,1)S(1)}, bf16[1536,768]{1,0:T(8,128)(2,1)}, u32[]{:S(2)}, u32[]{:S(2)}) collective-permute-start(bf16[1536,768]{1,0:T(8,128)(2,1)S(1)} %copy-done.3), channel_id=1, source_target_pairs={{0,8},{8,0},{1,9},{9,1},{2,10},{10,2},{3,11},{11,3},{4,12},{12,4},... | collective-permute-start | bytes 7077896 | tf_op jit(solution)/shard_map/ppermute | solution.py:174
  229.6 18.7 %all-to-all-start.2 = ((bf16[8,2,64,192]{3,2,1,0:T(8,128)(2,1)}), bf16[8,2,64,192]{3,2,1,0:T(8,128)(2,1)S(1)}, u32[]{:S(2)}, u32[]{:S(2)}) async-start(bf16[8,2,64,192]{3,2,1,0:T(8,128)(2,1)} %shard_map.82), calls=%async_computation.2 | async-start | bytes 1048576 | tf_op jit(solution)/shard_map/all_to_all | solution.py:173
Sparse Core Ops, SparseCore 0:
  19.8 83.0 all-gather.3
  134.3 72.0 all-gather.5

commit v19 on v18

--- a/solution.py
+++ b/solution.py
@@ -162,13 +162,15 @@
         "sdt,ed->set", normed, value_weight, preferred_element_type=jnp.float32
     ).astype(jnp.bfloat16)
     kv_rows = jnp.stack([key_rows, value_rows])
-    kv_tile = lax.all_gather(kv_rows, SEQ, axis=1)
-    batch_count = lax.axis_size(BATCH)
-    attended = flash_attention(queries, kv_tile, batch_count)
     row_start = lax.axis_index(BATCH) * own_rows
     own_hidden = jnp.transpose(
         lax.dynamic_slice_in_dim(hidden_full, row_start, own_rows, 2), (0, 2, 1)
     ).astype(jnp.float32)
+    kv_tile, own_hidden = lax.optimization_barrier(
+        (lax.all_gather(kv_rows, SEQ, axis=1), own_hidden)
+    )
+    batch_count = lax.axis_size(BATCH)
+    attended = flash_attention(queries, kv_tile, batch_count)
     head_width = attended.shape[3]
     arrived = lax.all_to_all(attended, BATCH, 0, 0, tiled=False)
     other_half = lax.ppermute(own_half, "core", [(0, 1), (1, 0)])

time: 260 us -> 265 us (1.019)
  local copies, waits for them, and re-layouts: 14.1 us -> 16.9 us
    all_gather x1, waiting for transfers between devices: 66.8 us -> 60.2 us  [shards(): lax.all_gather(kv_rows, SEQ, axis=1)]
    all_to_all x1, waiting for transfers between devices: 7.35 us -> 12 us  [shards(): arrived = lax.all_to_all(attended, BATCH, 0, 0, tiled=False)]
  transfers between devices with their start and end apart: 7 -> 7, of which waited for: 3 -> 3; matrix products, arithmetic and copies ran while one was open for 12% -> 13% of each run, Pallas kernels for 9% -> 9%
where the time goes in v19:
time: 265 us; the launch traced here: 264 us
  waiting for transfers between devices  114 us (43%)
  blocking collectives  44.5 us (17%)
  Pallas kernels  23.2 us (9%)
  starting transfers between devices  18.9 us (7%)
  matrix products  18.8 us (7%)
  local copies, waits for them, and re-layouts  16.9 us (6%)
  other arithmetic  13.9 us (5%)
  between operations  13.6 us (5%)
    all_gather x1, waiting for transfers between devices, shards(): lax.all_gather(kv_rows, SEQ, axis=1)  60.2 us
    all_to_all x1, blocking collectives, gather_batch(): arrived = lax.all_to_all(copies, BATCH, axis, axis, tiled=False)  44.5 us
    all_to_all x1, waiting for transfers between devices, gather_batch(): arrived = lax.all_to_all(copies, BATCH, axis, axis, tiled=False)  42.2 us
    pallas_call x1, Pallas kernels, flash_attention(): pl.pallas_call(flash_step, grid=(sample_count, source_count // sources_pe...  23.2 us
    all_to_all x1, waiting for transfers between devices, shards(): arrived = lax.all_to_all(attended, BATCH, 0, 0, tiled=False)  12 us
    dot_general x5, matrix products, shards(): jnp.einsum('std,ed->set', framed[:, offset:offset + seq_rows], conv_weigh...  8.16 us
    all_to_all x1, starting transfers between devices, gather_batch(): arrived = lax.all_to_all(copies, BATCH, axis, axis, tiled=False)  7.15 us
    all_to_all x1, starting transfers between devices, shards(): arrived = lax.all_to_all(attended, BATCH, 0, 0, tiled=False)  6.7 us
  transfers between devices with their start and end apart: 7, of which 3 were waited for; matrix products, arithmetic and copies ran while one was open for 13% of the time, Pallas kernels for 9%

profile of v19, /device:TPU:0, one launch (start us, length us, event | category | flops | bytes accessed | tf_op | source)
XLA Modules:
  0.0 264.3 jit_solution(6436330221507446286)
XLA Ops:
  6.5 3.0 %broadcast_in_dim.4 = bf16[2,8,64,1536]{3,2,0,1:T(8,128)(2,1)} broadcast(bf16[2,64,1536]{2,1,0:T(8,128)(2,1)} %param.8), dimensions={0,2,3} | broadcast | bytes 3538944 | tf_op jit(solution)/shard_map/broadcast_in_dim | solution.py:28
  9.6 7.1 %all-to-all-start = ((bf16[2,8,64,1536]{3,2,0,1:T(8,128)(2,1)}), bf16[2,8,64,1536]{3,2,0,1:T(8,128)(2,1)}, u32[]{:S(2)}, u32[]{:S(2)}) async-start(bf16[2,8,64,1536]{3,2,0,1:T(8,128)(2,1)} %broadcast_in_dim.4), calls=%async_computation | async-start | bytes 6291456 | tf_op jit(solution)/shard_map/all_to_all | solution.py:29
  17.6 42.2 %all-to-all-done = bf16[2,8,64,1536]{3,2,0,1:T(8,128)(2,1)} async-done(((bf16[2,8,64,1536]{3,2,0,1:T(8,128)(2,1)}), bf16[2,8,64,1536]{3,2,0,1:T(8,128)(2,1)}, u32[]{:S(2)}, u32[]{:S(2)}) %all-to-all-start) | async-done | bytes 3145760 | tf_op jit(solution)/shard_map/all_to_all | solution.py:29
  59.8 2.2 copy.72
  62.0 1.6 copy-done.2
  63.6 1.3 collective-permute-start.1
  64.9 3.0 %collective-permute-start = (bf16[2,2,1536]{2,1,0:T(2,128)(2,1)S(1)}, bf16[2,2,1536]{2,1,0:T(2,128)(2,1)S(1)}, u32[]{:S(2)}, u32[]{:S(2)}) collective-permute-start(bf16[2,2,1536]{2,1,0:T(2,128)(2,1)S(1)} %get-tuple-element.13), channel_id=1, source_target_pairs={{0,8},{8,16},{16,24},{24,32},{32,40},{40,48},{48,56},{56,64},{64,7... | collective-permute-start | bytes 36872 | tf_op jit(solution)/shard_map/ppermute | solution.py:20
  68.0 2.6 multiply_reduce_fusion
  70.6 5.3 %fusion.10 = bf16[2,512,1536]{2,1,0:T(8,128)(2,1)} fusion(f32[1536]{0:T(1024)S(1)} %copy-done.6, f32[2,512]{1,0:T(2,128)S(1)} %rsqrt.37, bf16[2,8,64,1536]{3,2,1,0:T(8,128)(2,1)} %copy-done.2), kind=kLoop, calls=%fused_computation.13 | loop fusion | flops 18874368 | bytes 6301696 | tf_op jit(solution)/shard_map/convert_element_type | solution.py:134
  76.0 1.4 constant_dynamic-slice_fusion.1
  78.0 3.3 %fusion.15 = f32[2,512,192]{1,2,0:T(8,128)S(1)} fusion(bf16[2,2,1536]{2,1,0:T(2,128)(2,1)S(1)} %get-tuple-element.15, bf16[2,512,1536]{2,1,0:T(8,128)(2,1)} %fusion.10, bf16[5,192,1536]{2,1,0:T(8,128)(2,1)} %param.10), kind=kOutput, calls=%fused_computation.22 | convolution fusion | flops 610271232 | bytes 4534272 | tf_op jit(solution)/shard_map/std,ed->set/dot_general | solution.py:140
  83.1 1.2 fusion.24
  85.5 1.2 fusion.29
  87.0 44.5 %all_to_all.15 = bf16[2,8,192,512]{3,2,0,1:T(8,128)(2,1)S(1)} all-to-all(bf16[2,8,192,512]{3,2,0,1:T(8,128)(2,1)S(1)} %broadcast_in_dim.5), channel_id=1, replica_groups=mesh['chip_x'=2,'chip_z'=4,'core'=2,'peer_y'=4,'peer_x'=2] {'peer_y','pe..., dimensions={1} | all-to-all | bytes 6291456 | tf_op jit(solution)/shard_map/all_to_all | solution.py:29
  131.6 1.9 copy.75
  133.5 2.7 %fusion = f32[2,512]{1,0:T(2,128)S(1)} fusion(bf16[2,1536,512]{2,1,0:T(8,128)(2,1)} %bitcast.66), kind=kLoop, calls=%fused_computation.3 | loop fusion | flops 4717568 | bytes 3149824 | tf_op jit(solution)/shard_map/reduce_sum | solution.py:152
  140.1 4.7 %copy.76 = bf16[2,1536,512]{1,2,0:T(8,128)(2,1)} copy(bf16[2,1536,512]{2,1,0:T(8,128)(2,1)} %bitcast.67) | data formatting | bytes 6291456 | tf_op jit(solution)/shard_map/optimization_barrier | solution.py:150
  145.9 4.2 %fusion.21.query_ref = bf16[2,512,192]{2,1,0:T(8,128)(2,1)} fusion(bf16[192,1536]{1,0:T(8,128)(2,1)S(1)} %copy-done.8, bf16[2,1536,512]{2,1,0:T(8,128)(2,1)} %bitcast.68, f32[1536]{0:T(1024)S(1)} %copy-done.9, f32[2,512]{1,0:T(2,128)S(1)} %add_rsqrt_fusion), kind=kOutput, calls=%fused_computation.30 | convolution fusion | flops 610664448 | bytes 4139008 | tf_op jit(solution)/shard_map/sdt,ed->ste/dot_general | solution.py:155
  150.0 60.2 %all-gather.6.cloned.1.call-done = bf16[2,32,192,512]{3,2,1,0:T(8,128)(2,1)} async-done(((bf16[2,2,192,512]{3,2,1,0:T(8,128)(2,1)}), bf16[2,32,192,512]{3,2,1,0:T(8,128)(2,1)}) %all-gather.6.cloned.1.call-update) | async-done | bytes 12582928 | tf_op jit(solution)/shard_map/all_gather | solution.py:170
  210.2 23.2 %shard_map.82 = bf16[8,2,64,192]{3,2,1,0:T(8,128)(2,1)} custom-call(bf16[2,512,192]{2,1,0:T(8,128)(2,1)} %fusion.21.query_ref, bf16[2,16,2,192,512]{4,3,2,1,0:T(8,128)(2,1)} %bitcast.64, bf16[2,16,2,192,512]{4,3,2,1,0:T(8,128)(2,1)} %bitcast.65), custom_call_target="tpu_custom_call" | custom-call | tf_op jit(solution)/shard_map/pallas_call | solution.py:77
  233.4 6.7 %all-to-all-start.2 = ((bf16[8,2,64,192]{3,2,1,0:T(8,128)(2,1)}), bf16[8,2,64,192]{3,2,1,0:T(8,128)(2,1)S(1)}, u32[]{:S(2)}, u32[]{:S(2)}) async-start(bf16[8,2,64,192]{3,2,1,0:T(8,128)(2,1)} %shard_map.82), calls=%async_computation.2 | async-start | bytes 1048576 | tf_op jit(solution)/shard_map/all_to_all | solution.py:175
  240.1 12.0 %all-to-all-done.2 = bf16[8,2,64,192]{3,2,1,0:T(8,128)(2,1)S(1)} async-done(((bf16[8,2,64,192]{3,2,1,0:T(8,128)(2,1)}), bf16[8,2,64,192]{3,2,1,0:T(8,128)(2,1)S(1)}, u32[]{:S(2)}, u32[]{:S(2)}) %all-to-all-start.2) | async-done | bytes 393248 | tf_op jit(solution)/shard_map/all_to_all | solution.py:175
  252.1 2.2 convolution_bitcast_fusion.1
  254.3 2.2 convolution_bitcast_fusion
  (47 shorter events, 10.6 us)
Async XLA Ops:
  6.5 129.7 %copy-start = (bf16[192,1536]{1,0:T(8,128)(2,1)S(1)}, bf16[192,1536]{1,0:T(8,128)(2,1)}, u32[]{:S(2)}) copy-start(bf16[192,1536]{1,0:T(8,128)(2,1)} %param.13) | copy-start | bytes 1769476
  9.6 7.2 %copy-start.4 = (bf16[192,1536]{1,0:T(8,128)(2,1)S(1)}, bf16[192,1536]{1,0:T(8,128)(2,1)}, u32[]{:S(2)}) copy-start(bf16[192,1536]{1,0:T(8,128)(2,1)} %param.15) | copy-start | bytes 1769476
  9.6 50.2 %all-to-all-start = ((bf16[2,8,64,1536]{3,2,0,1:T(8,128)(2,1)}), bf16[2,8,64,1536]{3,2,0,1:T(8,128)(2,1)}, u32[]{:S(2)}, u32[]{:S(2)}) async-start(bf16[2,8,64,1536]{3,2,0,1:T(8,128)(2,1)} %broadcast_in_dim.4), calls=%async_computation | async-start | bytes 6291456 | tf_op jit(solution)/shard_map/all_to_all | solution.py:29
  16.7 116.8 %all-gather.4.cloned.1.call-start = ((), (), s32[]{:S(2)}) async-start(), calls=%async_computation.3 | async-start | bytes 2654208 | tf_op jit(solution)/shard_map/all_gather | solution.py:125
  17.5 192.7 %all-gather.6.cloned.1.call-start = ((), (), s32[]{:S(2)}) async-start(), calls=%async_computation.4 | async-start | bytes 13369344 | tf_op jit(solution)/shard_map/all_gather | solution.py:170
  61.9 1.7 copy-start.2
  61.9 8.7 %copy-start.6 = (f32[1536]{0:T(1024)S(1)}, f32[1536]{0:T(1024)}, u32[]{:S(2)}) copy-start(f32[1536]{0:T(1024)} %param.9) | copy-start | bytes 18436
  63.6 13.9 %collective-permute-start.1 = (bf16[2,2,1536]{2,1,0:T(2,128)(2,1)S(1)}, bf16[2,2,1536]{2,1,0:T(2,128)(2,1)S(1)}, u32[]{:S(2)}, u32[]{:S(2)}) collective-permute-start(bf16[2,2,1536]{2,1,0:T(2,128)(2,1)S(1)} %get-tuple-element.14), channel_id=1, source_target_pairs={{8,0},{16,8},{24,16},{32,24},{40,32},{48,40},{56,48},{64,56},{72,6... | collective-permute-start | bytes 36872 | tf_op jit(solution)/shard_map/ppermute | solution.py:21
  64.9 12.7 %collective-permute-start = (bf16[2,2,1536]{2,1,0:T(2,128)(2,1)S(1)}, bf16[2,2,1536]{2,1,0:T(2,128)(2,1)S(1)}, u32[]{:S(2)}, u32[]{:S(2)}) collective-permute-start(bf16[2,2,1536]{2,1,0:T(2,128)(2,1)S(1)} %get-tuple-element.13), channel_id=1, source_target_pairs={{0,8},{8,16},{16,24},{24,32},{32,40},{40,48},{48,56},{56,64},{64,7... | collective-permute-start | bytes 36872 | tf_op jit(solution)/shard_map/ppermute | solution.py:20
  77.9 3.4 %copy-start.3 = (bf16[2,512,1536]{2,1,0:T(8,128)(2,1)S(1)}, bf16[2,512,1536]{2,1,0:T(8,128)(2,1)}, u32[]{:S(2)}) copy-start(bf16[2,512,1536]{2,1,0:T(8,128)(2,1)} %fusion.10) | copy-start | bytes 9437188
  77.9 3.9 %copy-start.5 = (bf16[5,192,1536]{2,1,0:T(8,128)(2,1)S(1)}, bf16[5,192,1536]{2,1,0:T(8,128)(2,1)}, u32[]{:S(2)}) copy-start(bf16[5,192,1536]{2,1,0:T(8,128)(2,1)} %param.10) | copy-start | bytes 8847364
  133.5 2.7 %copy-start.9 = (f32[1536]{0:T(1024)S(1)}, f32[1536]{0:T(1024)}, u32[]{:S(2)}) copy-start(f32[1536]{0:T(1024)} %param.11) | copy-start | bytes 18436
  133.5 2.8 %copy-start.1 = (bf16[2,8,192,512]{3,2,1,0:T(8,128)(2,1)S(1)}, bf16[2,8,192,512]{3,2,1,0:T(8,128)(2,1)}, u32[]{:S(2)}) copy-start(bf16[2,8,192,512]{3,2,1,0:T(8,128)(2,1)} %copy.75) | copy-start | bytes 9437188
  136.3 1.1 copy-start.7
  139.5 114.9 %collective-permute-start.2 = (bf16[1536,768]{1,0:T(8,128)(2,1)}, bf16[1536,768]{1,0:T(8,128)(2,1)}, u32[]{:S(2)}, u32[]{:S(2)}) collective-permute-start(bf16[1536,768]{1,0:T(8,128)(2,1)} %all-gather.4.cloned.1.call-done), channel_id=1, source_target_pairs={{0,8},{8,0},{1,9},{9,1},{2,10},{10,2},{3,11},{11,3},{4,12},{12,4},... | collective-permute-start | bytes 7077896 | tf_op jit(solution)/shard_map/ppermute | solution.py:176
  140.1 5.8 %copy-start.8 = (bf16[192,1536]{1,0:T(8,128)(2,1)S(1)}, bf16[192,1536]{1,0:T(8,128)(2,1)}, u32[]{:S(2)}) copy-start(bf16[192,1536]{1,0:T(8,128)(2,1)} %param.12) | copy-start | bytes 1769476
  233.4 18.7 %all-to-all-start.2 = ((bf16[8,2,64,192]{3,2,1,0:T(8,128)(2,1)}), bf16[8,2,64,192]{3,2,1,0:T(8,128)(2,1)S(1)}, u32[]{:S(2)}, u32[]{:S(2)}) async-start(bf16[8,2,64,192]{3,2,1,0:T(8,128)(2,1)} %shard_map.82), calls=%async_computation.2 | async-start | bytes 1048576 | tf_op jit(solution)/shard_map/all_to_all | solution.py:175
Sparse Core Ops, SparseCore 0:
  19.8 74.1 all-gather.3
  139.6 70.5 all-gather.5

commit v20 on v17

--- a/solution.py
+++ b/solution.py
@@ -77,7 +77,7 @@
         out_ref[:, 0] = finished.reshape(out_ref.shape[0], out_ref.shape[2], out_ref.shape[3])
 
 
-def flash_attention(queries, kv_tile, peers, sources_per_step=8):
+def flash_attention(queries, kv_tile, peers, sources_per_step=16):
     sample_count, query_count, head_width = queries.shape
     _, source_count, _, _, source_rows = kv_tile.shape
     sources_per_step = math.gcd(source_count, sources_per_step)

time: 260 us -> 260 us (level)
  no operation moved by 1% of the time
where the time goes in v20:
time: 260 us
  waiting for transfers between devices  118 us (45%)
  blocking collectives  43.6 us (17%)
  Pallas kernels  23.4 us (9%)
  starting transfers between devices  18.1 us (7%)
  local copies, waits for them, and re-layouts  15.2 us (6%)
  matrix products  14.9 us (6%)
  between operations  13.6 us (5%)
  other arithmetic  12.5 us (5%)
    all_gather x1, waiting for transfers between devices, shards(): kv_tile = lax.all_gather(kv_rows, SEQ, axis=1)  66 us
    all_to_all x1, blocking collectives, gather_batch(): arrived = lax.all_to_all(copies, BATCH, axis, axis, tiled=False)  43.6 us
    all_to_all x1, waiting for transfers between devices, gather_batch(): arrived = lax.all_to_all(copies, BATCH, axis, axis, tiled=False)  42.2 us
    pallas_call x1, Pallas kernels, flash_attention(): pl.pallas_call(flash_step, grid=(sample_count, source_count // sources_pe...  23.4 us
    all_to_all x1, waiting for transfers between devices, shards(): arrived = lax.all_to_all(attended, BATCH, 0, 0, tiled=False)  7.36 us
    all_to_all x1, starting transfers between devices, gather_batch(): arrived = lax.all_to_all(copies, BATCH, axis, axis, tiled=False)  7.15 us
    all_to_all x1, starting transfers between devices, shards(): arrived = lax.all_to_all(attended, BATCH, 0, 0, tiled=False)  6.7 us
    dot_general x5, matrix products, shards(): jnp.einsum('std,ed->set', framed[:, offset:offset + seq_rows], conv_weigh...  5.97 us
  transfers between devices with their start and end apart: 7, of which 4 were waited for; matrix products, arithmetic and copies ran while one was open for 11% of the time, Pallas kernels for 9%

profile of v20, /device:TPU:0, one launch (start us, length us, event | category | flops | bytes accessed | tf_op | source)
XLA Modules:
  0.0 259.6 jit_solution(14574055961091666427)
XLA Ops:
  6.5 3.0 %broadcast_in_dim.4 = bf16[2,8,64,1536]{3,2,0,1:T(8,128)(2,1)} broadcast(bf16[2,64,1536]{2,1,0:T(8,128)(2,1)} %param.8), dimensions={0,2,3} | broadcast | bytes 3538944 | tf_op jit(solution)/shard_map/broadcast_in_dim | solution.py:35
  9.6 7.1 %all-to-all-start = ((bf16[2,8,64,1536]{3,2,0,1:T(8,128)(2,1)}), bf16[2,8,64,1536]{3,2,0,1:T(8,128)(2,1)}, u32[]{:S(2)}, u32[]{:S(2)}) async-start(bf16[2,8,64,1536]{3,2,0,1:T(8,128)(2,1)} %broadcast_in_dim.4), calls=%async_computation | async-start | bytes 6291456 | tf_op jit(solution)/shard_map/all_to_all | solution.py:36
  17.6 42.2 %all-to-all-done = bf16[2,8,64,1536]{3,2,0,1:T(8,128)(2,1)} async-done(((bf16[2,8,64,1536]{3,2,0,1:T(8,128)(2,1)}), bf16[2,8,64,1536]{3,2,0,1:T(8,128)(2,1)}, u32[]{:S(2)}, u32[]{:S(2)}) %all-to-all-start) | async-done | bytes 3145760 | tf_op jit(solution)/shard_map/all_to_all | solution.py:36
  59.8 2.6 multiply_reduce_fusion
  62.5 2.2 copy.72
  64.6 1.6 copy-done.2
  66.7 4.4 %fusion.10 = bf16[2,512,1536]{2,1,0:T(8,128)(2,1)S(1)} fusion(f32[1536]{0:T(1024)S(1)} %copy-done.5, f32[2,512]{1,0:T(2,128)S(1)} %rsqrt.20, bf16[2,8,64,1536]{3,2,1,0:T(8,128)(2,1)} %copy-done.2), kind=kLoop, calls=%fused_computation.13 | loop fusion | flops 18874368 | bytes 6301696 | tf_op jit(solution)/shard_map/convert_element_type | solution.py:141
  71.1 1.3 collective-permute-start
  72.4 1.3 collective-permute-start.1
  74.9 2.7 %collective-permute-done.1 = bf16[2,2,1536]{2,1,0:T(2,128)(2,1)S(1)} collective-permute-done((bf16[2,2,1536]{2,1,0:T(2,128)(2,1)S(1)}, bf16[2,2,1536]{2,1,0:T(2,128)(2,1)S(1)}, u32[]{:S(2)}, u32[]{:S(2)}) %collective-permute-start.1) | collective-permute-done | bytes 12320 | tf_op jit(solution)/shard_map/ppermute | solution.py:25
  77.7 1.2 fusion.17
  81.2 1.3 fusion.42
  82.8 43.6 %all_to_all.15 = bf16[2,8,192,512]{3,2,0,1:T(8,128)(2,1)S(1)} all-to-all(bf16[2,8,192,512]{3,2,0,1:T(8,128)(2,1)S(1)} %broadcast_in_dim.5), channel_id=1, replica_groups=mesh['chip_x'=2,'chip_z'=4,'core'=2,'peer_y'=4,'peer_x'=2] {'peer_y','pe..., dimensions={1} | all-to-all | bytes 6291456 | tf_op jit(solution)/shard_map/all_to_all | solution.py:36
  126.4 1.9 copy.75
  128.4 2.7 %fusion = f32[2,512]{1,0:T(2,128)S(1)} fusion(bf16[2,1536,512]{2,1,0:T(8,128)(2,1)} %bitcast.66), kind=kLoop, calls=%fused_computation.3 | loop fusion | flops 4717568 | bytes 3149824 | tf_op jit(solution)/shard_map/reduce_sum | solution.py:158
  134.4 1.6 collective-permute-start.2
  136.0 4.1 %fusion.21.query_ref = bf16[2,512,192]{2,1,0:T(8,128)(2,1)} fusion(bf16[192,1536]{1,0:T(8,128)(2,1)S(1)} %copy-done.8, bf16[2,1536,512]{2,1,0:T(8,128)(2,1)} %bitcast.67, f32[1536]{0:T(1024)S(1)} %copy-done.9, f32[2,512]{1,0:T(2,128)S(1)} %add_rsqrt_fusion), kind=kOutput, calls=%fused_computation.30 | convolution fusion | flops 610664448 | bytes 4139008 | tf_op jit(solution)/shard_map/sdt,ed->ste/dot_general | solution.py:161
  140.0 66.0 %all-gather.6.cloned.1.call-done = bf16[2,32,192,512]{3,2,1,0:T(8,128)(2,1)} async-done(((bf16[2,2,192,512]{3,2,1,0:T(8,128)(2,1)}), bf16[2,32,192,512]{3,2,1,0:T(8,128)(2,1)}) %all-gather.6.cloned.1.call-update) | async-done | bytes 12582928 | tf_op jit(solution)/shard_map/all_gather | solution.py:171
  206.0 23.4 %shard_map.82 = bf16[8,2,64,192]{3,2,1,0:T(8,128)(2,1)} custom-call(bf16[2,512,192]{2,1,0:T(8,128)(2,1)} %fusion.21.query_ref, bf16[2,16,2,192,512]{4,3,2,1,0:T(8,128)(2,1)} %bitcast.64, bf16[2,16,2,192,512]{4,3,2,1,0:T(8,128)(2,1)} %bitcast.65), custom_call_target="tpu_custom_call" | custom-call | tf_op jit(solution)/shard_map/pallas_call | solution.py:84
  229.5 6.7 %all-to-all-start.2 = ((bf16[8,2,64,192]{3,2,1,0:T(8,128)(2,1)}), bf16[8,2,64,192]{3,2,1,0:T(8,128)(2,1)S(1)}, u32[]{:S(2)}, u32[]{:S(2)}) async-start(bf16[8,2,64,192]{3,2,1,0:T(8,128)(2,1)} %shard_map.82), calls=%async_computation.2 | async-start | bytes 1048576 | tf_op jit(solution)/shard_map/all_to_all | solution.py:179
  236.2 4.6 %copy.76 = bf16[2,1536,512]{1,2,0:T(8,128)(2,1)} copy(bf16[2,1536,512]{2,1,0:T(8,128)(2,1)} %bitcast.68) | data formatting | bytes 6291456 | tf_op jit(solution)/shard_map/optimization_barrier | solution.py:156
  240.8 7.4 %all-to-all-done.2 = bf16[8,2,64,192]{3,2,1,0:T(8,128)(2,1)S(1)} async-done(((bf16[8,2,64,192]{3,2,1,0:T(8,128)(2,1)}), bf16[8,2,64,192]{3,2,1,0:T(8,128)(2,1)S(1)}, u32[]{:S(2)}, u32[]{:S(2)}) %all-to-all-start.2) | async-done | bytes 393248 | tf_op jit(solution)/shard_map/all_to_all | solution.py:179
  248.7 2.2 convolution_bitcast_fusion
  250.9 1.9 fusion.46
  (41 shorter events, 9.0 us)
Async XLA Ops:
  6.5 124.6 %copy-start = (bf16[192,1536]{1,0:T(8,128)(2,1)S(1)}, bf16[192,1536]{1,0:T(8,128)(2,1)}, u32[]{:S(2)}) copy-start(bf16[192,1536]{1,0:T(8,128)(2,1)} %param.14) | copy-start | bytes 1769476
  9.6 7.2 %copy-start.4 = (bf16[192,1536]{1,0:T(8,128)(2,1)S(1)}, bf16[192,1536]{1,0:T(8,128)(2,1)}, u32[]{:S(2)}) copy-start(bf16[192,1536]{1,0:T(8,128)(2,1)} %param.15) | copy-start | bytes 1769476
  9.6 50.2 %all-to-all-start = ((bf16[2,8,64,1536]{3,2,0,1:T(8,128)(2,1)}), bf16[2,8,64,1536]{3,2,0,1:T(8,128)(2,1)}, u32[]{:S(2)}, u32[]{:S(2)}) async-start(bf16[2,8,64,1536]{3,2,0,1:T(8,128)(2,1)} %broadcast_in_dim.4), calls=%async_computation | async-start | bytes 6291456 | tf_op jit(solution)/shard_map/all_to_all | solution.py:36
  16.7 111.7 %all-gather.4.cloned.1.call-start = ((), (), s32[]{:S(2)}) async-start(), calls=%async_computation.3 | async-start | bytes 2654208 | tf_op jit(solution)/shard_map/all_gather | solution.py:132
  17.6 188.5 %all-gather.6.cloned.1.call-start = ((), (), s32[]{:S(2)}) async-start(), calls=%async_computation.4 | async-start | bytes 13369344 | tf_op jit(solution)/shard_map/all_gather | solution.py:171
  62.5 4.3 %copy-start.5 = (f32[1536]{0:T(1024)S(1)}, f32[1536]{0:T(1024)}, u32[]{:S(2)}) copy-start(f32[1536]{0:T(1024)} %param.9) | copy-start | bytes 18436
  64.6 1.6 copy-start.2
  66.7 7.0 %copy-start.6 = (bf16[5,192,1536]{2,1,0:T(8,128)(2,1)S(1)}, bf16[5,192,1536]{2,1,0:T(8,128)(2,1)}, u32[]{:S(2)}) copy-start(bf16[5,192,1536]{2,1,0:T(8,128)(2,1)} %param.10) | copy-start | bytes 8847364
  71.1 7.7 %collective-permute-start = (bf16[2,2,1536]{2,1,0:T(2,128)(2,1)S(1)}, bf16[2,2,1536]{2,1,0:T(2,128)(2,1)S(1)}, u32[]{:S(2)}, u32[]{:S(2)}) collective-permute-start(bf16[2,2,1536]{2,1,0:T(2,128)(2,1)S(1)} %get-tuple-element.9), channel_id=1, source_target_pairs={{0,8},{8,16},{16,24},{24,32},{32,40},{40,48},{48,56},{56,64},{64,7... | collective-permute-start | bytes 36872 | tf_op jit(solution)/shard_map/ppermute | solution.py:23
  72.4 5.2 %collective-permute-start.1 = (bf16[2,2,1536]{2,1,0:T(2,128)(2,1)S(1)}, bf16[2,2,1536]{2,1,0:T(2,128)(2,1)S(1)}, u32[]{:S(2)}, u32[]{:S(2)}) collective-permute-start(bf16[2,2,1536]{2,1,0:T(2,128)(2,1)S(1)} %get-tuple-element.10), channel_id=1, source_target_pairs={{8,0},{16,8},{24,16},{32,24},{40,32},{48,40},{56,48},{64,56},{72,6... | collective-permute-start | bytes 36872 | tf_op jit(solution)/shard_map/ppermute | solution.py:25
  128.4 2.7 %copy-start.9 = (f32[1536]{0:T(1024)S(1)}, f32[1536]{0:T(1024)}, u32[]{:S(2)}) copy-start(f32[1536]{0:T(1024)} %param.11) | copy-start | bytes 18436
  128.4 2.8 %copy-start.1 = (bf16[2,8,192,512]{3,2,1,0:T(8,128)(2,1)S(1)}, bf16[2,8,192,512]{3,2,1,0:T(8,128)(2,1)}, u32[]{:S(2)}) copy-start(bf16[2,8,192,512]{3,2,1,0:T(8,128)(2,1)} %copy.75) | copy-start | bytes 9437188
  131.2 1.1 copy-start.7
  132.3 2.1 copy-start.3
  132.3 3.7 %copy-start.8 = (bf16[192,1536]{1,0:T(8,128)(2,1)S(1)}, bf16[192,1536]{1,0:T(8,128)(2,1)}, u32[]{:S(2)}) copy-start(bf16[192,1536]{1,0:T(8,128)(2,1)} %param.12) | copy-start | bytes 1769476
  134.4 114.3 %collective-permute-start.2 = (bf16[1536,768]{1,0:T(8,128)(2,1)S(1)}, bf16[1536,768]{1,0:T(8,128)(2,1)}, u32[]{:S(2)}, u32[]{:S(2)}) collective-permute-start(bf16[1536,768]{1,0:T(8,128)(2,1)S(1)} %copy-done.3), channel_id=1, source_target_pairs={{0,8},{8,0},{1,9},{9,1},{2,10},{10,2},{3,11},{11,3},{4,12},{12,4},... | collective-permute-start | bytes 7077896 | tf_op jit(solution)/shard_map/ppermute | solution.py:180
  229.5 18.7 %all-to-all-start.2 = ((bf16[8,2,64,192]{3,2,1,0:T(8,128)(2,1)}), bf16[8,2,64,192]{3,2,1,0:T(8,128)(2,1)S(1)}, u32[]{:S(2)}, u32[]{:S(2)}) async-start(bf16[8,2,64,192]{3,2,1,0:T(8,128)(2,1)} %shard_map.82), calls=%async_computation.2 | async-start | bytes 1048576 | tf_op jit(solution)/shard_map/all_to_all | solution.py:179
Sparse Core Ops, SparseCore 0:
  19.9 79.5 all-gather.3
  134.5 71.4 all-gather.5

commit v21 on v17

--- a/solution.py
+++ b/solution.py
@@ -178,22 +178,16 @@
     head_width = attended.shape[3]
     arrived = lax.all_to_all(attended, BATCH, 0, 0, tiled=False)
     other_half = lax.ppermute(own_half, "core", [(0, 1), (1, 0)])
-    own_part = jnp.einsum(
+    full_output_weight = jnp.where(
+        mine == 0,
+        jnp.concatenate([own_half, other_half], axis=1),
+        jnp.concatenate([other_half, own_half], axis=1),
+    )
+    branch_rows = jnp.einsum(
         "hstd,hdf->stf",
         arrived,
-        own_half.reshape(batch_count, head_width, -1),
+        full_output_weight.reshape(batch_count, head_width, -1),
         preferred_element_type=jnp.float32,
-    )
-    other_part = jnp.einsum(
-        "hstd,hdf->stf",
-        arrived,
-        other_half.reshape(batch_count, head_width, -1),
-        preferred_element_type=jnp.float32,
-    )
-    branch_rows = jnp.where(
-        mine == 0,
-        jnp.concatenate([own_part, other_part], axis=2),
-        jnp.concatenate([other_part, own_part], axis=2),
     )
     result = own_hidden + branch_rows
     return result.astype(jnp.bfloat16)

time: 260 us -> 260 us (level)
  no operation moved by 1% of the time
where the time goes in v21:
time: 260 us
  waiting for transfers between devices  118 us (45%)
  blocking collectives  43.6 us (17%)
  Pallas kernels  23.2 us (9%)
  starting transfers between devices  18.1 us (7%)
  matrix products  17.1 us (7%)
  local copies, waits for them, and re-layouts  15.2 us (6%)
  between operations  13.6 us (5%)
  other arithmetic  10.6 us (4%)
    all_gather x1, waiting for transfers between devices, shards(): kv_tile = lax.all_gather(kv_rows, SEQ, axis=1)  65.9 us
    all_to_all x1, blocking collectives, gather_batch(): arrived = lax.all_to_all(copies, BATCH, axis, axis, tiled=False)  43.6 us
    all_to_all x1, waiting for transfers between devices, gather_batch(): arrived = lax.all_to_all(copies, BATCH, axis, axis, tiled=False)  42.2 us
    pallas_call x1, Pallas kernels, flash_attention(): pl.pallas_call(flash_step, grid=(sample_count, source_count // sources_pe...  23.2 us
    all_to_all x1, waiting for transfers between devices, shards(): arrived = lax.all_to_all(attended, BATCH, 0, 0, tiled=False)  7.35 us
    all_to_all x1, starting transfers between devices, gather_batch(): arrived = lax.all_to_all(copies, BATCH, axis, axis, tiled=False)  7.15 us
    all_to_all x1, starting transfers between devices, shards(): arrived = lax.all_to_all(attended, BATCH, 0, 0, tiled=False)  6.7 us
    dot_general x5, matrix products, shards(): jnp.einsum('std,ed->set', framed[:, offset:offset + seq_rows], conv_weigh...  5.97 us
  transfers between devices with their start and end apart: 7, of which 4 were waited for; matrix products, arithmetic and copies ran while one was open for 11% of the time, Pallas kernels for 9%

profile of v21, /device:TPU:0, one launch (start us, length us, event | category | flops | bytes accessed | tf_op | source)
XLA Modules:
  0.0 259.7 jit_solution(12451226523315732407)
XLA Ops:
  6.5 3.0 %broadcast_in_dim.4 = bf16[2,8,64,1536]{3,2,0,1:T(8,128)(2,1)} broadcast(bf16[2,64,1536]{2,1,0:T(8,128)(2,1)} %param.8), dimensions={0,2,3} | broadcast | bytes 3538944 | tf_op jit(solution)/shard_map/broadcast_in_dim | solution.py:35
  9.6 7.1 %all-to-all-start = ((bf16[2,8,64,1536]{3,2,0,1:T(8,128)(2,1)}), bf16[2,8,64,1536]{3,2,0,1:T(8,128)(2,1)}, u32[]{:S(2)}, u32[]{:S(2)}) async-start(bf16[2,8,64,1536]{3,2,0,1:T(8,128)(2,1)} %broadcast_in_dim.4), calls=%async_computation | async-start | bytes 6291456 | tf_op jit(solution)/shard_map/all_to_all | solution.py:36
  17.6 42.2 %all-to-all-done = bf16[2,8,64,1536]{3,2,0,1:T(8,128)(2,1)} async-done(((bf16[2,8,64,1536]{3,2,0,1:T(8,128)(2,1)}), bf16[2,8,64,1536]{3,2,0,1:T(8,128)(2,1)}, u32[]{:S(2)}, u32[]{:S(2)}) %all-to-all-start) | async-done | bytes 3145760 | tf_op jit(solution)/shard_map/all_to_all | solution.py:36
  59.8 2.6 multiply_reduce_fusion
  62.5 2.2 copy.67
  64.7 1.6 copy-done.2
  66.7 4.4 %fusion.10 = bf16[2,512,1536]{2,1,0:T(8,128)(2,1)S(1)} fusion(f32[1536]{0:T(1024)S(1)} %copy-done.4, f32[2,512]{1,0:T(2,128)S(1)} %rsqrt.20, bf16[2,8,64,1536]{3,2,1,0:T(8,128)(2,1)} %copy-done.2), kind=kLoop, calls=%fused_computation.13 | loop fusion | flops 18874368 | bytes 6301696 | tf_op jit(solution)/shard_map/convert_element_type | solution.py:141
  71.1 1.3 collective-permute-start
  72.4 1.3 collective-permute-start.1
  74.9 2.7 %collective-permute-done.1 = bf16[2,2,1536]{2,1,0:T(2,128)(2,1)S(1)} collective-permute-done((bf16[2,2,1536]{2,1,0:T(2,128)(2,1)S(1)}, bf16[2,2,1536]{2,1,0:T(2,128)(2,1)S(1)}, u32[]{:S(2)}, u32[]{:S(2)}) %collective-permute-start.1) | collective-permute-done | bytes 12320 | tf_op jit(solution)/shard_map/ppermute | solution.py:25
  77.7 1.2 fusion.21
  80.0 1.2 fusion.16
  81.2 1.3 fusion.55
  82.8 43.6 %all_to_all.15 = bf16[2,8,192,512]{3,2,0,1:T(8,128)(2,1)S(1)} all-to-all(bf16[2,8,192,512]{3,2,0,1:T(8,128)(2,1)S(1)} %broadcast_in_dim.5), channel_id=1, replica_groups=mesh['chip_x'=2,'chip_z'=4,'core'=2,'peer_y'=4,'peer_x'=2] {'peer_y','pe..., dimensions={1} | all-to-all | bytes 6291456 | tf_op jit(solution)/shard_map/all_to_all | solution.py:36
  126.4 1.9 copy.70
  128.4 2.7 %fusion = f32[2,512]{1,0:T(2,128)S(1)} fusion(bf16[2,1536,512]{2,1,0:T(8,128)(2,1)} %bitcast.68), kind=kLoop, calls=%fused_computation.3 | loop fusion | flops 4717568 | bytes 3149824 | tf_op jit(solution)/shard_map/reduce_sum | solution.py:158
  134.4 1.6 collective-permute-start.2
  136.0 4.2 %fusion.34.query_ref = bf16[2,512,192]{2,1,0:T(8,128)(2,1)} fusion(bf16[192,1536]{1,0:T(8,128)(2,1)} %param.12, bf16[2,1536,512]{2,1,0:T(8,128)(2,1)} %bitcast.69, f32[1536]{0:T(1024)S(1)} %copy-done.8, f32[2,512]{1,0:T(2,128)S(1)} %add_rsqrt_fusion), kind=kOutput, calls=%fused_computation.37 | convolution fusion | flops 610664448 | bytes 4139008 | tf_op jit(solution)/shard_map/sdt,ed->ste/dot_general | solution.py:161
  140.1 65.9 %all-gather.6.cloned.1.call-done = bf16[2,32,192,512]{3,2,1,0:T(8,128)(2,1)} async-done(((bf16[2,2,192,512]{3,2,1,0:T(8,128)(2,1)}), bf16[2,32,192,512]{3,2,1,0:T(8,128)(2,1)}) %all-gather.6.cloned.1.call-update) | async-done | bytes 12582928 | tf_op jit(solution)/shard_map/all_gather | solution.py:171
  206.0 23.2 %shard_map.82 = bf16[8,2,64,192]{3,2,1,0:T(8,128)(2,1)} custom-call(bf16[2,512,192]{2,1,0:T(8,128)(2,1)} %fusion.34.query_ref, bf16[2,16,2,192,512]{4,3,2,1,0:T(8,128)(2,1)} %bitcast.66, bf16[2,16,2,192,512]{4,3,2,1,0:T(8,128)(2,1)} %bitcast.67), custom_call_target="tpu_custom_call" | custom-call | tf_op jit(solution)/shard_map/pallas_call | solution.py:84
  229.3 6.7 %all-to-all-start.2 = ((bf16[8,2,64,192]{3,2,1,0:T(8,128)(2,1)}), bf16[8,2,64,192]{3,2,1,0:T(8,128)(2,1)S(1)}, u32[]{:S(2)}, u32[]{:S(2)}) async-start(bf16[8,2,64,192]{3,2,1,0:T(8,128)(2,1)} %shard_map.82), calls=%async_computation.2 | async-start | bytes 1048576 | tf_op jit(solution)/shard_map/all_to_all | solution.py:179
  236.0 4.7 %copy.71 = bf16[2,1536,512]{1,2,0:T(8,128)(2,1)} copy(bf16[2,1536,512]{2,1,0:T(8,128)(2,1)} %bitcast.70) | data formatting | bytes 6291456 | tf_op jit(solution)/shard_map/optimization_barrier | solution.py:156
  240.6 7.3 %all-to-all-done.2 = bf16[8,2,64,192]{3,2,1,0:T(8,128)(2,1)S(1)} async-done(((bf16[8,2,64,192]{3,2,1,0:T(8,128)(2,1)}), bf16[8,2,64,192]{3,2,1,0:T(8,128)(2,1)S(1)}, u32[]{:S(2)}, u32[]{:S(2)}) %all-to-all-start.2) | async-done | bytes 393248 | tf_op jit(solution)/shard_map/all_to_all | solution.py:179
  248.0 4.9 %fusion.31 = bf16[2,64,1536]{2,1,0:T(8,128)(2,1)} fusion(bf16[8,2,64,192]{3,2,1,0:T(8,128)(2,1)S(1)} %all-to-all-done.2, bf16[8,192,768]{2,1,0:T(8,128)(2,1)} %bitcast.23, bf16[8,192,768]{2,1,0:T(8,128)(2,1)S(1)} %bitcast.74, pred[]{:T(512)S(6)} %eq.3, bf16[2,1536,512]{1,2,0:T(8,128)(2,1)} %copy.71, s32[]{:T(128)S(6)} %select_n.20), kind=kOutput, calls=%fused_computation.35 | convolution fusion | flops 625803264 | bytes 5898245 | tf_op jit(solution)/shard_map/hstd,hdf->stf/dot_general | solution.py:186
  (37 shorter events, 7.3 us)
Async XLA Ops:
  6.5 124.6 %copy-start = (bf16[192,1536]{1,0:T(8,128)(2,1)S(1)}, bf16[192,1536]{1,0:T(8,128)(2,1)}, u32[]{:S(2)}) copy-start(bf16[192,1536]{1,0:T(8,128)(2,1)} %param.14) | copy-start | bytes 1769476
  9.6 7.2 %copy-start.3 = (bf16[192,1536]{1,0:T(8,128)(2,1)S(1)}, bf16[192,1536]{1,0:T(8,128)(2,1)}, u32[]{:S(2)}) copy-start(bf16[192,1536]{1,0:T(8,128)(2,1)} %param.15) | copy-start | bytes 1769476
  9.6 50.2 %all-to-all-start = ((bf16[2,8,64,1536]{3,2,0,1:T(8,128)(2,1)}), bf16[2,8,64,1536]{3,2,0,1:T(8,128)(2,1)}, u32[]{:S(2)}, u32[]{:S(2)}) async-start(bf16[2,8,64,1536]{3,2,0,1:T(8,128)(2,1)} %broadcast_in_dim.4), calls=%async_computation | async-start | bytes 6291456 | tf_op jit(solution)/shard_map/all_to_all | solution.py:36
  16.7 111.6 %all-gather.4.cloned.1.call-start = ((), (), s32[]{:S(2)}) async-start(), calls=%async_computation.3 | async-start | bytes 2654208 | tf_op jit(solution)/shard_map/all_gather | solution.py:132
  17.6 188.5 %all-gather.6.cloned.1.call-start = ((), (), s32[]{:S(2)}) async-start(), calls=%async_computation.4 | async-start | bytes 13369344 | tf_op jit(solution)/shard_map/all_gather | solution.py:171
  62.5 4.3 %copy-start.4 = (f32[1536]{0:T(1024)S(1)}, f32[1536]{0:T(1024)}, u32[]{:S(2)}) copy-start(f32[1536]{0:T(1024)} %param.9) | copy-start | bytes 18436
  64.6 1.7 copy-start.2
  66.7 7.0 %copy-start.5 = (bf16[5,192,1536]{2,1,0:T(8,128)(2,1)S(1)}, bf16[5,192,1536]{2,1,0:T(8,128)(2,1)}, u32[]{:S(2)}) copy-start(bf16[5,192,1536]{2,1,0:T(8,128)(2,1)} %param.10) | copy-start | bytes 8847364
  71.1 7.7 %collective-permute-start = (bf16[2,2,1536]{2,1,0:T(2,128)(2,1)S(1)}, bf16[2,2,1536]{2,1,0:T(2,128)(2,1)S(1)}, u32[]{:S(2)}, u32[]{:S(2)}) collective-permute-start(bf16[2,2,1536]{2,1,0:T(2,128)(2,1)S(1)} %get-tuple-element.9), channel_id=1, source_target_pairs={{0,8},{8,16},{16,24},{24,32},{32,40},{40,48},{48,56},{56,64},{64,7... | collective-permute-start | bytes 36872 | tf_op jit(solution)/shard_map/ppermute | solution.py:23
  72.4 5.2 %collective-permute-start.1 = (bf16[2,2,1536]{2,1,0:T(2,128)(2,1)S(1)}, bf16[2,2,1536]{2,1,0:T(2,128)(2,1)S(1)}, u32[]{:S(2)}, u32[]{:S(2)}) collective-permute-start(bf16[2,2,1536]{2,1,0:T(2,128)(2,1)S(1)} %get-tuple-element.10), channel_id=1, source_target_pairs={{8,0},{16,8},{24,16},{32,24},{40,32},{48,40},{56,48},{64,56},{72,6... | collective-permute-start | bytes 36872 | tf_op jit(solution)/shard_map/ppermute | solution.py:25
  128.4 2.7 %copy-start.8 = (f32[1536]{0:T(1024)S(1)}, f32[1536]{0:T(1024)}, u32[]{:S(2)}) copy-start(f32[1536]{0:T(1024)} %param.11) | copy-start | bytes 18436
  128.4 2.8 %copy-start.1 = (bf16[2,8,192,512]{3,2,1,0:T(8,128)(2,1)S(1)}, bf16[2,8,192,512]{3,2,1,0:T(8,128)(2,1)}, u32[]{:S(2)}) copy-start(bf16[2,8,192,512]{3,2,1,0:T(8,128)(2,1)} %copy.70) | copy-start | bytes 9437188
  131.2 1.1 copy-start.7
  132.3 2.1 copy-start.6
  134.4 106.3 %collective-permute-start.2 = (bf16[1536,768]{1,0:T(8,128)(2,1)S(1)}, bf16[1536,768]{1,0:T(8,128)(2,1)}, u32[]{:S(2)}, u32[]{:S(2)}) collective-permute-start(bf16[1536,768]{1,0:T(8,128)(2,1)S(1)} %copy-done.6), channel_id=1, source_target_pairs={{0,8},{8,0},{1,9},{9,1},{2,10},{10,2},{3,11},{11,3},{4,12},{12,4},... | collective-permute-start | bytes 7077896 | tf_op jit(solution)/shard_map/ppermute | solution.py:180
  229.3 18.7 %all-to-all-start.2 = ((bf16[8,2,64,192]{3,2,1,0:T(8,128)(2,1)}), bf16[8,2,64,192]{3,2,1,0:T(8,128)(2,1)S(1)}, u32[]{:S(2)}, u32[]{:S(2)}) async-start(bf16[8,2,64,192]{3,2,1,0:T(8,128)(2,1)} %shard_map.82), calls=%async_computation.2 | async-start | bytes 1048576 | tf_op jit(solution)/shard_map/all_to_all | solution.py:179
Sparse Core Ops, SparseCore 0:
  19.9 79.5 all-gather.3
  134.5 71.5 all-gather.5

commit v22 on v17

--- a/solution.py
+++ b/solution.py
@@ -176,7 +176,19 @@
         lax.dynamic_slice_in_dim(hidden_full, row_start, own_rows, 2), (0, 2, 1)
     ).astype(jnp.float32)
     head_width = attended.shape[3]
-    arrived = lax.all_to_all(attended, BATCH, 0, 0, tiled=False)
+    peer = lax.axis_index(BATCH)
+    by_shift = [lax.dynamic_index_in_dim(attended, peer, 0, keepdims=False)]
+    for shift in range(1, batch_count):
+        by_shift.append(
+            lax.ppermute(
+                lax.dynamic_index_in_dim(attended, (peer + shift) % batch_count, 0, keepdims=False),
+                BATCH,
+                [(index, (index + shift) % batch_count) for index in range(batch_count)],
+            )
+        )
+    arrived = jnp.take(
+        jnp.stack(by_shift), (peer - jnp.arange(batch_count)) % batch_count, axis=0
+    )
     other_half = lax.ppermute(own_half, "core", [(0, 1), (1, 0)])
     own_part = jnp.einsum(
         "hstd,hdf->stf",

time: 260 us -> 271 us (1.042)
  starting transfers between devices: 18.1 us -> 25.5 us
    ppermute x0 -> x7, starting transfers between devices: none -> 14.8 us  [shards(): lax.ppermute(lax.dynamic_index_in_dim(attended, (peer + shift) % batch_co...]
    all_to_all x1 -> x0, waiting for transfers between devices: 7.36 us -> none  [shards(): arrived = lax.all_to_all(attended, BATCH, 0, 0, tiled=False)]
    all_to_all x1 -> x0, starting transfers between devices: 6.7 us -> none  [shards(): arrived = lax.all_to_all(attended, BATCH, 0, 0, tiled=False)]
    ppermute x0 -> x7, waiting for transfers between devices: none -> 5.71 us  [shards(): lax.ppermute(lax.dynamic_index_in_dim(attended, (peer + shift) % batch_co...]
  transfers between devices with their start and end apart: 7 -> 13, of which waited for: 4 -> 6; matrix products, arithmetic and copies ran while one was open for 11% -> 12% of each run, Pallas kernels for 9% -> 9%
where the time goes in v22:
time: 271 us; the launch traced here: 270 us
  waiting for transfers between devices  116 us (43%)
  blocking collectives  45 us (17%)
  starting transfers between devices  25.5 us (9%)
  Pallas kernels  23.2 us (9%)
  local copies, waits for them, and re-layouts  16.9 us (6%)
  matrix products  16.6 us (6%)
  between operations  13.8 us (5%)
  other arithmetic  12.5 us (5%)
    all_gather x1, waiting for transfers between devices, shards(): kv_tile = lax.all_gather(kv_rows, SEQ, axis=1)  66.9 us
    all_to_all x1, blocking collectives, gather_batch(): arrived = lax.all_to_all(copies, BATCH, axis, axis, tiled=False)  45 us
    all_to_all x1, waiting for transfers between devices, gather_batch(): arrived = lax.all_to_all(copies, BATCH, axis, axis, tiled=False)  42.2 us
    pallas_call x1, Pallas kernels, flash_attention(): pl.pallas_call(flash_step, grid=(sample_count, source_count // sources_pe...  23.2 us
    ppermute x7, starting transfers between devices, shards(): lax.ppermute(lax.dynamic_index_in_dim(attended, (peer + shift) % batch_co...  14.8 us
    all_to_all x1, starting transfers between devices, gather_batch(): arrived = lax.all_to_all(copies, BATCH, axis, axis, tiled=False)  7.15 us
    dot_general x5, matrix products, shards(): jnp.einsum('std,ed->set', framed[:, offset:offset + seq_rows], conv_weigh...  5.97 us
    ppermute x7, waiting for transfers between devices, shards(): lax.ppermute(lax.dynamic_index_in_dim(attended, (peer + shift) % batch_co...  5.71 us
  transfers between devices with their start and end apart: 13, of which 6 were waited for; matrix products, arithmetic and copies ran while one was open for 12% of the time, Pallas kernels for 9%

profile of v22, /device:TPU:0, one launch (start us, length us, event | category | flops | bytes accessed | tf_op | source)
XLA Modules:
  0.0 269.9 jit_solution(9262796873989937964)
XLA Ops:
  6.5 3.0 %broadcast_in_dim.11 = bf16[2,8,64,1536]{3,2,0,1:T(8,128)(2,1)} broadcast(bf16[2,64,1536]{2,1,0:T(8,128)(2,1)} %param.8), dimensions={0,2,3} | broadcast | bytes 3538944 | tf_op jit(solution)/shard_map/broadcast_in_dim | solution.py:35
  9.6 7.1 %all-to-all-start = ((bf16[2,8,64,1536]{3,2,0,1:T(8,128)(2,1)}), bf16[2,8,64,1536]{3,2,0,1:T(8,128)(2,1)}, u32[]{:S(2)}, u32[]{:S(2)}) async-start(bf16[2,8,64,1536]{3,2,0,1:T(8,128)(2,1)} %broadcast_in_dim.11), calls=%async_computation | async-start | bytes 6291456 | tf_op jit(solution)/shard_map/all_to_all | solution.py:36
  17.6 42.2 %all-to-all-done = bf16[2,8,64,1536]{3,2,0,1:T(8,128)(2,1)} async-done(((bf16[2,8,64,1536]{3,2,0,1:T(8,128)(2,1)}), bf16[2,8,64,1536]{3,2,0,1:T(8,128)(2,1)}, u32[]{:S(2)}, u32[]{:S(2)}) %all-to-all-start) | async-done | bytes 3145760 | tf_op jit(solution)/shard_map/all_to_all | solution.py:36
  59.8 2.2 copy.72
  62.0 1.6 copy-done.2
  64.0 2.6 multiply_reduce_fusion
  66.7 4.4 %fusion.10 = bf16[2,512,1536]{2,1,0:T(8,128)(2,1)S(1)} fusion(f32[1536]{0:T(1024)S(1)} %copy-done.4, f32[2,512]{1,0:T(2,128)S(1)} %rsqrt.20, bf16[2,8,64,1536]{3,2,1,0:T(8,128)(2,1)} %copy-done.2), kind=kLoop, calls=%fused_computation.14 | loop fusion | flops 18874368 | bytes 6301696 | tf_op jit(solution)/shard_map/convert_element_type | solution.py:141
  76.1 1.6 collective-permute-done.1
  81.6 45.0 %all_to_all.10 = bf16[2,8,192,512]{3,2,0,1:T(8,128)(2,1)S(1)} all-to-all(bf16[2,8,192,512]{3,2,0,1:T(8,128)(2,1)S(1)} %broadcast_in_dim.12), channel_id=1, replica_groups=mesh['chip_x'=2,'chip_z'=4,'core'=2,'peer_y'=4,'peer_x'=2] {'peer_y','pe..., dimensions={1} | all-to-all | bytes 6291456 | tf_op jit(solution)/shard_map/all_to_all | solution.py:36
  126.6 1.9 copy.75
  128.5 2.7 fusion
  135.6 4.0 %fusion.21.query_ref = bf16[2,512,192]{2,1,0:T(8,128)(2,1)} fusion(bf16[192,1536]{1,0:T(8,128)(2,1)S(1)} %copy-done.7, bf16[2,1536,512]{2,1,0:T(8,128)(2,1)} %bitcast.95, f32[1536]{0:T(1024)S(1)} %copy-done.8, f32[2,512]{1,0:T(2,128)S(1)} %add_rsqrt_fusion), kind=kOutput, calls=%fused_computation.31 | convolution fusion | flops 610664448 | bytes 4139008 | tf_op jit(solution)/shard_map/sdt,ed->ste/dot_general | solution.py:161
  139.6 66.9 %all-gather.6.cloned.1.call-done = bf16[2,32,192,512]{3,2,1,0:T(8,128)(2,1)} async-done(((bf16[2,2,192,512]{3,2,1,0:T(8,128)(2,1)}), bf16[2,32,192,512]{3,2,1,0:T(8,128)(2,1)}) %all-gather.6.cloned.1.call-update) | async-done | bytes 12582928 | tf_op jit(solution)/shard_map/all_gather | solution.py:171
  206.5 23.2 %shard_map.82 = bf16[8,2,64,192]{3,2,1,0:T(8,128)(2,1)} custom-call(bf16[2,512,192]{2,1,0:T(8,128)(2,1)} %fusion.21.query_ref, bf16[2,16,2,192,512]{4,3,2,1,0:T(8,128)(2,1)} %bitcast.92, bf16[2,16,2,192,512]{4,3,2,1,0:T(8,128)(2,1)} %bitcast.93), custom_call_target="tpu_custom_call" | custom-call | tf_op jit(solution)/shard_map/pallas_call | solution.py:84
  230.8 3.1 %collective-permute-start.2 = (bf16[2,64,192]{2,1,0:T(8,128)(2,1)S(1)}, bf16[2,64,192]{2,1,0:T(8,128)(2,1)S(1)}, u32[]{:S(2)}, u32[]{:S(2)}) collective-permute-start(bf16[2,64,192]{2,1,0:T(8,128)(2,1)S(1)} %get-tuple-element.17), channel_id=1, source_target_pairs={{0,1},{1,2},{2,3},{3,4},{4,5},{5,6},{6,7},{7,0},{8,9},{9,10},{10,1... | collective-permute-start | bytes 147464 | tf_op jit(solution)/shard_map/ppermute | solution.py:183
  233.8 4.7 %copy.76 = bf16[2,1536,512]{1,2,0:T(8,128)(2,1)} copy(bf16[2,1536,512]{2,1,0:T(8,128)(2,1)} %bitcast.96) | data formatting | bytes 6291456 | tf_op jit(solution)/shard_map/optimization_barrier | solution.py:156
  240.0 2.1 collective-permute-start.4
  242.1 2.0 collective-permute-start.5
  244.1 4.5 %collective-permute-start.6 = (bf16[2,64,192]{2,1,0:T(8,128)(2,1)S(1)}, bf16[2,64,192]{2,1,0:T(8,128)(2,1)S(1)}, u32[]{:S(2)}, u32[]{:S(2)}) collective-permute-start(bf16[2,64,192]{2,1,0:T(8,128)(2,1)S(1)} %get-tuple-element.13), channel_id=1, source_target_pairs={{0,5},{1,6},{2,7},{3,0},{4,1},{5,2},{6,3},{7,4},{8,13},{9,14},{10,... | collective-permute-start | bytes 147464 | tf_op jit(solution)/shard_map/ppermute | solution.py:183
  250.8 2.1 collective-permute-done.7
  253.0 3.0 %collective-permute-done.8 = bf16[2,64,192]{2,1,0:T(8,128)(2,1)S(1)} collective-permute-done((bf16[2,64,192]{2,1,0:T(8,128)(2,1)S(1)}, bf16[2,64,192]{2,1,0:T(8,128)(2,1)S(1)}, u32[]{:S(2)}, u32[]{:S(2)}) %collective-permute-start.8) | collective-permute-done | bytes 49184 | tf_op jit(solution)/shard_map/ppermute | solution.py:183
  256.6 2.3 convolution_bitcast_fusion.1
  258.9 2.3 convolution_bitcast_fusion
  261.2 1.9 fusion.46
  (63 shorter events, 19.8 us)
Async XLA Ops:
  6.5 124.7 %copy-start = (bf16[192,1536]{1,0:T(8,128)(2,1)S(1)}, bf16[192,1536]{1,0:T(8,128)(2,1)}, u32[]{:S(2)}) copy-start(bf16[192,1536]{1,0:T(8,128)(2,1)} %param.13) | copy-start | bytes 1769476
  9.6 7.2 %copy-start.3 = (bf16[192,1536]{1,0:T(8,128)(2,1)S(1)}, bf16[192,1536]{1,0:T(8,128)(2,1)}, u32[]{:S(2)}) copy-start(bf16[192,1536]{1,0:T(8,128)(2,1)} %param.15) | copy-start | bytes 1769476
  9.6 50.2 %all-to-all-start = ((bf16[2,8,64,1536]{3,2,0,1:T(8,128)(2,1)}), bf16[2,8,64,1536]{3,2,0,1:T(8,128)(2,1)}, u32[]{:S(2)}, u32[]{:S(2)}) async-start(bf16[2,8,64,1536]{3,2,0,1:T(8,128)(2,1)} %broadcast_in_dim.11), calls=%async_computation | async-start | bytes 6291456 | tf_op jit(solution)/shard_map/all_to_all | solution.py:36
  16.7 111.8 %all-gather.4.cloned.1.call-start = ((), (), s32[]{:S(2)}) async-start(), calls=%async_computation.2 | async-start | bytes 2654208 | tf_op jit(solution)/shard_map/all_gather | solution.py:132
  17.5 188.9 %all-gather.6.cloned.1.call-start = ((), (), s32[]{:S(2)}) async-start(), calls=%async_computation.3 | async-start | bytes 13369344 | tf_op jit(solution)/shard_map/all_gather | solution.py:171
  61.9 1.7 copy-start.2
  61.9 4.8 %copy-start.4 = (f32[1536]{0:T(1024)S(1)}, f32[1536]{0:T(1024)}, u32[]{:S(2)}) copy-start(f32[1536]{0:T(1024)} %param.9) | copy-start | bytes 18436
  66.7 7.0 %copy-start.5 = (bf16[5,192,1536]{2,1,0:T(8,128)(2,1)S(1)}, bf16[5,192,1536]{2,1,0:T(8,128)(2,1)}, u32[]{:S(2)}) copy-start(bf16[5,192,1536]{2,1,0:T(8,128)(2,1)} %param.10) | copy-start | bytes 8847364
  71.1 3.8 %collective-permute-start = (bf16[2,2,1536]{2,1,0:T(2,128)(2,1)S(1)}, bf16[2,2,1536]{2,1,0:T(2,128)(2,1)S(1)}, u32[]{:S(2)}, u32[]{:S(2)}) collective-permute-start(bf16[2,2,1536]{2,1,0:T(2,128)(2,1)S(1)} %get-tuple-element.9), channel_id=1, source_target_pairs={{0,8},{8,16},{16,24},{24,32},{32,40},{40,48},{48,56},{56,64},{64,7... | collective-permute-start | bytes 36872 | tf_op jit(solution)/shard_map/ppermute | solution.py:23
  72.4 5.2 %collective-permute-start.1 = (bf16[2,2,1536]{2,1,0:T(2,128)(2,1)S(1)}, bf16[2,2,1536]{2,1,0:T(2,128)(2,1)S(1)}, u32[]{:S(2)}, u32[]{:S(2)}) collective-permute-start(bf16[2,2,1536]{2,1,0:T(2,128)(2,1)S(1)} %get-tuple-element.10), channel_id=1, source_target_pairs={{8,0},{16,8},{24,16},{32,24},{40,32},{48,40},{56,48},{64,56},{72,6... | collective-permute-start | bytes 36872 | tf_op jit(solution)/shard_map/ppermute | solution.py:25
  128.5 2.7 %copy-start.8 = (f32[1536]{0:T(1024)S(1)}, f32[1536]{0:T(1024)}, u32[]{:S(2)}) copy-start(f32[1536]{0:T(1024)} %param.11) | copy-start | bytes 18436
  128.5 2.8 %copy-start.1 = (bf16[2,8,192,512]{3,2,1,0:T(8,128)(2,1)S(1)}, bf16[2,8,192,512]{3,2,1,0:T(8,128)(2,1)}, u32[]{:S(2)}) copy-start(bf16[2,8,192,512]{3,2,1,0:T(8,128)(2,1)} %copy.75) | copy-start | bytes 9437188
  131.4 1.1 copy-start.6
  132.4 3.1 %copy-start.7 = (bf16[192,1536]{1,0:T(8,128)(2,1)S(1)}, bf16[192,1536]{1,0:T(8,128)(2,1)}, u32[]{:S(2)}) copy-start(bf16[192,1536]{1,0:T(8,128)(2,1)} %param.12) | copy-start | bytes 1769476
  134.6 124.2 %collective-permute-start.9 = (bf16[1536,768]{1,0:T(8,128)(2,1)}, bf16[1536,768]{1,0:T(8,128)(2,1)}, u32[]{:S(2)}, u32[]{:S(2)}) collective-permute-start(bf16[1536,768]{1,0:T(8,128)(2,1)} %all-gather.4.cloned.1.call-done), channel_id=1, source_target_pairs={{0,8},{8,0},{1,9},{9,1},{2,10},{10,2},{3,11},{11,3},{4,12},{12,4},... | collective-permute-start | bytes 7077896 | tf_op jit(solution)/shard_map/ppermute | solution.py:192
  230.8 13.3 %collective-permute-start.2 = (bf16[2,64,192]{2,1,0:T(8,128)(2,1)S(1)}, bf16[2,64,192]{2,1,0:T(8,128)(2,1)S(1)}, u32[]{:S(2)}, u32[]{:S(2)}) collective-permute-start(bf16[2,64,192]{2,1,0:T(8,128)(2,1)S(1)} %get-tuple-element.17), channel_id=1, source_target_pairs={{0,1},{1,2},{2,3},{3,4},{4,5},{5,6},{6,7},{7,0},{8,9},{9,10},{10,1... | collective-permute-start | bytes 147464 | tf_op jit(solution)/shard_map/ppermute | solution.py:183
  238.5 10.2 %collective-permute-start.3 = (bf16[2,64,192]{2,1,0:T(8,128)(2,1)S(1)}, bf16[2,64,192]{2,1,0:T(8,128)(2,1)S(1)}, u32[]{:S(2)}, u32[]{:S(2)}) collective-permute-start(bf16[2,64,192]{2,1,0:T(8,128)(2,1)S(1)} %get-tuple-element.16), channel_id=1, source_target_pairs={{0,2},{1,3},{2,4},{3,5},{4,6},{5,7},{6,0},{7,1},{8,10},{9,11},{10,... | collective-permute-start | bytes 147464 | tf_op jit(solution)/shard_map/ppermute | solution.py:183
  240.0 10.2 %collective-permute-start.4 = (bf16[2,64,192]{2,1,0:T(8,128)(2,1)S(1)}, bf16[2,64,192]{2,1,0:T(8,128)(2,1)S(1)}, u32[]{:S(2)}, u32[]{:S(2)}) collective-permute-start(bf16[2,64,192]{2,1,0:T(8,128)(2,1)S(1)} %get-tuple-element.15), channel_id=1, source_target_pairs={{0,3},{1,4},{2,5},{3,6},{4,7},{5,0},{6,1},{7,2},{8,11},{9,12},{10,... | collective-permute-start | bytes 147464 | tf_op jit(solution)/shard_map/ppermute | solution.py:183
  242.1 8.2 %collective-permute-start.5 = (bf16[2,64,192]{2,1,0:T(8,128)(2,1)S(1)}, bf16[2,64,192]{2,1,0:T(8,128)(2,1)S(1)}, u32[]{:S(2)}, u32[]{:S(2)}) collective-permute-start(bf16[2,64,192]{2,1,0:T(8,128)(2,1)S(1)} %get-tuple-element.14), channel_id=1, source_target_pairs={{0,4},{1,5},{2,6},{3,7},{4,0},{5,1},{6,2},{7,3},{8,12},{9,13},{10,... | collective-permute-start | bytes 147464 | tf_op jit(solution)/shard_map/ppermute | solution.py:183
  244.1 6.7 %collective-permute-start.6 = (bf16[2,64,192]{2,1,0:T(8,128)(2,1)S(1)}, bf16[2,64,192]{2,1,0:T(8,128)(2,1)S(1)}, u32[]{:S(2)}, u32[]{:S(2)}) collective-permute-start(bf16[2,64,192]{2,1,0:T(8,128)(2,1)S(1)} %get-tuple-element.13), channel_id=1, source_target_pairs={{0,5},{1,6},{2,7},{3,0},{4,1},{5,2},{6,3},{7,4},{8,13},{9,14},{10,... | collective-permute-start | bytes 147464 | tf_op jit(solution)/shard_map/ppermute | solution.py:183
  248.6 4.3 %collective-permute-start.7 = (bf16[2,64,192]{2,1,0:T(8,128)(2,1)S(1)}, bf16[2,64,192]{2,1,0:T(8,128)(2,1)S(1)}, u32[]{:S(2)}, u32[]{:S(2)}) collective-permute-start(bf16[2,64,192]{2,1,0:T(8,128)(2,1)S(1)} %get-tuple-element.12), channel_id=1, source_target_pairs={{0,6},{1,7},{2,0},{3,1},{4,2},{5,3},{6,4},{7,5},{8,14},{9,15},{10,... | collective-permute-start | bytes 147464 | tf_op jit(solution)/shard_map/ppermute | solution.py:183
  250.2 5.8 %collective-permute-start.8 = (bf16[2,64,192]{2,1,0:T(8,128)(2,1)S(1)}, bf16[2,64,192]{2,1,0:T(8,128)(2,1)S(1)}, u32[]{:S(2)}, u32[]{:S(2)}) collective-permute-start(bf16[2,64,192]{2,1,0:T(8,128)(2,1)S(1)} %get-tuple-element.11), channel_id=1, source_target_pairs={{0,7},{1,0},{2,1},{3,2},{4,3},{5,4},{6,5},{7,6},{8,15},{9,8},{10,9... | collective-permute-start | bytes 147464 | tf_op jit(solution)/shard_map/ppermute | solution.py:183
Sparse Core Ops, SparseCore 0:
  19.8 84.8 all-gather.3
  134.6 71.7 all-gather.5

commit v23 on v20

--- a/solution.py
+++ b/solution.py
@@ -38,7 +38,7 @@
 
 
 def flash_step(query_ref, key_ref, value_ref, out_ref, peak_ref, total_ref, summed_ref):
-    block = pl.program_id(1)
+    block = pl.program_id(2)
 
     @pl.when(block == 0)
     def _():
@@ -71,40 +71,47 @@
     summed_ref[...] = summed
     peak_ref[...] = new_peak
 
-    @pl.when(block == pl.num_programs(1) - 1)
+    @pl.when(block == pl.num_programs(2) - 1)
     def _():
         finished = (summed_ref[...] / total_ref[...]).astype(out_ref.dtype)
         out_ref[:, 0] = finished.reshape(out_ref.shape[0], out_ref.shape[2], out_ref.shape[3])
 
 
-def flash_attention(queries, kv_tile, peers, sources_per_step=16):
+def flash_attention(queries, kv_tile, peers, sources_per_step=16, query_splits=2):
     sample_count, query_count, head_width = queries.shape
     _, source_count, _, _, source_rows = kv_tile.shape
     sources_per_step = math.gcd(source_count, sources_per_step)
+    query_splits = math.gcd(peers, query_splits)
+    query_block = query_count // query_splits
+    peer_block = peers // query_splits
     return pl.pallas_call(
         flash_step,
-        grid=(sample_count, source_count // sources_per_step),
+        grid=(sample_count, query_splits, source_count // sources_per_step),
         in_specs=[
-            pl.BlockSpec((1, query_count, head_width), lambda s, k: (s, 0, 0)),
+            pl.BlockSpec((1, query_block, head_width), lambda s, q, k: (s, q, 0)),
             pl.BlockSpec(
-                (1, sources_per_step, 1, head_width, source_rows), lambda s, k: (0, k, s, 0, 0)
+                (1, sources_per_step, 1, head_width, source_rows),
+                lambda s, q, k: (0, k, s, 0, 0),
             ),
             pl.BlockSpec(
-                (1, sources_per_step, 1, head_width, source_rows), lambda s, k: (1, k, s, 0, 0)
+                (1, sources_per_step, 1, head_width, source_rows),
+                lambda s, q, k: (1, k, s, 0, 0),
             ),
         ],
         out_specs=pl.BlockSpec(
-            (peers, 1, query_count // peers, head_width), lambda s, k: (0, s, 0, 0)
+            (peer_block, 1, query_count // peers, head_width), lambda s, q, k: (q, s, 0, 0)
         ),
         out_shape=jax.ShapeDtypeStruct(
             (peers, sample_count, query_count // peers, head_width), jnp.bfloat16
         ),
         scratch_shapes=[
-            pltpu.VMEM((query_count, 1), jnp.float32),
-            pltpu.VMEM((query_count, 1), jnp.float32),
-            pltpu.VMEM((query_count, head_width), jnp.float32),
+            pltpu.VMEM((query_block, 1), jnp.float32),
+            pltpu.VMEM((query_block, 1), jnp.float32),
+            pltpu.VMEM((query_block, head_width), jnp.float32),
         ],
-        compiler_params=pltpu.CompilerParams(dimension_semantics=("parallel", "arbitrary")),
+        compiler_params=pltpu.CompilerParams(
+            dimension_semantics=("parallel", "parallel", "arbitrary")
+        ),
     )(queries, kv_tile, kv_tile)
 
 

time: 260 us -> 262 us (level)
  no operation moved by 1% of the time
where the time goes in v23:
time: 262 us; the launch traced here: 261 us
  waiting for transfers between devices  118 us (45%)
  blocking collectives  43.6 us (17%)
  Pallas kernels  24.7 us (9%)
  starting transfers between devices  18.1 us (7%)
  local copies, waits for them, and re-layouts  15.2 us (6%)
  matrix products  14.9 us (6%)
  between operations  13.6 us (5%)
  other arithmetic  12.5 us (5%)
    all_gather x1, waiting for transfers between devices, shards(): kv_tile = lax.all_gather(kv_rows, SEQ, axis=1)  66 us
    all_to_all x1, blocking collectives, gather_batch(): arrived = lax.all_to_all(copies, BATCH, axis, axis, tiled=False)  43.6 us
    all_to_all x1, waiting for transfers between devices, gather_batch(): arrived = lax.all_to_all(copies, BATCH, axis, axis, tiled=False)  42.2 us
    pallas_call x1, Pallas kernels, flash_attention(): pl.pallas_call(flash_step, grid=(sample_count, query_splits, source_count...  24.7 us
    all_to_all x1, waiting for transfers between devices, shards(): arrived = lax.all_to_all(attended, BATCH, 0, 0, tiled=False)  7.36 us
    all_to_all x1, starting transfers between devices, gather_batch(): arrived = lax.all_to_all(copies, BATCH, axis, axis, tiled=False)  7.15 us
    all_to_all x1, starting transfers between devices, shards(): arrived = lax.all_to_all(attended, BATCH, 0, 0, tiled=False)  6.7 us
    dot_general x5, matrix products, shards(): jnp.einsum('std,ed->set', framed[:, offset:offset + seq_rows], conv_weigh...  5.97 us
  transfers between devices with their start and end apart: 7, of which 4 were waited for; matrix products, arithmetic and copies ran while one was open for 11% of the time, Pallas kernels for 9%

profile of v23, /device:TPU:0, one launch (start us, length us, event | category | flops | bytes accessed | tf_op | source)
XLA Modules:
  0.0 260.9 jit_solution(5276421641681470703)
XLA Ops:
  6.5 3.0 %broadcast_in_dim.4 = bf16[2,8,64,1536]{3,2,0,1:T(8,128)(2,1)} broadcast(bf16[2,64,1536]{2,1,0:T(8,128)(2,1)} %param.8), dimensions={0,2,3} | broadcast | bytes 3538944 | tf_op jit(solution)/shard_map/broadcast_in_dim | solution.py:35
  9.6 7.1 %all-to-all-start = ((bf16[2,8,64,1536]{3,2,0,1:T(8,128)(2,1)}), bf16[2,8,64,1536]{3,2,0,1:T(8,128)(2,1)}, u32[]{:S(2)}, u32[]{:S(2)}) async-start(bf16[2,8,64,1536]{3,2,0,1:T(8,128)(2,1)} %broadcast_in_dim.4), calls=%async_computation | async-start | bytes 6291456 | tf_op jit(solution)/shard_map/all_to_all | solution.py:36
  17.6 42.2 %all-to-all-done = bf16[2,8,64,1536]{3,2,0,1:T(8,128)(2,1)} async-done(((bf16[2,8,64,1536]{3,2,0,1:T(8,128)(2,1)}), bf16[2,8,64,1536]{3,2,0,1:T(8,128)(2,1)}, u32[]{:S(2)}, u32[]{:S(2)}) %all-to-all-start) | async-done | bytes 3145760 | tf_op jit(solution)/shard_map/all_to_all | solution.py:36
  59.8 2.6 multiply_reduce_fusion
  62.5 2.2 copy.72
  64.6 1.6 copy-done.2
  66.7 4.4 %fusion.10 = bf16[2,512,1536]{2,1,0:T(8,128)(2,1)S(1)} fusion(f32[1536]{0:T(1024)S(1)} %copy-done.5, f32[2,512]{1,0:T(2,128)S(1)} %rsqrt.20, bf16[2,8,64,1536]{3,2,1,0:T(8,128)(2,1)} %copy-done.2), kind=kLoop, calls=%fused_computation.13 | loop fusion | flops 18874368 | bytes 6301696 | tf_op jit(solution)/shard_map/convert_element_type | solution.py:148
  71.1 1.3 collective-permute-start
  72.4 1.3 collective-permute-start.1
  74.9 2.7 %collective-permute-done.1 = bf16[2,2,1536]{2,1,0:T(2,128)(2,1)S(1)} collective-permute-done((bf16[2,2,1536]{2,1,0:T(2,128)(2,1)S(1)}, bf16[2,2,1536]{2,1,0:T(2,128)(2,1)S(1)}, u32[]{:S(2)}, u32[]{:S(2)}) %collective-permute-start.1) | collective-permute-done | bytes 12320 | tf_op jit(solution)/shard_map/ppermute | solution.py:25
  77.7 1.2 fusion.17
  81.2 1.3 fusion.42
  82.8 43.6 %all_to_all.15 = bf16[2,8,192,512]{3,2,0,1:T(8,128)(2,1)S(1)} all-to-all(bf16[2,8,192,512]{3,2,0,1:T(8,128)(2,1)S(1)} %broadcast_in_dim.5), channel_id=1, replica_groups=mesh['chip_x'=2,'chip_z'=4,'core'=2,'peer_y'=4,'peer_x'=2] {'peer_y','pe..., dimensions={1} | all-to-all | bytes 6291456 | tf_op jit(solution)/shard_map/all_to_all | solution.py:36
  126.4 1.9 copy.75
  128.4 2.7 %fusion = f32[2,512]{1,0:T(2,128)S(1)} fusion(bf16[2,1536,512]{2,1,0:T(8,128)(2,1)} %bitcast.66), kind=kLoop, calls=%fused_computation.3 | loop fusion | flops 4717568 | bytes 3149824 | tf_op jit(solution)/shard_map/reduce_sum | solution.py:165
  134.4 1.6 collective-permute-start.2
  136.0 4.1 %fusion.21.query_ref = bf16[2,512,192]{2,1,0:T(8,128)(2,1)} fusion(bf16[192,1536]{1,0:T(8,128)(2,1)S(1)} %copy-done.8, bf16[2,1536,512]{2,1,0:T(8,128)(2,1)} %bitcast.67, f32[1536]{0:T(1024)S(1)} %copy-done.9, f32[2,512]{1,0:T(2,128)S(1)} %add_rsqrt_fusion), kind=kOutput, calls=%fused_computation.30 | convolution fusion | flops 610664448 | bytes 4139008 | tf_op jit(solution)/shard_map/sdt,ed->ste/dot_general | solution.py:168
  140.0 66.0 %all-gather.6.cloned.1.call-done = bf16[2,32,192,512]{3,2,1,0:T(8,128)(2,1)} async-done(((bf16[2,2,192,512]{3,2,1,0:T(8,128)(2,1)}), bf16[2,32,192,512]{3,2,1,0:T(8,128)(2,1)}) %all-gather.6.cloned.1.call-update) | async-done | bytes 12582928 | tf_op jit(solution)/shard_map/all_gather | solution.py:178
  206.0 24.7 %shard_map.82 = bf16[8,2,64,192]{3,2,1,0:T(8,128)(2,1)} custom-call(bf16[2,512,192]{2,1,0:T(8,128)(2,1)} %fusion.21.query_ref, bf16[2,16,2,192,512]{4,3,2,1,0:T(8,128)(2,1)} %bitcast.64, bf16[2,16,2,192,512]{4,3,2,1,0:T(8,128)(2,1)} %bitcast.65), custom_call_target="tpu_custom_call" | custom-call | tf_op jit(solution)/shard_map/pallas_call | solution.py:87
  230.7 6.7 %all-to-all-start.2 = ((bf16[8,2,64,192]{3,2,1,0:T(8,128)(2,1)}), bf16[8,2,64,192]{3,2,1,0:T(8,128)(2,1)S(1)}, u32[]{:S(2)}, u32[]{:S(2)}) async-start(bf16[8,2,64,192]{3,2,1,0:T(8,128)(2,1)} %shard_map.82), calls=%async_computation.2 | async-start | bytes 1048576 | tf_op jit(solution)/shard_map/all_to_all | solution.py:186
  237.4 4.6 %copy.76 = bf16[2,1536,512]{1,2,0:T(8,128)(2,1)} copy(bf16[2,1536,512]{2,1,0:T(8,128)(2,1)} %bitcast.68) | data formatting | bytes 6291456 | tf_op jit(solution)/shard_map/optimization_barrier | solution.py:163
  242.0 7.4 %all-to-all-done.2 = bf16[8,2,64,192]{3,2,1,0:T(8,128)(2,1)S(1)} async-done(((bf16[8,2,64,192]{3,2,1,0:T(8,128)(2,1)}), bf16[8,2,64,192]{3,2,1,0:T(8,128)(2,1)S(1)}, u32[]{:S(2)}, u32[]{:S(2)}) %all-to-all-start.2) | async-done | bytes 393248 | tf_op jit(solution)/shard_map/all_to_all | solution.py:186
  249.9 2.2 convolution_bitcast_fusion
  252.1 1.9 fusion.46
  (41 shorter events, 9.0 us)
Async XLA Ops:
  6.5 124.6 %copy-start = (bf16[192,1536]{1,0:T(8,128)(2,1)S(1)}, bf16[192,1536]{1,0:T(8,128)(2,1)}, u32[]{:S(2)}) copy-start(bf16[192,1536]{1,0:T(8,128)(2,1)} %param.14) | copy-start | bytes 1769476
  9.6 7.2 %copy-start.4 = (bf16[192,1536]{1,0:T(8,128)(2,1)S(1)}, bf16[192,1536]{1,0:T(8,128)(2,1)}, u32[]{:S(2)}) copy-start(bf16[192,1536]{1,0:T(8,128)(2,1)} %param.15) | copy-start | bytes 1769476
  9.6 50.2 %all-to-all-start = ((bf16[2,8,64,1536]{3,2,0,1:T(8,128)(2,1)}), bf16[2,8,64,1536]{3,2,0,1:T(8,128)(2,1)}, u32[]{:S(2)}, u32[]{:S(2)}) async-start(bf16[2,8,64,1536]{3,2,0,1:T(8,128)(2,1)} %broadcast_in_dim.4), calls=%async_computation | async-start | bytes 6291456 | tf_op jit(solution)/shard_map/all_to_all | solution.py:36
  16.7 111.7 %all-gather.4.cloned.1.call-start = ((), (), s32[]{:S(2)}) async-start(), calls=%async_computation.3 | async-start | bytes 2654208 | tf_op jit(solution)/shard_map/all_gather | solution.py:139
  17.6 188.5 %all-gather.6.cloned.1.call-start = ((), (), s32[]{:S(2)}) async-start(), calls=%async_computation.4 | async-start | bytes 13369344 | tf_op jit(solution)/shard_map/all_gather | solution.py:178
  62.5 4.3 %copy-start.5 = (f32[1536]{0:T(1024)S(1)}, f32[1536]{0:T(1024)}, u32[]{:S(2)}) copy-start(f32[1536]{0:T(1024)} %param.9) | copy-start | bytes 18436
  64.6 1.6 copy-start.2
  66.7 7.0 %copy-start.6 = (bf16[5,192,1536]{2,1,0:T(8,128)(2,1)S(1)}, bf16[5,192,1536]{2,1,0:T(8,128)(2,1)}, u32[]{:S(2)}) copy-start(bf16[5,192,1536]{2,1,0:T(8,128)(2,1)} %param.10) | copy-start | bytes 8847364
  71.1 7.7 %collective-permute-start = (bf16[2,2,1536]{2,1,0:T(2,128)(2,1)S(1)}, bf16[2,2,1536]{2,1,0:T(2,128)(2,1)S(1)}, u32[]{:S(2)}, u32[]{:S(2)}) collective-permute-start(bf16[2,2,1536]{2,1,0:T(2,128)(2,1)S(1)} %get-tuple-element.9), channel_id=1, source_target_pairs={{0,8},{8,16},{16,24},{24,32},{32,40},{40,48},{48,56},{56,64},{64,7... | collective-permute-start | bytes 36872 | tf_op jit(solution)/shard_map/ppermute | solution.py:23
  72.4 5.2 %collective-permute-start.1 = (bf16[2,2,1536]{2,1,0:T(2,128)(2,1)S(1)}, bf16[2,2,1536]{2,1,0:T(2,128)(2,1)S(1)}, u32[]{:S(2)}, u32[]{:S(2)}) collective-permute-start(bf16[2,2,1536]{2,1,0:T(2,128)(2,1)S(1)} %get-tuple-element.10), channel_id=1, source_target_pairs={{8,0},{16,8},{24,16},{32,24},{40,32},{48,40},{56,48},{64,56},{72,6... | collective-permute-start | bytes 36872 | tf_op jit(solution)/shard_map/ppermute | solution.py:25
  128.4 2.7 %copy-start.9 = (f32[1536]{0:T(1024)S(1)}, f32[1536]{0:T(1024)}, u32[]{:S(2)}) copy-start(f32[1536]{0:T(1024)} %param.11) | copy-start | bytes 18436
  128.4 2.8 %copy-start.1 = (bf16[2,8,192,512]{3,2,1,0:T(8,128)(2,1)S(1)}, bf16[2,8,192,512]{3,2,1,0:T(8,128)(2,1)}, u32[]{:S(2)}) copy-start(bf16[2,8,192,512]{3,2,1,0:T(8,128)(2,1)} %copy.75) | copy-start | bytes 9437188
  131.2 1.1 copy-start.7
  132.3 2.1 copy-start.3
  132.3 3.7 %copy-start.8 = (bf16[192,1536]{1,0:T(8,128)(2,1)S(1)}, bf16[192,1536]{1,0:T(8,128)(2,1)}, u32[]{:S(2)}) copy-start(bf16[192,1536]{1,0:T(8,128)(2,1)} %param.12) | copy-start | bytes 1769476
  134.4 115.6 %collective-permute-start.2 = (bf16[1536,768]{1,0:T(8,128)(2,1)S(1)}, bf16[1536,768]{1,0:T(8,128)(2,1)}, u32[]{:S(2)}, u32[]{:S(2)}) collective-permute-start(bf16[1536,768]{1,0:T(8,128)(2,1)S(1)} %copy-done.3), channel_id=1, source_target_pairs={{0,8},{8,0},{1,9},{9,1},{2,10},{10,2},{3,11},{11,3},{4,12},{12,4},... | collective-permute-start | bytes 7077896 | tf_op jit(solution)/shard_map/ppermute | solution.py:187
  230.7 18.7 %all-to-all-start.2 = ((bf16[8,2,64,192]{3,2,1,0:T(8,128)(2,1)}), bf16[8,2,64,192]{3,2,1,0:T(8,128)(2,1)S(1)}, u32[]{:S(2)}, u32[]{:S(2)}) async-start(bf16[8,2,64,192]{3,2,1,0:T(8,128)(2,1)} %shard_map.82), calls=%async_computation.2 | async-start | bytes 1048576 | tf_op jit(solution)/shard_map/all_to_all | solution.py:186
Sparse Core Ops, SparseCore 0:
  19.9 79.5 all-gather.3
  134.5 71.4 all-gather.5

commit v24 on v18

--- a/solution.py
+++ b/solution.py
@@ -172,22 +172,16 @@
     head_width = attended.shape[3]
     arrived = lax.all_to_all(attended, BATCH, 0, 0, tiled=False)
     other_half = lax.ppermute(own_half, "core", [(0, 1), (1, 0)])
-    own_part = jnp.einsum(
+    full_output_weight = jnp.where(
+        mine == 0,
+        jnp.concatenate([own_half, other_half], axis=1),
+        jnp.concatenate([other_half, own_half], axis=1),
+    )
+    branch_rows = jnp.einsum(
         "hstd,hdf->stf",
         arrived,
-        own_half.reshape(batch_count, head_width, -1),
+        full_output_weight.reshape(batch_count, head_width, -1),
         preferred_element_type=jnp.float32,
-    )
-    other_part = jnp.einsum(
-        "hstd,hdf->stf",
-        arrived,
-        other_half.reshape(batch_count, head_width, -1),
-        preferred_element_type=jnp.float32,
-    )
-    branch_rows = jnp.where(
-        mine == 0,
-        jnp.concatenate([own_part, other_part], axis=2),
-        jnp.concatenate([other_part, own_part], axis=2),
     )
     result = own_hidden + branch_rows
     return result.astype(jnp.bfloat16)

time: 260 us -> 260 us (level)
  transfers between devices with their start and end apart: 7 -> 7, of which waited for: 3 -> 3; matrix products, arithmetic and copies ran while one was open for 12% -> 11% of each run, Pallas kernels for 9% -> 9%
where the time goes in v24:
time: 260 us
  waiting for transfers between devices  116 us (45%)
  blocking collectives  44.9 us (17%)
  Pallas kernels  23.3 us (9%)
  matrix products  19.2 us (7%)
  starting transfers between devices  17.8 us (7%)
  local copies, waits for them, and re-layouts  14.1 us (5%)
  between operations  13.6 us (5%)
  other arithmetic  10.8 us (4%)
    all_gather x1, waiting for transfers between devices, shards(): kv_tile = lax.all_gather(kv_rows, SEQ, axis=1)  66.7 us
    all_to_all x1, blocking collectives, gather_batch(): arrived = lax.all_to_all(copies, BATCH, axis, axis, tiled=False)  44.9 us
    all_to_all x1, waiting for transfers between devices, gather_batch(): arrived = lax.all_to_all(copies, BATCH, axis, axis, tiled=False)  42.2 us
    pallas_call x1, Pallas kernels, flash_attention(): pl.pallas_call(flash_step, grid=(sample_count, source_count // sources_pe...  23.3 us
    dot_general x5, matrix products, shards(): jnp.einsum('std,ed->set', framed[:, offset:offset + seq_rows], conv_weigh...  8.16 us
    all_to_all x1, waiting for transfers between devices, shards(): arrived = lax.all_to_all(attended, BATCH, 0, 0, tiled=False)  7.36 us
    all_to_all x1, starting transfers between devices, gather_batch(): arrived = lax.all_to_all(copies, BATCH, axis, axis, tiled=False)  7.15 us
    all_to_all x1, starting transfers between devices, shards(): arrived = lax.all_to_all(attended, BATCH, 0, 0, tiled=False)  6.7 us
  transfers between devices with their start and end apart: 7, of which 3 were waited for; matrix products, arithmetic and copies ran while one was open for 11% of the time, Pallas kernels for 9%

profile of v24, /device:TPU:0, one launch (start us, length us, event | category | flops | bytes accessed | tf_op | source)
XLA Modules:
  0.0 260.0 jit_solution(7774651701191752126)
XLA Ops:
  6.5 3.0 %broadcast_in_dim.4 = bf16[2,8,64,1536]{3,2,0,1:T(8,128)(2,1)} broadcast(bf16[2,64,1536]{2,1,0:T(8,128)(2,1)} %param.8), dimensions={0,2,3} | broadcast | bytes 3538944 | tf_op jit(solution)/shard_map/broadcast_in_dim | solution.py:28
  9.6 7.1 %all-to-all-start = ((bf16[2,8,64,1536]{3,2,0,1:T(8,128)(2,1)}), bf16[2,8,64,1536]{3,2,0,1:T(8,128)(2,1)}, u32[]{:S(2)}, u32[]{:S(2)}) async-start(bf16[2,8,64,1536]{3,2,0,1:T(8,128)(2,1)} %broadcast_in_dim.4), calls=%async_computation | async-start | bytes 6291456 | tf_op jit(solution)/shard_map/all_to_all | solution.py:29
  17.6 42.2 %all-to-all-done = bf16[2,8,64,1536]{3,2,0,1:T(8,128)(2,1)} async-done(((bf16[2,8,64,1536]{3,2,0,1:T(8,128)(2,1)}), bf16[2,8,64,1536]{3,2,0,1:T(8,128)(2,1)}, u32[]{:S(2)}, u32[]{:S(2)}) %all-to-all-start) | async-done | bytes 3145760 | tf_op jit(solution)/shard_map/all_to_all | solution.py:29
  59.8 2.6 multiply_reduce_fusion
  62.4 2.2 copy.67
  64.7 1.3 collective-permute-start
  66.0 1.3 collective-permute-start.1
  67.3 4.1 %fusion.10 = bf16[2,512,1536]{2,1,0:T(8,128)(2,1)} fusion(f32[1536]{0:T(1024)S(1)} %copy-done.5, f32[2,512]{1,0:T(2,128)S(1)} %rsqrt.37, bf16[2,8,64,1536]{3,2,1,0:T(8,128)(2,1)S(1)} %copy.67), kind=kLoop, calls=%fused_computation.13 | loop fusion | flops 18874368 | bytes 6301696 | tf_op jit(solution)/shard_map/convert_element_type | solution.py:134
  72.3 3.3 %fusion.19 = f32[2,512,192]{1,2,0:T(8,128)S(1)} fusion(bf16[2,2,1536]{2,1,0:T(2,128)(2,1)S(1)} %get-tuple-element.11, bf16[2,512,1536]{2,1,0:T(8,128)(2,1)} %fusion.10, bf16[5,192,1536]{2,1,0:T(8,128)(2,1)} %param.10), kind=kOutput, calls=%fused_computation.26 | convolution fusion | flops 610271232 | bytes 4534272 | tf_op jit(solution)/shard_map/std,ed->set/dot_general | solution.py:140
  76.2 1.2 fusion.21
  77.4 1.2 fusion.37
  78.6 1.2 fusion.16
  79.8 1.2 fusion.42
  81.3 44.9 %all_to_all.15 = bf16[2,8,192,512]{3,2,0,1:T(8,128)(2,1)S(1)} all-to-all(bf16[2,8,192,512]{3,2,0,1:T(8,128)(2,1)S(1)} %broadcast_in_dim.5), channel_id=1, replica_groups=mesh['chip_x'=2,'chip_z'=4,'core'=2,'peer_y'=4,'peer_x'=2] {'peer_y','pe..., dimensions={1} | all-to-all | bytes 6291456 | tf_op jit(solution)/shard_map/all_to_all | solution.py:29
  126.3 1.9 copy.70
  128.2 2.7 %fusion = f32[2,512]{1,0:T(2,128)S(1)} fusion(bf16[2,1536,512]{2,1,0:T(8,128)(2,1)} %bitcast.68), kind=kLoop, calls=%fused_computation.3 | loop fusion | flops 4717568 | bytes 3149824 | tf_op jit(solution)/shard_map/reduce_sum | solution.py:152
  134.2 1.3 collective-permute-start.2
  135.5 4.2 %fusion.34.query_ref = bf16[2,512,192]{2,1,0:T(8,128)(2,1)} fusion(bf16[192,1536]{1,0:T(8,128)(2,1)} %param.12, bf16[2,1536,512]{2,1,0:T(8,128)(2,1)} %bitcast.69, f32[1536]{0:T(1024)S(1)} %copy-done.8, f32[2,512]{1,0:T(2,128)S(1)} %add_rsqrt_fusion), kind=kOutput, calls=%fused_computation.37 | convolution fusion | flops 610664448 | bytes 4139008 | tf_op jit(solution)/shard_map/sdt,ed->ste/dot_general | solution.py:155
  139.6 66.7 %all-gather.6.cloned.1.call-done = bf16[2,32,192,512]{3,2,1,0:T(8,128)(2,1)} async-done(((bf16[2,2,192,512]{3,2,1,0:T(8,128)(2,1)}), bf16[2,32,192,512]{3,2,1,0:T(8,128)(2,1)}) %all-gather.6.cloned.1.call-update) | async-done | bytes 12582928 | tf_op jit(solution)/shard_map/all_gather | solution.py:165
  206.3 23.3 %shard_map.82 = bf16[8,2,64,192]{3,2,1,0:T(8,128)(2,1)} custom-call(bf16[2,512,192]{2,1,0:T(8,128)(2,1)} %fusion.34.query_ref, bf16[2,16,2,192,512]{4,3,2,1,0:T(8,128)(2,1)} %bitcast.66, bf16[2,16,2,192,512]{4,3,2,1,0:T(8,128)(2,1)} %bitcast.67), custom_call_target="tpu_custom_call" | custom-call | tf_op jit(solution)/shard_map/pallas_call | solution.py:77
  229.6 6.7 %all-to-all-start.2 = ((bf16[8,2,64,192]{3,2,1,0:T(8,128)(2,1)}), bf16[8,2,64,192]{3,2,1,0:T(8,128)(2,1)S(1)}, u32[]{:S(2)}, u32[]{:S(2)}) async-start(bf16[8,2,64,192]{3,2,1,0:T(8,128)(2,1)} %shard_map.82), calls=%async_computation.2 | async-start | bytes 1048576 | tf_op jit(solution)/shard_map/all_to_all | solution.py:173
  236.3 4.6 %copy.71 = bf16[2,1536,512]{1,2,0:T(8,128)(2,1)} copy(bf16[2,1536,512]{2,1,0:T(8,128)(2,1)} %bitcast.70) | data formatting | bytes 6291456 | tf_op jit(solution)/shard_map/optimization_barrier | solution.py:150
  240.9 7.4 %all-to-all-done.2 = bf16[8,2,64,192]{3,2,1,0:T(8,128)(2,1)S(1)} async-done(((bf16[8,2,64,192]{3,2,1,0:T(8,128)(2,1)}), bf16[8,2,64,192]{3,2,1,0:T(8,128)(2,1)S(1)}, u32[]{:S(2)}, u32[]{:S(2)}) %all-to-all-start.2) | async-done | bytes 393248 | tf_op jit(solution)/shard_map/all_to_all | solution.py:173
  248.3 4.8 %fusion.31 = bf16[2,64,1536]{2,1,0:T(8,128)(2,1)} fusion(bf16[8,2,64,192]{3,2,1,0:T(8,128)(2,1)S(1)} %all-to-all-done.2, bf16[8,192,768]{2,1,0:T(8,128)(2,1)} %bitcast.23, bf16[8,192,768]{2,1,0:T(8,128)(2,1)S(1)} %bitcast.75, pred[]{:T(512)S(6)} %eq.3, bf16[2,1536,512]{1,2,0:T(8,128)(2,1)} %copy.71, s32[]{:T(128)S(6)} %select_n.20), kind=kOutput, calls=%fused_computation.35 | convolution fusion | flops 625803264 | bytes 5898245 | tf_op jit(solution)/shard_map/hstd,hdf->stf/dot_general | solution.py:180
  (42 shorter events, 5.9 us)
Async XLA Ops:
  6.5 124.4 %copy-start = (bf16[192,1536]{1,0:T(8,128)(2,1)S(1)}, bf16[192,1536]{1,0:T(8,128)(2,1)}, u32[]{:S(2)}) copy-start(bf16[192,1536]{1,0:T(8,128)(2,1)} %param.14) | copy-start | bytes 1769476
  9.6 7.2 %copy-start.3 = (bf16[192,1536]{1,0:T(8,128)(2,1)S(1)}, bf16[192,1536]{1,0:T(8,128)(2,1)}, u32[]{:S(2)}) copy-start(bf16[192,1536]{1,0:T(8,128)(2,1)} %param.15) | copy-start | bytes 1769476
  9.6 50.2 %all-to-all-start = ((bf16[2,8,64,1536]{3,2,0,1:T(8,128)(2,1)}), bf16[2,8,64,1536]{3,2,0,1:T(8,128)(2,1)}, u32[]{:S(2)}, u32[]{:S(2)}) async-start(bf16[2,8,64,1536]{3,2,0,1:T(8,128)(2,1)} %broadcast_in_dim.4), calls=%async_computation | async-start | bytes 6291456 | tf_op jit(solution)/shard_map/all_to_all | solution.py:29
  16.7 111.5 %all-gather.4.cloned.1.call-start = ((), (), s32[]{:S(2)}) async-start(), calls=%async_computation.3 | async-start | bytes 2654208 | tf_op jit(solution)/shard_map/all_gather | solution.py:125
  17.5 188.8 %all-gather.6.cloned.1.call-start = ((), (), s32[]{:S(2)}) async-start(), calls=%async_computation.4 | async-start | bytes 13369344 | tf_op jit(solution)/shard_map/all_gather | solution.py:165
  62.4 4.8 %copy-start.5 = (f32[1536]{0:T(1024)S(1)}, f32[1536]{0:T(1024)}, u32[]{:S(2)}) copy-start(f32[1536]{0:T(1024)} %param.9) | copy-start | bytes 18436
  64.7 7.2 %collective-permute-start = (bf16[2,2,1536]{2,1,0:T(2,128)(2,1)S(1)}, bf16[2,2,1536]{2,1,0:T(2,128)(2,1)S(1)}, u32[]{:S(2)}, u32[]{:S(2)}) collective-permute-start(bf16[2,2,1536]{2,1,0:T(2,128)(2,1)S(1)} %get-tuple-element.9), channel_id=1, source_target_pairs={{0,8},{8,16},{16,24},{24,32},{32,40},{40,48},{48,56},{56,64},{64,7... | collective-permute-start | bytes 36872 | tf_op jit(solution)/shard_map/ppermute | solution.py:20
  66.0 6.0 %collective-permute-start.1 = (bf16[2,2,1536]{2,1,0:T(2,128)(2,1)S(1)}, bf16[2,2,1536]{2,1,0:T(2,128)(2,1)S(1)}, u32[]{:S(2)}, u32[]{:S(2)}) collective-permute-start(bf16[2,2,1536]{2,1,0:T(2,128)(2,1)S(1)} %get-tuple-element.10), channel_id=1, source_target_pairs={{8,0},{16,8},{24,16},{32,24},{40,32},{48,40},{56,48},{64,56},{72,6... | collective-permute-start | bytes 36872 | tf_op jit(solution)/shard_map/ppermute | solution.py:21
  72.2 3.4 %copy-start.2 = (bf16[2,512,1536]{2,1,0:T(8,128)(2,1)S(1)}, bf16[2,512,1536]{2,1,0:T(8,128)(2,1)}, u32[]{:S(2)}) copy-start(bf16[2,512,1536]{2,1,0:T(8,128)(2,1)} %fusion.10) | copy-start | bytes 9437188
  72.3 3.9 %copy-start.4 = (bf16[5,192,1536]{2,1,0:T(8,128)(2,1)S(1)}, bf16[5,192,1536]{2,1,0:T(8,128)(2,1)}, u32[]{:S(2)}) copy-start(bf16[5,192,1536]{2,1,0:T(8,128)(2,1)} %param.10) | copy-start | bytes 8847364
  128.2 2.7 %copy-start.8 = (f32[1536]{0:T(1024)S(1)}, f32[1536]{0:T(1024)}, u32[]{:S(2)}) copy-start(f32[1536]{0:T(1024)} %param.11) | copy-start | bytes 18436
  128.2 2.8 %copy-start.1 = (bf16[2,8,192,512]{3,2,1,0:T(8,128)(2,1)S(1)}, bf16[2,8,192,512]{3,2,1,0:T(8,128)(2,1)}, u32[]{:S(2)}) copy-start(bf16[2,8,192,512]{3,2,1,0:T(8,128)(2,1)} %copy.70) | copy-start | bytes 9437188
  131.0 1.1 copy-start.7
  132.1 2.1 copy-start.6
  134.2 106.8 %collective-permute-start.2 = (bf16[1536,768]{1,0:T(8,128)(2,1)S(1)}, bf16[1536,768]{1,0:T(8,128)(2,1)}, u32[]{:S(2)}, u32[]{:S(2)}) collective-permute-start(bf16[1536,768]{1,0:T(8,128)(2,1)S(1)} %copy-done.6), channel_id=1, source_target_pairs={{0,8},{8,0},{1,9},{9,1},{2,10},{10,2},{3,11},{11,3},{4,12},{12,4},... | collective-permute-start | bytes 7077896 | tf_op jit(solution)/shard_map/ppermute | solution.py:174
  229.6 18.7 %all-to-all-start.2 = ((bf16[8,2,64,192]{3,2,1,0:T(8,128)(2,1)}), bf16[8,2,64,192]{3,2,1,0:T(8,128)(2,1)S(1)}, u32[]{:S(2)}, u32[]{:S(2)}) async-start(bf16[8,2,64,192]{3,2,1,0:T(8,128)(2,1)} %shard_map.82), calls=%async_computation.2 | async-start | bytes 1048576 | tf_op jit(solution)/shard_map/all_to_all | solution.py:173
Sparse Core Ops, SparseCore 0:
  19.9 84.1 all-gather.3
  134.3 72.0 all-gather.5

commit v25 on v20

--- a/solution.py
+++ b/solution.py
@@ -77,7 +77,7 @@
         out_ref[:, 0] = finished.reshape(out_ref.shape[0], out_ref.shape[2], out_ref.shape[3])
 
 
-def flash_attention(queries, kv_tile, peers, sources_per_step=16):
+def flash_attention(queries, kv_tile, peers, sources_per_step=4):
     sample_count, query_count, head_width = queries.shape
     _, source_count, _, _, source_rows = kv_tile.shape
     sources_per_step = math.gcd(source_count, sources_per_step)

time: 260 us -> 261 us (level)
  no operation moved by 1% of the time
where the time goes in v25:
time: 261 us; the launch traced here: 260 us
  waiting for transfers between devices  118 us (45%)
  blocking collectives  43.6 us (17%)
  Pallas kernels  24.1 us (9%)
  starting transfers between devices  18.1 us (7%)
  local copies, waits for them, and re-layouts  15.2 us (6%)
  matrix products  14.9 us (6%)
  between operations  13.6 us (5%)
  other arithmetic  12.5 us (5%)
    all_gather x1, waiting for transfers between devices, shards(): kv_tile = lax.all_gather(kv_rows, SEQ, axis=1)  66 us
    all_to_all x1, blocking collectives, gather_batch(): arrived = lax.all_to_all(copies, BATCH, axis, axis, tiled=False)  43.6 us
    all_to_all x1, waiting for transfers between devices, gather_batch(): arrived = lax.all_to_all(copies, BATCH, axis, axis, tiled=False)  42.2 us
    pallas_call x1, Pallas kernels, flash_attention(): pl.pallas_call(flash_step, grid=(sample_count, source_count // sources_pe...  24.1 us
    all_to_all x1, waiting for transfers between devices, shards(): arrived = lax.all_to_all(attended, BATCH, 0, 0, tiled=False)  7.36 us
    all_to_all x1, starting transfers between devices, gather_batch(): arrived = lax.all_to_all(copies, BATCH, axis, axis, tiled=False)  7.15 us
    all_to_all x1, starting transfers between devices, shards(): arrived = lax.all_to_all(attended, BATCH, 0, 0, tiled=False)  6.71 us
    dot_general x5, matrix products, shards(): jnp.einsum('std,ed->set', framed[:, offset:offset + seq_rows], conv_weigh...  5.97 us
  transfers between devices with their start and end apart: 7, of which 4 were waited for; matrix products, arithmetic and copies ran while one was open for 11% of the time, Pallas kernels for 9%

profile of v25, /device:TPU:0, one launch (start us, length us, event | category | flops | bytes accessed | tf_op | source)
XLA Modules:
  0.0 260.3 jit_solution(13880777229701861468)
XLA Ops:
  6.5 3.0 %broadcast_in_dim.4 = bf16[2,8,64,1536]{3,2,0,1:T(8,128)(2,1)} broadcast(bf16[2,64,1536]{2,1,0:T(8,128)(2,1)} %param.8), dimensions={0,2,3} | broadcast | bytes 3538944 | tf_op jit(solution)/shard_map/broadcast_in_dim | solution.py:35
  9.6 7.1 %all-to-all-start = ((bf16[2,8,64,1536]{3,2,0,1:T(8,128)(2,1)}), bf16[2,8,64,1536]{3,2,0,1:T(8,128)(2,1)}, u32[]{:S(2)}, u32[]{:S(2)}) async-start(bf16[2,8,64,1536]{3,2,0,1:T(8,128)(2,1)} %broadcast_in_dim.4), calls=%async_computation | async-start | bytes 6291456 | tf_op jit(solution)/shard_map/all_to_all | solution.py:36
  17.6 42.2 %all-to-all-done = bf16[2,8,64,1536]{3,2,0,1:T(8,128)(2,1)} async-done(((bf16[2,8,64,1536]{3,2,0,1:T(8,128)(2,1)}), bf16[2,8,64,1536]{3,2,0,1:T(8,128)(2,1)}, u32[]{:S(2)}, u32[]{:S(2)}) %all-to-all-start) | async-done | bytes 3145760 | tf_op jit(solution)/shard_map/all_to_all | solution.py:36
  59.8 2.6 multiply_reduce_fusion
  62.5 2.2 copy.72
  64.6 1.6 copy-done.2
  66.7 4.4 %fusion.10 = bf16[2,512,1536]{2,1,0:T(8,128)(2,1)S(1)} fusion(f32[1536]{0:T(1024)S(1)} %copy-done.5, f32[2,512]{1,0:T(2,128)S(1)} %rsqrt.20, bf16[2,8,64,1536]{3,2,1,0:T(8,128)(2,1)} %copy-done.2), kind=kLoop, calls=%fused_computation.13 | loop fusion | flops 18874368 | bytes 6301696 | tf_op jit(solution)/shard_map/convert_element_type | solution.py:141
  71.1 1.3 collective-permute-start
  72.4 1.3 collective-permute-start.1
  74.9 2.7 %collective-permute-done.1 = bf16[2,2,1536]{2,1,0:T(2,128)(2,1)S(1)} collective-permute-done((bf16[2,2,1536]{2,1,0:T(2,128)(2,1)S(1)}, bf16[2,2,1536]{2,1,0:T(2,128)(2,1)S(1)}, u32[]{:S(2)}, u32[]{:S(2)}) %collective-permute-start.1) | collective-permute-done | bytes 12320 | tf_op jit(solution)/shard_map/ppermute | solution.py:25
  77.7 1.2 fusion.17
  81.2 1.3 fusion.42
  82.8 43.6 %all_to_all.15 = bf16[2,8,192,512]{3,2,0,1:T(8,128)(2,1)S(1)} all-to-all(bf16[2,8,192,512]{3,2,0,1:T(8,128)(2,1)S(1)} %broadcast_in_dim.5), channel_id=1, replica_groups=mesh['chip_x'=2,'chip_z'=4,'core'=2,'peer_y'=4,'peer_x'=2] {'peer_y','pe..., dimensions={1} | all-to-all | bytes 6291456 | tf_op jit(solution)/shard_map/all_to_all | solution.py:36
  126.4 1.9 copy.75
  128.4 2.7 %fusion = f32[2,512]{1,0:T(2,128)S(1)} fusion(bf16[2,1536,512]{2,1,0:T(8,128)(2,1)} %bitcast.66), kind=kLoop, calls=%fused_computation.3 | loop fusion | flops 4717568 | bytes 3149824 | tf_op jit(solution)/shard_map/reduce_sum | solution.py:158
  134.4 1.6 collective-permute-start.2
  136.0 4.1 %fusion.21.query_ref = bf16[2,512,192]{2,1,0:T(8,128)(2,1)} fusion(bf16[192,1536]{1,0:T(8,128)(2,1)S(1)} %copy-done.8, bf16[2,1536,512]{2,1,0:T(8,128)(2,1)} %bitcast.67, f32[1536]{0:T(1024)S(1)} %copy-done.9, f32[2,512]{1,0:T(2,128)S(1)} %add_rsqrt_fusion), kind=kOutput, calls=%fused_computation.30 | convolution fusion | flops 610664448 | bytes 4139008 | tf_op jit(solution)/shard_map/sdt,ed->ste/dot_general | solution.py:161
  140.0 66.0 %all-gather.6.cloned.1.call-done = bf16[2,32,192,512]{3,2,1,0:T(8,128)(2,1)} async-done(((bf16[2,2,192,512]{3,2,1,0:T(8,128)(2,1)}), bf16[2,32,192,512]{3,2,1,0:T(8,128)(2,1)}) %all-gather.6.cloned.1.call-update) | async-done | bytes 12582928 | tf_op jit(solution)/shard_map/all_gather | solution.py:171
  206.0 24.1 %shard_map.82 = bf16[8,2,64,192]{3,2,1,0:T(8,128)(2,1)} custom-call(bf16[2,512,192]{2,1,0:T(8,128)(2,1)} %fusion.21.query_ref, bf16[2,16,2,192,512]{4,3,2,1,0:T(8,128)(2,1)} %bitcast.64, bf16[2,16,2,192,512]{4,3,2,1,0:T(8,128)(2,1)} %bitcast.65), custom_call_target="tpu_custom_call" | custom-call | tf_op jit(solution)/shard_map/pallas_call | solution.py:84
  230.2 6.7 %all-to-all-start.2 = ((bf16[8,2,64,192]{3,2,1,0:T(8,128)(2,1)}), bf16[8,2,64,192]{3,2,1,0:T(8,128)(2,1)S(1)}, u32[]{:S(2)}, u32[]{:S(2)}) async-start(bf16[8,2,64,192]{3,2,1,0:T(8,128)(2,1)} %shard_map.82), calls=%async_computation.2 | async-start | bytes 1048576 | tf_op jit(solution)/shard_map/all_to_all | solution.py:179
  236.9 4.6 %copy.76 = bf16[2,1536,512]{1,2,0:T(8,128)(2,1)} copy(bf16[2,1536,512]{2,1,0:T(8,128)(2,1)} %bitcast.68) | data formatting | bytes 6291456 | tf_op jit(solution)/shard_map/optimization_barrier | solution.py:156
  241.5 7.4 %all-to-all-done.2 = bf16[8,2,64,192]{3,2,1,0:T(8,128)(2,1)S(1)} async-done(((bf16[8,2,64,192]{3,2,1,0:T(8,128)(2,1)}), bf16[8,2,64,192]{3,2,1,0:T(8,128)(2,1)S(1)}, u32[]{:S(2)}, u32[]{:S(2)}) %all-to-all-start.2) | async-done | bytes 393248 | tf_op jit(solution)/shard_map/all_to_all | solution.py:179
  249.4 2.2 convolution_bitcast_fusion
  251.6 1.9 fusion.46
  (41 shorter events, 9.0 us)
Async XLA Ops:
  6.5 124.6 %copy-start = (bf16[192,1536]{1,0:T(8,128)(2,1)S(1)}, bf16[192,1536]{1,0:T(8,128)(2,1)}, u32[]{:S(2)}) copy-start(bf16[192,1536]{1,0:T(8,128)(2,1)} %param.14) | copy-start | bytes 1769476
  9.6 7.2 %copy-start.4 = (bf16[192,1536]{1,0:T(8,128)(2,1)S(1)}, bf16[192,1536]{1,0:T(8,128)(2,1)}, u32[]{:S(2)}) copy-start(bf16[192,1536]{1,0:T(8,128)(2,1)} %param.15) | copy-start | bytes 1769476
  9.6 50.2 %all-to-all-start = ((bf16[2,8,64,1536]{3,2,0,1:T(8,128)(2,1)}), bf16[2,8,64,1536]{3,2,0,1:T(8,128)(2,1)}, u32[]{:S(2)}, u32[]{:S(2)}) async-start(bf16[2,8,64,1536]{3,2,0,1:T(8,128)(2,1)} %broadcast_in_dim.4), calls=%async_computation | async-start | bytes 6291456 | tf_op jit(solution)/shard_map/all_to_all | solution.py:36
  16.7 111.7 %all-gather.4.cloned.1.call-start = ((), (), s32[]{:S(2)}) async-start(), calls=%async_computation.3 | async-start | bytes 2654208 | tf_op jit(solution)/shard_map/all_gather | solution.py:132
  17.6 188.5 %all-gather.6.cloned.1.call-start = ((), (), s32[]{:S(2)}) async-start(), calls=%async_computation.4 | async-start | bytes 13369344 | tf_op jit(solution)/shard_map/all_gather | solution.py:171
  62.5 4.3 %copy-start.5 = (f32[1536]{0:T(1024)S(1)}, f32[1536]{0:T(1024)}, u32[]{:S(2)}) copy-start(f32[1536]{0:T(1024)} %param.9) | copy-start | bytes 18436
  64.6 1.6 copy-start.2
  66.7 7.0 %copy-start.6 = (bf16[5,192,1536]{2,1,0:T(8,128)(2,1)S(1)}, bf16[5,192,1536]{2,1,0:T(8,128)(2,1)}, u32[]{:S(2)}) copy-start(bf16[5,192,1536]{2,1,0:T(8,128)(2,1)} %param.10) | copy-start | bytes 8847364
  71.1 7.7 %collective-permute-start = (bf16[2,2,1536]{2,1,0:T(2,128)(2,1)S(1)}, bf16[2,2,1536]{2,1,0:T(2,128)(2,1)S(1)}, u32[]{:S(2)}, u32[]{:S(2)}) collective-permute-start(bf16[2,2,1536]{2,1,0:T(2,128)(2,1)S(1)} %get-tuple-element.9), channel_id=1, source_target_pairs={{0,8},{8,16},{16,24},{24,32},{32,40},{40,48},{48,56},{56,64},{64,7... | collective-permute-start | bytes 36872 | tf_op jit(solution)/shard_map/ppermute | solution.py:23
  72.4 5.2 %collective-permute-start.1 = (bf16[2,2,1536]{2,1,0:T(2,128)(2,1)S(1)}, bf16[2,2,1536]{2,1,0:T(2,128)(2,1)S(1)}, u32[]{:S(2)}, u32[]{:S(2)}) collective-permute-start(bf16[2,2,1536]{2,1,0:T(2,128)(2,1)S(1)} %get-tuple-element.10), channel_id=1, source_target_pairs={{8,0},{16,8},{24,16},{32,24},{40,32},{48,40},{56,48},{64,56},{72,6... | collective-permute-start | bytes 36872 | tf_op jit(solution)/shard_map/ppermute | solution.py:25
  128.4 2.7 %copy-start.9 = (f32[1536]{0:T(1024)S(1)}, f32[1536]{0:T(1024)}, u32[]{:S(2)}) copy-start(f32[1536]{0:T(1024)} %param.11) | copy-start | bytes 18436
  128.4 2.8 %copy-start.1 = (bf16[2,8,192,512]{3,2,1,0:T(8,128)(2,1)S(1)}, bf16[2,8,192,512]{3,2,1,0:T(8,128)(2,1)}, u32[]{:S(2)}) copy-start(bf16[2,8,192,512]{3,2,1,0:T(8,128)(2,1)} %copy.75) | copy-start | bytes 9437188
  131.2 1.1 copy-start.7
  132.3 2.1 copy-start.3
  132.3 3.7 %copy-start.8 = (bf16[192,1536]{1,0:T(8,128)(2,1)S(1)}, bf16[192,1536]{1,0:T(8,128)(2,1)}, u32[]{:S(2)}) copy-start(bf16[192,1536]{1,0:T(8,128)(2,1)} %param.12) | copy-start | bytes 1769476
  134.4 115.0 %collective-permute-start.2 = (bf16[1536,768]{1,0:T(8,128)(2,1)S(1)}, bf16[1536,768]{1,0:T(8,128)(2,1)}, u32[]{:S(2)}, u32[]{:S(2)}) collective-permute-start(bf16[1536,768]{1,0:T(8,128)(2,1)S(1)} %copy-done.3), channel_id=1, source_target_pairs={{0,8},{8,0},{1,9},{9,1},{2,10},{10,2},{3,11},{11,3},{4,12},{12,4},... | collective-permute-start | bytes 7077896 | tf_op jit(solution)/shard_map/ppermute | solution.py:180
  230.2 18.7 %all-to-all-start.2 = ((bf16[8,2,64,192]{3,2,1,0:T(8,128)(2,1)}), bf16[8,2,64,192]{3,2,1,0:T(8,128)(2,1)S(1)}, u32[]{:S(2)}, u32[]{:S(2)}) async-start(bf16[8,2,64,192]{3,2,1,0:T(8,128)(2,1)} %shard_map.82), calls=%async_computation.2 | async-start | bytes 1048576 | tf_op jit(solution)/shard_map/all_to_all | solution.py:179
Sparse Core Ops, SparseCore 0:
  19.9 79.5 all-gather.3
  134.5 71.4 all-gather.5

commit v26 on v17

--- a/solution.py
+++ b/solution.py
@@ -161,13 +161,12 @@
         jnp.einsum("sdt,ed->ste", normed, query_weight, preferred_element_type=jnp.float32)
         * HD ** (-0.5)
     ).astype(jnp.bfloat16)
-    key_rows = jnp.einsum(
-        "sdt,ed->set", normed, key_weight, preferred_element_type=jnp.float32
+    kv_rows = jnp.einsum(
+        "sdt,ked->kset",
+        normed,
+        jnp.stack([key_weight, value_weight]),
+        preferred_element_type=jnp.float32,
     ).astype(jnp.bfloat16)
-    value_rows = jnp.einsum(
-        "sdt,ed->set", normed, value_weight, preferred_element_type=jnp.float32
-    ).astype(jnp.bfloat16)
-    kv_rows = jnp.stack([key_rows, value_rows])
     kv_tile = lax.all_gather(kv_rows, SEQ, axis=1)
     batch_count = lax.axis_size(BATCH)
     attended = flash_attention(queries, kv_tile, batch_count)

time: 260 us -> 261 us (level)
  no operation moved by 1% of the time
where the time goes in v26:
time: 261 us; the launch traced here: 260 us
  waiting for transfers between devices  118 us (45%)
  blocking collectives  45 us (17%)
  Pallas kernels  23.2 us (9%)
  starting transfers between devices  17.4 us (7%)
  matrix products  16.4 us (6%)
  local copies, waits for them, and re-layouts  15.2 us (6%)
  between operations  13.6 us (5%)
  other arithmetic  11.5 us (4%)
    all_gather x1, waiting for transfers between devices, shards(): kv_tile = lax.all_gather(kv_rows, SEQ, axis=1)  67 us
    all_to_all x1, blocking collectives, gather_batch(): arrived = lax.all_to_all(copies, BATCH, axis, axis, tiled=False)  45 us
    all_to_all x1, waiting for transfers between devices, gather_batch(): arrived = lax.all_to_all(copies, BATCH, axis, axis, tiled=False)  42.2 us
    pallas_call x1, Pallas kernels, flash_attention(): pl.pallas_call(flash_step, grid=(sample_count, source_count // sources_pe...  23.2 us
    all_to_all x1, waiting for transfers between devices, shards(): arrived = lax.all_to_all(attended, BATCH, 0, 0, tiled=False)  7.35 us
    all_to_all x1, starting transfers between devices, gather_batch(): arrived = lax.all_to_all(copies, BATCH, axis, axis, tiled=False)  7.15 us
    all_to_all x1, starting transfers between devices, shards(): arrived = lax.all_to_all(attended, BATCH, 0, 0, tiled=False)  6.7 us
    dot_general x5, matrix products, shards(): jnp.einsum('std,ed->set', framed[:, offset:offset + seq_rows], conv_weigh...  5.97 us
  transfers between devices with their start and end apart: 7, of which 4 were waited for; matrix products, arithmetic and copies ran while one was open for 11% of the time, Pallas kernels for 9%

profile of v26, /device:TPU:0, one launch (start us, length us, event | category | flops | bytes accessed | tf_op | source)
XLA Modules:
  0.0 260.5 jit_solution(7997532007294166776)
XLA Ops:
  6.5 3.0 %broadcast_in_dim.4 = bf16[2,8,64,1536]{3,2,0,1:T(8,128)(2,1)} broadcast(bf16[2,64,1536]{2,1,0:T(8,128)(2,1)} %param.8), dimensions={0,2,3} | broadcast | bytes 3538944 | tf_op jit(solution)/shard_map/broadcast_in_dim | solution.py:35
  9.6 7.1 %all-to-all-start = ((bf16[2,8,64,1536]{3,2,0,1:T(8,128)(2,1)}), bf16[2,8,64,1536]{3,2,0,1:T(8,128)(2,1)}, u32[]{:S(2)}, u32[]{:S(2)}) async-start(bf16[2,8,64,1536]{3,2,0,1:T(8,128)(2,1)} %broadcast_in_dim.4), calls=%async_computation | async-start | bytes 6291456 | tf_op jit(solution)/shard_map/all_to_all | solution.py:36
  17.6 42.2 %all-to-all-done = bf16[2,8,64,1536]{3,2,0,1:T(8,128)(2,1)} async-done(((bf16[2,8,64,1536]{3,2,0,1:T(8,128)(2,1)}), bf16[2,8,64,1536]{3,2,0,1:T(8,128)(2,1)}, u32[]{:S(2)}, u32[]{:S(2)}) %all-to-all-start) | async-done | bytes 3145760 | tf_op jit(solution)/shard_map/all_to_all | solution.py:36
  59.8 2.2 copy.71
  62.0 1.7 copy-done.2
  64.1 2.6 multiply_reduce_fusion
  66.7 4.4 %fusion.10 = bf16[2,512,1536]{2,1,0:T(8,128)(2,1)S(1)} fusion(f32[1536]{0:T(1024)S(1)} %copy-done.5, f32[2,512]{1,0:T(2,128)S(1)} %rsqrt.20, bf16[2,8,64,1536]{3,2,1,0:T(8,128)(2,1)} %copy-done.2), kind=kLoop, calls=%fused_computation.13 | loop fusion | flops 18874368 | bytes 6301696 | tf_op jit(solution)/shard_map/convert_element_type | solution.py:141
  71.1 1.3 collective-permute-start
  72.4 1.3 collective-permute-start.1
  76.1 1.6 collective-permute-done.1
  77.7 1.2 fusion.17
  80.0 1.3 fusion.48
  81.6 45.0 %all_to_all.15 = bf16[2,8,192,512]{3,2,0,1:T(8,128)(2,1)S(1)} all-to-all(bf16[2,8,192,512]{3,2,0,1:T(8,128)(2,1)S(1)} %broadcast_in_dim.5), channel_id=1, replica_groups=mesh['chip_x'=2,'chip_z'=4,'core'=2,'peer_y'=4,'peer_x'=2] {'peer_y','pe..., dimensions={1} | all-to-all | bytes 6291456 | tf_op jit(solution)/shard_map/all_to_all | solution.py:36
  126.6 1.9 copy.74
  128.6 2.7 %fusion = f32[2,512]{1,0:T(2,128)S(1)} fusion(bf16[2,1536,512]{2,1,0:T(8,128)(2,1)} %bitcast.68), kind=kLoop, calls=%fused_computation.3 | loop fusion | flops 4717568 | bytes 3149824 | tf_op jit(solution)/shard_map/reduce_sum | solution.py:158
  131.4 3.7 %fusion.27 = bf16[2,2,192,512]{3,2,1,0:T(8,128)(2,1)} fusion(bf16[1,192,1536]{2,1,0:T(8,128)(2,1)S(1)} %bitcast.74, bf16[1,192,1536]{2,1,0:T(8,128)(2,1)} %bitcast.75, bf16[2,1536,512]{2,1,0:T(8,128)(2,1)S(1)} %bitcast.71, f32[1536]{0:T(1024)S(1)} %copy-done.8, f32[2,512]{1,0:T(2,128)S(1)} %add_rsqrt_fusion), kind=kOutput, calls=%fused_computation.34 | convolution fusion | flops 1217003520 | bytes 5122048 | tf_op jit(solution)/shard_map/sdt,ked->kset/dot_general | solution.py:164
  136.0 4.0 %fusion.26.query_ref = bf16[2,512,192]{2,1,0:T(8,128)(2,1)} fusion(bf16[2,1536,512]{2,1,0:T(8,128)(2,1)} %bitcast.69, f32[1536]{0:T(1024)S(1)} %copy-done.8, f32[2,512]{1,0:T(2,128)S(1)} %add_rsqrt_fusion, bf16[192,1536]{1,0:T(8,128)(2,1)S(1)} %copy-done), kind=kOutput, calls=%fused_computation.33 | convolution fusion | flops 610664448 | bytes 4139008 | tf_op jit(solution)/shard_map/sdt,ed->ste/dot_general | solution.py:161
  140.1 67.0 %all-gather.6.cloned.1.call-done = bf16[2,32,192,512]{3,2,1,0:T(8,128)(2,1)} async-done(((bf16[2,2,192,512]{3,2,1,0:T(8,128)(2,1)}), bf16[2,32,192,512]{3,2,1,0:T(8,128)(2,1)}) %all-gather.6.cloned.1.call-update) | async-done | bytes 12582928 | tf_op jit(solution)/shard_map/all_gather | solution.py:170
  207.1 23.2 %shard_map.82 = bf16[8,2,64,192]{3,2,1,0:T(8,128)(2,1)} custom-call(bf16[2,512,192]{2,1,0:T(8,128)(2,1)} %fusion.26.query_ref, bf16[2,16,2,192,512]{4,3,2,1,0:T(8,128)(2,1)} %bitcast.66, bf16[2,16,2,192,512]{4,3,2,1,0:T(8,128)(2,1)} %bitcast.67), custom_call_target="tpu_custom_call" | custom-call | tf_op jit(solution)/shard_map/pallas_call | solution.py:84
  230.3 6.7 %all-to-all-start.2 = ((bf16[8,2,64,192]{3,2,1,0:T(8,128)(2,1)}), bf16[8,2,64,192]{3,2,1,0:T(8,128)(2,1)S(1)}, u32[]{:S(2)}, u32[]{:S(2)}) async-start(bf16[8,2,64,192]{3,2,1,0:T(8,128)(2,1)} %shard_map.82), calls=%async_computation.2 | async-start | bytes 1048576 | tf_op jit(solution)/shard_map/all_to_all | solution.py:178
  237.0 4.7 %copy.75 = bf16[2,1536,512]{1,2,0:T(8,128)(2,1)} copy(bf16[2,1536,512]{2,1,0:T(8,128)(2,1)} %bitcast.70) | data formatting | bytes 6291456 | tf_op jit(solution)/shard_map/optimization_barrier | solution.py:156
  241.6 7.4 %all-to-all-done.2 = bf16[8,2,64,192]{3,2,1,0:T(8,128)(2,1)S(1)} async-done(((bf16[8,2,64,192]{3,2,1,0:T(8,128)(2,1)}), bf16[8,2,64,192]{3,2,1,0:T(8,128)(2,1)S(1)}, u32[]{:S(2)}, u32[]{:S(2)}) %all-to-all-start.2) | async-done | bytes 393248 | tf_op jit(solution)/shard_map/all_to_all | solution.py:178
  249.5 2.2 convolution_bitcast_fusion
  251.7 1.9 fusion.56
  (37 shorter events, 6.8 us)
Async XLA Ops:
  6.5 129.5 %copy-start = (bf16[192,1536]{1,0:T(8,128)(2,1)S(1)}, bf16[192,1536]{1,0:T(8,128)(2,1)}, u32[]{:S(2)}) copy-start(bf16[192,1536]{1,0:T(8,128)(2,1)} %param.12) | copy-start | bytes 1769476
  9.6 7.2 %copy-start.4 = (bf16[192,1536]{1,0:T(8,128)(2,1)S(1)}, bf16[192,1536]{1,0:T(8,128)(2,1)}, u32[]{:S(2)}) copy-start(bf16[192,1536]{1,0:T(8,128)(2,1)} %param.15) | copy-start | bytes 1769476
  9.6 50.2 %all-to-all-start = ((bf16[2,8,64,1536]{3,2,0,1:T(8,128)(2,1)}), bf16[2,8,64,1536]{3,2,0,1:T(8,128)(2,1)}, u32[]{:S(2)}, u32[]{:S(2)}) async-start(bf16[2,8,64,1536]{3,2,0,1:T(8,128)(2,1)} %broadcast_in_dim.4), calls=%async_computation | async-start | bytes 6291456 | tf_op jit(solution)/shard_map/all_to_all | solution.py:36
  16.7 111.8 %all-gather.4.cloned.1.call-start = ((), (), s32[]{:S(2)}) async-start(), calls=%async_computation.3 | async-start | bytes 2654208 | tf_op jit(solution)/shard_map/all_gather | solution.py:132
  17.6 189.5 %all-gather.6.cloned.1.call-start = ((), (), s32[]{:S(2)}) async-start(), calls=%async_computation.4 | async-start | bytes 13369344 | tf_op jit(solution)/shard_map/all_gather | solution.py:170
  62.0 1.7 copy-start.2
  62.0 4.8 %copy-start.5 = (f32[1536]{0:T(1024)S(1)}, f32[1536]{0:T(1024)}, u32[]{:S(2)}) copy-start(f32[1536]{0:T(1024)} %param.9) | copy-start | bytes 18436
  66.7 7.0 %copy-start.6 = (bf16[5,192,1536]{2,1,0:T(8,128)(2,1)S(1)}, bf16[5,192,1536]{2,1,0:T(8,128)(2,1)}, u32[]{:S(2)}) copy-start(bf16[5,192,1536]{2,1,0:T(8,128)(2,1)} %param.10) | copy-start | bytes 8847364
  71.1 3.8 %collective-permute-start = (bf16[2,2,1536]{2,1,0:T(2,128)(2,1)S(1)}, bf16[2,2,1536]{2,1,0:T(2,128)(2,1)S(1)}, u32[]{:S(2)}, u32[]{:S(2)}) collective-permute-start(bf16[2,2,1536]{2,1,0:T(2,128)(2,1)S(1)} %get-tuple-element.9), channel_id=1, source_target_pairs={{0,8},{8,16},{16,24},{24,32},{32,40},{40,48},{48,56},{56,64},{64,7... | collective-permute-start | bytes 36872 | tf_op jit(solution)/shard_map/ppermute | solution.py:23
  72.4 5.2 %collective-permute-start.1 = (bf16[2,2,1536]{2,1,0:T(2,128)(2,1)S(1)}, bf16[2,2,1536]{2,1,0:T(2,128)(2,1)S(1)}, u32[]{:S(2)}, u32[]{:S(2)}) collective-permute-start(bf16[2,2,1536]{2,1,0:T(2,128)(2,1)S(1)} %get-tuple-element.10), channel_id=1, source_target_pairs={{8,0},{16,8},{24,16},{32,24},{40,32},{48,40},{56,48},{64,56},{72,6... | collective-permute-start | bytes 36872 | tf_op jit(solution)/shard_map/ppermute | solution.py:25
  126.6 4.7 %copy-start.7 = (bf16[192,1536]{1,0:T(8,128)(2,1)S(1)}, bf16[192,1536]{1,0:T(8,128)(2,1)}, u32[]{:S(2)}) copy-start(bf16[192,1536]{1,0:T(8,128)(2,1)} %param.14) | copy-start | bytes 1769476
  128.5 2.7 %copy-start.8 = (f32[1536]{0:T(1024)S(1)}, f32[1536]{0:T(1024)}, u32[]{:S(2)}) copy-start(f32[1536]{0:T(1024)} %param.11) | copy-start | bytes 18436
  128.6 2.8 %copy-start.1 = (bf16[2,8,192,512]{3,2,1,0:T(8,128)(2,1)S(1)}, bf16[2,8,192,512]{3,2,1,0:T(8,128)(2,1)}, u32[]{:S(2)}) copy-start(bf16[2,8,192,512]{3,2,1,0:T(8,128)(2,1)} %copy.74) | copy-start | bytes 9437188
  131.4 3.7 %copy-start.3 = (bf16[1536,768]{1,0:T(8,128)(2,1)S(1)}, bf16[1536,768]{1,0:T(8,128)(2,1)}, u32[]{:S(2)}) copy-start(bf16[1536,768]{1,0:T(8,128)(2,1)} %all-gather.4.cloned.1.call-done) | copy-start | bytes 7077892
  135.1 114.4 %collective-permute-start.2 = (bf16[1536,768]{1,0:T(8,128)(2,1)S(1)}, bf16[1536,768]{1,0:T(8,128)(2,1)}, u32[]{:S(2)}, u32[]{:S(2)}) collective-permute-start(bf16[1536,768]{1,0:T(8,128)(2,1)S(1)} %copy-done.3), channel_id=1, source_target_pairs={{0,8},{8,0},{1,9},{9,1},{2,10},{10,2},{3,11},{11,3},{4,12},{12,4},... | collective-permute-start | bytes 7077896 | tf_op jit(solution)/shard_map/ppermute | solution.py:179
  230.3 18.7 %all-to-all-start.2 = ((bf16[8,2,64,192]{3,2,1,0:T(8,128)(2,1)}), bf16[8,2,64,192]{3,2,1,0:T(8,128)(2,1)S(1)}, u32[]{:S(2)}, u32[]{:S(2)}) async-start(bf16[8,2,64,192]{3,2,1,0:T(8,128)(2,1)} %shard_map.82), calls=%async_computation.2 | async-start | bytes 1048576 | tf_op jit(solution)/shard_map/all_to_all | solution.py:178
Sparse Core Ops, SparseCore 0:
  19.9 84.7 all-gather.3
  135.2 71.8 all-gather.5

commit v27 on v24

--- a/solution.py
+++ b/solution.py
@@ -155,13 +155,12 @@
         jnp.einsum("sdt,ed->ste", normed, query_weight, preferred_element_type=jnp.float32)
         * HD ** (-0.5)
     ).astype(jnp.bfloat16)
-    key_rows = jnp.einsum(
-        "sdt,ed->set", normed, key_weight, preferred_element_type=jnp.float32
+    kv_rows = jnp.einsum(
+        "sdt,ked->kset",
+        normed,
+        jnp.stack([key_weight, value_weight]),
+        preferred_element_type=jnp.float32,
     ).astype(jnp.bfloat16)
-    value_rows = jnp.einsum(
-        "sdt,ed->set", normed, value_weight, preferred_element_type=jnp.float32
-    ).astype(jnp.bfloat16)
-    kv_rows = jnp.stack([key_rows, value_rows])
     kv_tile = lax.all_gather(kv_rows, SEQ, axis=1)
     batch_count = lax.axis_size(BATCH)
     attended = flash_attention(queries, kv_tile, batch_count)

time: 260 us -> 261 us (level)
  no operation moved by 1% of the time
where the time goes in v27:
time: 261 us
  waiting for transfers between devices  116 us (44%)
  blocking collectives  44.9 us (17%)
  Pallas kernels  23.2 us (9%)
  matrix products  20.8 us (8%)
  starting transfers between devices  17.8 us (7%)
  local copies, waits for them, and re-layouts  14 us (5%)
  between operations  13.6 us (5%)
  other arithmetic  9.82 us (4%)
    all_gather x1, waiting for transfers between devices, shards(): kv_tile = lax.all_gather(kv_rows, SEQ, axis=1)  66.9 us
    all_to_all x1, blocking collectives, gather_batch(): arrived = lax.all_to_all(copies, BATCH, axis, axis, tiled=False)  44.9 us
    all_to_all x1, waiting for transfers between devices, gather_batch(): arrived = lax.all_to_all(copies, BATCH, axis, axis, tiled=False)  42.2 us
    pallas_call x1, Pallas kernels, flash_attention(): pl.pallas_call(flash_step, grid=(sample_count, source_count // sources_pe...  23.2 us
    dot_general x5, matrix products, shards(): jnp.einsum('std,ed->set', framed[:, offset:offset + seq_rows], conv_weigh...  8.15 us
    all_to_all x1, waiting for transfers between devices, shards(): arrived = lax.all_to_all(attended, BATCH, 0, 0, tiled=False)  7.35 us
    all_to_all x1, starting transfers between devices, gather_batch(): arrived = lax.all_to_all(copies, BATCH, axis, axis, tiled=False)  7.15 us
    all_to_all x1, starting transfers between devices, shards(): arrived = lax.all_to_all(attended, BATCH, 0, 0, tiled=False)  6.71 us
  transfers between devices with their start and end apart: 7, of which 3 were waited for; matrix products, arithmetic and copies ran while one was open for 11% of the time, Pallas kernels for 9%

profile of v27, /device:TPU:0, one launch (start us, length us, event | category | flops | bytes accessed | tf_op | source)
XLA Modules:
  0.0 260.6 jit_solution(3576301211549569841)
XLA Ops:
  6.5 3.0 %broadcast_in_dim.4 = bf16[2,8,64,1536]{3,2,0,1:T(8,128)(2,1)} broadcast(bf16[2,64,1536]{2,1,0:T(8,128)(2,1)} %param.8), dimensions={0,2,3} | broadcast | bytes 3538944 | tf_op jit(solution)/shard_map/broadcast_in_dim | solution.py:28
  9.6 7.1 %all-to-all-start = ((bf16[2,8,64,1536]{3,2,0,1:T(8,128)(2,1)}), bf16[2,8,64,1536]{3,2,0,1:T(8,128)(2,1)}, u32[]{:S(2)}, u32[]{:S(2)}) async-start(bf16[2,8,64,1536]{3,2,0,1:T(8,128)(2,1)} %broadcast_in_dim.4), calls=%async_computation | async-start | bytes 6291456 | tf_op jit(solution)/shard_map/all_to_all | solution.py:29
  17.6 42.2 %all-to-all-done = bf16[2,8,64,1536]{3,2,0,1:T(8,128)(2,1)} async-done(((bf16[2,8,64,1536]{3,2,0,1:T(8,128)(2,1)}), bf16[2,8,64,1536]{3,2,0,1:T(8,128)(2,1)}, u32[]{:S(2)}, u32[]{:S(2)}) %all-to-all-start) | async-done | bytes 3145760 | tf_op jit(solution)/shard_map/all_to_all | solution.py:29
  59.8 2.6 multiply_reduce_fusion
  62.4 2.2 copy.66
  64.7 1.3 collective-permute-start
  66.0 1.3 collective-permute-start.1
  67.3 4.1 %fusion.10 = bf16[2,512,1536]{2,1,0:T(8,128)(2,1)} fusion(f32[1536]{0:T(1024)S(1)} %copy-done.5, f32[2,512]{1,0:T(2,128)S(1)} %rsqrt.37, bf16[2,8,64,1536]{3,2,1,0:T(8,128)(2,1)S(1)} %copy.66), kind=kLoop, calls=%fused_computation.13 | loop fusion | flops 18874368 | bytes 6301696 | tf_op jit(solution)/shard_map/convert_element_type | solution.py:134
  72.3 3.3 %fusion.19 = f32[2,512,192]{1,2,0:T(8,128)S(1)} fusion(bf16[2,2,1536]{2,1,0:T(2,128)(2,1)S(1)} %get-tuple-element.11, bf16[2,512,1536]{2,1,0:T(8,128)(2,1)} %fusion.10, bf16[5,192,1536]{2,1,0:T(8,128)(2,1)} %param.10), kind=kOutput, calls=%fused_computation.26 | convolution fusion | flops 610271232 | bytes 4534272 | tf_op jit(solution)/shard_map/std,ed->set/dot_general | solution.py:140
  76.2 1.2 fusion.21
  77.4 1.2 fusion.45
  79.8 1.2 fusion.48
  81.3 44.9 %all_to_all.15 = bf16[2,8,192,512]{3,2,0,1:T(8,128)(2,1)S(1)} all-to-all(bf16[2,8,192,512]{3,2,0,1:T(8,128)(2,1)S(1)} %broadcast_in_dim.5), channel_id=1, replica_groups=mesh['chip_x'=2,'chip_z'=4,'core'=2,'peer_y'=4,'peer_x'=2] {'peer_y','pe..., dimensions={1} | all-to-all | bytes 6291456 | tf_op jit(solution)/shard_map/all_to_all | solution.py:29
  126.3 1.9 copy.69
  128.2 2.7 %fusion = f32[2,512]{1,0:T(2,128)S(1)} fusion(bf16[2,1536,512]{2,1,0:T(8,128)(2,1)} %bitcast.70), kind=kLoop, calls=%fused_computation.3 | loop fusion | flops 4717568 | bytes 3149824 | tf_op jit(solution)/shard_map/reduce_sum | solution.py:152
  131.0 3.8 %fusion.40 = bf16[2,2,192,512]{3,2,1,0:T(8,128)(2,1)} fusion(bf16[1,192,1536]{2,1,0:T(8,128)(2,1)} %bitcast.77, bf16[1,192,1536]{2,1,0:T(8,128)(2,1)} %bitcast.78, bf16[2,1536,512]{2,1,0:T(8,128)(2,1)S(1)} %bitcast.73, f32[1536]{0:T(1024)S(1)} %copy-done.7, f32[2,512]{1,0:T(2,128)S(1)} %add_rsqrt_fusion), kind=kOutput, calls=%fused_computation.41 | convolution fusion | flops 1217003520 | bytes 5122048 | tf_op jit(solution)/shard_map/sdt,ked->kset/dot_general | solution.py:158
  134.9 1.3 collective-permute-start.2
  136.2 4.0 %fusion.39.query_ref = bf16[2,512,192]{2,1,0:T(8,128)(2,1)} fusion(bf16[2,1536,512]{2,1,0:T(8,128)(2,1)} %bitcast.71, f32[1536]{0:T(1024)S(1)} %copy-done.7, f32[2,512]{1,0:T(2,128)S(1)} %add_rsqrt_fusion, bf16[192,1536]{1,0:T(8,128)(2,1)S(1)} %copy-done), kind=kOutput, calls=%fused_computation.40 | convolution fusion | flops 610664448 | bytes 4139008 | tf_op jit(solution)/shard_map/sdt,ed->ste/dot_general | solution.py:155
  140.2 66.9 %all-gather.6.cloned.1.call-done = bf16[2,32,192,512]{3,2,1,0:T(8,128)(2,1)} async-done(((bf16[2,2,192,512]{3,2,1,0:T(8,128)(2,1)}), bf16[2,32,192,512]{3,2,1,0:T(8,128)(2,1)}) %all-gather.6.cloned.1.call-update) | async-done | bytes 12582928 | tf_op jit(solution)/shard_map/all_gather | solution.py:164
  207.0 23.2 %shard_map.82 = bf16[8,2,64,192]{3,2,1,0:T(8,128)(2,1)} custom-call(bf16[2,512,192]{2,1,0:T(8,128)(2,1)} %fusion.39.query_ref, bf16[2,16,2,192,512]{4,3,2,1,0:T(8,128)(2,1)} %bitcast.68, bf16[2,16,2,192,512]{4,3,2,1,0:T(8,128)(2,1)} %bitcast.69), custom_call_target="tpu_custom_call" | custom-call | tf_op jit(solution)/shard_map/pallas_call | solution.py:77
  230.2 6.7 %all-to-all-start.2 = ((bf16[8,2,64,192]{3,2,1,0:T(8,128)(2,1)}), bf16[8,2,64,192]{3,2,1,0:T(8,128)(2,1)S(1)}, u32[]{:S(2)}, u32[]{:S(2)}) async-start(bf16[8,2,64,192]{3,2,1,0:T(8,128)(2,1)} %shard_map.82), calls=%async_computation.2 | async-start | bytes 1048576 | tf_op jit(solution)/shard_map/all_to_all | solution.py:172
  237.0 4.7 %copy.70 = bf16[2,1536,512]{1,2,0:T(8,128)(2,1)} copy(bf16[2,1536,512]{2,1,0:T(8,128)(2,1)} %bitcast.72) | data formatting | bytes 6291456 | tf_op jit(solution)/shard_map/optimization_barrier | solution.py:150
  241.6 7.4 %all-to-all-done.2 = bf16[8,2,64,192]{3,2,1,0:T(8,128)(2,1)S(1)} async-done(((bf16[8,2,64,192]{3,2,1,0:T(8,128)(2,1)}), bf16[8,2,64,192]{3,2,1,0:T(8,128)(2,1)S(1)}, u32[]{:S(2)}, u32[]{:S(2)}) %all-to-all-start.2) | async-done | bytes 393248 | tf_op jit(solution)/shard_map/all_to_all | solution.py:172
  249.0 4.8 %fusion.33 = bf16[2,64,1536]{2,1,0:T(8,128)(2,1)} fusion(bf16[8,2,64,192]{3,2,1,0:T(8,128)(2,1)S(1)} %all-to-all-done.2, bf16[8,192,768]{2,1,0:T(8,128)(2,1)} %bitcast.23, bf16[8,192,768]{2,1,0:T(8,128)(2,1)S(1)} %bitcast.76, pred[]{:T(512)S(6)} %eq.3, bf16[2,1536,512]{1,2,0:T(8,128)(2,1)} %copy.70, s32[]{:T(128)S(6)} %select_n.20), kind=kOutput, calls=%fused_computation.37 | convolution fusion | flops 625803264 | bytes 5898245 | tf_op jit(solution)/shard_map/hstd,hdf->stf/dot_general | solution.py:179
  (38 shorter events, 4.0 us)
Async XLA Ops:
  6.5 129.6 %copy-start = (bf16[192,1536]{1,0:T(8,128)(2,1)S(1)}, bf16[192,1536]{1,0:T(8,128)(2,1)}, u32[]{:S(2)}) copy-start(bf16[192,1536]{1,0:T(8,128)(2,1)} %param.12) | copy-start | bytes 1769476
  9.6 7.2 %copy-start.3 = (bf16[192,1536]{1,0:T(8,128)(2,1)S(1)}, bf16[192,1536]{1,0:T(8,128)(2,1)}, u32[]{:S(2)}) copy-start(bf16[192,1536]{1,0:T(8,128)(2,1)} %param.15) | copy-start | bytes 1769476
  9.6 50.2 %all-to-all-start = ((bf16[2,8,64,1536]{3,2,0,1:T(8,128)(2,1)}), bf16[2,8,64,1536]{3,2,0,1:T(8,128)(2,1)}, u32[]{:S(2)}, u32[]{:S(2)}) async-start(bf16[2,8,64,1536]{3,2,0,1:T(8,128)(2,1)} %broadcast_in_dim.4), calls=%async_computation | async-start | bytes 6291456 | tf_op jit(solution)/shard_map/all_to_all | solution.py:29
  16.7 111.5 %all-gather.4.cloned.1.call-start = ((), (), s32[]{:S(2)}) async-start(), calls=%async_computation.3 | async-start | bytes 2654208 | tf_op jit(solution)/shard_map/all_gather | solution.py:125
  17.5 189.5 %all-gather.6.cloned.1.call-start = ((), (), s32[]{:S(2)}) async-start(), calls=%async_computation.4 | async-start | bytes 13369344 | tf_op jit(solution)/shard_map/all_gather | solution.py:164
  62.4 4.8 %copy-start.5 = (f32[1536]{0:T(1024)S(1)}, f32[1536]{0:T(1024)}, u32[]{:S(2)}) copy-start(f32[1536]{0:T(1024)} %param.9) | copy-start | bytes 18436
  64.7 7.2 %collective-permute-start = (bf16[2,2,1536]{2,1,0:T(2,128)(2,1)S(1)}, bf16[2,2,1536]{2,1,0:T(2,128)(2,1)S(1)}, u32[]{:S(2)}, u32[]{:S(2)}) collective-permute-start(bf16[2,2,1536]{2,1,0:T(2,128)(2,1)S(1)} %get-tuple-element.9), channel_id=1, source_target_pairs={{0,8},{8,16},{16,24},{24,32},{32,40},{40,48},{48,56},{56,64},{64,7... | collective-permute-start | bytes 36872 | tf_op jit(solution)/shard_map/ppermute | solution.py:20
  66.0 6.0 %collective-permute-start.1 = (bf16[2,2,1536]{2,1,0:T(2,128)(2,1)S(1)}, bf16[2,2,1536]{2,1,0:T(2,128)(2,1)S(1)}, u32[]{:S(2)}, u32[]{:S(2)}) collective-permute-start(bf16[2,2,1536]{2,1,0:T(2,128)(2,1)S(1)} %get-tuple-element.10), channel_id=1, source_target_pairs={{8,0},{16,8},{24,16},{32,24},{40,32},{48,40},{56,48},{64,56},{72,6... | collective-permute-start | bytes 36872 | tf_op jit(solution)/shard_map/ppermute | solution.py:21
  72.2 3.4 %copy-start.2 = (bf16[2,512,1536]{2,1,0:T(8,128)(2,1)S(1)}, bf16[2,512,1536]{2,1,0:T(8,128)(2,1)}, u32[]{:S(2)}) copy-start(bf16[2,512,1536]{2,1,0:T(8,128)(2,1)} %fusion.10) | copy-start | bytes 9437188
  72.3 3.9 %copy-start.4 = (bf16[5,192,1536]{2,1,0:T(8,128)(2,1)S(1)}, bf16[5,192,1536]{2,1,0:T(8,128)(2,1)}, u32[]{:S(2)}) copy-start(bf16[5,192,1536]{2,1,0:T(8,128)(2,1)} %param.10) | copy-start | bytes 8847364
  128.2 2.7 %copy-start.7 = (f32[1536]{0:T(1024)S(1)}, f32[1536]{0:T(1024)}, u32[]{:S(2)}) copy-start(f32[1536]{0:T(1024)} %param.11) | copy-start | bytes 18436
  128.2 2.8 %copy-start.1 = (bf16[2,8,192,512]{3,2,1,0:T(8,128)(2,1)S(1)}, bf16[2,8,192,512]{3,2,1,0:T(8,128)(2,1)}, u32[]{:S(2)}) copy-start(bf16[2,8,192,512]{3,2,1,0:T(8,128)(2,1)} %copy.69) | copy-start | bytes 9437188
  131.0 3.8 %copy-start.6 = (bf16[1536,768]{1,0:T(8,128)(2,1)S(1)}, bf16[1536,768]{1,0:T(8,128)(2,1)}, u32[]{:S(2)}) copy-start(bf16[1536,768]{1,0:T(8,128)(2,1)} %all-gather.4.cloned.1.call-done) | copy-start | bytes 7077892
  134.9 106.7 %collective-permute-start.2 = (bf16[1536,768]{1,0:T(8,128)(2,1)S(1)}, bf16[1536,768]{1,0:T(8,128)(2,1)}, u32[]{:S(2)}, u32[]{:S(2)}) collective-permute-start(bf16[1536,768]{1,0:T(8,128)(2,1)S(1)} %copy-done.6), channel_id=1, source_target_pairs={{0,8},{8,0},{1,9},{9,1},{2,10},{10,2},{3,11},{11,3},{4,12},{12,4},... | collective-permute-start | bytes 7077896 | tf_op jit(solution)/shard_map/ppermute | solution.py:173
  230.2 18.7 %all-to-all-start.2 = ((bf16[8,2,64,192]{3,2,1,0:T(8,128)(2,1)}), bf16[8,2,64,192]{3,2,1,0:T(8,128)(2,1)S(1)}, u32[]{:S(2)}, u32[]{:S(2)}) async-start(bf16[8,2,64,192]{3,2,1,0:T(8,128)(2,1)} %shard_map.82), calls=%async_computation.2 | async-start | bytes 1048576 | tf_op jit(solution)/shard_map/all_to_all | solution.py:172
Sparse Core Ops, SparseCore 0:
  19.9 84.1 all-gather.3
  135.0 71.9 all-gather.5
